TPU v7x, 32 devices: a whole 2x2x4 slice. The times are simulated.
32 devices in a mesh: space: 8 (over z, y), chan: 4 (over x, core).
Axes of the slice: x: 2, y: 2, z: 4, core: 2. Of those that a mesh axis runs over, the one named last changes fastest.
Arguments:
- positions: float32 [3, 2048], P(None, 'space'), may hold values from 0 to 2
- features: bfloat16 [128, 2048], P('chan', 'space'), may hold values from -6 to 6
- send_rows: int32 [24, 128], P('space'), may hold values from 0 to 255, as said below
- pair_tiles: int32 [64, 2], P('space'), may hold values from 0 to 4, as said below
- tile_live: int32 [64], P('space'), may hold values from 0 to 1, as said below
- radial_weight: float32 [128, 8], P('chan'), may hold values from -1 to 1
- mix_weight: bfloat16 [3, 128, 128], replicated, may hold values from -0.5 to 0.5
- out_grad: bfloat16 [128, 9, 2048], P('chan', None, 'space'), may hold values from -6 to 6
Outputs:
- output: bfloat16 [128, 9, 2048], P('chan', None, 'space')
- grad_features: bfloat16 [128, 2048], P('chan', 'space')
- forces: float32 [3, 2048], P(None, 'space')
- grad_radial: float32 [128, 8], P('chan')
Inputs may be any that keep to these rules, and one draw needn't show every extreme that they name: `send_rows`: row s * 3 + b lists 128 distinct atoms of domain s, numbered within the domain, that domain s sends to domain s xor 2^b. `pair_tiles`: row s * 8 + t holds domain s's tile t: a target block below 2 among its own blocks, then a source block below 5 among its source blocks. `tile_live`: on each domain the live tiles come first; each domain has 2 or more live tiles, and some domain has all 8.
All inputs are finite; a program needn't handle non-finite values.
Results may differ from a plain program's by a relative error of at most 0.025.
Values may be sent and summed in bfloat16 or wider, within the bound.
No kernel may reach another device: no remote copies, remote signals or barrier semaphores. Data moves between devices by JAX's collectives and lax.ppermute only.
A program may use at most 64 MiB of HBM per device.

v0:
```python
import math

import jax
import jax.numpy as jnp
from jax import lax
from jax.sharding import PartitionSpec as P

SOFTENING = 0.25
CUTOFF = 2.5
CUTOFF_SQ = 6.25
SHARPNESS = 10.0
ROOT_THREE = math.sqrt(3.0)
ORDER_OF = (0, 1, 1, 1, 2, 2, 2, 2, 2)


def partner(value, axis, bit):
    mask = 2**bit
    pairs = [(source, source ^ mask) for source in range(lax.axis_size(axis))]
    return lax.ppermute(value, axis, pairs)


def geometry(target_pos, source_pos, pair_keep, radial_count):
    offset = source_pos[:, None, :] - target_pos[:, :, None]
    dist_sq = jnp.sum(offset * offset, axis=0) + SOFTENING
    distance = jnp.sqrt(dist_sq)
    along_x = offset[0] / distance
    along_y = offset[1] / distance
    along_z = offset[2] / distance
    harmonics = jnp.stack(
        [
            jnp.ones_like(along_x),
            along_x,
            along_y,
            along_z,
            ROOT_THREE * along_x * along_y,
            ROOT_THREE * along_y * along_z,
            ROOT_THREE * along_x * along_z,
            0.5 * (3.0 * along_z * along_z - 1.0),
            0.5 * ROOT_THREE * (along_x * along_x - along_y * along_y),
        ]
    )
    envelope = jnp.square(jnp.maximum(1.0 - dist_sq / CUTOFF_SQ, 0.0)) * pair_keep
    centers = (jnp.arange(radial_count, dtype=jnp.float32) + 0.5) * (CUTOFF / radial_count)
    radial = (
        jnp.exp(-SHARPNESS * jnp.square(distance[None] - centers[:, None, None])) * envelope[None]
    )
    return (harmonics, radial)


def take_block(array, blk_index, block_size):
    return lax.dynamic_slice_in_dim(array, blk_index * block_size, block_size, array.ndim - 1)


def add_block(array, blk_index, value, block_size):
    current = take_block(array, blk_index, block_size)
    return lax.dynamic_update_slice_in_dim(
        array, current + value, blk_index * block_size, array.ndim - 1
    )


def body(
    positions, features, send_rows, pair_tiles, tile_live, radial_weight, mix_weight, out_grad
):
    block_size = send_rows.shape[1]
    atoms_dev = positions.shape[1]
    chan_dev = features.shape[0]
    radial_count = radial_weight.shape[1]
    components = out_grad.shape[1]
    levels = lax.axis_size("space").bit_length() - 1
    pos_list = [positions]
    feat_list = [features]
    for level_bit in range(levels):
        sent_rows = send_rows[level_bit]
        got_feat, got_pos = (
            partner(
                jnp.take(features, sent_rows, axis=1).astype(jnp.float32), "space", level_bit
            ).astype(jnp.bfloat16),
            partner(jnp.take(positions, sent_rows, axis=1), "space", level_bit),
        )
        feat_list.append(got_feat)
        pos_list.append(got_pos)
    src_pos = jnp.concatenate(pos_list, axis=1)
    src_feat = jnp.concatenate(feat_list, axis=1)
    src_atoms = src_pos.shape[1]
    live_count = jnp.sum(tile_live)

    def tile_parts(tile_index):
        target_blk = pair_tiles[tile_index, 0]
        source_blk = pair_tiles[tile_index, 1]
        same = (target_blk == source_blk).astype(jnp.float32)
        pair_keep = 1.0 - same * jnp.eye(block_size, dtype=jnp.float32)
        target_pos = take_block(src_pos, target_blk, block_size)
        source_pos = take_block(src_pos, source_blk, block_size)

        def geo_fn(first_pos, second_pos):
            return geometry(first_pos, second_pos, pair_keep, radial_count)

        return (target_blk, source_blk, target_pos, source_pos, geo_fn)

    def forward_tile(tile_index, moments):
        target_blk, source_blk, target_pos, source_pos, geo_fn = tile_parts(tile_index)
        harmonics, radial = geo_fn(target_pos, source_pos)
        source_feat = take_block(src_feat, source_blk, block_size)
        pieces_list = []
        for harmonic in range(components):
            pair_values = (harmonics[harmonic][None] * radial).astype(jnp.bfloat16)
            message = jnp.einsum(
                "kij,cj->cki", pair_values, source_feat, preferred_element_type=jnp.float32
            )
            pieces_list.append(jnp.einsum("cki,ck->ci", message, radial_weight))
        contrib = jnp.stack(pieces_list, axis=1)
        return add_block(moments, target_blk, contrib, block_size)

    moments = lax.fori_loop(
        0, live_count, forward_tile, jnp.zeros((chan_dev, components, atoms_dev), jnp.float32)
    )
    packed = moments.astype(jnp.bfloat16)
    mixing = jnp.take(mix_weight, jnp.array(ORDER_OF, dtype=jnp.int32), axis=0)
    offset = lax.axis_index("chan") * chan_dev
    gathered_piece = lax.all_gather(packed, "chan", axis=0, tiled=True)
    weight_part = lax.dynamic_slice(
        mixing, (0, offset, 0), (components, chan_dev, gathered_piece.shape[0])
    )
    mixed_out = jnp.einsum(
        "lxc,cli->xli", weight_part, gathered_piece, preferred_element_type=jnp.float32
    )
    scalar_part = mixed_out[:, 0, :]
    gate_value = jax.nn.sigmoid(scalar_part)
    result = jnp.concatenate(
        [(scalar_part * gate_value)[:, None, :], mixed_out[:, 1:, :] * gate_value[:, None, :]],
        axis=1,
    ).astype(jnp.bfloat16)
    upstream = out_grad.astype(jnp.float32)
    scalar_grad = upstream[:, 0, :] * (
        gate_value * (1.0 + scalar_part * (1.0 - gate_value))
    ) + gate_value * (1.0 - gate_value) * jnp.sum(upstream[:, 1:, :] * mixed_out[:, 1:, :], axis=1)
    rest_grad = upstream[:, 1:, :] * gate_value[:, None, :]
    dz_packed = jnp.concatenate([scalar_grad[:, None, :], rest_grad], axis=1).astype(jnp.bfloat16)
    gathered_piece = lax.all_gather(dz_packed, "chan", axis=0, tiled=True)
    weight_part = lax.dynamic_slice(
        mixing, (0, 0, offset), (components, gathered_piece.shape[0], chan_dev)
    )
    moment_grad_all = jnp.einsum(
        "lxc,xli->cli", weight_part, gathered_piece, preferred_element_type=jnp.float32
    )

    def backward_tile(tile_index, running):
        grad_src, dpos_src, grad_rad = running
        target_blk, source_blk, target_pos, source_pos, geo_fn = tile_parts(tile_index)
        (harmonics, radial), pullback = jax.vjp(geo_fn, target_pos, source_pos)
        source_feat = take_block(src_feat, source_blk, block_size)
        moment_grad = take_block(moment_grad_all, target_blk, block_size)
        grad_source = jnp.zeros((chan_dev, block_size), jnp.float32)
        rad_grad = jnp.zeros_like(radial)
        harm_list = []
        for harmonic in range(components):
            pair_values = (harmonics[harmonic][None] * radial).astype(jnp.bfloat16)
            message = jnp.einsum(
                "kij,cj->cki", pair_values, source_feat, preferred_element_type=jnp.float32
            )
            grad_rad = grad_rad + jnp.einsum("cki,ci->ck", message, moment_grad[:, harmonic, :])
            weighted = (radial_weight[:, :, None] * moment_grad[:, harmonic, None, :]).astype(
                jnp.bfloat16
            )
            grad_source = grad_source + jnp.einsum(
                "cki,kij->cj", weighted, pair_values, preferred_element_type=jnp.float32
            )
            value_grad = jnp.einsum(
                "cki,cj->kij", weighted, source_feat, preferred_element_type=jnp.float32
            )
            harm_list.append(jnp.sum(value_grad * radial, axis=0))
            rad_grad = rad_grad + value_grad * harmonics[harmonic][None]
        target_grad, source_grad_pos = pullback((jnp.stack(harm_list), rad_grad))
        grad_src = add_block(grad_src, source_blk, grad_source, block_size)
        dpos_src = add_block(dpos_src, target_blk, target_grad, block_size)
        dpos_src = add_block(dpos_src, source_blk, source_grad_pos, block_size)
        return (grad_src, dpos_src, grad_rad)

    init = (
        jnp.zeros((chan_dev, src_atoms), jnp.float32),
        jnp.zeros((3, src_atoms), jnp.float32),
        jnp.zeros((chan_dev, radial_count), jnp.float32),
    )
    grad_src, dpos_src, grad_rad = lax.fori_loop(0, live_count, backward_tile, init)
    dpos_src = lax.psum(dpos_src, "chan")
    own_grad = grad_src[:, :atoms_dev]
    own_dpos = dpos_src[:, :atoms_dev]
    for level_bit in range(levels):
        low = atoms_dev + level_bit * block_size
        back_grad, back_pos = partner(
            (grad_src[:, low : low + block_size], dpos_src[:, low : low + block_size]),
            "space",
            level_bit,
        )
        sent_rows = send_rows[level_bit]
        own_grad = own_grad.at[:, sent_rows].add(back_grad)
        own_dpos = own_dpos.at[:, sent_rows].add(back_pos)
    grad_radial = lax.psum(grad_rad, "space")
    return (result, own_grad.astype(jnp.bfloat16), -own_dpos, grad_radial)


def solution(mesh):
    placed = (
        P(None, "space"),
        P("chan", "space"),
        P("space", None),
        P("space", None),
        P("space"),
        P("chan", None),
        P(),
        P("chan", None, "space"),
    )
    return jax.shard_map(
        body,
        mesh=mesh,
        in_specs=placed,
        out_specs=(P("chan", None, "space"), P("chan", "space"), P(None, "space"), P("chan", None)),
        check_vma=False,
    )
```

profile of v0, /device:TPU:0, one launch (start us, length us, event | category | flops | bytes accessed | tf_op | source)
XLA Modules:
  0.0 354.6 jit_solution(2762358216147547025)
XLA Ops:
  0.7 0.9 copy.55
  1.6 0.7 gather_fusion.3
  2.4 4.1 %collective-permute-start.2 = (bf16[32,128]{1,0:T(8,128)(2,1)S(1)}, bf16[32,128]{1,0:T(8,128)(2,1)S(1)}, u32[]{:S(2)}, u32[]{:S(2)}) collective-permute-start(bf16[32,128]{1,0:T(8,128)(2,1)S(1)} %bitcast_convert_fusion), channel_id=1, source_target_pairs={{0,16},{4,20},{8,24},{12,28},{16,0},{20,4},{24,8},{28,12},{1,17},{... | collective-permute-start | bytes 24584 | tf_op jit(solution)/shard_map/ppermute | solution.py:19
  6.5 0.7 gather_fusion.2
  7.3 1.6 collective-permute-start.1
  9.1 0.7 gather_fusion.6
  9.8 0.4 collective-permute-start.5
  10.2 0.6 gather_fusion.5
  11.0 0.7 collective-permute-start.4
  11.6 0.6 gather_fusion.4
  12.4 1.6 collective-permute-start.3
  14.0 0.7 gather_fusion.1
  14.8 0.7 copy-done.11
  15.5 0.6 copy-done.12
  16.1 0.6 reduce_sum.216
  16.7 0.6 gather_fusion
  17.4 0.6 collective-permute-start
  18.2 2.9 collective-permute-done
  21.1 0.6 copy-done.7
  21.8 19.3 %while.28 = (s32[]{:T(128)}, f32[32,9,256]{2,0,1:T(8,128)S(1)}, s32[]{:T(128)}, s32[8,2]{0,1:T(2,128)S(1)}, bf16[32,640]{1,0:T(8,128)(2,1)S(1)}, /*index=5*/f32[...) while((s32[]{:T(128)}, f32[32,9,256]{2,0,1:T(8,128)S(1)}, ...), condition=%wide.region_3.6_spmd, body=%wide.region_1.5_spmd.sunk | while | flops 83677216 | bytes 5811606 | solution.py:114
  22.4 0.7 constant_dynamic-slice_fusion.55
  31.8 0.7 constant_dynamic-slice_fusion.55
  41.1 0.6 copy-done.2
  41.7 7.5 %all_gather.6 = bf16[128,9,256]{2,0,1:T(8,128)(2,1)S(1)} all-gather(bf16[32,9,256]{2,0,1:T(8,128)(2,1)S(1)} %convert_element_type.217), channel_id=1, replica_groups=mesh['space'=8,'chan'=4] {'chan'}, dimensions={0}, use_global_device_ids=true | all-gather | bytes 737280 | tf_op jit(solution)/shard_map/all_gather | solution.py:120
  49.6 7.6 %all_gather.7 = bf16[128,9,256]{2,0,1:T(8,128)(2,1)S(1)} all-gather(bf16[32,9,256]{2,0,1:T(8,128)(2,1)S(1)} %pad_maximum_fusion.1), channel_id=1, replica_groups=mesh['space'=8,'chan'=4] {'chan'}, dimensions={0}, use_global_device_ids=true | all-gather | bytes 737280 | tf_op jit(solution)/shard_map/all_gather | solution.py:139
  57.7 47.3 %while.29 = (s32[]{:T(128)}, f32[32,640]{1,0:T(8,128)S(1)}, f32[3,640]{1,0:T(4,128)S(1)}, f32[32,8]{0,1:T(8,128)S(1)}, s32[]{:T(128)}, /*index=5*/s32[8,2]{0,1:T...) while((s32[]{:T(128)}, f32[32,640]{1,0:T(8,128)S(1)}, ...), condition=%wide.region_19.22_spmd, body=%wide.region_5.21_spmd.sunk | while | flops 250567328 | bytes 19222200 | solution.py:184
  58.5 0.7 constant_dynamic-slice_fusion.58
  65.2 0.4 copy-done.3
  68.5 1.3 fusion.574
  70.3 1.0 fusion.578
  71.6 1.0 fusion.580
  72.9 1.0 fusion.582
  74.1 1.0 fusion.584
  75.4 1.0 fusion.586
  76.7 1.0 fusion.588
  77.9 1.0 fusion.590
  79.2 1.0 fusion.592
  81.7 0.7 constant_dynamic-slice_fusion.58
  88.4 0.4 copy-done.3
  91.7 1.3 fusion.574
  93.5 1.0 fusion.578
  94.8 1.0 fusion.580
  96.1 1.0 fusion.582
  97.4 1.0 fusion.584
  98.6 1.0 fusion.586
  99.9 1.0 fusion.588
  101.2 1.0 fusion.590
  102.4 1.0 fusion.592
  105.1 14.2 %psum.14 = f32[3,640]{0,1:T(8,128)S(1)} all-reduce(f32[3,640]{0,1:T(8,128)S(1)} %copy.73), channel_id=1, replica_groups=mesh['space'=8,'chan'=4] {'chan'}, use_global_device_ids=true, to_apply=%region_23.26 | all-reduce | flops 1920 | bytes 15360 | tf_op jit(solution)/shard_map/psum | solution.py:185
  119.4 195.8 %collective-permute-start.9 = (f32[3,128]{0,1:T(8,128)S(1)}, f32[3,128]{0,1:T(8,128)S(1)}, u32[]{:S(2)}, u32[]{:S(2)}) collective-permute-start(f32[3,128]{0,1:T(8,128)S(1)} %get-tuple-element.342), channel_id=1, source_target_pairs={{0,4},{4,0},{8,12},{12,8},{16,20},{20,16},{24,28},{28,24},{1,5},{5... | collective-permute-start | bytes 4616 | tf_op jit(solution)/shard_map/ppermute | solution.py:19
  315.3 4.0 %collective-permute-start.8 = (f32[32,128]{1,0:T(8,128)S(1)}, f32[32,128]{1,0:T(8,128)S(1)}, u32[]{:S(2)}, u32[]{:S(2)}) collective-permute-start(f32[32,128]{1,0:T(8,128)S(1)} %get-tuple-element.346), channel_id=1, source_target_pairs={{0,16},{4,20},{8,24},{12,28},{16,0},{20,4},{24,8},{28,12},{1,17},{... | collective-permute-start | bytes 49160 | tf_op jit(solution)/shard_map/ppermute | solution.py:19
  319.3 0.6 collective-permute-start.10
  320.2 0.7 pad_maximum_fusion
  321.1 0.7 copy-done.4
  321.8 22.5 %psum.15 = f32[32,8]{0,1:T(8,128)} all-reduce(f32[32,8]{0,1:T(8,128)S(1)} %get-tuple-element.231), channel_id=1, replica_groups=mesh['space'=8,'chan'=4] {'space'}, use_global_device_ids=true, to_apply=%region_27.30 | all-reduce | flops 256 | bytes 2048 | tf_op jit(solution)/shard_map/psum | solution.py:198
  344.3 1.3 scatter_custom_fusion.3
  345.6 1.3 scatter_custom_fusion.4
  347.0 1.3 scatter_custom_fusion.5
  348.3 0.7 copy.75
  349.3 0.6 slice-done
  349.9 1.3 scatter_fusion
  351.2 1.3 scatter_fusion.1
  352.5 1.3 scatter_fusion.2
  353.9 0.7 copy.74
  (233 shorter events, 31.2 us)
Async XLA Ops:
  0.6 16.1 %copy-start = (bf16[3,128,128]{2,1,0:T(8,128)(2,1)S(1)}, bf16[3,128,128]{2,1,0:T(8,128)(2,1)}, u32[]{:S(2)}) copy-start(bf16[3,128,128]{2,1,0:T(8,128)(2,1)} %param.23) | copy-start | bytes 294916
  0.6 0.9 copy-start.10
  2.4 15.8 %collective-permute-start.2 = (bf16[32,128]{1,0:T(8,128)(2,1)S(1)}, bf16[32,128]{1,0:T(8,128)(2,1)S(1)}, u32[]{:S(2)}, u32[]{:S(2)}) collective-permute-start(bf16[32,128]{1,0:T(8,128)(2,1)S(1)} %bitcast_convert_fusion), channel_id=1, source_target_pairs={{0,16},{4,20},{8,24},{12,28},{16,0},{20,4},{24,8},{28,12},{1,17},{... | collective-permute-start | bytes 24584 | tf_op jit(solution)/shard_map/ppermute | solution.py:19
  7.3 1.7 copy-start.9
  7.3 10.9 %collective-permute-start.1 = (bf16[32,128]{1,0:T(8,128)(2,1)S(1)}, bf16[32,128]{1,0:T(8,128)(2,1)S(1)}, u32[]{:S(2)}, u32[]{:S(2)}) collective-permute-start(bf16[32,128]{1,0:T(8,128)(2,1)S(1)} %bitcast_convert_fusion.1), channel_id=1, source_target_pairs={{0,8},{4,12},{8,0},{12,4},{16,24},{20,28},{24,16},{28,20},{1,9},{5... | collective-permute-start | bytes 24584 | tf_op jit(solution)/shard_map/ppermute | solution.py:19
  9.8 7.5 %collective-permute-start.5 = (f32[3,128]{0,1:T(8,128)S(1)}, f32[3,128]{0,1:T(8,128)S(1)}, u32[]{:S(2)}, u32[]{:S(2)}) collective-permute-start(f32[3,128]{0,1:T(8,128)S(1)} %select_bitcast_fusion), channel_id=1, source_target_pairs={{0,16},{4,20},{8,24},{12,28},{16,0},{20,4},{24,8},{28,12},{1,17},{... | collective-permute-start | bytes 4616 | tf_op jit(solution)/shard_map/ppermute | solution.py:19
  11.0 7.0 %collective-permute-start.4 = (f32[3,128]{0,1:T(8,128)S(1)}, f32[3,128]{0,1:T(8,128)S(1)}, u32[]{:S(2)}, u32[]{:S(2)}) collective-permute-start(f32[3,128]{0,1:T(8,128)S(1)} %select_bitcast_fusion.1), channel_id=1, source_target_pairs={{0,8},{4,12},{8,0},{12,4},{16,24},{20,28},{24,16},{28,20},{1,9},{5... | collective-permute-start | bytes 4616 | tf_op jit(solution)/shard_map/ppermute | solution.py:19
  11.6 3.8 %copy-start.6 = (bf16[32,9,256]{2,0,1:T(8,128)(2,1)S(1)}, bf16[32,9,256]{2,0,1:T(8,128)(2,1)}, u32[]{:S(2)}) copy-start(bf16[32,9,256]{2,0,1:T(8,128)(2,1)} %param.24) | copy-start | bytes 442372
  12.4 5.7 %collective-permute-start.3 = (f32[3,128]{0,1:T(8,128)S(1)}, f32[3,128]{0,1:T(8,128)S(1)}, u32[]{:S(2)}, u32[]{:S(2)}) collective-permute-start(f32[3,128]{0,1:T(8,128)S(1)} %select_bitcast_fusion.2), channel_id=1, source_target_pairs={{0,4},{4,0},{8,12},{12,8},{16,20},{20,16},{24,28},{28,24},{1,5},{5... | collective-permute-start | bytes 4616 | tf_op jit(solution)/shard_map/ppermute | solution.py:19
  14.7 0.7 copy-start.11
  15.4 0.7 copy-start.12
  15.4 1.3 copy-start.1
  17.4 3.7 %collective-permute-start = (bf16[32,128]{1,0:T(8,128)(2,1)S(1)}, bf16[32,128]{1,0:T(8,128)(2,1)S(1)}, u32[]{:S(2)}, u32[]{:S(2)}) collective-permute-start(bf16[32,128]{1,0:T(8,128)(2,1)S(1)} %bitcast_convert_fusion.2), channel_id=1, source_target_pairs={{0,4},{4,0},{8,12},{12,8},{16,20},{20,16},{24,28},{28,24},{1,5},{5... | collective-permute-start | bytes 24584 | tf_op jit(solution)/shard_map/ppermute | solution.py:19
  18.1 2.9 copy-start.8
  21.1 0.7 copy-start.7
  41.1 0.6 copy-start.2
  64.9 0.8 copy-start.3
  88.1 0.8 copy-start.3
  119.3 201.7 %copy-start.5 = (f32[3,640]{0,1:T(8,128)}, f32[3,640]{0,1:T(8,128)S(1)}, u32[]{:S(2)}) copy-start(f32[3,640]{0,1:T(8,128)S(1)} %psum.14) | copy-start | bytes 23044
  119.4 200.5 %collective-permute-start.9 = (f32[3,128]{0,1:T(8,128)S(1)}, f32[3,128]{0,1:T(8,128)S(1)}, u32[]{:S(2)}, u32[]{:S(2)}) collective-permute-start(f32[3,128]{0,1:T(8,128)S(1)} %get-tuple-element.342), channel_id=1, source_target_pairs={{0,4},{4,0},{8,12},{12,8},{16,20},{20,16},{24,28},{28,24},{1,5},{5... | collective-permute-start | bytes 4616 | tf_op jit(solution)/shard_map/ppermute | solution.py:19
  315.2 33.8 %collective-permute-start.6 = (f32[32,128]{1,0:T(8,128)S(1)}, f32[32,128]{1,0:T(8,128)S(1)}, u32[]{:S(2)}, u32[]{:S(2)}) collective-permute-start(f32[32,128]{1,0:T(8,128)S(1)} %get-tuple-element.348), channel_id=1, source_target_pairs={{0,4},{4,0},{8,12},{12,8},{16,20},{20,16},{24,28},{28,24},{1,5},{5... | collective-permute-start | bytes 49160 | tf_op jit(solution)/shard_map/ppermute | solution.py:19
  315.3 33.8 %collective-permute-start.7 = (f32[32,128]{1,0:T(8,128)S(1)}, f32[32,128]{1,0:T(8,128)S(1)}, u32[]{:S(2)}, u32[]{:S(2)}) collective-permute-start(f32[32,128]{1,0:T(8,128)S(1)} %get-tuple-element.347), channel_id=1, source_target_pairs={{0,8},{4,12},{8,0},{12,4},{16,24},{20,28},{24,16},{28,20},{1,9},{5... | collective-permute-start | bytes 49160 | tf_op jit(solution)/shard_map/ppermute | solution.py:19
  315.3 33.9 %collective-permute-start.8 = (f32[32,128]{1,0:T(8,128)S(1)}, f32[32,128]{1,0:T(8,128)S(1)}, u32[]{:S(2)}, u32[]{:S(2)}) collective-permute-start(f32[32,128]{1,0:T(8,128)S(1)} %get-tuple-element.346), channel_id=1, source_target_pairs={{0,16},{4,20},{8,24},{12,28},{16,0},{20,4},{24,8},{28,12},{1,17},{... | collective-permute-start | bytes 49160 | tf_op jit(solution)/shard_map/ppermute | solution.py:19
  319.3 26.3 %collective-permute-start.10 = (f32[3,128]{0,1:T(8,128)S(1)}, f32[3,128]{0,1:T(8,128)S(1)}, u32[]{:S(2)}, u32[]{:S(2)}) collective-permute-start(f32[3,128]{0,1:T(8,128)S(1)} %get-tuple-element.341), channel_id=1, source_target_pairs={{0,8},{4,12},{8,0},{12,4},{16,24},{20,28},{24,16},{28,20},{1,9},{5... | collective-permute-start | bytes 4616 | tf_op jit(solution)/shard_map/ppermute | solution.py:19
  319.9 27.0 %collective-permute-start.11 = (f32[3,128]{0,1:T(8,128)S(1)}, f32[3,128]{0,1:T(8,128)S(1)}, u32[]{:S(2)}, u32[]{:S(2)}) collective-permute-start(f32[3,128]{0,1:T(8,128)S(1)} %get-tuple-element.340), channel_id=1, source_target_pairs={{0,16},{4,20},{8,24},{12,28},{16,0},{20,4},{24,8},{28,12},{1,17},{... | collective-permute-start | bytes 4616 | tf_op jit(solution)/shard_map/ppermute | solution.py:19
  321.1 0.7 copy-start.4
  321.1 23.2 %slice-start.1 = ((f32[3,640]{0,1:T(8,128)}), f32[3,256]{0,1:T(8,128)S(1)}, s32[]{:S(2)}) async-start(f32[3,640]{0,1:T(8,128)} %copy-done.5), calls=%async_computation.1 | async-start | bytes 262144 | tf_op jit(solution)/shard_map/slice | solution.py:187
  349.0 0.9 slice-start
where the time goes:
time: 359 us; the launch traced here: 355 us
  starting transfers between devices  210 us (58%)
  blocking collectives  51.8 us (14%)
  matrix products  43.8 us (12%)
  local copies, waits for them, and re-layouts  17.6 us (5%)
  loops' own time  15.4 us (4%)
  other arithmetic  12.2 us (3%)
    ppermute x12, starting transfers between devices, partner(): return lax.ppermute(value, axis, pairs)  210 us
    psum x1, blocking collectives, body(): grad_radial = lax.psum(grad_rad, 'space')  22.5 us
    dot_general x18, matrix products, backward_tile(): jnp.einsum('kij,cj->cki', pair_values, source_feat, preferred_element_typ...  17.4 us
    psum x1, blocking collectives, body(): dpos_src = lax.psum(dpos_src, 'chan')  14.2 us
    dot_general x18, matrix products, backward_tile(): jnp.einsum('cki,cj->kij', weighted, source_feat, preferred_element_type=j...  8.14 us
    another operation x1, loops' own time, body(): lax.fori_loop(0, live_count, backward_tile, init)  7.83 us
    all_gather x1, blocking collectives, body(): gathered_piece = lax.all_gather(dz_packed, 'chan', axis=0, tiled=True)  7.65 us
    another operation x1, loops' own time, body(): lax.fori_loop(0, live_count, forward_tile, jnp.zeros((chan_dev, component...  7.56 us
  transfers between devices with their start and end apart: 12, of which 1 were waited for; matrix products, arithmetic and copies ran while one was open for 3% of the time, Pallas kernels for 0%

commit v1 on v0

--- a/solution.py
+++ b/solution.py
@@ -97,23 +97,23 @@
 
         return (target_blk, source_blk, target_pos, source_pos, geo_fn)
 
-    def forward_tile(tile_index, moments):
+    def forward_tile(tile_index, msg_acc):
         target_blk, source_blk, target_pos, source_pos, geo_fn = tile_parts(tile_index)
         harmonics, radial = geo_fn(target_pos, source_pos)
         source_feat = take_block(src_feat, source_blk, block_size)
-        pieces_list = []
-        for harmonic in range(components):
-            pair_values = (harmonics[harmonic][None] * radial).astype(jnp.bfloat16)
-            message = jnp.einsum(
-                "kij,cj->cki", pair_values, source_feat, preferred_element_type=jnp.float32
-            )
-            pieces_list.append(jnp.einsum("cki,ck->ci", message, radial_weight))
-        contrib = jnp.stack(pieces_list, axis=1)
-        return add_block(moments, target_blk, contrib, block_size)
-
-    moments = lax.fori_loop(
-        0, live_count, forward_tile, jnp.zeros((chan_dev, components, atoms_dev), jnp.float32)
-    )
+        pair_values = (harmonics[:, None] * radial[None]).astype(jnp.bfloat16)
+        message = jnp.einsum(
+            "lkij,cj->clki", pair_values, source_feat, preferred_element_type=jnp.float32
+        )
+        return add_block(msg_acc, target_blk, message, block_size)
+
+    msg_acc = lax.fori_loop(
+        0,
+        live_count,
+        forward_tile,
+        jnp.zeros((chan_dev, components, radial_count, atoms_dev), jnp.float32),
+    )
+    moments = jnp.einsum("clki,ck->cli", msg_acc, radial_weight)
     packed = moments.astype(jnp.bfloat16)
     mixing = jnp.take(mix_weight, jnp.array(ORDER_OF, dtype=jnp.int32), axis=0)
     offset = lax.axis_index("chan") * chan_dev
@@ -143,45 +143,37 @@
     moment_grad_all = jnp.einsum(
         "lxc,xli->cli", weight_part, gathered_piece, preferred_element_type=jnp.float32
     )
+    grad_rad = jnp.einsum("clki,cli->ck", msg_acc, moment_grad_all)
+    weighted_all = (radial_weight[:, None, :, None] * moment_grad_all[:, :, None, :]).astype(
+        jnp.bfloat16
+    )
 
     def backward_tile(tile_index, running):
-        grad_src, dpos_src, grad_rad = running
+        grad_src, dpos_src = running
         target_blk, source_blk, target_pos, source_pos, geo_fn = tile_parts(tile_index)
         (harmonics, radial), pullback = jax.vjp(geo_fn, target_pos, source_pos)
         source_feat = take_block(src_feat, source_blk, block_size)
-        moment_grad = take_block(moment_grad_all, target_blk, block_size)
-        grad_source = jnp.zeros((chan_dev, block_size), jnp.float32)
-        rad_grad = jnp.zeros_like(radial)
-        harm_list = []
-        for harmonic in range(components):
-            pair_values = (harmonics[harmonic][None] * radial).astype(jnp.bfloat16)
-            message = jnp.einsum(
-                "kij,cj->cki", pair_values, source_feat, preferred_element_type=jnp.float32
-            )
-            grad_rad = grad_rad + jnp.einsum("cki,ci->ck", message, moment_grad[:, harmonic, :])
-            weighted = (radial_weight[:, :, None] * moment_grad[:, harmonic, None, :]).astype(
-                jnp.bfloat16
-            )
-            grad_source = grad_source + jnp.einsum(
-                "cki,kij->cj", weighted, pair_values, preferred_element_type=jnp.float32
-            )
-            value_grad = jnp.einsum(
-                "cki,cj->kij", weighted, source_feat, preferred_element_type=jnp.float32
-            )
-            harm_list.append(jnp.sum(value_grad * radial, axis=0))
-            rad_grad = rad_grad + value_grad * harmonics[harmonic][None]
-        target_grad, source_grad_pos = pullback((jnp.stack(harm_list), rad_grad))
+        weighted = take_block(weighted_all, target_blk, block_size)
+        pair_values = (harmonics[:, None] * radial[None]).astype(jnp.bfloat16)
+        grad_source = jnp.einsum(
+            "clki,lkij->cj", weighted, pair_values, preferred_element_type=jnp.float32
+        )
+        value_grad = jnp.einsum(
+            "clki,cj->lkij", weighted, source_feat, preferred_element_type=jnp.float32
+        )
+        harm_grad = jnp.sum(value_grad * radial[None], axis=1)
+        rad_grad = jnp.sum(value_grad * harmonics[:, None], axis=0)
+        target_grad, source_grad_pos = pullback((harm_grad, rad_grad))
         grad_src = add_block(grad_src, source_blk, grad_source, block_size)
         dpos_src = add_block(dpos_src, target_blk, target_grad, block_size)
         dpos_src = add_block(dpos_src, source_blk, source_grad_pos, block_size)
-        return (grad_src, dpos_src, grad_rad)
+        return (grad_src, dpos_src)
 
     init = (
         jnp.zeros((chan_dev, src_atoms), jnp.float32),
         jnp.zeros((3, src_atoms), jnp.float32),
-        jnp.zeros((chan_dev, radial_count), jnp.float32),
-    )
-    grad_src, dpos_src, grad_rad = lax.fori_loop(0, live_count, backward_tile, init)
+    )
+    grad_src, dpos_src = lax.fori_loop(0, live_count, backward_tile, init)
     dpos_src = lax.psum(dpos_src, "chan")
     own_grad = grad_src[:, :atoms_dev]
     own_dpos = dpos_src[:, :atoms_dev]

time: 359 us -> 220 us (0.61)
  starting transfers between devices: 210 us -> 75.2 us
  matrix products: 43.8 us -> 14.7 us
  loops' own time: 15.4 us -> 28 us
  other arithmetic: 12.2 us -> 22.4 us
  local copies, waits for them, and re-layouts: 17.6 us -> 22.8 us
    ppermute x12, starting transfers between devices: 210 us -> 75.2 us  [partner(): return lax.ppermute(value, axis, pairs)]
    dot_general x108 -> x14, matrix products: 43.2 us -> 14.1 us  [the longest x4 7.05 us: backward_tile(): jnp.einsum('clki,cj->lkij', weighted, source_feat, preferred_element_type...]
    another operation x1, loops' own time: 7.83 us -> 14.3 us  [body(): grad_src, dpos_src = lax.fori_loop(0, live_count, backward_tile, init)]
    another operation x1, loops' own time: 7.56 us -> 13.6 us  [body(): lax.fori_loop(0, live_count, forward_tile, jnp.zeros((chan_dev, component...]
  transfers between devices with their start and end apart: 12 -> 12, of which waited for: 1 -> 1; matrix products, arithmetic and copies ran while one was open for 3% -> 8% of each run, Pallas kernels for 0% -> 0%
where the time goes in v1:
time: 220 us; the launch traced here: 218 us
  starting transfers between devices  75.2 us (34%)
  blocking collectives  49.8 us (23%)
  loops' own time  28 us (13%)
  local copies, waits for them, and re-layouts  22.8 us (10%)
  other arithmetic  22.4 us (10%)
  matrix products  14.7 us (7%)
  waiting for transfers between devices  4.29 us (2%)
    ppermute x12, starting transfers between devices, partner(): return lax.ppermute(value, axis, pairs)  75.2 us
    psum x1, blocking collectives, body(): grad_radial = lax.psum(grad_rad, 'space')  20.5 us
    another operation x1, loops' own time, body(): grad_src, dpos_src = lax.fori_loop(0, live_count, backward_tile, init)  14.3 us
    psum x1, blocking collectives, body(): dpos_src = lax.psum(dpos_src, 'chan')  14.2 us
    another operation x1, loops' own time, body(): lax.fori_loop(0, live_count, forward_tile, jnp.zeros((chan_dev, component...  13.6 us
    all_gather x1, blocking collectives, body(): gathered_piece = lax.all_gather(dz_packed, 'chan', axis=0, tiled=True)  7.65 us
    all_gather x1, blocking collectives, body(): gathered_piece = lax.all_gather(packed, 'chan', axis=0, tiled=True)  7.53 us
    dot_general x4, matrix products, backward_tile(): jnp.einsum('clki,cj->lkij', weighted, source_feat, preferred_element_type...  7.05 us
  transfers between devices with their start and end apart: 12, of which 1 were waited for; matrix products, arithmetic and copies ran while one was open for 8% of the time, Pallas kernels for 0%

profile of v1, /device:TPU:0, one launch (start us, length us, event | category | flops | bytes accessed | tf_op | source)
XLA Modules:
  0.0 218.1 jit_solution(12961454209003522048)
XLA Ops:
  0.7 0.8 compare_and_fusion.2
  1.5 0.8 copy.43
  2.3 0.6 gather_fusion.4
  3.1 3.0 %collective-permute-start.3 = (f32[3,128]{0,1:T(8,128)S(1)}, f32[3,128]{0,1:T(8,128)S(1)}, u32[]{:S(2)}, u32[]{:S(2)}) collective-permute-start(f32[3,128]{0,1:T(8,128)S(1)} %select_bitcast_fusion.2), channel_id=1, source_target_pairs={{0,4},{4,0},{8,12},{12,8},{16,20},{20,16},{24,28},{28,24},{1,5},{5... | collective-permute-start | bytes 4616 | tf_op jit(solution)/shard_map/ppermute | solution.py:19
  6.1 0.6 gather_fusion.5
  6.8 1.6 collective-permute-start.4
  8.5 0.6 gather_fusion.6
  9.2 2.7 %collective-permute-start.5 = (f32[3,128]{0,1:T(8,128)S(1)}, f32[3,128]{0,1:T(8,128)S(1)}, u32[]{:S(2)}, u32[]{:S(2)}) collective-permute-start(f32[3,128]{0,1:T(8,128)S(1)} %select_bitcast_fusion), channel_id=1, source_target_pairs={{0,16},{4,20},{8,24},{12,28},{16,0},{20,4},{24,8},{28,12},{1,17},{... | collective-permute-start | bytes 4616 | tf_op jit(solution)/shard_map/ppermute | solution.py:19
  11.9 0.8 copy.37
  12.7 0.7 gather_fusion.1
  14.1 0.7 gather_fusion.2
  15.4 0.7 gather_fusion.3
  16.1 0.8 fusion.99
  17.0 0.7 pad_clamp_fusion.3
  17.7 1.3 reduce_sum.132
  19.0 0.8 copy.61
  19.7 0.9 convert_element_type.71
  20.7 1.3 gather_fusion
  22.3 4.3 %collective-permute-done.2 = bf16[32,128]{1,0:T(8,128)(2,1)S(1)} collective-permute-done((bf16[32,128]{1,0:T(8,128)(2,1)S(1)}, bf16[32,128]{1,0:T(8,128)(2,1)S(1)}, u32[]{:S(2)}, u32[]{:S(2)}) %collective-permute-start.2) | collective-permute-done | bytes 8224 | tf_op jit(solution)/shard_map/ppermute | solution.py:19
  26.7 29.7 %while.26 = (s32[]{:T(128)}, f32[32,9,8,256]{3,2,1,0:T(8,128)S(1)}, s32[]{:T(128)}, s32[8,2]{0,1:T(2,128)S(1)}, bf16[32,640]{1,0:T(8,128)(2,1)S(1)}, /*index=5*/...) while((s32[]{:T(128)}, f32[32,9,8,256]{3,2,1,0:T(8,128)S(1)}, ...), condition=%wide.region_3.6_spmd, body=%wide.region_1.5_spmd.sunk | while | flops 79511584 | bytes 15943102 | solution.py:110
  27.4 0.6 constant_dynamic-slice_fusion.21
  31.3 1.0 copy-done.2
  32.2 1.0 fusion.132
  33.2 0.8 copy_dynamic-update-slice_fusion.2
  34.7 0.6 constant_dynamic-slice_fusion.21
  38.5 1.0 copy-done.2
  39.5 1.0 fusion.132
  40.4 0.8 copy_dynamic-update-slice_fusion.2
  41.9 0.6 constant_dynamic-slice_fusion.21
  45.8 1.0 copy-done.2
  46.7 1.0 fusion.132
  47.7 0.8 copy_dynamic-update-slice_fusion.2
  49.2 0.6 constant_dynamic-slice_fusion.21
  53.0 1.0 copy-done.2
  54.0 1.0 fusion.132
  54.9 0.8 copy_dynamic-update-slice_fusion.2
  56.9 7.5 %all_gather.6 = bf16[128,9,256]{2,0,1:T(8,128)(2,1)S(1)} all-gather(bf16[32,9,256]{2,0,1:T(8,128)(2,1)S(1)} %bitcast.335), channel_id=1, replica_groups=mesh['space'=8,'chan'=4] {'chan'}, dimensions={0}, use_global_device_ids=true | all-gather | bytes 737280 | tf_op jit(solution)/shard_map/all_gather | solution.py:120
  64.8 7.7 %all_gather.7 = bf16[128,9,256]{2,0,1:T(8,128)(2,1)S(1)} all-gather(bf16[32,9,256]{2,0,1:T(8,128)(2,1)S(1)} %pad_maximum_fusion.1), channel_id=1, replica_groups=mesh['space'=8,'chan'=4] {'chan'}, dimensions={0}, use_global_device_ids=true | all-gather | bytes 737280 | tf_op jit(solution)/shard_map/all_gather | solution.py:139
  72.9 0.7 fusion.80
  73.9 31.8 %while.27 = (s32[]{:T(128)}, f32[32,640]{1,0:T(8,128)S(1)}, f32[3,640]{1,0:T(4,128)S(1)}, s32[]{:T(128)}, s32[8,2]{0,1:T(2,128)S(1)}, /*index=5*/bf16[32,9,8,256...) while((s32[]{:T(128)}, f32[32,640]{1,0:T(8,128)S(1)}, ...), condition=%wide.region_13.16_spmd, body=%wide.region_5.15_spmd.sunk | while | flops 162828704 | bytes 14683590 | solution.py:176
  74.6 0.6 constant_dynamic-slice_fusion.25
  78.5 1.8 multiply_reduce_fusion.6
  82.4 0.6 constant_dynamic-slice_fusion.25
  86.3 1.8 multiply_reduce_fusion.6
  90.2 0.6 constant_dynamic-slice_fusion.25
  94.1 1.8 multiply_reduce_fusion.6
  97.9 0.6 constant_dynamic-slice_fusion.25
  101.9 1.8 multiply_reduce_fusion.6
  105.9 14.2 %psum.14 = f32[3,640]{0,1:T(8,128)S(1)} all-reduce(f32[3,640]{0,1:T(8,128)S(1)} %copy.54), channel_id=1, replica_groups=mesh['space'=8,'chan'=4] {'chan'}, use_global_device_ids=true, to_apply=%region_17.20 | all-reduce | flops 1920 | bytes 15360 | tf_op jit(solution)/shard_map/psum | solution.py:177
  120.1 1.6 collective-permute-start.9
  121.7 60.3 %collective-permute-start.10 = (f32[3,128]{0,1:T(8,128)S(1)}, f32[3,128]{0,1:T(8,128)S(1)}, u32[]{:S(2)}, u32[]{:S(2)}) collective-permute-start(f32[3,128]{0,1:T(8,128)S(1)} %get-tuple-element.262), channel_id=1, source_target_pairs={{0,8},{4,12},{8,0},{12,4},{16,24},{20,28},{24,16},{28,20},{1,9},{5... | collective-permute-start | bytes 4616 | tf_op jit(solution)/shard_map/ppermute | solution.py:19
  181.9 1.8 collective-permute-start.11
  184.0 0.7 collective-permute-start.7
  184.7 2.1 collective-permute-start.8
  186.8 0.7 pad_maximum_fusion
  187.8 20.5 %psum.15 = f32[32,8]{0,1:T(8,128)} all-reduce(f32[32,8]{0,1:T(8,128)S(1)} %bitcast.340), channel_id=1, replica_groups=mesh['space'=8,'chan'=4] {'space'}, use_global_device_ids=true, to_apply=%region_21.24 | all-reduce | flops 256 | bytes 2048 | tf_op jit(solution)/shard_map/psum | solution.py:190
  208.2 1.3 scatter_custom_fusion.3
  209.6 1.5 scatter_custom_fusion.4
  211.1 1.3 scatter_custom_fusion.5
  212.4 0.7 copy.56
  213.4 1.3 scatter_fusion
  214.8 1.3 scatter_fusion.1
  216.1 1.3 scatter_fusion.2
  217.4 0.7 copy.55
  (228 shorter events, 15.4 us)
Async XLA Ops:
  0.6 20.1 %copy-start = (bf16[3,128,128]{2,1,0:T(8,128)(2,1)S(1)}, bf16[3,128,128]{2,1,0:T(8,128)(2,1)}, u32[]{:S(2)}) copy-start(bf16[3,128,128]{2,1,0:T(8,128)(2,1)} %param.23) | copy-start | bytes 294916
  0.6 21.6 %copy-start.7 = (f32[3,256]{1,0:T(4,128)S(1)}, f32[3,256]{1,0:T(4,128)}, u32[]{:S(2)}) copy-start(f32[3,256]{1,0:T(4,128)} %param.17) | copy-start | bytes 9220
  0.7 25.9 %copy-start.5 = (bf16[32,256]{1,0:T(8,128)(2,1)S(1)}, bf16[32,256]{1,0:T(8,128)(2,1)}, u32[]{:S(2)}) copy-start(bf16[32,256]{1,0:T(8,128)(2,1)} %param.18) | copy-start | bytes 49156
  2.3 24.4 %copy-start.4 = (s32[8,2]{0,1:T(2,128)S(1)}, s32[8,2]{0,1:T(2,128)}, u32[]{:S(2)}) copy-start(s32[8,2]{0,1:T(2,128)} %param.20) | copy-start | bytes 196
  3.1 18.9 %collective-permute-start.3 = (f32[3,128]{0,1:T(8,128)S(1)}, f32[3,128]{0,1:T(8,128)S(1)}, u32[]{:S(2)}, u32[]{:S(2)}) collective-permute-start(f32[3,128]{0,1:T(8,128)S(1)} %select_bitcast_fusion.2), channel_id=1, source_target_pairs={{0,4},{4,0},{8,12},{12,8},{16,20},{20,16},{24,28},{28,24},{1,5},{5... | collective-permute-start | bytes 4616 | tf_op jit(solution)/shard_map/ppermute | solution.py:19
  6.8 15.2 %collective-permute-start.4 = (f32[3,128]{0,1:T(8,128)S(1)}, f32[3,128]{0,1:T(8,128)S(1)}, u32[]{:S(2)}, u32[]{:S(2)}) collective-permute-start(f32[3,128]{0,1:T(8,128)S(1)} %select_bitcast_fusion.1), channel_id=1, source_target_pairs={{0,8},{4,12},{8,0},{12,4},{16,24},{20,28},{24,16},{28,20},{1,9},{5... | collective-permute-start | bytes 4616 | tf_op jit(solution)/shard_map/ppermute | solution.py:19
  9.2 12.9 %collective-permute-start.5 = (f32[3,128]{0,1:T(8,128)S(1)}, f32[3,128]{0,1:T(8,128)S(1)}, u32[]{:S(2)}, u32[]{:S(2)}) collective-permute-start(f32[3,128]{0,1:T(8,128)S(1)} %select_bitcast_fusion), channel_id=1, source_target_pairs={{0,16},{4,20},{8,24},{12,28},{16,0},{20,4},{24,8},{28,12},{1,17},{... | collective-permute-start | bytes 4616 | tf_op jit(solution)/shard_map/ppermute | solution.py:19
  13.5 8.8 %collective-permute-start = (bf16[32,128]{1,0:T(8,128)(2,1)S(1)}, bf16[32,128]{1,0:T(8,128)(2,1)S(1)}, u32[]{:S(2)}, u32[]{:S(2)}) collective-permute-start(bf16[32,128]{1,0:T(8,128)(2,1)S(1)} %bitcast_convert_fusion.3), channel_id=1, source_target_pairs={{0,4},{4,0},{8,12},{12,8},{16,20},{20,16},{24,28},{28,24},{1,5},{5... | collective-permute-start | bytes 24584 | tf_op jit(solution)/shard_map/ppermute | solution.py:19
  14.9 7.4 %collective-permute-start.1 = (bf16[32,128]{1,0:T(8,128)(2,1)S(1)}, bf16[32,128]{1,0:T(8,128)(2,1)S(1)}, u32[]{:S(2)}, u32[]{:S(2)}) collective-permute-start(bf16[32,128]{1,0:T(8,128)(2,1)S(1)} %bitcast_convert_fusion.2), channel_id=1, source_target_pairs={{0,8},{4,12},{8,0},{12,4},{16,24},{20,28},{24,16},{28,20},{1,9},{5... | collective-permute-start | bytes 24584 | tf_op jit(solution)/shard_map/ppermute | solution.py:19
  22.0 4.6 %collective-permute-start.2 = (bf16[32,128]{1,0:T(8,128)(2,1)S(1)}, bf16[32,128]{1,0:T(8,128)(2,1)S(1)}, u32[]{:S(2)}, u32[]{:S(2)}) collective-permute-start(bf16[32,128]{1,0:T(8,128)(2,1)S(1)} %bitcast_convert_fusion.1), channel_id=1, source_target_pairs={{0,16},{4,20},{8,24},{12,28},{16,0},{20,4},{24,8},{28,12},{1,17},{... | collective-permute-start | bytes 24584 | tf_op jit(solution)/shard_map/ppermute | solution.py:19
  29.7 1.3 copy-start.1
  31.2 1.1 copy-start.2
  36.9 1.3 copy-start.1
  38.4 1.1 copy-start.2
  44.2 1.3 copy-start.1
  45.7 1.1 copy-start.2
  51.4 1.3 copy-start.1
  52.9 1.1 copy-start.2
  56.4 8.0 %copy-start.3 = (bf16[9,128,128]{2,1,0:T(8,128)(2,1)S(1)}, bf16[9,128,128]{2,1,0:T(8,128)(2,1)}, u32[]{:S(2)}) copy-start(bf16[9,128,128]{2,1,0:T(8,128)(2,1)} %gather_fusion) | copy-start | bytes 884740
  64.8 8.8 %copy-start.6 = (f32[32,8]{0,1:T(8,128)S(1)}, f32[32,8]{0,1:T(8,128)}, u32[]{:S(2)}) copy-start(f32[32,8]{0,1:T(8,128)} %param.22) | copy-start | bytes 3076
  120.1 64.6 %collective-permute-start.9 = (f32[3,128]{0,1:T(8,128)S(1)}, f32[3,128]{0,1:T(8,128)S(1)}, u32[]{:S(2)}, u32[]{:S(2)}) collective-permute-start(f32[3,128]{0,1:T(8,128)S(1)} %get-tuple-element.263), channel_id=1, source_target_pairs={{0,4},{4,0},{8,12},{12,8},{16,20},{20,16},{24,28},{28,24},{1,5},{5... | collective-permute-start | bytes 4616 | tf_op jit(solution)/shard_map/ppermute | solution.py:19
  121.7 87.9 %collective-permute-start.10 = (f32[3,128]{0,1:T(8,128)S(1)}, f32[3,128]{0,1:T(8,128)S(1)}, u32[]{:S(2)}, u32[]{:S(2)}) collective-permute-start(f32[3,128]{0,1:T(8,128)S(1)} %get-tuple-element.262), channel_id=1, source_target_pairs={{0,8},{4,12},{8,0},{12,4},{16,24},{20,28},{24,16},{28,20},{1,9},{5... | collective-permute-start | bytes 4616 | tf_op jit(solution)/shard_map/ppermute | solution.py:19
  181.9 29.1 %collective-permute-start.11 = (f32[3,128]{0,1:T(8,128)S(1)}, f32[3,128]{0,1:T(8,128)S(1)}, u32[]{:S(2)}, u32[]{:S(2)}) collective-permute-start(f32[3,128]{0,1:T(8,128)S(1)} %get-tuple-element.261), channel_id=1, source_target_pairs={{0,16},{4,20},{8,24},{12,28},{16,0},{20,4},{24,8},{28,12},{1,17},{... | collective-permute-start | bytes 4616 | tf_op jit(solution)/shard_map/ppermute | solution.py:19
  183.7 29.4 %collective-permute-start.6 = (f32[32,128]{1,0:T(8,128)S(1)}, f32[32,128]{1,0:T(8,128)S(1)}, u32[]{:S(2)}, u32[]{:S(2)}) collective-permute-start(f32[32,128]{1,0:T(8,128)S(1)} %get-tuple-element.269), channel_id=1, source_target_pairs={{0,4},{4,0},{8,12},{12,8},{16,20},{20,16},{24,28},{28,24},{1,5},{5... | collective-permute-start | bytes 49160 | tf_op jit(solution)/shard_map/ppermute | solution.py:19
  184.0 29.3 %collective-permute-start.7 = (f32[32,128]{1,0:T(8,128)S(1)}, f32[32,128]{1,0:T(8,128)S(1)}, u32[]{:S(2)}, u32[]{:S(2)}) collective-permute-start(f32[32,128]{1,0:T(8,128)S(1)} %get-tuple-element.268), channel_id=1, source_target_pairs={{0,8},{4,12},{8,0},{12,4},{16,24},{20,28},{24,16},{28,20},{1,9},{5... | collective-permute-start | bytes 49160 | tf_op jit(solution)/shard_map/ppermute | solution.py:19
  184.7 28.6 %collective-permute-start.8 = (f32[32,128]{1,0:T(8,128)S(1)}, f32[32,128]{1,0:T(8,128)S(1)}, u32[]{:S(2)}, u32[]{:S(2)}) collective-permute-start(f32[32,128]{1,0:T(8,128)S(1)} %get-tuple-element.267), channel_id=1, source_target_pairs={{0,16},{4,20},{8,24},{12,28},{16,0},{20,4},{24,8},{28,12},{1,17},{... | collective-permute-start | bytes 49160 | tf_op jit(solution)/shard_map/ppermute | solution.py:19

commit v2 on v1

--- a/solution.py
+++ b/solution.py
@@ -82,37 +82,54 @@
     src_pos = jnp.concatenate(pos_list, axis=1)
     src_feat = jnp.concatenate(feat_list, axis=1)
     src_atoms = src_pos.shape[1]
-    live_count = jnp.sum(tile_live)
+    src_blocks = src_atoms // block_size
+    own_blocks = atoms_dev // block_size
+    tile_count = pair_tiles.shape[0]
+    target_idx = pair_tiles[:, 0]
+    source_idx = pair_tiles[:, 1]
+    live = tile_live.astype(jnp.float32)
+    block_ids = jnp.arange(src_blocks, dtype=jnp.int32)
+    target_hot = (target_idx[:, None] == block_ids[None]).astype(jnp.float32) * live[:, None]
+    source_hot = (source_idx[:, None] == block_ids[None]).astype(jnp.float32) * live[:, None]
+    same = (target_idx == source_idx).astype(jnp.float32)
+    eye = jnp.eye(block_size, dtype=jnp.float32)
+    keep_all = live[:, None, None] * (1.0 - same[:, None, None] * eye[None])
+    pos_blocks = jnp.moveaxis(src_pos.reshape(3, src_blocks, block_size), 1, 0)
+    feat_blocks = jnp.moveaxis(src_feat.reshape(chan_dev, src_blocks, block_size), 1, 0)
+    target_pos_all = jnp.take(pos_blocks, target_idx, axis=0)
+    source_pos_all = jnp.take(pos_blocks, source_idx, axis=0)
+    source_feat_all = jnp.take(feat_blocks, source_idx, axis=0)
+
+    def pick(array, tile_index):
+        return lax.dynamic_index_in_dim(array, tile_index, 0, keepdims=False)
 
     def tile_parts(tile_index):
-        target_blk = pair_tiles[tile_index, 0]
-        source_blk = pair_tiles[tile_index, 1]
-        same = (target_blk == source_blk).astype(jnp.float32)
-        pair_keep = 1.0 - same * jnp.eye(block_size, dtype=jnp.float32)
-        target_pos = take_block(src_pos, target_blk, block_size)
-        source_pos = take_block(src_pos, source_blk, block_size)
+        pair_keep = pick(keep_all, tile_index)
+        target_pos = pick(target_pos_all, tile_index)
+        source_pos = pick(source_pos_all, tile_index)
 
         def geo_fn(first_pos, second_pos):
             return geometry(first_pos, second_pos, pair_keep, radial_count)
 
-        return (target_blk, source_blk, target_pos, source_pos, geo_fn)
+        return (target_pos, source_pos, geo_fn)
 
     def forward_tile(tile_index, msg_acc):
-        target_blk, source_blk, target_pos, source_pos, geo_fn = tile_parts(tile_index)
+        target_pos, source_pos, geo_fn = tile_parts(tile_index)
         harmonics, radial = geo_fn(target_pos, source_pos)
-        source_feat = take_block(src_feat, source_blk, block_size)
+        source_feat = pick(source_feat_all, tile_index)
         pair_values = (harmonics[:, None] * radial[None]).astype(jnp.bfloat16)
         message = jnp.einsum(
             "lkij,cj->clki", pair_values, source_feat, preferred_element_type=jnp.float32
         )
-        return add_block(msg_acc, target_blk, message, block_size)
+        hot = pick(target_hot, tile_index)[:own_blocks]
+        return msg_acc + hot[None, None, None, :, None] * message[:, :, :, None, :]
 
     msg_acc = lax.fori_loop(
         0,
-        live_count,
+        tile_count,
         forward_tile,
-        jnp.zeros((chan_dev, components, radial_count, atoms_dev), jnp.float32),
-    )
+        jnp.zeros((chan_dev, components, radial_count, own_blocks, block_size), jnp.float32),
+    ).reshape(chan_dev, components, radial_count, atoms_dev)
     moments = jnp.einsum("clki,ck->cli", msg_acc, radial_weight)
     packed = moments.astype(jnp.bfloat16)
     mixing = jnp.take(mix_weight, jnp.array(ORDER_OF, dtype=jnp.int32), axis=0)
@@ -147,13 +164,17 @@
     weighted_all = (radial_weight[:, None, :, None] * moment_grad_all[:, :, None, :]).astype(
         jnp.bfloat16
     )
+    weighted_blocks = jnp.moveaxis(
+        weighted_all.reshape(chan_dev, components, radial_count, own_blocks, block_size), 3, 0
+    )
+    weighted_tiles = jnp.take(weighted_blocks, jnp.minimum(target_idx, own_blocks - 1), axis=0)
 
     def backward_tile(tile_index, running):
-        grad_src, dpos_src = running
-        target_blk, source_blk, target_pos, source_pos, geo_fn = tile_parts(tile_index)
+        grad_tiles, target_grads, source_grads = running
+        target_pos, source_pos, geo_fn = tile_parts(tile_index)
         (harmonics, radial), pullback = jax.vjp(geo_fn, target_pos, source_pos)
-        source_feat = take_block(src_feat, source_blk, block_size)
-        weighted = take_block(weighted_all, target_blk, block_size)
+        source_feat = pick(source_feat_all, tile_index)
+        weighted = pick(weighted_tiles, tile_index)
         pair_values = (harmonics[:, None] * radial[None]).astype(jnp.bfloat16)
         grad_source = jnp.einsum(
             "clki,lkij->cj", weighted, pair_values, preferred_element_type=jnp.float32
@@ -164,31 +185,44 @@
         harm_grad = jnp.sum(value_grad * radial[None], axis=1)
         rad_grad = jnp.sum(value_grad * harmonics[:, None], axis=0)
         target_grad, source_grad_pos = pullback((harm_grad, rad_grad))
-        grad_src = add_block(grad_src, source_blk, grad_source, block_size)
-        dpos_src = add_block(dpos_src, target_blk, target_grad, block_size)
-        dpos_src = add_block(dpos_src, source_blk, source_grad_pos, block_size)
-        return (grad_src, dpos_src)
+        grad_tiles = lax.dynamic_update_index_in_dim(grad_tiles, grad_source, tile_index, 0)
+        target_grads = lax.dynamic_update_index_in_dim(target_grads, target_grad, tile_index, 0)
+        source_grads = lax.dynamic_update_index_in_dim(
+            source_grads, source_grad_pos, tile_index, 0
+        )
+        return (grad_tiles, target_grads, source_grads)
 
     init = (
-        jnp.zeros((chan_dev, src_atoms), jnp.float32),
-        jnp.zeros((3, src_atoms), jnp.float32),
-    )
-    grad_src, dpos_src = lax.fori_loop(0, live_count, backward_tile, init)
-    dpos_src = lax.psum(dpos_src, "chan")
-    own_grad = grad_src[:, :atoms_dev]
-    own_dpos = dpos_src[:, :atoms_dev]
+        jnp.zeros((tile_count, chan_dev, block_size), jnp.float32),
+        jnp.zeros((tile_count, 3, block_size), jnp.float32),
+        jnp.zeros((tile_count, 3, block_size), jnp.float32),
+    )
+    grad_tiles, target_grads, source_grads = lax.fori_loop(0, tile_count, backward_tile, init)
+    grad_src = jnp.sum(
+        source_hot[:, None, :, None] * grad_tiles[:, :, None, :], axis=0
+    ).reshape(chan_dev, src_atoms)
+    dpos_src = jnp.sum(
+        target_hot[:, None, :, None] * target_grads[:, :, None, :]
+        + source_hot[:, None, :, None] * source_grads[:, :, None, :],
+        axis=0,
+    ).reshape(3, src_atoms)
+    for chan_bit in range(lax.axis_size("chan").bit_length() - 1):
+        dpos_src = dpos_src + partner(dpos_src, "chan", chan_bit)
+    own_both = jnp.concatenate([grad_src[:, :atoms_dev], dpos_src[:, :atoms_dev]], axis=0)
+    back_list = []
     for level_bit in range(levels):
         low = atoms_dev + level_bit * block_size
-        back_grad, back_pos = partner(
-            (grad_src[:, low : low + block_size], dpos_src[:, low : low + block_size]),
-            "space",
-            level_bit,
-        )
-        sent_rows = send_rows[level_bit]
-        own_grad = own_grad.at[:, sent_rows].add(back_grad)
-        own_dpos = own_dpos.at[:, sent_rows].add(back_pos)
-    grad_radial = lax.psum(grad_rad, "space")
-    return (result, own_grad.astype(jnp.bfloat16), -own_dpos, grad_radial)
+        ghost_both = jnp.concatenate(
+            [grad_src[:, low : low + block_size], dpos_src[:, low : low + block_size]], axis=0
+        )
+        back_both, other_rad = partner((ghost_both, grad_rad), "space", level_bit)
+        grad_rad = grad_rad + other_rad
+        back_list.append(back_both)
+    all_rows = send_rows[:levels].reshape(-1)
+    own_both = own_both.at[:, all_rows].add(jnp.concatenate(back_list, axis=1))
+    own_grad = own_both[:chan_dev]
+    own_dpos = own_both[chan_dev:]
+    return (result, own_grad.astype(jnp.bfloat16), -own_dpos, grad_rad)
 
 
 def solution(mesh):

time: 220 us -> 188 us (0.85)
  starting transfers between devices: 75.2 us -> 16.5 us
  other arithmetic: 22.4 us -> 68.7 us
  blocking collectives: 49.8 us -> 15.4 us
  loops' own time: 28 us -> 2.37 us
  local copies, waits for them, and re-layouts: 22.8 us -> 43.3 us
  matrix products: 14.7 us -> 28 us
  waiting for transfers between devices: 4.29 us -> 10.9 us
    ppermute x12 -> x14, starting transfers between devices: 75.2 us -> 16.5 us  [partner(): return lax.ppermute(value, axis, pairs)]
    add x0 -> x13, other arithmetic: none -> 36.4 us  [the longest x8 35.8 us: forward_tile(): return msg_acc + hot[None, None, None, :, None] * message[:, :, :, None, :]]
    psum x2 -> x0, blocking collectives: 34.6 us -> none  [the longest x1 20.5 us: body(): grad_radial = lax.psum(grad_rad, 'space')]
    another operation x2, loops' own time: 28 us -> 2.37 us  [the longest x1 1.42 us: body(): lax.fori_loop(0, tile_count, backward_tile, init)]
    squeeze x0 -> x8, local copies, waits for them, and re-layouts: none -> 8.93 us  [pick(): return lax.dynamic_index_in_dim(array, tile_index, 0, keepdims=False)]
    dot_general x4 -> x8, matrix products: 7.05 us -> 15.2 us  [backward_tile(): jnp.einsum('clki,cj->lkij', weighted, source_feat, preferred_element_type...]
    ppermute x12 -> x14, waiting for transfers between devices: 4.29 us -> 10.9 us  [partner(): return lax.ppermute(value, axis, pairs)]
    dot_general x0 -> x8, local copies, waits for them, and re-layouts: none -> 5.5 us  [forward_tile(): jnp.einsum('lkij,cj->clki', pair_values, source_feat, preferred_element_t...]
  transfers between devices with their start and end apart: 12 -> 14, of which waited for: 1 -> 5; matrix products, arithmetic and copies ran while one was open for 8% -> 40% of each run, Pallas kernels for 0% -> 0%
where the time goes in v2:
time: 188 us; the launch traced here: 186 us
  other arithmetic  68.7 us (37%)
  local copies, waits for them, and re-layouts  43.3 us (23%)
  matrix products  28 us (15%)
  starting transfers between devices  16.5 us (9%)
  blocking collectives  15.4 us (8%)
  waiting for transfers between devices  10.9 us (6%)
  loops' own time  2.37 us (1%)
    add x8, other arithmetic, forward_tile(): return msg_acc + hot[None, None, None, :, None] * message[:, :, :, None, :]  35.8 us
    ppermute x14, starting transfers between devices, partner(): return lax.ppermute(value, axis, pairs)  16.5 us
    dot_general x8, matrix products, backward_tile(): jnp.einsum('clki,cj->lkij', weighted, source_feat, preferred_element_type...  15.2 us
    ppermute x14, waiting for transfers between devices, partner(): return lax.ppermute(value, axis, pairs)  10.9 us
    dynamic_slice x16, local copies, waits for them, and re-layouts, pick(): return lax.dynamic_index_in_dim(array, tile_index, 0, keepdims=False)  9.01 us
    squeeze x8, local copies, waits for them, and re-layouts, pick(): return lax.dynamic_index_in_dim(array, tile_index, 0, keepdims=False)  8.93 us
    all_gather x1, blocking collectives, body(): gathered_piece = lax.all_gather(dz_packed, 'chan', axis=0, tiled=True)  7.83 us
    all_gather x1, blocking collectives, body(): gathered_piece = lax.all_gather(packed, 'chan', axis=0, tiled=True)  7.53 us
  transfers between devices with their start and end apart: 14, of which 5 were waited for; matrix products, arithmetic and copies ran while one was open for 40% of the time, Pallas kernels for 0%

profile of v2, /device:TPU:0, one launch (start us, length us, event | category | flops | bytes accessed | tf_op | source)
XLA Modules:
  0.0 186.2 jit_solution(3019772393678737669)
XLA Ops:
  0.7 0.8 compare_and_fusion.4
  1.5 0.8 copy.146
  3.1 3.0 %collective-permute-start.3 = (f32[3,128]{0,1:T(8,128)S(1)}, f32[3,128]{0,1:T(8,128)S(1)}, u32[]{:S(2)}, u32[]{:S(2)}) collective-permute-start(f32[3,128]{0,1:T(8,128)S(1)} %select_bitcast_fusion.2), channel_id=1, source_target_pairs={{0,4},{4,0},{8,12},{12,8},{16,20},{20,16},{24,28},{28,24},{1,5},{5... | collective-permute-start | bytes 4616 | tf_op jit(solution)/shard_map/ppermute | solution.py:19
  6.8 1.6 collective-permute-start.4
  9.2 2.7 %collective-permute-start.5 = (f32[3,128]{0,1:T(8,128)S(1)}, f32[3,128]{0,1:T(8,128)S(1)}, u32[]{:S(2)}, u32[]{:S(2)}) collective-permute-start(f32[3,128]{0,1:T(8,128)S(1)} %select_bitcast_fusion), channel_id=1, source_target_pairs={{0,16},{4,20},{8,24},{12,28},{16,0},{20,4},{24,8},{28,12},{1,17},{... | collective-permute-start | bytes 4616 | tf_op jit(solution)/shard_map/ppermute | solution.py:19
  11.9 0.8 copy.139
  21.6 0.8 copy.169
  22.4 0.9 convert_element_type.81
  25.7 3.0 %collective-permute-done.2 = bf16[32,128]{1,0:T(8,128)(2,1)S(1)} collective-permute-done((bf16[32,128]{1,0:T(8,128)(2,1)S(1)}, bf16[32,128]{1,0:T(8,128)(2,1)S(1)}, u32[]{:S(2)}, u32[]{:S(2)}) %collective-permute-start.2) | collective-permute-done | bytes 8224 | tf_op jit(solution)/shard_map/ppermute | solution.py:19
  29.4 54.5 %while.36 = (s32[]{:T(128)}, f32[32,9,8,2,128]{4,3,2,1,0:T(2,128)}, f32[8,5]{1,0:T(8,128)S(1)}, bf16[8,32,128]{2,1,0:T(8,128)(2,1)S(1)}, f32[8,3,128]{2,1,0:T(4,...) while((s32[]{:T(128)}, f32[32,9,8,2,128]{4,3,2,1,0:T(2,128)}, ...), condition=%wide.region_2.6_spmd.clone, body=%wide.region_0.5_spmd.clone.sunk | while | flops 80936976 | bytes 13649143 | solution.py:127
  30.1 0.9 fusion.141
  31.7 3.0 %select_add_fusion.2 = f32[32,9,8,2,128]{4,3,2,1,0:T(2,128)} fusion(f32[32,9,8,2,128]{4,3,2,1,0:T(2,128)} %get-tuple-element.744, pred[]{:T(512)S(6)} %compare.6, f32[32,9,8,128]{3,2,1,0:T(8,128)S(1)} %copy.221, f32[2]{0:T(128)S(1)} %slice_bitcast_fusion.4), kind=kLoop, calls=%fused_computation.127.clone.1 | loop fusion | flops 1769472 | bytes 5898249 | tf_op jit(solution)/shard_map/while/body/eval_jaxpr/add | solution.py:125
  35.4 0.9 fusion.141
  37.1 4.7 %select_add_fusion.2 = f32[32,9,8,2,128]{4,3,2,1,0:T(2,128)} fusion(f32[32,9,8,2,128]{4,3,2,1,0:T(2,128)} %get-tuple-element.744, pred[]{:T(512)S(6)} %compare.6, f32[32,9,8,128]{3,2,1,0:T(8,128)S(1)} %copy.221, f32[2]{0:T(128)S(1)} %slice_bitcast_fusion.4), kind=kLoop, calls=%fused_computation.127.clone.1 | loop fusion | flops 1769472 | bytes 5898249 | tf_op jit(solution)/shard_map/while/body/eval_jaxpr/add | solution.py:125
  42.4 0.9 fusion.141
  44.1 4.7 %select_add_fusion.2 = f32[32,9,8,2,128]{4,3,2,1,0:T(2,128)} fusion(f32[32,9,8,2,128]{4,3,2,1,0:T(2,128)} %get-tuple-element.744, pred[]{:T(512)S(6)} %compare.6, f32[32,9,8,128]{3,2,1,0:T(8,128)S(1)} %copy.221, f32[2]{0:T(128)S(1)} %slice_bitcast_fusion.4), kind=kLoop, calls=%fused_computation.127.clone.1 | loop fusion | flops 1769472 | bytes 5898249 | tf_op jit(solution)/shard_map/while/body/eval_jaxpr/add | solution.py:125
  49.5 0.9 fusion.141
  51.1 4.7 %select_add_fusion.2 = f32[32,9,8,2,128]{4,3,2,1,0:T(2,128)} fusion(f32[32,9,8,2,128]{4,3,2,1,0:T(2,128)} %get-tuple-element.744, pred[]{:T(512)S(6)} %compare.6, f32[32,9,8,128]{3,2,1,0:T(8,128)S(1)} %copy.221, f32[2]{0:T(128)S(1)} %slice_bitcast_fusion.4), kind=kLoop, calls=%fused_computation.127.clone.1 | loop fusion | flops 1769472 | bytes 5898249 | tf_op jit(solution)/shard_map/while/body/eval_jaxpr/add | solution.py:125
  56.5 0.9 fusion.141
  58.1 4.7 %select_add_fusion.2 = f32[32,9,8,2,128]{4,3,2,1,0:T(2,128)} fusion(f32[32,9,8,2,128]{4,3,2,1,0:T(2,128)} %get-tuple-element.744, pred[]{:T(512)S(6)} %compare.6, f32[32,9,8,128]{3,2,1,0:T(8,128)S(1)} %copy.221, f32[2]{0:T(128)S(1)} %slice_bitcast_fusion.4), kind=kLoop, calls=%fused_computation.127.clone.1 | loop fusion | flops 1769472 | bytes 5898249 | tf_op jit(solution)/shard_map/while/body/eval_jaxpr/add | solution.py:125
  63.5 0.9 fusion.141
  65.1 4.7 %select_add_fusion.2 = f32[32,9,8,2,128]{4,3,2,1,0:T(2,128)} fusion(f32[32,9,8,2,128]{4,3,2,1,0:T(2,128)} %get-tuple-element.744, pred[]{:T(512)S(6)} %compare.6, f32[32,9,8,128]{3,2,1,0:T(8,128)S(1)} %copy.221, f32[2]{0:T(128)S(1)} %slice_bitcast_fusion.4), kind=kLoop, calls=%fused_computation.127.clone.1 | loop fusion | flops 1769472 | bytes 5898249 | tf_op jit(solution)/shard_map/while/body/eval_jaxpr/add | solution.py:125
  70.5 0.9 fusion.141
  72.2 4.7 %select_add_fusion.2 = f32[32,9,8,2,128]{4,3,2,1,0:T(2,128)} fusion(f32[32,9,8,2,128]{4,3,2,1,0:T(2,128)} %get-tuple-element.744, pred[]{:T(512)S(6)} %compare.6, f32[32,9,8,128]{3,2,1,0:T(8,128)S(1)} %copy.221, f32[2]{0:T(128)S(1)} %slice_bitcast_fusion.4), kind=kLoop, calls=%fused_computation.127.clone.1 | loop fusion | flops 1769472 | bytes 5898249 | tf_op jit(solution)/shard_map/while/body/eval_jaxpr/add | solution.py:125
  77.5 0.9 fusion.141
  79.2 4.7 %select_add_fusion.2 = f32[32,9,8,2,128]{4,3,2,1,0:T(2,128)} fusion(f32[32,9,8,2,128]{4,3,2,1,0:T(2,128)} %get-tuple-element.744, pred[]{:T(512)S(6)} %compare.6, f32[32,9,8,128]{3,2,1,0:T(8,128)S(1)} %copy.221, f32[2]{0:T(128)S(1)} %slice_bitcast_fusion.4), kind=kLoop, calls=%fused_computation.127.clone.1 | loop fusion | flops 1769472 | bytes 5898249 | tf_op jit(solution)/shard_map/while/body/eval_jaxpr/add | solution.py:125
  83.9 3.3 %reshape.438 = bf16[32,9,8,256]{3,2,1,0:T(8,128)(2,1)S(1)} reshape(f32[32,9,8,2,128]{4,3,2,1,0:T(2,128)} %get-tuple-element.405) | data formatting | bytes 3538944 | tf_op jit(solution)/shard_map/reshape | solution.py:132
  87.7 7.5 %all_gather.6 = bf16[128,9,256]{2,0,1:T(8,128)(2,1)S(1)} all-gather(bf16[32,9,256]{2,0,1:T(8,128)(2,1)S(1)} %bitcast.408), channel_id=1, replica_groups=mesh['space'=8,'chan'=4] {'chan'}, dimensions={0}, use_global_device_ids=true | all-gather | bytes 737280 | tf_op jit(solution)/shard_map/all_gather | solution.py:137
  95.6 7.8 %all_gather.7 = bf16[128,9,256]{2,0,1:T(8,128)(2,1)S(1)} all-gather(bf16[32,9,256]{2,0,1:T(8,128)(2,1)S(1)} %pad_maximum_fusion.1), channel_id=1, replica_groups=mesh['space'=8,'chan'=4] {'chan'}, dimensions={0}, use_global_device_ids=true | all-gather | bytes 737280 | tf_op jit(solution)/shard_map/all_gather | solution.py:156
  104.6 1.5 collective-permute-start.11
  106.8 3.3 %gather_fusion.2 = bf16[8,32,9,8,128]{4,3,2,1,0:T(8,128)(2,1)} fusion(bf16[2,32,9,8,128]{4,3,2,1,0:T(8,128)(2,1)S(1)} %multiply_convert_fusion.3, s32[1024]{0:T(1024)S(1)} %pad_clamp_fusion), kind=kCustom, calls=%fused_computation.10 | custom fusion | bytes 9437216 | tf_op jit(solution)/shard_map/jit(_take)/gather | solution.py:170
  110.1 5.0 %broadcast_select_fusion = bf16[8,32,9,8,128]{4,3,2,1,0:T(8,128)(2,1)} fusion(bf16[8,32,9,8,128]{4,3,2,1,0:T(8,128)(2,1)} %gather_fusion.2, pred[8]{0:T(512)(128)(4,1)S(1)} %get-tuple-element.584), kind=kLoop, calls=%fused_computation.162 | loop fusion | flops 2359296 | bytes 9437192 | tf_op jit(solution)/shard_map/jit(_take)/select_n | solution.py:170
  115.0 50.7 %while.35 = (s32[]{:T(128)}, f32[8,32,128]{2,1,0:T(8,128)S(1)}, f32[8,3,128]{2,0,1:T(8,128)S(1)}, f32[8,3,128]{2,0,1:T(8,128)S(1)}, bf16[8,32,9,8,128]{4,3,2,1,0...) while((s32[]{:T(128)}, f32[8,32,128]{2,1,0:T(8,128)S(1)}, ...), condition=%wide.region_12.16_spmd, body=%wide.region_4.15_spmd.sunk | while | flops 162725520 | bytes 17160432 | solution.py:200
  115.7 1.1 fusion.131
  116.8 1.9 %multiply_reduce_fusion.7 = (f32[9,128,128]{2,1,0:T(8,128)S(1)}, f32[8,128,128]{2,1,0:T(8,128)S(1)}, bf16[9,8,128,128]{3,2,1,0:T(8,128)(2,1)S(1)}) fusion(f32[8,128,128]{2,1,0:T(8,128)S(1)} %fusion.130, f32[9,128,128]{2,1,0:T(8,128)S(1)} %get-tuple-element.711, bf16[8,32,128]{2,1,0:T(8,128)(2,1)S(1)} %get-tuple-element.791, s32[]{:T(128)} %get-tuple-element.772, ...), kind=kOutput, calls=%fused_computation.13.clone.1 | convolution fusion | flops 82296832 | bytes 5185540 | tf_op jit(solution)/shard_map/while/body/eval_jaxpr/clki,cj->lkij/dot_general | solution.py:182
  119.8 1.1 constant_dynamic-slice_fusion.4
  122.1 1.1 fusion.131
  123.2 1.9 %multiply_reduce_fusion.7 = (f32[9,128,128]{2,1,0:T(8,128)S(1)}, f32[8,128,128]{2,1,0:T(8,128)S(1)}, bf16[9,8,128,128]{3,2,1,0:T(8,128)(2,1)S(1)}) fusion(f32[8,128,128]{2,1,0:T(8,128)S(1)} %fusion.130, f32[9,128,128]{2,1,0:T(8,128)S(1)} %get-tuple-element.711, bf16[8,32,128]{2,1,0:T(8,128)(2,1)S(1)} %get-tuple-element.791, s32[]{:T(128)} %get-tuple-element.772, ...), kind=kOutput, calls=%fused_computation.13.clone.1 | convolution fusion | flops 82296832 | bytes 5185540 | tf_op jit(solution)/shard_map/while/body/eval_jaxpr/clki,cj->lkij/dot_general | solution.py:182
  126.1 1.1 constant_dynamic-slice_fusion.4
  128.4 1.1 fusion.131
  129.5 1.9 %multiply_reduce_fusion.7 = (f32[9,128,128]{2,1,0:T(8,128)S(1)}, f32[8,128,128]{2,1,0:T(8,128)S(1)}, bf16[9,8,128,128]{3,2,1,0:T(8,128)(2,1)S(1)}) fusion(f32[8,128,128]{2,1,0:T(8,128)S(1)} %fusion.130, f32[9,128,128]{2,1,0:T(8,128)S(1)} %get-tuple-element.711, bf16[8,32,128]{2,1,0:T(8,128)(2,1)S(1)} %get-tuple-element.791, s32[]{:T(128)} %get-tuple-element.772, ...), kind=kOutput, calls=%fused_computation.13.clone.1 | convolution fusion | flops 82296832 | bytes 5185540 | tf_op jit(solution)/shard_map/while/body/eval_jaxpr/clki,cj->lkij/dot_general | solution.py:182
  132.4 1.1 constant_dynamic-slice_fusion.4
  134.7 1.1 fusion.131
  135.9 1.9 %multiply_reduce_fusion.7 = (f32[9,128,128]{2,1,0:T(8,128)S(1)}, f32[8,128,128]{2,1,0:T(8,128)S(1)}, bf16[9,8,128,128]{3,2,1,0:T(8,128)(2,1)S(1)}) fusion(f32[8,128,128]{2,1,0:T(8,128)S(1)} %fusion.130, f32[9,128,128]{2,1,0:T(8,128)S(1)} %get-tuple-element.711, bf16[8,32,128]{2,1,0:T(8,128)(2,1)S(1)} %get-tuple-element.791, s32[]{:T(128)} %get-tuple-element.772, ...), kind=kOutput, calls=%fused_computation.13.clone.1 | convolution fusion | flops 82296832 | bytes 5185540 | tf_op jit(solution)/shard_map/while/body/eval_jaxpr/clki,cj->lkij/dot_general | solution.py:182
  138.8 1.1 constant_dynamic-slice_fusion.4
  141.1 1.1 fusion.131
  142.2 1.9 %multiply_reduce_fusion.7 = (f32[9,128,128]{2,1,0:T(8,128)S(1)}, f32[8,128,128]{2,1,0:T(8,128)S(1)}, bf16[9,8,128,128]{3,2,1,0:T(8,128)(2,1)S(1)}) fusion(f32[8,128,128]{2,1,0:T(8,128)S(1)} %fusion.130, f32[9,128,128]{2,1,0:T(8,128)S(1)} %get-tuple-element.711, bf16[8,32,128]{2,1,0:T(8,128)(2,1)S(1)} %get-tuple-element.791, s32[]{:T(128)} %get-tuple-element.772, ...), kind=kOutput, calls=%fused_computation.13.clone.1 | convolution fusion | flops 82296832 | bytes 5185540 | tf_op jit(solution)/shard_map/while/body/eval_jaxpr/clki,cj->lkij/dot_general | solution.py:182
  145.1 1.1 constant_dynamic-slice_fusion.4
  147.4 1.1 fusion.131
  148.5 1.9 %multiply_reduce_fusion.7 = (f32[9,128,128]{2,1,0:T(8,128)S(1)}, f32[8,128,128]{2,1,0:T(8,128)S(1)}, bf16[9,8,128,128]{3,2,1,0:T(8,128)(2,1)S(1)}) fusion(f32[8,128,128]{2,1,0:T(8,128)S(1)} %fusion.130, f32[9,128,128]{2,1,0:T(8,128)S(1)} %get-tuple-element.711, bf16[8,32,128]{2,1,0:T(8,128)(2,1)S(1)} %get-tuple-element.791, s32[]{:T(128)} %get-tuple-element.772, ...), kind=kOutput, calls=%fused_computation.13.clone.1 | convolution fusion | flops 82296832 | bytes 5185540 | tf_op jit(solution)/shard_map/while/body/eval_jaxpr/clki,cj->lkij/dot_general | solution.py:182
  151.5 1.1 constant_dynamic-slice_fusion.4
  153.8 1.1 fusion.131
  154.9 1.9 %multiply_reduce_fusion.7 = (f32[9,128,128]{2,1,0:T(8,128)S(1)}, f32[8,128,128]{2,1,0:T(8,128)S(1)}, bf16[9,8,128,128]{3,2,1,0:T(8,128)(2,1)S(1)}) fusion(f32[8,128,128]{2,1,0:T(8,128)S(1)} %fusion.130, f32[9,128,128]{2,1,0:T(8,128)S(1)} %get-tuple-element.711, bf16[8,32,128]{2,1,0:T(8,128)(2,1)S(1)} %get-tuple-element.791, s32[]{:T(128)} %get-tuple-element.772, ...), kind=kOutput, calls=%fused_computation.13.clone.1 | convolution fusion | flops 82296832 | bytes 5185540 | tf_op jit(solution)/shard_map/while/body/eval_jaxpr/clki,cj->lkij/dot_general | solution.py:182
  157.8 1.1 constant_dynamic-slice_fusion.4
  160.1 1.1 fusion.131
  161.2 1.9 %multiply_reduce_fusion.7 = (f32[9,128,128]{2,1,0:T(8,128)S(1)}, f32[8,128,128]{2,1,0:T(8,128)S(1)}, bf16[9,8,128,128]{3,2,1,0:T(8,128)(2,1)S(1)}) fusion(f32[8,128,128]{2,1,0:T(8,128)S(1)} %fusion.130, f32[9,128,128]{2,1,0:T(8,128)S(1)} %get-tuple-element.711, bf16[8,32,128]{2,1,0:T(8,128)(2,1)S(1)} %get-tuple-element.791, s32[]{:T(128)} %get-tuple-element.772, ...), kind=kOutput, calls=%fused_computation.13.clone.1 | convolution fusion | flops 82296832 | bytes 5185540 | tf_op jit(solution)/shard_map/while/body/eval_jaxpr/clki,cj->lkij/dot_general | solution.py:182
  164.1 1.1 constant_dynamic-slice_fusion.4
  166.1 1.6 collective-permute-start.12
  167.7 2.0 %collective-permute-done.12 = f32[32,8]{0,1:T(8,128)S(1)} collective-permute-done((f32[32,8]{0,1:T(8,128)S(1)}, f32[32,8]{0,1:T(8,128)S(1)}, u32[]{:S(2)}, u32[]{:S(2)}) %collective-permute-start.12) | collective-permute-done | bytes 1056 | tf_op jit(solution)/shard_map/ppermute | solution.py:19
  171.5 2.8 %collective-permute-done.13 = f32[32,8]{0,1:T(8,128)S(1)} collective-permute-done((f32[32,8]{0,1:T(8,128)S(1)}, f32[32,8]{0,1:T(8,128)S(1)}, u32[]{:S(2)}, u32[]{:S(2)}) %collective-permute-start.13) | collective-permute-done | bytes 1056 | tf_op jit(solution)/shard_map/ppermute | solution.py:19
  175.5 1.6 collective-permute-start.9
  177.1 1.6 collective-permute-start.10
  179.3 2.6 %collective-permute-done.10 = f32[35,128]{1,0:T(8,128)S(1)} collective-permute-done((f32[35,128]{1,0:T(8,128)S(1)}, f32[35,128]{1,0:T(8,128)S(1)}, u32[]{:S(2)}, u32[]{:S(2)}) %collective-permute-start.10) | collective-permute-done | bytes 17952 | tf_op jit(solution)/shard_map/ppermute | solution.py:19
  182.0 2.7 %scatter_fusion = f32[35,256]{0,1:T(8,128)S(1)} fusion(f32[35,256]{0,1:T(8,128)S(1)} %copy.162, s32[384]{0:T(512)S(1)} %fusion.93, f32[384,35]{1,0:T(8,128)S(1)} %copy.163), kind=kCustom, calls=%fused_computation.11 | custom fusion | flops 13440 | bytes 162816 | tf_op jit(solution)/shard_map/scatter-add | solution.py:222
  (446 shorter events, 48.8 us)
Async XLA Ops:
  0.6 22.8 %copy-start = (bf16[3,128,128]{2,1,0:T(8,128)(2,1)S(1)}, bf16[3,128,128]{2,1,0:T(8,128)(2,1)}, u32[]{:S(2)}) copy-start(bf16[3,128,128]{2,1,0:T(8,128)(2,1)} %param.25) | copy-start | bytes 294916
  0.6 23.7 %copy-start.2 = (f32[3,256]{1,0:T(4,128)S(1)}, f32[3,256]{1,0:T(4,128)}, u32[]{:S(2)}) copy-start(f32[3,256]{1,0:T(4,128)} %param.19) | copy-start | bytes 9220
  0.7 28.0 %copy-start.1 = (bf16[32,256]{1,0:T(8,128)(2,1)S(1)}, bf16[32,256]{1,0:T(8,128)(2,1)}, u32[]{:S(2)}) copy-start(bf16[32,256]{1,0:T(8,128)(2,1)} %param.20) | copy-start | bytes 49156
  3.1 21.0 %collective-permute-start.3 = (f32[3,128]{0,1:T(8,128)S(1)}, f32[3,128]{0,1:T(8,128)S(1)}, u32[]{:S(2)}, u32[]{:S(2)}) collective-permute-start(f32[3,128]{0,1:T(8,128)S(1)} %select_bitcast_fusion.2), channel_id=1, source_target_pairs={{0,4},{4,0},{8,12},{12,8},{16,20},{20,16},{24,28},{28,24},{1,5},{5... | collective-permute-start | bytes 4616 | tf_op jit(solution)/shard_map/ppermute | solution.py:19
  6.8 17.4 %collective-permute-start.4 = (f32[3,128]{0,1:T(8,128)S(1)}, f32[3,128]{0,1:T(8,128)S(1)}, u32[]{:S(2)}, u32[]{:S(2)}) collective-permute-start(f32[3,128]{0,1:T(8,128)S(1)} %select_bitcast_fusion.1), channel_id=1, source_target_pairs={{0,8},{4,12},{8,0},{12,4},{16,24},{20,28},{24,16},{28,20},{1,9},{5... | collective-permute-start | bytes 4616 | tf_op jit(solution)/shard_map/ppermute | solution.py:19
  9.2 15.1 %collective-permute-start.5 = (f32[3,128]{0,1:T(8,128)S(1)}, f32[3,128]{0,1:T(8,128)S(1)}, u32[]{:S(2)}, u32[]{:S(2)}) collective-permute-start(f32[3,128]{0,1:T(8,128)S(1)} %select_bitcast_fusion), channel_id=1, source_target_pairs={{0,16},{4,20},{8,24},{12,28},{16,0},{20,4},{24,8},{28,12},{1,17},{... | collective-permute-start | bytes 4616 | tf_op jit(solution)/shard_map/ppermute | solution.py:19
  13.5 12.2 %collective-permute-start = (bf16[32,128]{1,0:T(8,128)(2,1)S(1)}, bf16[32,128]{1,0:T(8,128)(2,1)S(1)}, u32[]{:S(2)}, u32[]{:S(2)}) collective-permute-start(bf16[32,128]{1,0:T(8,128)(2,1)S(1)} %bitcast_convert_fusion.3), channel_id=1, source_target_pairs={{0,4},{4,0},{8,12},{12,8},{16,20},{20,16},{24,28},{28,24},{1,5},{5... | collective-permute-start | bytes 24584 | tf_op jit(solution)/shard_map/ppermute | solution.py:19
  14.9 10.8 %collective-permute-start.1 = (bf16[32,128]{1,0:T(8,128)(2,1)S(1)}, bf16[32,128]{1,0:T(8,128)(2,1)S(1)}, u32[]{:S(2)}, u32[]{:S(2)}) collective-permute-start(bf16[32,128]{1,0:T(8,128)(2,1)S(1)} %bitcast_convert_fusion.2), channel_id=1, source_target_pairs={{0,8},{4,12},{8,0},{12,4},{16,24},{20,28},{24,16},{28,20},{1,9},{5... | collective-permute-start | bytes 24584 | tf_op jit(solution)/shard_map/ppermute | solution.py:19
  24.1 4.6 %collective-permute-start.2 = (bf16[32,128]{1,0:T(8,128)(2,1)S(1)}, bf16[32,128]{1,0:T(8,128)(2,1)S(1)}, u32[]{:S(2)}, u32[]{:S(2)}) collective-permute-start(bf16[32,128]{1,0:T(8,128)(2,1)S(1)} %bitcast_convert_fusion.1), channel_id=1, source_target_pairs={{0,16},{4,20},{8,24},{12,28},{16,0},{20,4},{24,8},{28,12},{1,17},{... | collective-permute-start | bytes 24584 | tf_op jit(solution)/shard_map/ppermute | solution.py:19
  104.6 61.5 %collective-permute-start.11 = (f32[32,8]{0,1:T(8,128)S(1)}, f32[32,8]{0,1:T(8,128)S(1)}, u32[]{:S(2)}, u32[]{:S(2)}) collective-permute-start(f32[32,8]{0,1:T(8,128)S(1)} %bitcast.413), channel_id=1, source_target_pairs={{0,4},{4,0},{8,12},{12,8},{16,20},{20,16},{24,28},{28,24},{1,5},{5... | collective-permute-start | bytes 3080 | tf_op jit(solution)/shard_map/ppermute | solution.py:19
  166.0 4.1 %collective-permute-start.6 = (f32[3,640]{1,0:T(4,128)S(1)}, f32[3,640]{1,0:T(4,128)S(1)}, u32[]{:S(2)}, u32[]{:S(2)}) collective-permute-start(f32[3,640]{1,0:T(4,128)S(1)} %bitcast.414), channel_id=1, source_target_pairs={{0,1},{1,0},{2,3},{3,2},{4,5},{5,4},{6,7},{7,6},{8,9},{9,8},{10,11... | collective-permute-start | bytes 23048 | tf_op jit(solution)/shard_map/ppermute | solution.py:19
  166.1 3.6 %collective-permute-start.12 = (f32[32,8]{0,1:T(8,128)S(1)}, f32[32,8]{0,1:T(8,128)S(1)}, u32[]{:S(2)}, u32[]{:S(2)}) collective-permute-start(f32[32,8]{0,1:T(8,128)S(1)} %bitcast_add_fusion), channel_id=1, source_target_pairs={{0,8},{4,12},{8,0},{12,4},{16,24},{20,28},{24,16},{28,20},{1,9},{5... | collective-permute-start | bytes 3080 | tf_op jit(solution)/shard_map/ppermute | solution.py:19
  169.8 4.5 %collective-permute-start.13 = (f32[32,8]{0,1:T(8,128)S(1)}, f32[32,8]{0,1:T(8,128)S(1)}, u32[]{:S(2)}, u32[]{:S(2)}) collective-permute-start(f32[32,8]{0,1:T(8,128)S(1)} %add.378), channel_id=1, source_target_pairs={{0,16},{4,20},{8,24},{12,28},{16,0},{20,4},{24,8},{28,12},{1,17},{... | collective-permute-start | bytes 3080 | tf_op jit(solution)/shard_map/ppermute | solution.py:19
  170.1 4.8 %collective-permute-start.7 = (f32[3,640]{1,0:T(4,128)S(1)}, f32[3,640]{1,0:T(4,128)S(1)}, u32[]{:S(2)}, u32[]{:S(2)}) collective-permute-start(f32[3,640]{1,0:T(4,128)S(1)} %fusion.108), channel_id=1, source_target_pairs={{0,2},{1,3},{2,0},{3,1},{4,6},{5,7},{6,4},{7,5},{8,10},{9,11},{10,... | collective-permute-start | bytes 23048 | tf_op jit(solution)/shard_map/ppermute | solution.py:19
  174.9 3.8 %collective-permute-start.8 = (f32[35,128]{1,0:T(8,128)S(1)}, f32[35,128]{1,0:T(8,128)S(1)}, u32[]{:S(2)}, u32[]{:S(2)}) collective-permute-start(f32[35,128]{1,0:T(8,128)S(1)} %pad_maximum_fusion.3), channel_id=1, source_target_pairs={{0,4},{4,0},{8,12},{12,8},{16,20},{20,16},{24,28},{28,24},{1,5},{5... | collective-permute-start | bytes 53768 | tf_op jit(solution)/shard_map/ppermute | solution.py:19
  175.5 3.8 %collective-permute-start.9 = (f32[35,128]{1,0:T(8,128)S(1)}, f32[35,128]{1,0:T(8,128)S(1)}, u32[]{:S(2)}, u32[]{:S(2)}) collective-permute-start(f32[35,128]{1,0:T(8,128)S(1)} %pad_maximum_fusion.4), channel_id=1, source_target_pairs={{0,8},{4,12},{8,0},{12,4},{16,24},{20,28},{24,16},{28,20},{1,9},{5... | collective-permute-start | bytes 53768 | tf_op jit(solution)/shard_map/ppermute | solution.py:19
  177.1 4.8 %collective-permute-start.10 = (f32[35,128]{1,0:T(8,128)S(1)}, f32[35,128]{1,0:T(8,128)S(1)}, u32[]{:S(2)}, u32[]{:S(2)}) collective-permute-start(f32[35,128]{1,0:T(8,128)S(1)} %pad_maximum_fusion.5), channel_id=1, source_target_pairs={{0,16},{4,20},{8,24},{12,28},{16,0},{20,4},{24,8},{28,12},{1,17},{... | collective-permute-start | bytes 53768 | tf_op jit(solution)/shard_map/ppermute | solution.py:19

commit v3 on v2

--- a/solution.py
+++ b/solution.py
@@ -96,9 +96,9 @@
     keep_all = live[:, None, None] * (1.0 - same[:, None, None] * eye[None])
     pos_blocks = jnp.moveaxis(src_pos.reshape(3, src_blocks, block_size), 1, 0)
     feat_blocks = jnp.moveaxis(src_feat.reshape(chan_dev, src_blocks, block_size), 1, 0)
-    target_pos_all = jnp.take(pos_blocks, target_idx, axis=0)
-    source_pos_all = jnp.take(pos_blocks, source_idx, axis=0)
-    source_feat_all = jnp.take(feat_blocks, source_idx, axis=0)
+    target_pos_all = jnp.take(pos_blocks, target_idx, axis=0, mode="clip")
+    source_pos_all = jnp.take(pos_blocks, source_idx, axis=0, mode="clip")
+    source_feat_all = jnp.take(feat_blocks, source_idx, axis=0, mode="clip")
 
     def pick(array, tile_index):
         return lax.dynamic_index_in_dim(array, tile_index, 0, keepdims=False)
@@ -122,15 +122,17 @@
             "lkij,cj->clki", pair_values, source_feat, preferred_element_type=jnp.float32
         )
         hot = pick(target_hot, tile_index)[:own_blocks]
-        return msg_acc + hot[None, None, None, :, None] * message[:, :, :, None, :]
+        return msg_acc + hot[:, None, None, None, None] * message[None]
 
     msg_acc = lax.fori_loop(
         0,
         tile_count,
         forward_tile,
-        jnp.zeros((chan_dev, components, radial_count, own_blocks, block_size), jnp.float32),
-    ).reshape(chan_dev, components, radial_count, atoms_dev)
-    moments = jnp.einsum("clki,ck->cli", msg_acc, radial_weight)
+        jnp.zeros((own_blocks, chan_dev, components, radial_count, block_size), jnp.float32),
+    )
+    moments = jnp.einsum("bclki,ck->clbi", msg_acc, radial_weight).reshape(
+        chan_dev, components, atoms_dev
+    )
     packed = moments.astype(jnp.bfloat16)
     mixing = jnp.take(mix_weight, jnp.array(ORDER_OF, dtype=jnp.int32), axis=0)
     offset = lax.axis_index("chan") * chan_dev
@@ -160,21 +162,21 @@
     moment_grad_all = jnp.einsum(
         "lxc,xli->cli", weight_part, gathered_piece, preferred_element_type=jnp.float32
     )
-    grad_rad = jnp.einsum("clki,cli->ck", msg_acc, moment_grad_all)
-    weighted_all = (radial_weight[:, None, :, None] * moment_grad_all[:, :, None, :]).astype(
-        jnp.bfloat16
-    )
-    weighted_blocks = jnp.moveaxis(
-        weighted_all.reshape(chan_dev, components, radial_count, own_blocks, block_size), 3, 0
-    )
-    weighted_tiles = jnp.take(weighted_blocks, jnp.minimum(target_idx, own_blocks - 1), axis=0)
+    grad_blocks = jnp.moveaxis(
+        moment_grad_all.reshape(chan_dev, components, own_blocks, block_size), 2, 0
+    )
+    grad_rad = jnp.einsum("bclki,bcli->ck", msg_acc, grad_blocks)
+    grad_tiles_in = jnp.take(grad_blocks, target_idx, axis=0, mode="clip")
 
     def backward_tile(tile_index, running):
         grad_tiles, target_grads, source_grads = running
         target_pos, source_pos, geo_fn = tile_parts(tile_index)
         (harmonics, radial), pullback = jax.vjp(geo_fn, target_pos, source_pos)
         source_feat = pick(source_feat_all, tile_index)
-        weighted = pick(weighted_tiles, tile_index)
+        moment_grad = pick(grad_tiles_in, tile_index)
+        weighted = (radial_weight[:, None, :, None] * moment_grad[:, :, None, :]).astype(
+            jnp.bfloat16
+        )
         pair_values = (harmonics[:, None] * radial[None]).astype(jnp.bfloat16)
         grad_source = jnp.einsum(
             "clki,lkij->cj", weighted, pair_values, preferred_element_type=jnp.float32

time: 188 us -> 171 us (0.910)
  matrix products: 28 us -> 52.4 us
  local copies, waits for them, and re-layouts: 43.3 us -> 19.5 us
  other arithmetic: 68.7 us -> 51.5 us
    dot_general x8, matrix products: 3.66 us -> 17.4 us  [backward_tile(): jnp.einsum('clki,lkij->cj', weighted, pair_values, preferred_element_type...]
    add x8, other arithmetic: 35.8 us -> 25.4 us  [forward_tile(): return msg_acc + hot[:, None, None, None, None] * message[None]]
    squeeze x8 -> x0, local copies, waits for them, and re-layouts: 8.93 us -> none  [pick(): return lax.dynamic_index_in_dim(array, tile_index, 0, keepdims=False)]
    dynamic_slice x16 -> x8, local copies, waits for them, and re-layouts: 9.01 us -> 0.08 us  [pick(): return lax.dynamic_index_in_dim(array, tile_index, 0, keepdims=False)]
    dot_general x8, matrix products: 15.2 us -> 24.1 us  [backward_tile(): jnp.einsum('clki,cj->lkij', weighted, source_feat, preferred_element_type...]
    select_n x3 -> x0, other arithmetic: 5.13 us -> none  [the longest x1 4.97 us: body(): jnp.take(weighted_blocks, jnp.minimum(target_idx, own_blocks - 1), axis=0)]
    reshape x1 -> x2, local copies, waits for them, and re-layouts: 3.34 us -> 0.05 us  [body(): moment_grad_all.reshape(chan_dev, components, own_blocks, block_size)]
    gather x4, local copies, waits for them, and re-layouts: 4.99 us -> 2.34 us  [the longest x1 0.62 us: body(): grad_tiles_in = jnp.take(grad_blocks, target_idx, axis=0, mode='clip')]
  transfers between devices with their start and end apart: 14 -> 14, of which waited for: 5 -> 5; matrix products, arithmetic and copies ran while one was open for 40% -> 41% of each run, Pallas kernels for 0% -> 0%
where the time goes in v3:
time: 171 us; the launch traced here: 170 us
  matrix products  52.4 us (31%)
  other arithmetic  51.5 us (30%)
  local copies, waits for them, and re-layouts  19.5 us (11%)
  starting transfers between devices  16.5 us (10%)
  blocking collectives  15.3 us (9%)
  waiting for transfers between devices  11 us (6%)
  loops' own time  2.34 us (1%)
    add x8, other arithmetic, forward_tile(): return msg_acc + hot[:, None, None, None, None] * message[None]  25.4 us
    dot_general x8, matrix products, backward_tile(): jnp.einsum('clki,cj->lkij', weighted, source_feat, preferred_element_type...  24.1 us
    dot_general x8, matrix products, backward_tile(): jnp.einsum('clki,lkij->cj', weighted, pair_values, preferred_element_type...  17.4 us
    ppermute x14, starting transfers between devices, partner(): return lax.ppermute(value, axis, pairs)  16.5 us
    ppermute x14, waiting for transfers between devices, partner(): return lax.ppermute(value, axis, pairs)  11 us
    all_gather x1, blocking collectives, body(): gathered_piece = lax.all_gather(dz_packed, 'chan', axis=0, tiled=True)  7.78 us
    all_gather x1, blocking collectives, body(): gathered_piece = lax.all_gather(packed, 'chan', axis=0, tiled=True)  7.53 us
    dot_general x8, matrix products, forward_tile(): jnp.einsum('lkij,cj->clki', pair_values, source_feat, preferred_element_t...  7.31 us
  transfers between devices with their start and end apart: 14, of which 5 were waited for; matrix products, arithmetic and copies ran while one was open for 41% of the time, Pallas kernels for 0%

profile of v3, /device:TPU:0, one launch (start us, length us, event | category | flops | bytes accessed | tf_op | source)
XLA Modules:
  0.0 169.6 jit_solution(14007038120060681130)
XLA Ops:
  0.7 0.8 compare_and_fusion.2
  1.5 0.8 copy.136
  3.1 3.0 %collective-permute-start.3 = (f32[3,128]{0,1:T(8,128)S(1)}, f32[3,128]{0,1:T(8,128)S(1)}, u32[]{:S(2)}, u32[]{:S(2)}) collective-permute-start(f32[3,128]{0,1:T(8,128)S(1)} %select_bitcast_fusion.2), channel_id=1, source_target_pairs={{0,4},{4,0},{8,12},{12,8},{16,20},{20,16},{24,28},{28,24},{1,5},{5... | collective-permute-start | bytes 4616 | tf_op jit(solution)/shard_map/ppermute | solution.py:19
  6.8 1.6 collective-permute-start.4
  9.2 2.7 %collective-permute-start.5 = (f32[3,128]{0,1:T(8,128)S(1)}, f32[3,128]{0,1:T(8,128)S(1)}, u32[]{:S(2)}, u32[]{:S(2)}) collective-permute-start(f32[3,128]{0,1:T(8,128)S(1)} %select_bitcast_fusion), channel_id=1, source_target_pairs={{0,16},{4,20},{8,24},{12,28},{16,0},{20,4},{24,8},{28,12},{1,17},{... | collective-permute-start | bytes 4616 | tf_op jit(solution)/shard_map/ppermute | solution.py:19
  11.9 0.8 copy.129
  12.7 0.7 gather_fusion.5
  14.1 0.7 gather_fusion.6
  15.4 0.7 gather_fusion.7
  16.1 0.8 slice_bitcast_fusion.1
  16.9 0.8 compare_convert_fusion
  18.5 0.7 fusion.95
  20.0 0.8 copy.158
  20.8 0.9 convert_element_type.94
  24.0 3.1 %collective-permute-done.2 = bf16[32,128]{1,0:T(8,128)(2,1)S(1)} collective-permute-done((bf16[32,128]{1,0:T(8,128)(2,1)S(1)}, bf16[32,128]{1,0:T(8,128)(2,1)S(1)}, u32[]{:S(2)}, u32[]{:S(2)}) %collective-permute-start.2) | collective-permute-done | bytes 8224 | tf_op jit(solution)/shard_map/ppermute | solution.py:19
  27.7 44.0 %while.36 = (s32[]{:T(128)}, f32[2,32,9,8,128]{4,3,2,1,0:T(8,128)}, f32[8,5]{1,0:T(8,128)S(1)}, bf16[8,32,128]{2,1,0:T(8,128)(2,1)S(1)}, f32[8,3,128]{2,1,0:T(4,...) while((s32[]{:T(128)}, f32[2,32,9,8,128]{4,3,2,1,0:T(8,128)}, ...), condition=%wide.region_2.5_spmd.clone, body=%wide.region_0.4_spmd.clone.sunk | while | flops 80936976 | bytes 13649143 | solution.py:127
  28.4 0.9 fusion.138
  29.3 0.7 copy.211
  30.0 1.7 %select_add_fusion.2 = f32[2,32,9,8,128]{4,3,2,1,0:T(8,128)} fusion(f32[2,32,9,8,128]{4,3,2,1,0:T(8,128)} %get-tuple-element.716, f32[32,9,8,128]{3,2,1,0:T(8,128)S(1)} %copy.211, f32[2]{0:T(128)S(1)} %slice_bitcast_fusion.4, pred[]{:T(512)S(6)} %compare.6), kind=kLoop, calls=%fused_computation.127.clone.1 | loop fusion | flops 1769472 | bytes 5898249 | tf_op jit(solution)/shard_map/while/body/eval_jaxpr/add | solution.py:125
  32.4 0.9 fusion.138
  34.1 3.4 %select_add_fusion.2 = f32[2,32,9,8,128]{4,3,2,1,0:T(8,128)} fusion(f32[2,32,9,8,128]{4,3,2,1,0:T(8,128)} %get-tuple-element.716, f32[32,9,8,128]{3,2,1,0:T(8,128)S(1)} %copy.211, f32[2]{0:T(128)S(1)} %slice_bitcast_fusion.4, pred[]{:T(512)S(6)} %compare.6), kind=kLoop, calls=%fused_computation.127.clone.1 | loop fusion | flops 1769472 | bytes 5898249 | tf_op jit(solution)/shard_map/while/body/eval_jaxpr/add | solution.py:125
  38.2 0.9 fusion.138
  39.8 3.4 %select_add_fusion.2 = f32[2,32,9,8,128]{4,3,2,1,0:T(8,128)} fusion(f32[2,32,9,8,128]{4,3,2,1,0:T(8,128)} %get-tuple-element.716, f32[32,9,8,128]{3,2,1,0:T(8,128)S(1)} %copy.211, f32[2]{0:T(128)S(1)} %slice_bitcast_fusion.4, pred[]{:T(512)S(6)} %compare.6), kind=kLoop, calls=%fused_computation.127.clone.1 | loop fusion | flops 1769472 | bytes 5898249 | tf_op jit(solution)/shard_map/while/body/eval_jaxpr/add | solution.py:125
  43.9 0.9 fusion.138
  45.5 3.4 %select_add_fusion.2 = f32[2,32,9,8,128]{4,3,2,1,0:T(8,128)} fusion(f32[2,32,9,8,128]{4,3,2,1,0:T(8,128)} %get-tuple-element.716, f32[32,9,8,128]{3,2,1,0:T(8,128)S(1)} %copy.211, f32[2]{0:T(128)S(1)} %slice_bitcast_fusion.4, pred[]{:T(512)S(6)} %compare.6), kind=kLoop, calls=%fused_computation.127.clone.1 | loop fusion | flops 1769472 | bytes 5898249 | tf_op jit(solution)/shard_map/while/body/eval_jaxpr/add | solution.py:125
  49.6 0.9 fusion.138
  51.2 3.4 %select_add_fusion.2 = f32[2,32,9,8,128]{4,3,2,1,0:T(8,128)} fusion(f32[2,32,9,8,128]{4,3,2,1,0:T(8,128)} %get-tuple-element.716, f32[32,9,8,128]{3,2,1,0:T(8,128)S(1)} %copy.211, f32[2]{0:T(128)S(1)} %slice_bitcast_fusion.4, pred[]{:T(512)S(6)} %compare.6), kind=kLoop, calls=%fused_computation.127.clone.1 | loop fusion | flops 1769472 | bytes 5898249 | tf_op jit(solution)/shard_map/while/body/eval_jaxpr/add | solution.py:125
  55.3 0.9 fusion.138
  56.9 3.4 %select_add_fusion.2 = f32[2,32,9,8,128]{4,3,2,1,0:T(8,128)} fusion(f32[2,32,9,8,128]{4,3,2,1,0:T(8,128)} %get-tuple-element.716, f32[32,9,8,128]{3,2,1,0:T(8,128)S(1)} %copy.211, f32[2]{0:T(128)S(1)} %slice_bitcast_fusion.4, pred[]{:T(512)S(6)} %compare.6), kind=kLoop, calls=%fused_computation.127.clone.1 | loop fusion | flops 1769472 | bytes 5898249 | tf_op jit(solution)/shard_map/while/body/eval_jaxpr/add | solution.py:125
  61.0 0.9 fusion.138
  62.6 3.4 %select_add_fusion.2 = f32[2,32,9,8,128]{4,3,2,1,0:T(8,128)} fusion(f32[2,32,9,8,128]{4,3,2,1,0:T(8,128)} %get-tuple-element.716, f32[32,9,8,128]{3,2,1,0:T(8,128)S(1)} %copy.211, f32[2]{0:T(128)S(1)} %slice_bitcast_fusion.4, pred[]{:T(512)S(6)} %compare.6), kind=kLoop, calls=%fused_computation.127.clone.1 | loop fusion | flops 1769472 | bytes 5898249 | tf_op jit(solution)/shard_map/while/body/eval_jaxpr/add | solution.py:125
  66.7 0.9 fusion.138
  68.3 3.4 %select_add_fusion.2 = f32[2,32,9,8,128]{4,3,2,1,0:T(8,128)} fusion(f32[2,32,9,8,128]{4,3,2,1,0:T(8,128)} %get-tuple-element.716, f32[32,9,8,128]{3,2,1,0:T(8,128)S(1)} %copy.211, f32[2]{0:T(128)S(1)} %slice_bitcast_fusion.4, pred[]{:T(512)S(6)} %compare.6), kind=kLoop, calls=%fused_computation.127.clone.1 | loop fusion | flops 1769472 | bytes 5898249 | tf_op jit(solution)/shard_map/while/body/eval_jaxpr/add | solution.py:125
  71.7 2.1 %fusion.79 = bf16[32,1,2,9,128]{4,1,3,2,0:T(2,128)(2,1)S(1)} fusion(bf16[32,8,1,1,1]{1,2,4,3,0:T(2,128)(2,1)S(1)} %copy.158, f32[2,32,9,8,128]{4,3,2,1,0:T(8,128)} %get-tuple-element.426), kind=kOutput, calls=%fused_computation.162 | convolution fusion | flops 1179648 | bytes 2507264 | tf_op jit(solution)/shard_map/bclki,ck->clbi/dot_general | solution.py:133
  74.1 7.5 %all_gather.6 = bf16[128,9,256]{2,0,1:T(8,128)(2,1)S(1)} all-gather(bf16[32,9,256]{2,0,1:T(8,128)(2,1)S(1)} %convert_element_type.93), channel_id=1, replica_groups=mesh['space'=8,'chan'=4] {'chan'}, dimensions={0}, use_global_device_ids=true | all-gather | bytes 737280 | tf_op jit(solution)/shard_map/all_gather | solution.py:139
  82.0 7.8 %all_gather.7 = bf16[128,9,256]{2,0,1:T(8,128)(2,1)S(1)} all-gather(bf16[32,9,256]{2,0,1:T(8,128)(2,1)S(1)} %pad_maximum_fusion.1), channel_id=1, replica_groups=mesh['space'=8,'chan'=4] {'chan'}, dimensions={0}, use_global_device_ids=true | all-gather | bytes 737280 | tf_op jit(solution)/shard_map/all_gather | solution.py:158
  90.3 0.8 fusion.81
  91.2 1.5 collective-permute-start.11
  93.4 55.8 %while.35 = (s32[]{:T(128)}, f32[8,32,128]{2,1,0:T(8,128)S(1)}, f32[8,3,128]{2,0,1:T(8,128)S(1)}, f32[8,3,128]{2,0,1:T(8,128)S(1)}, f32[32,8]{0,1:T(8,128)S(1)},...) while((s32[]{:T(128)}, f32[8,32,128]{2,1,0:T(8,128)S(1)}, ...), condition=%wide.region_12.15_spmd, body=%wide.region_4.0_spmd.sunk | while | flops 163905168 | bytes 14219509 | solution.py:202
  94.1 3.0 %multiply_reduce_fusion.7 = (f32[9,128,128]{2,1,0:T(8,128)S(1)}, f32[8,128,128]{2,1,0:T(8,128)S(1)}, bf16[9,8,128,128]{3,2,1,0:T(8,128)(2,1)}) fusion(f32[8,128,128]{2,1,0:T(8,128)S(1)} %fusion.128, f32[9,128,128]{2,1,0:T(8,128)S(1)} %get-tuple-element.683, bf16[8,32,128]{2,1,0:T(8,128)(2,1)S(1)} %get-tuple-element.766, s32[]{:T(128)} %get-tuple-element.745, ...), kind=kOutput, calls=%fused_computation.13.clone.1 | convolution fusion | flops 82886656 | bytes 4747268 | tf_op jit(solution)/shard_map/while/body/eval_jaxpr/clki,cj->lkij/dot_general | solution.py:184
  98.1 2.2 %fusion.129 = f32[8,32,128]{2,1,0:T(8,128)S(1)} fusion(f32[8,32,128]{2,1,0:T(8,128)S(1)} %get-tuple-element.746, s32[]{:T(128)} %get-tuple-element.745, bf16[9,8,128,128]{3,2,1,0:T(8,128)(2,1)} %get-tuple-element.684, f32[32,9,128]{2,0,1:T(8,128)S(1)} %dynamic-slice_bitcast_fusion.9, f32[32,8]{0,1:T(8,128)S(1)} %get-tuple-element.761), kind=kOutput, calls=%fused_computation.19.clone.1 | convolution fusion | flops 76087296 | bytes 2527236 | tf_op jit(solution)/shard_map/while/body/eval_jaxpr/clki,lkij->cj/dot_general | solution.py:181
  101.1 3.0 %multiply_reduce_fusion.7 = (f32[9,128,128]{2,1,0:T(8,128)S(1)}, f32[8,128,128]{2,1,0:T(8,128)S(1)}, bf16[9,8,128,128]{3,2,1,0:T(8,128)(2,1)}) fusion(f32[8,128,128]{2,1,0:T(8,128)S(1)} %fusion.128, f32[9,128,128]{2,1,0:T(8,128)S(1)} %get-tuple-element.683, bf16[8,32,128]{2,1,0:T(8,128)(2,1)S(1)} %get-tuple-element.766, s32[]{:T(128)} %get-tuple-element.745, ...), kind=kOutput, calls=%fused_computation.13.clone.1 | convolution fusion | flops 82886656 | bytes 4747268 | tf_op jit(solution)/shard_map/while/body/eval_jaxpr/clki,cj->lkij/dot_general | solution.py:184
  105.1 2.2 %fusion.129 = f32[8,32,128]{2,1,0:T(8,128)S(1)} fusion(f32[8,32,128]{2,1,0:T(8,128)S(1)} %get-tuple-element.746, s32[]{:T(128)} %get-tuple-element.745, bf16[9,8,128,128]{3,2,1,0:T(8,128)(2,1)} %get-tuple-element.684, f32[32,9,128]{2,0,1:T(8,128)S(1)} %dynamic-slice_bitcast_fusion.9, f32[32,8]{0,1:T(8,128)S(1)} %get-tuple-element.761), kind=kOutput, calls=%fused_computation.19.clone.1 | convolution fusion | flops 76087296 | bytes 2527236 | tf_op jit(solution)/shard_map/while/body/eval_jaxpr/clki,lkij->cj/dot_general | solution.py:181
  108.1 3.0 %multiply_reduce_fusion.7 = (f32[9,128,128]{2,1,0:T(8,128)S(1)}, f32[8,128,128]{2,1,0:T(8,128)S(1)}, bf16[9,8,128,128]{3,2,1,0:T(8,128)(2,1)}) fusion(f32[8,128,128]{2,1,0:T(8,128)S(1)} %fusion.128, f32[9,128,128]{2,1,0:T(8,128)S(1)} %get-tuple-element.683, bf16[8,32,128]{2,1,0:T(8,128)(2,1)S(1)} %get-tuple-element.766, s32[]{:T(128)} %get-tuple-element.745, ...), kind=kOutput, calls=%fused_computation.13.clone.1 | convolution fusion | flops 82886656 | bytes 4747268 | tf_op jit(solution)/shard_map/while/body/eval_jaxpr/clki,cj->lkij/dot_general | solution.py:184
  112.1 2.2 %fusion.129 = f32[8,32,128]{2,1,0:T(8,128)S(1)} fusion(f32[8,32,128]{2,1,0:T(8,128)S(1)} %get-tuple-element.746, s32[]{:T(128)} %get-tuple-element.745, bf16[9,8,128,128]{3,2,1,0:T(8,128)(2,1)} %get-tuple-element.684, f32[32,9,128]{2,0,1:T(8,128)S(1)} %dynamic-slice_bitcast_fusion.9, f32[32,8]{0,1:T(8,128)S(1)} %get-tuple-element.761), kind=kOutput, calls=%fused_computation.19.clone.1 | convolution fusion | flops 76087296 | bytes 2527236 | tf_op jit(solution)/shard_map/while/body/eval_jaxpr/clki,lkij->cj/dot_general | solution.py:181
  115.0 3.0 %multiply_reduce_fusion.7 = (f32[9,128,128]{2,1,0:T(8,128)S(1)}, f32[8,128,128]{2,1,0:T(8,128)S(1)}, bf16[9,8,128,128]{3,2,1,0:T(8,128)(2,1)}) fusion(f32[8,128,128]{2,1,0:T(8,128)S(1)} %fusion.128, f32[9,128,128]{2,1,0:T(8,128)S(1)} %get-tuple-element.683, bf16[8,32,128]{2,1,0:T(8,128)(2,1)S(1)} %get-tuple-element.766, s32[]{:T(128)} %get-tuple-element.745, ...), kind=kOutput, calls=%fused_computation.13.clone.1 | convolution fusion | flops 82886656 | bytes 4747268 | tf_op jit(solution)/shard_map/while/body/eval_jaxpr/clki,cj->lkij/dot_general | solution.py:184
  119.1 2.2 %fusion.129 = f32[8,32,128]{2,1,0:T(8,128)S(1)} fusion(f32[8,32,128]{2,1,0:T(8,128)S(1)} %get-tuple-element.746, s32[]{:T(128)} %get-tuple-element.745, bf16[9,8,128,128]{3,2,1,0:T(8,128)(2,1)} %get-tuple-element.684, f32[32,9,128]{2,0,1:T(8,128)S(1)} %dynamic-slice_bitcast_fusion.9, f32[32,8]{0,1:T(8,128)S(1)} %get-tuple-element.761), kind=kOutput, calls=%fused_computation.19.clone.1 | convolution fusion | flops 76087296 | bytes 2527236 | tf_op jit(solution)/shard_map/while/body/eval_jaxpr/clki,lkij->cj/dot_general | solution.py:181
  122.0 3.0 %multiply_reduce_fusion.7 = (f32[9,128,128]{2,1,0:T(8,128)S(1)}, f32[8,128,128]{2,1,0:T(8,128)S(1)}, bf16[9,8,128,128]{3,2,1,0:T(8,128)(2,1)}) fusion(f32[8,128,128]{2,1,0:T(8,128)S(1)} %fusion.128, f32[9,128,128]{2,1,0:T(8,128)S(1)} %get-tuple-element.683, bf16[8,32,128]{2,1,0:T(8,128)(2,1)S(1)} %get-tuple-element.766, s32[]{:T(128)} %get-tuple-element.745, ...), kind=kOutput, calls=%fused_computation.13.clone.1 | convolution fusion | flops 82886656 | bytes 4747268 | tf_op jit(solution)/shard_map/while/body/eval_jaxpr/clki,cj->lkij/dot_general | solution.py:184
  126.0 2.2 %fusion.129 = f32[8,32,128]{2,1,0:T(8,128)S(1)} fusion(f32[8,32,128]{2,1,0:T(8,128)S(1)} %get-tuple-element.746, s32[]{:T(128)} %get-tuple-element.745, bf16[9,8,128,128]{3,2,1,0:T(8,128)(2,1)} %get-tuple-element.684, f32[32,9,128]{2,0,1:T(8,128)S(1)} %dynamic-slice_bitcast_fusion.9, f32[32,8]{0,1:T(8,128)S(1)} %get-tuple-element.761), kind=kOutput, calls=%fused_computation.19.clone.1 | convolution fusion | flops 76087296 | bytes 2527236 | tf_op jit(solution)/shard_map/while/body/eval_jaxpr/clki,lkij->cj/dot_general | solution.py:181
  129.0 3.0 %multiply_reduce_fusion.7 = (f32[9,128,128]{2,1,0:T(8,128)S(1)}, f32[8,128,128]{2,1,0:T(8,128)S(1)}, bf16[9,8,128,128]{3,2,1,0:T(8,128)(2,1)}) fusion(f32[8,128,128]{2,1,0:T(8,128)S(1)} %fusion.128, f32[9,128,128]{2,1,0:T(8,128)S(1)} %get-tuple-element.683, bf16[8,32,128]{2,1,0:T(8,128)(2,1)S(1)} %get-tuple-element.766, s32[]{:T(128)} %get-tuple-element.745, ...), kind=kOutput, calls=%fused_computation.13.clone.1 | convolution fusion | flops 82886656 | bytes 4747268 | tf_op jit(solution)/shard_map/while/body/eval_jaxpr/clki,cj->lkij/dot_general | solution.py:184
  133.0 2.2 %fusion.129 = f32[8,32,128]{2,1,0:T(8,128)S(1)} fusion(f32[8,32,128]{2,1,0:T(8,128)S(1)} %get-tuple-element.746, s32[]{:T(128)} %get-tuple-element.745, bf16[9,8,128,128]{3,2,1,0:T(8,128)(2,1)} %get-tuple-element.684, f32[32,9,128]{2,0,1:T(8,128)S(1)} %dynamic-slice_bitcast_fusion.9, f32[32,8]{0,1:T(8,128)S(1)} %get-tuple-element.761), kind=kOutput, calls=%fused_computation.19.clone.1 | convolution fusion | flops 76087296 | bytes 2527236 | tf_op jit(solution)/shard_map/while/body/eval_jaxpr/clki,lkij->cj/dot_general | solution.py:181
  135.9 3.0 %multiply_reduce_fusion.7 = (f32[9,128,128]{2,1,0:T(8,128)S(1)}, f32[8,128,128]{2,1,0:T(8,128)S(1)}, bf16[9,8,128,128]{3,2,1,0:T(8,128)(2,1)}) fusion(f32[8,128,128]{2,1,0:T(8,128)S(1)} %fusion.128, f32[9,128,128]{2,1,0:T(8,128)S(1)} %get-tuple-element.683, bf16[8,32,128]{2,1,0:T(8,128)(2,1)S(1)} %get-tuple-element.766, s32[]{:T(128)} %get-tuple-element.745, ...), kind=kOutput, calls=%fused_computation.13.clone.1 | convolution fusion | flops 82886656 | bytes 4747268 | tf_op jit(solution)/shard_map/while/body/eval_jaxpr/clki,cj->lkij/dot_general | solution.py:184
  140.0 2.2 %fusion.129 = f32[8,32,128]{2,1,0:T(8,128)S(1)} fusion(f32[8,32,128]{2,1,0:T(8,128)S(1)} %get-tuple-element.746, s32[]{:T(128)} %get-tuple-element.745, bf16[9,8,128,128]{3,2,1,0:T(8,128)(2,1)} %get-tuple-element.684, f32[32,9,128]{2,0,1:T(8,128)S(1)} %dynamic-slice_bitcast_fusion.9, f32[32,8]{0,1:T(8,128)S(1)} %get-tuple-element.761), kind=kOutput, calls=%fused_computation.19.clone.1 | convolution fusion | flops 76087296 | bytes 2527236 | tf_op jit(solution)/shard_map/while/body/eval_jaxpr/clki,lkij->cj/dot_general | solution.py:181
  142.9 3.0 %multiply_reduce_fusion.7 = (f32[9,128,128]{2,1,0:T(8,128)S(1)}, f32[8,128,128]{2,1,0:T(8,128)S(1)}, bf16[9,8,128,128]{3,2,1,0:T(8,128)(2,1)}) fusion(f32[8,128,128]{2,1,0:T(8,128)S(1)} %fusion.128, f32[9,128,128]{2,1,0:T(8,128)S(1)} %get-tuple-element.683, bf16[8,32,128]{2,1,0:T(8,128)(2,1)S(1)} %get-tuple-element.766, s32[]{:T(128)} %get-tuple-element.745, ...), kind=kOutput, calls=%fused_computation.13.clone.1 | convolution fusion | flops 82886656 | bytes 4747268 | tf_op jit(solution)/shard_map/while/body/eval_jaxpr/clki,cj->lkij/dot_general | solution.py:184
  147.0 2.2 %fusion.129 = f32[8,32,128]{2,1,0:T(8,128)S(1)} fusion(f32[8,32,128]{2,1,0:T(8,128)S(1)} %get-tuple-element.746, s32[]{:T(128)} %get-tuple-element.745, bf16[9,8,128,128]{3,2,1,0:T(8,128)(2,1)} %get-tuple-element.684, f32[32,9,128]{2,0,1:T(8,128)S(1)} %dynamic-slice_bitcast_fusion.9, f32[32,8]{0,1:T(8,128)S(1)} %get-tuple-element.761), kind=kOutput, calls=%fused_computation.19.clone.1 | convolution fusion | flops 76087296 | bytes 2527236 | tf_op jit(solution)/shard_map/while/body/eval_jaxpr/clki,lkij->cj/dot_general | solution.py:181
  149.5 1.6 collective-permute-start.12
  151.2 2.0 %collective-permute-done.12 = f32[32,8]{0,1:T(8,128)S(1)} collective-permute-done((f32[32,8]{0,1:T(8,128)S(1)}, f32[32,8]{0,1:T(8,128)S(1)}, u32[]{:S(2)}, u32[]{:S(2)}) %collective-permute-start.12) | collective-permute-done | bytes 1056 | tf_op jit(solution)/shard_map/ppermute | solution.py:19
  153.5 0.7 collective-permute-start.7
  154.9 2.8 %collective-permute-done.13 = f32[32,8]{0,1:T(8,128)S(1)} collective-permute-done((f32[32,8]{0,1:T(8,128)S(1)}, f32[32,8]{0,1:T(8,128)S(1)}, u32[]{:S(2)}, u32[]{:S(2)}) %collective-permute-start.13) | collective-permute-done | bytes 1056 | tf_op jit(solution)/shard_map/ppermute | solution.py:19
  158.9 1.6 collective-permute-start.9
  160.5 1.6 collective-permute-start.10
  162.7 2.6 %collective-permute-done.10 = f32[35,128]{1,0:T(8,128)S(1)} collective-permute-done((f32[35,128]{1,0:T(8,128)S(1)}, f32[35,128]{1,0:T(8,128)S(1)}, u32[]{:S(2)}, u32[]{:S(2)}) %collective-permute-start.10) | collective-permute-done | bytes 17952 | tf_op jit(solution)/shard_map/ppermute | solution.py:19
  165.4 2.7 %scatter_fusion = f32[35,256]{0,1:T(8,128)S(1)} fusion(f32[35,256]{0,1:T(8,128)S(1)} %copy.150, s32[384]{0:T(512)S(1)} %fusion.95, f32[384,35]{1,0:T(8,128)S(1)} %copy.151), kind=kCustom, calls=%fused_computation.11 | custom fusion | flops 13440 | bytes 162816 | tf_op jit(solution)/shard_map/scatter-add | solution.py:224
  168.9 0.7 copy.152
  (434 shorter events, 36.4 us)
Async XLA Ops:
  0.6 21.2 %copy-start = (bf16[3,128,128]{2,1,0:T(8,128)(2,1)S(1)}, bf16[3,128,128]{2,1,0:T(8,128)(2,1)}, u32[]{:S(2)}) copy-start(bf16[3,128,128]{2,1,0:T(8,128)(2,1)} %param.23) | copy-start | bytes 294916
  0.6 22.2 %copy-start.3 = (f32[3,256]{1,0:T(4,128)S(1)}, f32[3,256]{1,0:T(4,128)}, u32[]{:S(2)}) copy-start(f32[3,256]{1,0:T(4,128)} %param.17) | copy-start | bytes 9220
  0.7 26.4 %copy-start.2 = (bf16[32,256]{1,0:T(8,128)(2,1)S(1)}, bf16[32,256]{1,0:T(8,128)(2,1)}, u32[]{:S(2)}) copy-start(bf16[32,256]{1,0:T(8,128)(2,1)} %param.18) | copy-start | bytes 49156
  3.1 19.4 %collective-permute-start.3 = (f32[3,128]{0,1:T(8,128)S(1)}, f32[3,128]{0,1:T(8,128)S(1)}, u32[]{:S(2)}, u32[]{:S(2)}) collective-permute-start(f32[3,128]{0,1:T(8,128)S(1)} %select_bitcast_fusion.2), channel_id=1, source_target_pairs={{0,4},{4,0},{8,12},{12,8},{16,20},{20,16},{24,28},{28,24},{1,5},{5... | collective-permute-start | bytes 4616 | tf_op jit(solution)/shard_map/ppermute | solution.py:19
  6.8 15.8 %collective-permute-start.4 = (f32[3,128]{0,1:T(8,128)S(1)}, f32[3,128]{0,1:T(8,128)S(1)}, u32[]{:S(2)}, u32[]{:S(2)}) collective-permute-start(f32[3,128]{0,1:T(8,128)S(1)} %select_bitcast_fusion.1), channel_id=1, source_target_pairs={{0,8},{4,12},{8,0},{12,4},{16,24},{20,28},{24,16},{28,20},{1,9},{5... | collective-permute-start | bytes 4616 | tf_op jit(solution)/shard_map/ppermute | solution.py:19
  9.2 13.5 %collective-permute-start.5 = (f32[3,128]{0,1:T(8,128)S(1)}, f32[3,128]{0,1:T(8,128)S(1)}, u32[]{:S(2)}, u32[]{:S(2)}) collective-permute-start(f32[3,128]{0,1:T(8,128)S(1)} %select_bitcast_fusion), channel_id=1, source_target_pairs={{0,16},{4,20},{8,24},{12,28},{16,0},{20,4},{24,8},{28,12},{1,17},{... | collective-permute-start | bytes 4616 | tf_op jit(solution)/shard_map/ppermute | solution.py:19
  13.5 10.5 %collective-permute-start = (bf16[32,128]{1,0:T(8,128)(2,1)S(1)}, bf16[32,128]{1,0:T(8,128)(2,1)S(1)}, u32[]{:S(2)}, u32[]{:S(2)}) collective-permute-start(bf16[32,128]{1,0:T(8,128)(2,1)S(1)} %bitcast_convert_fusion.3), channel_id=1, source_target_pairs={{0,4},{4,0},{8,12},{12,8},{16,20},{20,16},{24,28},{28,24},{1,5},{5... | collective-permute-start | bytes 24584 | tf_op jit(solution)/shard_map/ppermute | solution.py:19
  14.9 9.1 %collective-permute-start.1 = (bf16[32,128]{1,0:T(8,128)(2,1)S(1)}, bf16[32,128]{1,0:T(8,128)(2,1)S(1)}, u32[]{:S(2)}, u32[]{:S(2)}) collective-permute-start(bf16[32,128]{1,0:T(8,128)(2,1)S(1)} %bitcast_convert_fusion.2), channel_id=1, source_target_pairs={{0,8},{4,12},{8,0},{12,4},{16,24},{20,28},{24,16},{28,20},{1,9},{5... | collective-permute-start | bytes 24584 | tf_op jit(solution)/shard_map/ppermute | solution.py:19
  22.5 4.6 %collective-permute-start.2 = (bf16[32,128]{1,0:T(8,128)(2,1)S(1)}, bf16[32,128]{1,0:T(8,128)(2,1)S(1)}, u32[]{:S(2)}, u32[]{:S(2)}) collective-permute-start(bf16[32,128]{1,0:T(8,128)(2,1)S(1)} %bitcast_convert_fusion.1), channel_id=1, source_target_pairs={{0,16},{4,20},{8,24},{12,28},{16,0},{20,4},{24,8},{28,12},{1,17},{... | collective-permute-start | bytes 24584 | tf_op jit(solution)/shard_map/ppermute | solution.py:19
  81.9 8.4 %copy-start.1 = (f32[2,32,9,8,128]{4,3,2,1,0:T(8,128)S(1)}, f32[2,32,9,8,128]{4,3,2,1,0:T(8,128)}, u32[]{:S(2)}) copy-start(f32[2,32,9,8,128]{4,3,2,1,0:T(8,128)} %get-tuple-element.426) | copy-start | bytes 7077892
  91.1 2.2 %copy-start.4 = (f32[32,8]{0,1:T(8,128)S(1)}, f32[32,8]{0,1:T(8,128)}, u32[]{:S(2)}) copy-start(f32[32,8]{0,1:T(8,128)} %param.22) | copy-start | bytes 3076
  91.2 58.4 %collective-permute-start.11 = (f32[32,8]{0,1:T(8,128)S(1)}, f32[32,8]{0,1:T(8,128)S(1)}, u32[]{:S(2)}, u32[]{:S(2)}) collective-permute-start(f32[32,8]{0,1:T(8,128)S(1)} %bitcast.407), channel_id=1, source_target_pairs={{0,4},{4,0},{8,12},{12,8},{16,20},{20,16},{24,28},{28,24},{1,5},{5... | collective-permute-start | bytes 3080 | tf_op jit(solution)/shard_map/ppermute | solution.py:19
  149.4 4.1 %collective-permute-start.6 = (f32[3,640]{1,0:T(4,128)S(1)}, f32[3,640]{1,0:T(4,128)S(1)}, u32[]{:S(2)}, u32[]{:S(2)}) collective-permute-start(f32[3,640]{1,0:T(4,128)S(1)} %bitcast.408), channel_id=1, source_target_pairs={{0,1},{1,0},{2,3},{3,2},{4,5},{5,4},{6,7},{7,6},{8,9},{9,8},{10,11... | collective-permute-start | bytes 23048 | tf_op jit(solution)/shard_map/ppermute | solution.py:19
  149.5 3.6 %collective-permute-start.12 = (f32[32,8]{0,1:T(8,128)S(1)}, f32[32,8]{0,1:T(8,128)S(1)}, u32[]{:S(2)}, u32[]{:S(2)}) collective-permute-start(f32[32,8]{0,1:T(8,128)S(1)} %bitcast_add_fusion), channel_id=1, source_target_pairs={{0,8},{4,12},{8,0},{12,4},{16,24},{20,28},{24,16},{28,20},{1,9},{5... | collective-permute-start | bytes 3080 | tf_op jit(solution)/shard_map/ppermute | solution.py:19
  153.2 4.5 %collective-permute-start.13 = (f32[32,8]{0,1:T(8,128)S(1)}, f32[32,8]{0,1:T(8,128)S(1)}, u32[]{:S(2)}, u32[]{:S(2)}) collective-permute-start(f32[32,8]{0,1:T(8,128)S(1)} %add.361), channel_id=1, source_target_pairs={{0,16},{4,20},{8,24},{12,28},{16,0},{20,4},{24,8},{28,12},{1,17},{... | collective-permute-start | bytes 3080 | tf_op jit(solution)/shard_map/ppermute | solution.py:19
  153.5 4.8 %collective-permute-start.7 = (f32[3,640]{1,0:T(4,128)S(1)}, f32[3,640]{1,0:T(4,128)S(1)}, u32[]{:S(2)}, u32[]{:S(2)}) collective-permute-start(f32[3,640]{1,0:T(4,128)S(1)} %fusion.105), channel_id=1, source_target_pairs={{0,2},{1,3},{2,0},{3,1},{4,6},{5,7},{6,4},{7,5},{8,10},{9,11},{10,... | collective-permute-start | bytes 23048 | tf_op jit(solution)/shard_map/ppermute | solution.py:19
  158.3 3.8 %collective-permute-start.8 = (f32[35,128]{1,0:T(8,128)S(1)}, f32[35,128]{1,0:T(8,128)S(1)}, u32[]{:S(2)}, u32[]{:S(2)}) collective-permute-start(f32[35,128]{1,0:T(8,128)S(1)} %pad_maximum_fusion.3), channel_id=1, source_target_pairs={{0,4},{4,0},{8,12},{12,8},{16,20},{20,16},{24,28},{28,24},{1,5},{5... | collective-permute-start | bytes 53768 | tf_op jit(solution)/shard_map/ppermute | solution.py:19
  158.9 3.8 %collective-permute-start.9 = (f32[35,128]{1,0:T(8,128)S(1)}, f32[35,128]{1,0:T(8,128)S(1)}, u32[]{:S(2)}, u32[]{:S(2)}) collective-permute-start(f32[35,128]{1,0:T(8,128)S(1)} %pad_maximum_fusion.4), channel_id=1, source_target_pairs={{0,8},{4,12},{8,0},{12,4},{16,24},{20,28},{24,16},{28,20},{1,9},{5... | collective-permute-start | bytes 53768 | tf_op jit(solution)/shard_map/ppermute | solution.py:19
  160.5 4.8 %collective-permute-start.10 = (f32[35,128]{1,0:T(8,128)S(1)}, f32[35,128]{1,0:T(8,128)S(1)}, u32[]{:S(2)}, u32[]{:S(2)}) collective-permute-start(f32[35,128]{1,0:T(8,128)S(1)} %pad_maximum_fusion.5), channel_id=1, source_target_pairs={{0,16},{4,20},{8,24},{12,28},{16,0},{20,4},{24,8},{28,12},{1,17},{... | collective-permute-start | bytes 53768 | tf_op jit(solution)/shard_map/ppermute | solution.py:19

commit v4 on v3

v4 whole, which is shorter than its diff:
```python
import math

import jax
import jax.numpy as jnp
from jax import lax
from jax.sharding import PartitionSpec as P

SOFTENING = 0.25
CUTOFF = 2.5
CUTOFF_SQ = 6.25
SHARPNESS = 10.0
ROOT_THREE = math.sqrt(3.0)
ORDER_OF = (0, 1, 1, 1, 2, 2, 2, 2, 2)


def partner(value, axis, bit):
    mask = 2**bit
    pairs = [(source, source ^ mask) for source in range(lax.axis_size(axis))]
    return lax.ppermute(value, axis, pairs)


def geometry(target_pos, source_pos, pair_keep, radial_count):
    offset = source_pos[:, :, None, :] - target_pos[:, :, :, None]
    dist_sq = jnp.sum(offset * offset, axis=1) + SOFTENING
    distance = jnp.sqrt(dist_sq)
    along_x = offset[:, 0] / distance
    along_y = offset[:, 1] / distance
    along_z = offset[:, 2] / distance
    harmonics = jnp.stack(
        [
            jnp.ones_like(along_x),
            along_x,
            along_y,
            along_z,
            ROOT_THREE * along_x * along_y,
            ROOT_THREE * along_y * along_z,
            ROOT_THREE * along_x * along_z,
            0.5 * (3.0 * along_z * along_z - 1.0),
            0.5 * ROOT_THREE * (along_x * along_x - along_y * along_y),
        ]
    )
    envelope = jnp.square(jnp.maximum(1.0 - dist_sq / CUTOFF_SQ, 0.0)) * pair_keep
    centers = (jnp.arange(radial_count, dtype=jnp.float32) + 0.5) * (CUTOFF / radial_count)
    radial = (
        jnp.exp(-SHARPNESS * jnp.square(distance[None] - centers[:, None, None, None]))
        * envelope[None]
    )
    return (harmonics, radial)


def take_block(array, blk_index, block_size):
    return lax.dynamic_slice_in_dim(array, blk_index * block_size, block_size, array.ndim - 1)


def add_block(array, blk_index, value, block_size):
    current = take_block(array, blk_index, block_size)
    return lax.dynamic_update_slice_in_dim(
        array, current + value, blk_index * block_size, array.ndim - 1
    )


def body(
    positions, features, send_rows, pair_tiles, tile_live, radial_weight, mix_weight, out_grad
):
    block_size = send_rows.shape[1]
    atoms_dev = positions.shape[1]
    chan_dev = features.shape[0]
    radial_count = radial_weight.shape[1]
    components = out_grad.shape[1]
    levels = lax.axis_size("space").bit_length() - 1
    chan_count = lax.axis_size("chan")
    chan_index = lax.axis_index("chan")
    pos_list = [positions]
    feat_list = [features]
    for level_bit in range(levels):
        sent_rows = send_rows[level_bit]
        got_feat, got_pos = partner(
            (jnp.take(features, sent_rows, axis=1), jnp.take(positions, sent_rows, axis=1)),
            "space",
            level_bit,
        )
        feat_list.append(got_feat)
        pos_list.append(got_pos)
    src_pos = jnp.concatenate(pos_list, axis=1)
    src_feat = jnp.concatenate(feat_list, axis=1)
    full_feat = lax.all_gather(src_feat, "chan", axis=0, tiled=True)
    full_weight = lax.all_gather(radial_weight, "chan", axis=0, tiled=True)
    all_chan = full_feat.shape[0]
    src_atoms = src_pos.shape[1]
    src_blocks = src_atoms // block_size
    own_blocks = atoms_dev // block_size
    tiles_here = pair_tiles.shape[0] // chan_count
    my_tiles = chan_index * tiles_here + jnp.arange(tiles_here, dtype=jnp.int32)
    my_pairs = jnp.take(pair_tiles, my_tiles, axis=0, mode="clip")
    target_idx = my_pairs[:, 0]
    source_idx = my_pairs[:, 1]
    live = jnp.take(tile_live, my_tiles, mode="clip").astype(jnp.float32)
    block_ids = jnp.arange(src_blocks, dtype=jnp.int32)
    target_hot = (target_idx[:, None] == block_ids[None]).astype(jnp.float32) * live[:, None]
    source_hot = (source_idx[:, None] == block_ids[None]).astype(jnp.float32) * live[:, None]
    same = (target_idx == source_idx).astype(jnp.float32)
    eye = jnp.eye(block_size, dtype=jnp.float32)
    pair_keep = live[:, None, None] * (1.0 - same[:, None, None] * eye[None])
    pos_blocks = jnp.moveaxis(src_pos.reshape(3, src_blocks, block_size), 1, 0)
    feat_blocks = jnp.moveaxis(full_feat.reshape(all_chan, src_blocks, block_size), 1, 0)
    target_pos = jnp.take(pos_blocks, target_idx, axis=0, mode="clip")
    source_pos = jnp.take(pos_blocks, source_idx, axis=0, mode="clip")
    source_feat = jnp.take(feat_blocks, source_idx, axis=0, mode="clip")

    def geo_fn(first_pos, second_pos):
        return geometry(first_pos, second_pos, pair_keep, radial_count)

    (harmonics, radial), pullback = jax.vjp(geo_fn, target_pos, source_pos)
    pair_values = (harmonics[:, None] * radial[None]).astype(jnp.bfloat16)
    routed_feat = (
        target_hot[:, :own_blocks, None, None] * source_feat[:, None].astype(jnp.float32)
    ).astype(jnp.bfloat16)
    msg_acc = jnp.einsum(
        "lktij,tbcj->bclki", pair_values, routed_feat, preferred_element_type=jnp.float32
    )
    moment_part = jnp.einsum("bclki,ck->clbi", msg_acc, full_weight).reshape(
        all_chan, components, atoms_dev
    )
    moments = lax.psum_scatter(moment_part, "chan", scatter_dimension=0, tiled=True)
    packed = moments.astype(jnp.bfloat16)
    mixing = jnp.take(mix_weight, jnp.array(ORDER_OF, dtype=jnp.int32), axis=0)
    offset = chan_index * chan_dev
    gathered_piece = lax.all_gather(packed, "chan", axis=0, tiled=True)
    weight_part = lax.dynamic_slice(
        mixing, (0, offset, 0), (components, chan_dev, gathered_piece.shape[0])
    )
    mixed_out = jnp.einsum(
        "lxc,cli->xli", weight_part, gathered_piece, preferred_element_type=jnp.float32
    )
    scalar_part = mixed_out[:, 0, :]
    gate_value = jax.nn.sigmoid(scalar_part)
    result = jnp.concatenate(
        [(scalar_part * gate_value)[:, None, :], mixed_out[:, 1:, :] * gate_value[:, None, :]],
        axis=1,
    ).astype(jnp.bfloat16)
    upstream = out_grad.astype(jnp.float32)
    scalar_grad = upstream[:, 0, :] * (
        gate_value * (1.0 + scalar_part * (1.0 - gate_value))
    ) + gate_value * (1.0 - gate_value) * jnp.sum(upstream[:, 1:, :] * mixed_out[:, 1:, :], axis=1)
    rest_grad = upstream[:, 1:, :] * gate_value[:, None, :]
    dz_packed = jnp.concatenate([scalar_grad[:, None, :], rest_grad], axis=1).astype(jnp.bfloat16)
    gathered_piece = lax.all_gather(dz_packed, "chan", axis=0, tiled=True)
    moment_grad_all = jnp.einsum(
        "lxc,xli->cli", mixing, gathered_piece, preferred_element_type=jnp.float32
    )
    grad_blocks = jnp.moveaxis(
        moment_grad_all.reshape(all_chan, components, own_blocks, block_size), 2, 0
    )
    grad_rad = jnp.einsum("bclki,bcli->ck", msg_acc, grad_blocks)
    tile_grad = jnp.take(grad_blocks, target_idx, axis=0, mode="clip")
    weighted = (
        live[:, None, None, None, None]
        * full_weight[None, :, None, :, None]
        * tile_grad[:, :, :, None, :]
    ).astype(jnp.bfloat16)
    grad_source = jnp.einsum(
        "tclki,lktij->tcj", weighted, pair_values, preferred_element_type=jnp.float32
    )
    value_grad = jnp.einsum(
        "tclki,tcj->lktij", weighted, source_feat, preferred_element_type=jnp.float32
    )
    harm_grad = jnp.sum(value_grad * radial[None], axis=1)
    rad_grad = jnp.sum(value_grad * harmonics[:, None], axis=0)
    target_grad, source_grad_pos = pullback((harm_grad, rad_grad))
    grad_part = jnp.sum(
        source_hot[:, None, :, None] * grad_source[:, :, None, :], axis=0
    ).reshape(all_chan, src_atoms)
    dpos_src = jnp.sum(
        target_hot[:, None, :, None] * target_grad[:, :, None, :]
        + source_hot[:, None, :, None] * source_grad_pos[:, :, None, :],
        axis=0,
    ).reshape(3, src_atoms)
    grad_src = lax.psum_scatter(grad_part, "chan", scatter_dimension=0, tiled=True)
    for chan_bit in range(chan_count.bit_length() - 1):
        other_pos, other_rad = partner((dpos_src, grad_rad), "chan", chan_bit)
        dpos_src = dpos_src + other_pos
        grad_rad = grad_rad + other_rad
    grad_rad = lax.dynamic_slice_in_dim(grad_rad, offset, chan_dev, 0)
    own_both = jnp.concatenate([grad_src[:, :atoms_dev], dpos_src[:, :atoms_dev]], axis=0)
    back_list = []
    for level_bit in range(levels):
        low = atoms_dev + level_bit * block_size
        ghost_both = jnp.concatenate(
            [grad_src[:, low : low + block_size], dpos_src[:, low : low + block_size]], axis=0
        )
        back_both, other_rad = partner((ghost_both, grad_rad), "space", level_bit)
        grad_rad = grad_rad + other_rad
        back_list.append(back_both)
    all_rows = send_rows[:levels].reshape(-1)
    own_both = own_both.at[:, all_rows].add(jnp.concatenate(back_list, axis=1))
    own_grad = own_both[:chan_dev]
    own_dpos = own_both[chan_dev:]
    return (result, own_grad.astype(jnp.bfloat16), -own_dpos, grad_rad)


def solution(mesh):
    placed = (
        P(None, "space"),
        P("chan", "space"),
        P("space", None),
        P("space", None),
        P("space"),
        P("chan", None),
        P(),
        P("chan", None, "space"),
    )
    return jax.shard_map(
        body,
        mesh=mesh,
        in_specs=placed,
        out_specs=(P("chan", None, "space"), P("chan", "space"), P(None, "space"), P("chan", None)),
        check_vma=False,
    )
```

time: 171 us -> 167 us (0.977)
  other arithmetic: 51.5 us -> 20.2 us
  matrix products: 52.4 us -> 21.9 us
  waiting for transfers between devices: 11 us -> 36.4 us
  between operations: 1.02 us -> 14.8 us
  blocking collectives: 15.3 us -> 25.8 us
  local copies, waits for them, and re-layouts: 19.5 us -> 25.8 us
  starting transfers between devices: 16.5 us -> 21.9 us
  loops' own time: 2.34 us -> 0 us
    dot_general x27 -> x5, matrix products: 52.2 us -> 21.7 us  [the longest x1 7.93 us: body(): jnp.einsum('bclki,ck->clbi', msg_acc, full_weight)]
    add x10 -> x3, other arithmetic: 25.4 us -> 0.01 us  [the longest x2 0.01 us: body(): dpos_src = dpos_src + other_pos]
    reduce_scatter x0 -> x1, waiting for transfers between devices: none -> 23.6 us  [body(): lax.psum_scatter(moment_part, 'chan', scatter_dimension=0, tiled=True)]
    all_gather x0 -> x2, blocking collectives: none -> 10.9 us  [the longest x1 5.7 us: body(): full_feat = lax.all_gather(src_feat, 'chan', axis=0, tiled=True)]
    ppermute x14 -> x16, starting transfers between devices: 16.5 us -> 21.8 us  [partner(): return lax.ppermute(value, axis, pairs)]
    dot_general x10 -> x1, local copies, waits for them, and re-layouts: 5.72 us -> 0.61 us  [body(): jnp.einsum('bclki,ck->clbi', msg_acc, full_weight)]
    dot_general x0 -> x1, other arithmetic: none -> 4.96 us  [body(): grad_rad = jnp.einsum('bclki,bcli->ck', msg_acc, grad_blocks)]
    unnamed x16 -> x78, local copies, waits for them, and re-layouts: 3.82 us -> 8.14 us
  transfers between devices with their start and end apart: 14 -> 18, of which waited for: 5 -> 8; matrix products, arithmetic and copies ran while one was open for 41% -> 14% of each run, Pallas kernels for 0% -> 0%
where the time goes in v4:
time: 167 us
  waiting for transfers between devices  36.4 us (22%)
  local copies, waits for them, and re-layouts  25.8 us (15%)
  blocking collectives  25.8 us (15%)
  starting transfers between devices  21.9 us (13%)
  matrix products  21.9 us (13%)
  other arithmetic  20.2 us (12%)
  between operations  14.8 us (9%)
    reduce_scatter x1, waiting for transfers between devices, body(): lax.psum_scatter(moment_part, 'chan', scatter_dimension=0, tiled=True)  23.6 us
    ppermute x16, starting transfers between devices, partner(): return lax.ppermute(value, axis, pairs)  21.8 us
    ppermute x16, waiting for transfers between devices, partner(): return lax.ppermute(value, axis, pairs)  10.3 us
    unnamed x78, local copies, waits for them, and re-layouts  8.14 us
    dot_general x1, matrix products, body(): jnp.einsum('bclki,ck->clbi', msg_acc, full_weight)  7.93 us
    dot_general x1, matrix products, body(): jnp.einsum('tclki,tcj->lktij', weighted, source_feat, preferred_element_t...  7.81 us
    all_gather x1, blocking collectives, body(): gathered_piece = lax.all_gather(dz_packed, 'chan', axis=0, tiled=True)  7.65 us
    all_gather x1, blocking collectives, body(): gathered_piece = lax.all_gather(packed, 'chan', axis=0, tiled=True)  7.33 us
  transfers between devices with their start and end apart: 18, of which 8 were waited for; matrix products, arithmetic and copies ran while one was open for 14% of the time, Pallas kernels for 0%

profile of v4, /device:TPU:0, one launch (start us, length us, event | category | flops | bytes accessed | tf_op | source)
XLA Modules:
  0.0 166.9 jit_solution(12453427088656397232)
XLA Ops:
  7.3 0.8 compare_and_fusion.2
  8.1 0.8 copy.268
  8.9 0.6 gather_fusion.10
  9.6 3.0 %collective-permute-start.3 = (f32[3,128]{0,1:T(8,128)S(1)}, f32[3,128]{0,1:T(8,128)S(1)}, u32[]{:S(2)}, u32[]{:S(2)}) collective-permute-start(f32[3,128]{0,1:T(8,128)S(1)} %select_bitcast_fusion.2), channel_id=1, source_target_pairs={{0,4},{4,0},{8,12},{12,8},{16,20},{20,16},{24,28},{28,24},{1,5},{5... | collective-permute-start | bytes 4616 | tf_op jit(solution)/shard_map/ppermute | solution.py:19
  12.7 0.6 gather_fusion.11
  13.4 1.6 collective-permute-start.4
  15.1 0.6 gather_fusion.12
  15.8 2.7 %collective-permute-start.5 = (f32[3,128]{0,1:T(8,128)S(1)}, f32[3,128]{0,1:T(8,128)S(1)}, u32[]{:S(2)}, u32[]{:S(2)}) collective-permute-start(f32[3,128]{0,1:T(8,128)S(1)} %select_bitcast_fusion), channel_id=1, source_target_pairs={{0,16},{4,20},{8,24},{12,28},{16,0},{20,4},{24,8},{28,12},{1,17},{... | collective-permute-start | bytes 4616 | tf_op jit(solution)/shard_map/ppermute | solution.py:19
  18.5 0.8 copy.260
  19.3 0.7 gather_fusion.7
  20.7 0.7 gather_fusion.8
  22.0 0.8 copy.259
  23.5 0.6 pad_clamp_fusion
  24.8 0.7 gather_fusion.9
  25.5 0.6 gather_fusion.1
  26.1 0.7 select_bitcast_fusion.3
  28.0 5.2 %all-gather = f32[4,32,8]{1,2,0:T(8,128)S(1)} all-gather(f32[1,32,8]{1,2,0:T(8,128)S(1)} %bitcast.382), channel_id=1, replica_groups=mesh['space'=8,'chan'=4] {'chan'}, dimensions={0}, use_global_device_ids=true | all-gather | bytes 5120 | tf_op jit(solution)/shard_map/all_gather | solution.py:87
  33.2 0.7 copy.317
  36.9 2.1 %collective-permute-done.2 = bf16[32,128]{0,1:T(8,128)(2,1)S(1)} collective-permute-done((bf16[32,128]{0,1:T(8,128)(2,1)}, bf16[32,128]{0,1:T(8,128)(2,1)S(1)}, u32[]{:S(2)}, u32[]{:S(2)}) %collective-permute-start.2) | collective-permute-done | bytes 8224 | tf_op jit(solution)/shard_map/ppermute | solution.py:19
  39.1 5.7 %all_gather.12 = bf16[128,640]{1,0:T(8,128)(2,1)S(1)} all-gather(bf16[32,640]{1,0:T(8,128)(2,1)S(1)} %pad_maximum_fusion.3), channel_id=1, replica_groups=mesh['space'=8,'chan'=4] {'chan'}, dimensions={0}, use_global_device_ids=true | all-gather | bytes 204800 | tf_op jit(solution)/shard_map/all_gather | solution.py:86
  44.8 0.8 copy.266
  45.6 1.1 copy.267
  46.6 0.7 gather_fusion.2
  47.4 2.1 %fusion.7 = f32[2,128,9,8,128,1]{4,1,3,2,5,0:T(8,128)S(1)} fusion(f32[2,128,128]{2,1,0:T(8,128)S(1)} %convert_element_type.58, f32[2,2]{0,1:T(2,128)} %slice.73, f32[8,2,128,128]{2,3,0,1:T(8,128)S(1)} %fusion.19, f32[9,2,128,128]{2,3,1,0:T(8,128)S(1)} %multiply_dynamic-update-slice_fusion), kind=kOutput, calls=%fused_computation.26 | convolution fusion | flops 1212809216 | bytes 11796496 | tf_op jit(solution)/shard_map/lktij,tbcj->bclki/dot_general | solution.py:118
  49.5 7.9 %fusion.3 = f32[128,1,2,9,128]{4,1,3,2,0:T(1,128)S(1)} fusion(f32[128,8,1,1,1]{1,2,4,3,0:T(1,128)S(1)} %bitcast.379, f32[2,128,9,8,128]{4,1,3,2,0:T(8,128)S(1)} %bitcast.370), kind=kOutput, calls=%fused_computation.20 | convolution fusion | flops 4718592 | bytes 10620928 | tf_op jit(solution)/shard_map/bclki,ck->clbi/dot_general | solution.py:121
  57.5 0.6 copy.359
  58.1 2.0 %reshape.464 = f32[128,9,256]{2,0,1:T(8,128)} reshape(f32[128,9,2,128]{3,2,0,1:T(2,128)S(1)} %bitcast.373) | data formatting | bytes 2359296 | tf_op jit(solution)/shard_map/reshape | solution.py:121
  60.2 0.8 copy-done.10
  61.2 0.6 gather_fusion.5
  61.9 23.6 %reduce-scatter.5.cloned.1.call-done = f32[32,9,256]{2,0,1:T(8,128)} async-done(((f32[128,9,256]{2,0,1:T(8,128)}), f32[32,9,256]{2,0,1:T(8,128)}) %reduce-scatter.5.cloned.1.call-update) | async-done | bytes 294928 | tf_op jit(solution)/shard_map/reduce_scatter | solution.py:124
  85.5 1.0 convert_element_type.63
  86.5 7.3 %all_gather.14 = bf16[128,9,256]{2,0,1:T(8,128)(2,1)S(1)} all-gather(bf16[32,9,256]{2,0,1:T(8,128)(2,1)S(1)} %convert_element_type.63), channel_id=1, replica_groups=mesh['space'=8,'chan'=4] {'chan'}, dimensions={0}, use_global_device_ids=true | all-gather | bytes 737280 | tf_op jit(solution)/shard_map/all_gather | solution.py:128
  94.1 0.7 multiply_convert_fusion.2
  94.9 7.6 %all_gather.15 = bf16[128,9,256]{2,0,1:T(8,128)(2,1)S(1)} all-gather(bf16[32,9,256]{2,0,1:T(8,128)(2,1)S(1)} %pad_maximum_fusion.1), channel_id=1, replica_groups=mesh['space'=8,'chan'=4] {'chan'}, dimensions={0}, use_global_device_ids=true | all-gather | bytes 737280 | tf_op jit(solution)/shard_map/all_gather | solution.py:147
  102.9 0.7 gather_fusion.6
  103.6 1.4 copy.281
  105.1 7.8 %fusion.1 = (f32[9,2,128,128]{2,3,0,1:T(8,128)S(1)}, f32[8,2,128,128]{2,3,0,1:T(8,128)}, bf16[9,8,2,128,128]{3,4,1,0,2:T(8,128)(2,1)}) fusion(f32[8,2,128,128]{2,3,0,1:T(8,128)} %copy-done.3, f32[2,128,9,128]{3,1,2,0:T(8,128)} %copy.281, f32[2,128,8]{1,2,0:T(8,128)S(1)} %broadcast_multiply_fusion, bf16[2,128,128]{2,1,0:T(8,128)(2,1)S(1)} %gather_fusion.2, ...), kind=kOutput, calls=%fused_computation.18 | convolution fusion | flops 622297088 | bytes 10428416 | tf_op jit(solution)/shard_map/tclki,tcj->lktij/dot_general | solution.py:164
  112.9 0.8 fusion.29
  113.7 0.9 fusion.63
  114.5 1.4 copy.335
  115.9 5.0 %fusion = f32[128,8]{0,1:T(8,128)S(1)} fusion(f32[2,128,9,8,128,1]{4,1,3,2,5,0:T(8,128)} %copy-done.2, f32[128,2,128,9]{2,0,3,1:T(8,128)} %copy.335), kind=kLoop, calls=%fused_computation.15 | loop fusion | flops 4717568 | bytes 10620928 | tf_op jit(solution)/shard_map/bclki,bcli->ck/dot_general | solution.py:154
  121.3 3.4 %fusion.10 = f32[2,128,128]{2,1,0:T(8,128)S(1)} fusion(bf16[9,8,2,128,128]{3,4,1,0,2:T(8,128)(2,1)} %get-tuple-element.48, f32[2,128,9,128]{3,1,2,0:T(8,128)S(1)} %copy-done.5, f32[2,128,8]{1,2,0:T(8,128)S(1)} %broadcast_multiply_fusion), kind=kOutput, calls=%fused_computation.33 | convolution fusion | flops 608698368 | bytes 6037504 | tf_op jit(solution)/shard_map/tclki,lktij->tcj/dot_general | solution.py:161
  125.0 0.9 copy.321
  126.0 1.8 %fusion.20 = (f32[2,128,128]{1,2,0:T(8,128)S(1)}, f32[2,128,128]{1,2,0:T(8,128)S(1)}) fusion(f32[8,2,128,128]{2,3,0,1:T(8,128)} %get-tuple-element.35, f32[8]{0:T(128)S(1)} %copy-done.31, f32[2,128,128]{1,2,0:T(8,128)S(1)} %get-tuple-element.54, f32[2,128,128]{1,2,0:T(8,128)S(1)} %get-tuple-element.55), kind=kLoop, calls=%fused_computation.39 | loop fusion | flops 2818048 | bytes 1572896 | tf_op jit(solution)/shard_map/transpose(jvp())/reduce_sum | solution.py:45
  128.2 1.0 collective-permute-start.12
  129.6 2.3 %collective-permute-done.12 = f32[128,8]{0,1:T(8,128)S(1)} collective-permute-done((f32[128,8]{0,1:T(8,128)S(1)}, f32[128,8]{0,1:T(8,128)S(1)}, u32[]{:S(2)}, u32[]{:S(2)}) %collective-permute-start.12) | collective-permute-done | bytes 4128 | tf_op jit(solution)/shard_map/ppermute | solution.py:19
  131.9 1.5 collective-permute-start.13
  133.6 1.9 %collective-permute-done.13 = f32[32,8]{0,1:T(8,128)S(1)} collective-permute-done((f32[32,8]{0,1:T(8,128)S(1)}, f32[32,8]{0,1:T(8,128)S(1)}, u32[]{:S(2)}, u32[]{:S(2)}) %collective-permute-start.13) | collective-permute-done | bytes 1056 | tf_op jit(solution)/shard_map/ppermute | solution.py:19
  135.6 1.5 collective-permute-start.14
  137.1 1.0 collective-permute-start.7
  138.1 1.1 collective-permute-done.14
  139.2 2.4 %collective-permute-start.15 = (f32[32,8]{0,1:T(8,128)S(1)}, f32[32,8]{0,1:T(8,128)S(1)}, u32[]{:S(2)}, u32[]{:S(2)}) collective-permute-start(f32[32,8]{0,1:T(8,128)S(1)} %add.187), channel_id=1, source_target_pairs={{0,16},{4,20},{8,24},{12,28},{16,0},{20,4},{24,8},{28,12},{1,17},{... | collective-permute-start | bytes 3080 | tf_op jit(solution)/shard_map/ppermute | solution.py:19
  141.7 0.7 pad_maximum_fusion
  142.3 1.4 collective-permute-done.15
  144.5 2.5 %reduce-scatter.7.cloned.1.call-done = f32[32,640]{1,0:T(8,128)} async-done(((f32[128,640]{1,0:T(8,128)}), f32[32,640]{1,0:T(8,128)}) %reduce-scatter.7.cloned.1.call-update) | async-done | bytes 81936
  147.0 0.8 fusion.95
  147.8 1.6 collective-permute-start.8
  149.3 1.5 collective-permute-start.9
  150.8 2.4 %collective-permute-start.10 = (f32[35,128]{1,0:T(8,128)S(1)}, f32[35,128]{1,0:T(8,128)S(1)}, u32[]{:S(2)}, u32[]{:S(2)}) collective-permute-start(f32[35,128]{1,0:T(8,128)S(1)} %pad_maximum_fusion.6), channel_id=1, source_target_pairs={{0,16},{4,20},{8,24},{12,28},{16,0},{20,4},{24,8},{28,12},{1,17},{... | collective-permute-start | bytes 53768 | tf_op jit(solution)/shard_map/ppermute | solution.py:19
  153.2 0.8 slice.128
  154.2 1.5 collective-permute-done.10
  155.8 2.7 %scatter_fusion = f32[35,256]{0,1:T(8,128)S(1)} fusion(f32[35,256]{0,1:T(8,128)S(1)} %pad_maximum_fusion.2, s32[384]{0:T(512)S(1)} %fusion.92, f32[384,35]{1,0:T(8,128)S(1)} %copy.297), kind=kCustom, calls=%fused_computation.13 | custom fusion | flops 13440 | bytes 162816 | tf_op jit(solution)/shard_map/scatter-add | solution.py:195
  158.6 0.7 copy.299
  159.3 0.7 copy.298
  (167 shorter events, 11.1 us)
Async XLA Ops:
  7.2 54.0 %copy-start = (bf16[3,128,128]{2,1,0:T(8,128)(2,1)S(1)}, bf16[3,128,128]{2,1,0:T(8,128)(2,1)}, u32[]{:S(2)}) copy-start(bf16[3,128,128]{2,1,0:T(8,128)(2,1)} %param.19) | copy-start | bytes 294916
  7.2 27.0 %copy-start.21 = (f32[3,256]{1,0:T(4,128)S(1)}, f32[3,256]{1,0:T(4,128)}, u32[]{:S(2)}) copy-start(f32[3,256]{1,0:T(4,128)} %param.13) | copy-start | bytes 9220
  7.2 18.3 %copy-start.1 = (s32[8]{0:T(128)S(1)}, s32[8]{0:T(128)}, u32[]{:S(2)}) copy-start(s32[8]{0:T(128)} %param.17) | copy-start | bytes 100
  7.2 20.8 %copy-start.27 = (f32[32,8]{0,1:T(8,128)S(1)}, f32[32,8]{0,1:T(8,128)}, u32[]{:S(2)}) copy-start(f32[32,8]{0,1:T(8,128)} %param.18) | copy-start | bytes 3076
  7.2 78.3 %reduce-scatter.5.cloned.1.call-start = ((), (), s32[]{:S(2)}) async-start(), calls=%async_computation.2 | async-start | bytes 1474560 | tf_op jit(solution)/shard_map/reduce_scatter | solution.py:124
  9.6 24.3 %collective-permute-start.3 = (f32[3,128]{0,1:T(8,128)S(1)}, f32[3,128]{0,1:T(8,128)S(1)}, u32[]{:S(2)}, u32[]{:S(2)}) collective-permute-start(f32[3,128]{0,1:T(8,128)S(1)} %select_bitcast_fusion.2), channel_id=1, source_target_pairs={{0,4},{4,0},{8,12},{12,8},{16,20},{20,16},{24,28},{28,24},{1,5},{5... | collective-permute-start | bytes 4616 | tf_op jit(solution)/shard_map/ppermute | solution.py:19
  13.4 20.6 %collective-permute-start.4 = (f32[3,128]{0,1:T(8,128)S(1)}, f32[3,128]{0,1:T(8,128)S(1)}, u32[]{:S(2)}, u32[]{:S(2)}) collective-permute-start(f32[3,128]{0,1:T(8,128)S(1)} %select_bitcast_fusion.1), channel_id=1, source_target_pairs={{0,8},{4,12},{8,0},{12,4},{16,24},{20,28},{24,16},{28,20},{1,9},{5... | collective-permute-start | bytes 4616 | tf_op jit(solution)/shard_map/ppermute | solution.py:19
  15.8 18.3 %collective-permute-start.5 = (f32[3,128]{0,1:T(8,128)S(1)}, f32[3,128]{0,1:T(8,128)S(1)}, u32[]{:S(2)}, u32[]{:S(2)}) collective-permute-start(f32[3,128]{0,1:T(8,128)S(1)} %select_bitcast_fusion), channel_id=1, source_target_pairs={{0,16},{4,20},{8,24},{12,28},{16,0},{20,4},{24,8},{28,12},{1,17},{... | collective-permute-start | bytes 4616 | tf_op jit(solution)/shard_map/ppermute | solution.py:19
  20.1 16.6 %collective-permute-start = (bf16[32,128]{0,1:T(8,128)(2,1)S(1)}, bf16[32,128]{0,1:T(8,128)(2,1)S(1)}, u32[]{:S(2)}, u32[]{:S(2)}) collective-permute-start(bf16[32,128]{0,1:T(8,128)(2,1)S(1)} %select_bitcast_fusion.5), channel_id=1, source_target_pairs={{0,4},{4,0},{8,12},{12,8},{16,20},{20,16},{24,28},{28,24},{1,5},{5... | collective-permute-start | bytes 24584 | tf_op jit(solution)/shard_map/ppermute | solution.py:19
  21.5 15.3 %collective-permute-start.1 = (bf16[32,128]{0,1:T(8,128)(2,1)S(1)}, bf16[32,128]{0,1:T(8,128)(2,1)S(1)}, u32[]{:S(2)}, u32[]{:S(2)}) collective-permute-start(bf16[32,128]{0,1:T(8,128)(2,1)S(1)} %select_bitcast_fusion.4), channel_id=1, source_target_pairs={{0,8},{4,12},{8,0},{12,4},{16,24},{20,28},{24,16},{28,20},{1,9},{5... | collective-permute-start | bytes 24584 | tf_op jit(solution)/shard_map/ppermute | solution.py:19
  24.1 11.5 %copy-start.25 = (s32[1024]{0:T(1024)}, s32[1024]{0:T(1024)S(1)}, u32[]{:S(2)}) copy-start(s32[1024]{0:T(1024)S(1)} %pad_clamp_fusion.2) | copy-start | bytes 12292
  24.2 11.9 %copy-start.28 = (f32[2]{0:T(128)}, f32[2]{0:T(128)S(1)}, u32[]{:S(2)}) copy-start(f32[2]{0:T(128)S(1)} %compare_convert_fusion) | copy-start | bytes 28
  26.1 9.9 %copy-start.22 = (f32[2]{0:T(128)}, f32[2]{0:T(128)S(1)}, u32[]{:S(2)}) copy-start(f32[2]{0:T(128)S(1)} %convert_element_type.57) | copy-start | bytes 28
  27.4 6.5 %copy-start.19 = (f32[2,5]{0,1:T(8,128)}, f32[2,5]{0,1:T(8,128)S(1)}, u32[]{:S(2)}) copy-start(f32[2,5]{0,1:T(8,128)S(1)} %get-tuple-element.71) | copy-start | bytes 124
  33.9 5.0 %collective-permute-start.2 = (bf16[32,128]{0,1:T(8,128)(2,1)}, bf16[32,128]{0,1:T(8,128)(2,1)S(1)}, u32[]{:S(2)}, u32[]{:S(2)}) collective-permute-start(bf16[32,128]{0,1:T(8,128)(2,1)} %select_bitcast_fusion.3), channel_id=1, source_target_pairs={{0,16},{4,20},{8,24},{12,28},{16,0},{20,4},{24,8},{28,12},{1,17},{... | collective-permute-start | bytes 24584 | tf_op jit(solution)/shard_map/ppermute | solution.py:19
  34.8 1.0 copy-start.15
  35.4 0.6 copy-start.17
  35.6 0.7 copy-start.30
  36.1 2.9 %copy-start.11 = (bf16[32,256]{1,0:T(8,128)(2,1)S(1)}, bf16[32,256]{1,0:T(8,128)(2,1)}, u32[]{:S(2)}) copy-start(bf16[32,256]{1,0:T(8,128)(2,1)} %param.14) | copy-start | bytes 49156
  36.6 12.9 %copy-start.3 = (f32[8,2,128,128]{2,3,0,1:T(8,128)}, f32[8,2,128,128]{2,3,0,1:T(8,128)S(1)}, u32[]{:S(2)}) copy-start(f32[8,2,128,128]{2,3,0,1:T(8,128)S(1)} %fusion.19) | copy-start | bytes 3145732
  36.7 12.8 %copy-start.4 = (f32[9,2,128,128]{2,3,1,0:T(8,128)}, f32[9,2,128,128]{2,3,1,0:T(8,128)S(1)}, u32[]{:S(2)}) copy-start(f32[9,2,128,128]{2,3,1,0:T(8,128)S(1)} %multiply_dynamic-update-slice_fusion) | copy-start | bytes 3538948
  47.3 2.2 %copy-start.12 = (f32[4,32,8]{2,1,0:T(8,128)S(1)}, f32[4,32,8]{2,1,0:T(8,128)}, u32[]{:S(2)}) copy-start(f32[4,32,8]{2,1,0:T(8,128)} %copy.317) | copy-start | bytes 12292
  49.5 8.6 %copy-start.2 = (f32[2,128,9,8,128,1]{4,1,3,2,5,0:T(8,128)}, f32[2,128,9,8,128,1]{4,1,3,2,5,0:T(8,128)S(1)}, u32[]{:S(2)}) copy-start(f32[2,128,9,8,128,1]{4,1,3,2,5,0:T(8,128)S(1)} %fusion.7) | copy-start | bytes 28311556
  60.1 0.9 copy-start.10
  60.1 1.0 copy-start.13
  60.1 1.1 copy-start.32
  60.1 1.7 %copy-start.26 = (s32[3,128]{1,0:T(4,128)S(1)}, s32[3,128]{1,0:T(4,128)}, u32[]{:S(2)}) copy-start(s32[3,128]{1,0:T(4,128)} %param.15) | copy-start | bytes 4612
  60.1 1.8 %copy-start.23 = (f32[2]{0:T(128)S(1)}, f32[2]{0:T(128)}, u32[]{:S(2)}) copy-start(f32[2]{0:T(128)} %copy-done.22) | copy-start | bytes 28
  60.1 86.9 %reduce-scatter.7.cloned.1.call-start = ((), (), s32[]{:S(2)}) async-start(), calls=%async_computation.3 | async-start | bytes 409600
  115.9 5.4 %copy-start.5 = (f32[2,128,9,128]{3,1,2,0:T(8,128)S(1)}, f32[2,128,9,128]{3,1,2,0:T(8,128)}, u32[]{:S(2)}) copy-start(f32[2,128,9,128]{3,1,2,0:T(8,128)} %copy.281) | copy-start | bytes 3538948
  120.9 7.3 %collective-permute-start.11 = (f32[128,8]{0,1:T(8,128)S(1)}, f32[128,8]{0,1:T(8,128)S(1)}, u32[]{:S(2)}, u32[]{:S(2)}) collective-permute-start(f32[128,8]{0,1:T(8,128)S(1)} %fusion), channel_id=1, source_target_pairs={{0,1},{1,0},{2,3},{3,2},{4,5},{5,4},{6,7},{7,6},{8,9},{9,8},{10,11... | collective-permute-start | bytes 12296 | tf_op jit(solution)/shard_map/ppermute | solution.py:19
  124.7 1.2 copy-start.31
  125.0 2.8 %copy-start.24 = (f32[2]{0:T(128)S(1)}, f32[2]{0:T(128)}, u32[]{:S(2)}) copy-start(f32[2]{0:T(128)} %copy-done.22) | copy-start | bytes 28
  125.0 2.8 %copy-start.29 = (f32[2]{0:T(128)S(1)}, f32[2]{0:T(128)}, u32[]{:S(2)}) copy-start(f32[2]{0:T(128)} %copy-done.28) | copy-start | bytes 28
  127.7 1.5 copy-start.7
  127.7 1.5 copy-start.8
  127.7 1.5 copy-start.9
  127.8 1.5 copy-start.16
  127.8 1.5 copy-start.18
  127.8 5.6 %copy-start.14 = (f32[2,5]{0,1:T(8,128)S(1)}, f32[2,5]{0,1:T(8,128)}, u32[]{:S(2)}) copy-start(f32[2,5]{0,1:T(8,128)} %get-tuple-element.70) | copy-start | bytes 124
  127.8 5.6 %copy-start.20 = (f32[2,5]{0,1:T(8,128)S(1)}, f32[2,5]{0,1:T(8,128)}, u32[]{:S(2)}) copy-start(f32[2,5]{0,1:T(8,128)} %copy-done.19) | copy-start | bytes 124
  127.8 13.9 %copy-start.6 = (bf16[32,8,256]{2,0,1:T(8,128)(2,1)S(1)}, bf16[32,8,256]{2,0,1:T(8,128)(2,1)}, u32[]{:S(2)}) copy-start(bf16[32,8,256]{2,0,1:T(8,128)(2,1)} %get-tuple-element.60) | copy-start | bytes 393220
  128.2 3.7 %collective-permute-start.12 = (f32[128,8]{0,1:T(8,128)S(1)}, f32[128,8]{0,1:T(8,128)S(1)}, u32[]{:S(2)}, u32[]{:S(2)}) collective-permute-start(f32[128,8]{0,1:T(8,128)S(1)} %add.184), channel_id=1, source_target_pairs={{0,2},{1,3},{2,0},{3,1},{4,6},{5,7},{6,4},{7,5},{8,10},{9,11},{10,... | collective-permute-start | bytes 12296 | tf_op jit(solution)/shard_map/ppermute | solution.py:19
  131.9 3.6 %collective-permute-start.13 = (f32[32,8]{0,1:T(8,128)S(1)}, f32[32,8]{0,1:T(8,128)S(1)}, u32[]{:S(2)}, u32[]{:S(2)}) collective-permute-start(f32[32,8]{0,1:T(8,128)S(1)} %constant_dynamic-slice_fusion), channel_id=1, source_target_pairs={{0,4},{4,0},{8,12},{12,8},{16,20},{20,16},{24,28},{28,24},{1,5},{5... | collective-permute-start | bytes 3080 | tf_op jit(solution)/shard_map/ppermute | solution.py:19
  133.5 3.6 %collective-permute-start.6 = (f32[3,640]{1,0:T(4,128)S(1)}, f32[3,640]{1,0:T(4,128)S(1)}, u32[]{:S(2)}, u32[]{:S(2)}) collective-permute-start(f32[3,640]{1,0:T(4,128)S(1)} %bitcast.380), channel_id=1, source_target_pairs={{0,1},{1,0},{2,3},{3,2},{4,5},{5,4},{6,7},{7,6},{8,9},{9,8},{10,11... | collective-permute-start | bytes 23048 | tf_op jit(solution)/shard_map/ppermute | solution.py:19
  135.6 3.6 %collective-permute-start.14 = (f32[32,8]{0,1:T(8,128)S(1)}, f32[32,8]{0,1:T(8,128)S(1)}, u32[]{:S(2)}, u32[]{:S(2)}) collective-permute-start(f32[32,8]{0,1:T(8,128)S(1)} %fusion.102), channel_id=1, source_target_pairs={{0,8},{4,12},{8,0},{12,4},{16,24},{20,28},{24,16},{28,20},{1,9},{5... | collective-permute-start | bytes 3080 | tf_op jit(solution)/shard_map/ppermute | solution.py:19
  137.1 7.2 %collective-permute-start.7 = (f32[3,640]{1,0:T(4,128)S(1)}, f32[3,640]{1,0:T(4,128)S(1)}, u32[]{:S(2)}, u32[]{:S(2)}) collective-permute-start(f32[3,640]{1,0:T(4,128)S(1)} %fusion.103), channel_id=1, source_target_pairs={{0,2},{1,3},{2,0},{3,1},{4,6},{5,7},{6,4},{7,5},{8,10},{9,11},{10,... | collective-permute-start | bytes 23048 | tf_op jit(solution)/shard_map/ppermute | solution.py:19
  139.2 4.5 %collective-permute-start.15 = (f32[32,8]{0,1:T(8,128)S(1)}, f32[32,8]{0,1:T(8,128)S(1)}, u32[]{:S(2)}, u32[]{:S(2)}) collective-permute-start(f32[32,8]{0,1:T(8,128)S(1)} %add.187), channel_id=1, source_target_pairs={{0,16},{4,20},{8,24},{12,28},{16,0},{20,4},{24,8},{28,12},{1,17},{... | collective-permute-start | bytes 3080 | tf_op jit(solution)/shard_map/ppermute | solution.py:19
  147.8 6.4 %collective-permute-start.8 = (f32[35,128]{1,0:T(8,128)S(1)}, f32[35,128]{1,0:T(8,128)S(1)}, u32[]{:S(2)}, u32[]{:S(2)}) collective-permute-start(f32[35,128]{1,0:T(8,128)S(1)} %pad_maximum_fusion.4), channel_id=1, source_target_pairs={{0,4},{4,0},{8,12},{12,8},{16,20},{20,16},{24,28},{28,24},{1,5},{5... | collective-permute-start | bytes 53768 | tf_op jit(solution)/shard_map/ppermute | solution.py:19
  149.3 4.9 %collective-permute-start.9 = (f32[35,128]{1,0:T(8,128)S(1)}, f32[35,128]{1,0:T(8,128)S(1)}, u32[]{:S(2)}, u32[]{:S(2)}) collective-permute-start(f32[35,128]{1,0:T(8,128)S(1)} %pad_maximum_fusion.5), channel_id=1, source_target_pairs={{0,8},{4,12},{8,0},{12,4},{16,24},{20,28},{24,16},{28,20},{1,9},{5... | collective-permute-start | bytes 53768 | tf_op jit(solution)/shard_map/ppermute | solution.py:19
  150.8 4.9 %collective-permute-start.10 = (f32[35,128]{1,0:T(8,128)S(1)}, f32[35,128]{1,0:T(8,128)S(1)}, u32[]{:S(2)}, u32[]{:S(2)}) collective-permute-start(f32[35,128]{1,0:T(8,128)S(1)} %pad_maximum_fusion.6), channel_id=1, source_target_pairs={{0,16},{4,20},{8,24},{12,28},{16,0},{20,4},{24,8},{28,12},{1,17},{... | collective-permute-start | bytes 53768 | tf_op jit(solution)/shard_map/ppermute | solution.py:19
Sparse Core Ops, SparseCore 0:
  60.3 25.2 reduce-scatter.4
  126.1 20.8 reduce-scatter.6

commit v5 on v4

--- a/solution.py
+++ b/solution.py
@@ -17,6 +17,17 @@
     mask = 2**bit
     pairs = [(source, source ^ mask) for source in range(lax.axis_size(axis))]
     return lax.ppermute(value, axis, pairs)
+
+
+def halving_sum(value, axis):
+    index = lax.axis_index(axis)
+    for bit in reversed(range(lax.axis_size(axis).bit_length() - 1)):
+        half = value.shape[0] // 2
+        mine = (index >> bit) & 1
+        keep = lax.dynamic_slice_in_dim(value, mine * half, half, 0)
+        give = lax.dynamic_slice_in_dim(value, (1 - mine) * half, half, 0)
+        value = keep + partner(give, axis, bit)
+    return value
 
 
 def geometry(target_pos, source_pos, pair_keep, radial_count):
@@ -121,7 +132,7 @@
     moment_part = jnp.einsum("bclki,ck->clbi", msg_acc, full_weight).reshape(
         all_chan, components, atoms_dev
     )
-    moments = lax.psum_scatter(moment_part, "chan", scatter_dimension=0, tiled=True)
+    moments = halving_sum(moment_part, "chan")
     packed = moments.astype(jnp.bfloat16)
     mixing = jnp.take(mix_weight, jnp.array(ORDER_OF, dtype=jnp.int32), axis=0)
     offset = chan_index * chan_dev

time: 167 us -> 156 us (0.934)
  waiting for transfers between devices: 36.4 us -> 23.3 us
  local copies, waits for them, and re-layouts: 25.8 us -> 23.2 us
  starting transfers between devices: 21.9 us -> 24.4 us
  other arithmetic: 20.2 us -> 22.3 us
    reduce_scatter x1 -> x0, waiting for transfers between devices: 23.6 us -> none  [body(): lax.psum_scatter(moment_part, 'chan', scatter_dimension=0, tiled=True)]
    ppermute x16 -> x18, waiting for transfers between devices: 10.3 us -> 20.8 us  [partner(): return lax.ppermute(value, axis, pairs)]
    ppermute x16 -> x18, starting transfers between devices: 21.8 us -> 24.3 us  [partner(): return lax.ppermute(value, axis, pairs)]
    unnamed x78 -> x82, local copies, waits for them, and re-layouts: 8.14 us -> 6.67 us
  transfers between devices with their start and end apart: 18 -> 19, of which waited for: 8 -> 9; matrix products, arithmetic and copies ran while one was open for 14% -> 17% of each run, Pallas kernels for 0% -> 0%
where the time goes in v5:
time: 156 us; the launch traced here: 155 us
  blocking collectives  26.1 us (17%)
  starting transfers between devices  24.4 us (16%)
  waiting for transfers between devices  23.3 us (15%)
  local copies, waits for them, and re-layouts  23.2 us (15%)
  other arithmetic  22.3 us (14%)
  matrix products  21.2 us (14%)
  between operations  14.9 us (10%)
    ppermute x18, starting transfers between devices, partner(): return lax.ppermute(value, axis, pairs)  24.3 us
    ppermute x18, waiting for transfers between devices, partner(): return lax.ppermute(value, axis, pairs)  20.8 us
    dot_general x1, matrix products, body(): jnp.einsum('bclki,ck->clbi', msg_acc, full_weight)  7.93 us
    dot_general x1, matrix products, body(): jnp.einsum('tclki,tcj->lktij', weighted, source_feat, preferred_element_t...  7.81 us
    all_gather x1, blocking collectives, body(): gathered_piece = lax.all_gather(dz_packed, 'chan', axis=0, tiled=True)  7.65 us
    all_gather x1, blocking collectives, body(): gathered_piece = lax.all_gather(packed, 'chan', axis=0, tiled=True)  7.53 us
    unnamed x82, local copies, waits for them, and re-layouts  6.67 us
    all_gather x1, blocking collectives, body(): full_feat = lax.all_gather(src_feat, 'chan', axis=0, tiled=True)  5.7 us
  transfers between devices with their start and end apart: 19, of which 9 were waited for; matrix products, arithmetic and copies ran while one was open for 17% of the time, Pallas kernels for 0%

profile of v5, /device:TPU:0, one launch (start us, length us, event | category | flops | bytes accessed | tf_op | source)
XLA Modules:
  0.0 155.3 jit_solution(12455476455145526079)
XLA Ops:
  7.3 0.8 compare_and_fusion.2
  8.1 0.8 copy.268
  8.9 0.6 gather_fusion.10
  9.6 3.0 %collective-permute-start.3 = (f32[3,128]{0,1:T(8,128)S(1)}, f32[3,128]{0,1:T(8,128)S(1)}, u32[]{:S(2)}, u32[]{:S(2)}) collective-permute-start(f32[3,128]{0,1:T(8,128)S(1)} %select_bitcast_fusion.2), channel_id=1, source_target_pairs={{0,4},{4,0},{8,12},{12,8},{16,20},{20,16},{24,28},{28,24},{1,5},{5... | collective-permute-start | bytes 4616 | tf_op jit(solution)/shard_map/ppermute | solution.py:19
  12.7 0.6 gather_fusion.11
  13.4 1.6 %collective-permute-start.4 = (f32[3,128]{0,1:T(8,128)S(1)}, f32[3,128]{0,1:T(8,128)S(1)}, u32[]{:S(2)}, u32[]{:S(2)}) collective-permute-start(f32[3,128]{0,1:T(8,128)S(1)} %select_bitcast_fusion.1), channel_id=1, source_target_pairs={{0,8},{4,12},{8,0},{12,4},{16,24},{20,28},{24,16},{28,20},{1,9},{5... | collective-permute-start | bytes 4616 | tf_op jit(solution)/shard_map/ppermute | solution.py:19
  15.1 0.6 gather_fusion.12
  15.8 2.7 %collective-permute-start.5 = (f32[3,128]{0,1:T(8,128)S(1)}, f32[3,128]{0,1:T(8,128)S(1)}, u32[]{:S(2)}, u32[]{:S(2)}) collective-permute-start(f32[3,128]{0,1:T(8,128)S(1)} %select_bitcast_fusion), channel_id=1, source_target_pairs={{0,16},{4,20},{8,24},{12,28},{16,0},{20,4},{24,8},{28,12},{1,17},{... | collective-permute-start | bytes 4616 | tf_op jit(solution)/shard_map/ppermute | solution.py:19
  18.5 0.8 copy.260
  19.3 0.7 gather_fusion.7
  20.0 0.7 select_bitcast_fusion.5
  21.2 0.7 gather_fusion.8
  21.9 0.7 select_bitcast_fusion.4
  23.1 0.8 copy.259
  25.8 0.7 gather_fusion.9
  26.5 0.6 gather_fusion.1
  27.2 0.7 select_bitcast_fusion.3
  27.9 5.2 %all-gather = f32[4,32,8]{1,2,0:T(8,128)S(1)} all-gather(f32[1,32,8]{1,2,0:T(8,128)S(1)} %bitcast.382), channel_id=1, replica_groups=mesh['space'=8,'chan'=4] {'chan'}, dimensions={0}, use_global_device_ids=true | all-gather | bytes 5120 | tf_op jit(solution)/shard_map/all_gather | solution.py:98
  35.9 0.9 copy.263
  36.8 0.8 copy.264
  37.6 0.6 collective-permute-done.2
  38.4 5.7 %all_gather.12 = bf16[128,640]{1,0:T(8,128)(2,1)S(1)} all-gather(bf16[32,640]{1,0:T(8,128)(2,1)S(1)} %pad_maximum_fusion.3), channel_id=1, replica_groups=mesh['space'=8,'chan'=4] {'chan'}, dimensions={0}, use_global_device_ids=true | all-gather | bytes 204800 | tf_op jit(solution)/shard_map/all_gather | solution.py:97
  45.0 1.5 fusion.7
  46.5 7.9 %fusion.3 = f32[128,1,2,9,128]{4,1,3,2,0:T(1,128)S(1)} fusion(f32[128,8,1,1,1]{1,2,4,3,0:T(1,128)S(1)} %bitcast.379, f32[2,128,9,8,128]{4,1,3,2,0:T(8,128)S(1)} %bitcast.370), kind=kOutput, calls=%fused_computation.20 | convolution fusion | flops 4718592 | bytes 10620928 | tf_op jit(solution)/shard_map/bclki,ck->clbi/dot_general | solution.py:132
  54.4 0.6 copy.359
  55.0 0.9 reshape.464
  56.1 1.5 collective-permute-start.6
  57.7 0.7 copy.280
  59.0 12.8 %collective-permute-done.6 = f32[64,9,256]{2,0,1:T(8,128)} collective-permute-done((f32[64,9,256]{2,0,1:T(8,128)S(1)}, f32[64,9,256]{2,0,1:T(8,128)}, u32[]{:S(2)}, u32[]{:S(2)}) %collective-permute-start.6) | collective-permute-done | bytes 589856 | tf_op jit(solution)/shard_map/ppermute | solution.py:19
  71.8 1.4 dynamic-slice_add_fusion
  73.3 0.6 fusion.92
  73.9 0.7 broadcast_multiply_fusion
  74.9 7.5 %all_gather.14 = bf16[128,9,256]{2,0,1:T(8,128)(2,1)S(1)} all-gather(bf16[32,9,256]{2,0,1:T(8,128)(2,1)S(1)} %add_convert_fusion), channel_id=1, replica_groups=mesh['space'=8,'chan'=4] {'chan'}, dimensions={0}, use_global_device_ids=true | all-gather | bytes 737280 | tf_op jit(solution)/shard_map/all_gather | solution.py:139
  82.7 0.7 multiply_convert_fusion.2
  83.5 7.7 %all_gather.15 = bf16[128,9,256]{2,0,1:T(8,128)(2,1)S(1)} all-gather(bf16[32,9,256]{2,0,1:T(8,128)(2,1)S(1)} %pad_maximum_fusion.1), channel_id=1, replica_groups=mesh['space'=8,'chan'=4] {'chan'}, dimensions={0}, use_global_device_ids=true | all-gather | bytes 737280 | tf_op jit(solution)/shard_map/all_gather | solution.py:158
  91.5 0.7 gather_fusion.6
  92.3 1.4 copy.281
  93.7 7.8 %fusion.1 = (f32[9,2,128,128]{2,3,0,1:T(8,128)S(1)}, f32[8,2,128,128]{2,3,0,1:T(8,128)}, bf16[9,8,2,128,128]{3,4,1,0,2:T(8,128)(2,1)}) fusion(f32[8,2,128,128]{2,3,0,1:T(8,128)} %copy-done.3, f32[2,128,9,128]{3,1,2,0:T(8,128)} %copy.281, f32[2,128,8]{1,2,0:T(8,128)S(1)} %copy-done.26, bf16[2,128,128]{2,1,0:T(8,128)(2,1)S(1)} %copy-done.11, ...), kind=kOutput, calls=%fused_computation.18 | convolution fusion | flops 622297088 | bytes 10428416 | tf_op jit(solution)/shard_map/tclki,tcj->lktij/dot_general | solution.py:175
  101.6 0.8 fusion.63
  102.4 1.4 copy.335
  103.8 5.0 %fusion = f32[128,8]{0,1:T(8,128)S(1)} fusion(f32[2,128,9,8,128,1]{4,1,3,2,5,0:T(8,128)} %copy-done.2, f32[128,2,128,9]{2,0,3,1:T(8,128)} %copy.335), kind=kLoop, calls=%fused_computation.15 | loop fusion | flops 4717568 | bytes 10620928 | tf_op jit(solution)/shard_map/bclki,bcli->ck/dot_general | solution.py:165
  109.2 3.4 %fusion.10 = f32[2,128,128]{2,1,0:T(8,128)S(1)} fusion(bf16[9,8,2,128,128]{3,4,1,0,2:T(8,128)(2,1)} %get-tuple-element.48, f32[2,128,9,128]{3,1,2,0:T(8,128)S(1)} %copy-done.5, f32[2,128,8]{1,2,0:T(8,128)S(1)} %copy-done.26), kind=kOutput, calls=%fused_computation.33 | convolution fusion | flops 608698368 | bytes 6037504 | tf_op jit(solution)/shard_map/tclki,lktij->tcj/dot_general | solution.py:172
  113.0 0.9 copy.321
  113.9 1.8 %fusion.20 = (f32[2,128,128]{1,2,0:T(8,128)S(1)}, f32[2,128,128]{1,2,0:T(8,128)S(1)}) fusion(f32[8,2,128,128]{2,3,0,1:T(8,128)} %get-tuple-element.35, f32[8]{0:T(128)S(1)} %copy-done.33, f32[2,128,128]{1,2,0:T(8,128)S(1)} %get-tuple-element.54, f32[2,128,128]{1,2,0:T(8,128)S(1)} %get-tuple-element.55), kind=kLoop, calls=%fused_computation.39 | loop fusion | flops 2818048 | bytes 1572896 | tf_op jit(solution)/shard_map/transpose(jvp())/reduce_sum | solution.py:56
  116.1 0.7 add.206
  116.8 1.5 collective-permute-start.14
  118.6 1.8 %collective-permute-done.14 = f32[128,8]{0,1:T(8,128)S(1)} collective-permute-done((f32[128,8]{0,1:T(8,128)S(1)}, f32[128,8]{0,1:T(8,128)S(1)}, u32[]{:S(2)}, u32[]{:S(2)}) %collective-permute-start.14) | collective-permute-done | bytes 4128 | tf_op jit(solution)/shard_map/ppermute | solution.py:19
  120.5 1.5 collective-permute-start.15
  122.2 1.9 %collective-permute-done.15 = f32[32,8]{0,1:T(8,128)S(1)} collective-permute-done((f32[32,8]{0,1:T(8,128)S(1)}, f32[32,8]{0,1:T(8,128)S(1)}, u32[]{:S(2)}, u32[]{:S(2)}) %collective-permute-start.15) | collective-permute-done | bytes 1056 | tf_op jit(solution)/shard_map/ppermute | solution.py:19
  124.2 1.6 %collective-permute-start.16 = (f32[32,8]{0,1:T(8,128)S(1)}, f32[32,8]{0,1:T(8,128)S(1)}, u32[]{:S(2)}, u32[]{:S(2)}) collective-permute-start(f32[32,8]{0,1:T(8,128)S(1)} %fusion.102), channel_id=1, source_target_pairs={{0,8},{4,12},{8,0},{12,4},{16,24},{20,28},{24,16},{28,20},{1,9},{5... | collective-permute-start | bytes 3080 | tf_op jit(solution)/shard_map/ppermute | solution.py:19
  125.7 1.5 collective-permute-start.9
  127.8 2.3 %collective-permute-start.17 = (f32[32,8]{0,1:T(8,128)S(1)}, f32[32,8]{0,1:T(8,128)S(1)}, u32[]{:S(2)}, u32[]{:S(2)}) collective-permute-start(f32[32,8]{0,1:T(8,128)S(1)} %add.209), channel_id=1, source_target_pairs={{0,16},{4,20},{8,24},{12,28},{16,0},{20,4},{24,8},{28,12},{1,17},{... | collective-permute-start | bytes 3080 | tf_op jit(solution)/shard_map/ppermute | solution.py:19
  130.1 0.7 pad_maximum_fusion
  130.8 1.5 collective-permute-done.17
  133.0 2.4 %reduce-scatter.4.cloned.1.call-done = f32[32,640]{1,0:T(8,128)} async-done(((f32[128,640]{1,0:T(8,128)}), f32[32,640]{1,0:T(8,128)}) %reduce-scatter.4.cloned.1.call-update) | async-done | bytes 81936
  135.5 0.8 fusion.95
  136.2 1.5 collective-permute-start.10
  137.8 1.5 collective-permute-start.11
  139.3 2.4 %collective-permute-start.12 = (f32[35,128]{1,0:T(8,128)S(1)}, f32[35,128]{1,0:T(8,128)S(1)}, u32[]{:S(2)}, u32[]{:S(2)}) collective-permute-start(f32[35,128]{1,0:T(8,128)S(1)} %pad_maximum_fusion.6), channel_id=1, source_target_pairs={{0,16},{4,20},{8,24},{12,28},{16,0},{20,4},{24,8},{28,12},{1,17},{... | collective-permute-start | bytes 53768 | tf_op jit(solution)/shard_map/ppermute | solution.py:19
  141.7 0.8 slice.128
  142.7 1.5 collective-permute-done.12
  144.3 2.7 %scatter_fusion = f32[35,256]{0,1:T(8,128)S(1)} fusion(f32[35,256]{0,1:T(8,128)S(1)} %pad_maximum_fusion.2, s32[384]{0:T(512)S(1)} %copy-done.25, f32[384,35]{1,0:T(8,128)S(1)} %copy.297), kind=kCustom, calls=%fused_computation.13 | custom fusion | flops 13440 | bytes 162816 | tf_op jit(solution)/shard_map/scatter-add | solution.py:206
  147.1 0.7 copy.299
  147.8 0.7 copy.298
  (175 shorter events, 12.4 us)
Async XLA Ops:
  7.2 51.2 %copy-start = (bf16[3,128,128]{2,1,0:T(8,128)(2,1)S(1)}, bf16[3,128,128]{2,1,0:T(8,128)(2,1)}, u32[]{:S(2)}) copy-start(bf16[3,128,128]{2,1,0:T(8,128)(2,1)} %param.19) | copy-start | bytes 294916
  7.2 26.3 %copy-start.22 = (f32[3,256]{1,0:T(4,128)S(1)}, f32[3,256]{1,0:T(4,128)}, u32[]{:S(2)}) copy-start(f32[3,256]{1,0:T(4,128)} %param.13) | copy-start | bytes 9220
  7.2 19.3 %copy-start.1 = (s32[8]{0:T(128)S(1)}, s32[8]{0:T(128)}, u32[]{:S(2)}) copy-start(s32[8]{0:T(128)} %param.17) | copy-start | bytes 100
  7.2 20.7 %copy-start.29 = (f32[32,8]{0,1:T(8,128)S(1)}, f32[32,8]{0,1:T(8,128)}, u32[]{:S(2)}) copy-start(f32[32,8]{0,1:T(8,128)} %param.18) | copy-start | bytes 3076
  7.2 128.2 %reduce-scatter.4.cloned.1.call-start = ((), (), s32[]{:S(2)}) async-start(), calls=%async_computation.1 | async-start | bytes 409600
  9.6 23.5 %collective-permute-start.3 = (f32[3,128]{0,1:T(8,128)S(1)}, f32[3,128]{0,1:T(8,128)S(1)}, u32[]{:S(2)}, u32[]{:S(2)}) collective-permute-start(f32[3,128]{0,1:T(8,128)S(1)} %select_bitcast_fusion.2), channel_id=1, source_target_pairs={{0,4},{4,0},{8,12},{12,8},{16,20},{20,16},{24,28},{28,24},{1,5},{5... | collective-permute-start | bytes 4616 | tf_op jit(solution)/shard_map/ppermute | solution.py:19
  13.4 19.9 %collective-permute-start.4 = (f32[3,128]{0,1:T(8,128)S(1)}, f32[3,128]{0,1:T(8,128)S(1)}, u32[]{:S(2)}, u32[]{:S(2)}) collective-permute-start(f32[3,128]{0,1:T(8,128)S(1)} %select_bitcast_fusion.1), channel_id=1, source_target_pairs={{0,8},{4,12},{8,0},{12,4},{16,24},{20,28},{24,16},{28,20},{1,9},{5... | collective-permute-start | bytes 4616 | tf_op jit(solution)/shard_map/ppermute | solution.py:19
  15.8 17.6 %collective-permute-start.5 = (f32[3,128]{0,1:T(8,128)S(1)}, f32[3,128]{0,1:T(8,128)S(1)}, u32[]{:S(2)}, u32[]{:S(2)}) collective-permute-start(f32[3,128]{0,1:T(8,128)S(1)} %select_bitcast_fusion), channel_id=1, source_target_pairs={{0,16},{4,20},{8,24},{12,28},{16,0},{20,4},{24,8},{28,12},{1,17},{... | collective-permute-start | bytes 4616 | tf_op jit(solution)/shard_map/ppermute | solution.py:19
  20.7 15.2 %collective-permute-start = (bf16[32,128]{0,1:T(8,128)(2,1)}, bf16[32,128]{0,1:T(8,128)(2,1)}, u32[]{:S(2)}, u32[]{:S(2)}) collective-permute-start(bf16[32,128]{0,1:T(8,128)(2,1)} %select_bitcast_fusion.5), channel_id=1, source_target_pairs={{0,4},{4,0},{8,12},{12,8},{16,20},{20,16},{24,28},{28,24},{1,5},{5... | collective-permute-start | bytes 24584 | tf_op jit(solution)/shard_map/ppermute | solution.py:19
  22.6 14.2 %collective-permute-start.1 = (bf16[32,128]{0,1:T(8,128)(2,1)}, bf16[32,128]{0,1:T(8,128)(2,1)}, u32[]{:S(2)}, u32[]{:S(2)}) collective-permute-start(bf16[32,128]{0,1:T(8,128)(2,1)} %select_bitcast_fusion.4), channel_id=1, source_target_pairs={{0,8},{4,12},{8,0},{12,4},{16,24},{20,28},{24,16},{28,20},{1,9},{5... | collective-permute-start | bytes 24584 | tf_op jit(solution)/shard_map/ppermute | solution.py:19
  25.2 10.1 %copy-start.30 = (f32[2]{0:T(128)}, f32[2]{0:T(128)S(1)}, u32[]{:S(2)}) copy-start(f32[2]{0:T(128)S(1)} %compare_convert_fusion) | copy-start | bytes 28
  25.3 10.1 %copy-start.6 = (f32[128,128]{0,1:T(8,128)}, f32[128,128]{0,1:T(8,128)S(1)}, u32[]{:S(2)}) copy-start(f32[128,128]{0,1:T(8,128)S(1)} %fusion.82) | copy-start | bytes 196612
  27.2 46.8 %copy-start.23 = (f32[2]{0:T(128)}, f32[2]{0:T(128)S(1)}, u32[]{:S(2)}) copy-start(f32[2]{0:T(128)S(1)} %convert_element_type.57) | copy-start | bytes 28
  27.9 5.5 %copy-start.20 = (f32[2,5]{0,1:T(8,128)}, f32[2,5]{0,1:T(8,128)S(1)}, u32[]{:S(2)}) copy-start(f32[2,5]{0,1:T(8,128)S(1)} %get-tuple-element.71) | copy-start | bytes 124
  27.9 29.9 %copy-start.14 = (f32[2,5]{0,1:T(8,128)}, f32[2,5]{0,1:T(8,128)S(1)}, u32[]{:S(2)}) copy-start(f32[2,5]{0,1:T(8,128)S(1)} %get-tuple-element.70) | copy-start | bytes 124
  33.2 5.1 %collective-permute-start.2 = (bf16[32,128]{0,1:T(8,128)(2,1)}, bf16[32,128]{0,1:T(8,128)(2,1)S(1)}, u32[]{:S(2)}, u32[]{:S(2)}) collective-permute-start(bf16[32,128]{0,1:T(8,128)(2,1)} %select_bitcast_fusion.3), channel_id=1, source_target_pairs={{0,16},{4,20},{8,24},{12,28},{16,0},{20,4},{24,8},{28,12},{1,17},{... | collective-permute-start | bytes 24584 | tf_op jit(solution)/shard_map/ppermute | solution.py:19
  34.1 1.0 copy-start.16
  34.7 0.6 copy-start.18
  34.9 0.6 copy-start.32
  35.4 2.9 %copy-start.13 = (bf16[32,256]{1,0:T(8,128)(2,1)S(1)}, bf16[32,256]{1,0:T(8,128)(2,1)}, u32[]{:S(2)}) copy-start(bf16[32,256]{1,0:T(8,128)(2,1)} %param.14) | copy-start | bytes 49156
  35.8 10.6 %copy-start.3 = (f32[8,2,128,128]{2,3,0,1:T(8,128)}, f32[8,2,128,128]{2,3,0,1:T(8,128)S(1)}, u32[]{:S(2)}) copy-start(f32[8,2,128,128]{2,3,0,1:T(8,128)S(1)} %fusion.19) | copy-start | bytes 3145732
  35.9 10.6 %copy-start.4 = (f32[9,2,128,128]{2,3,1,0:T(8,128)}, f32[9,2,128,128]{2,3,1,0:T(8,128)S(1)}, u32[]{:S(2)}) copy-start(f32[9,2,128,128]{2,3,1,0:T(8,128)S(1)} %multiply_dynamic-update-slice_fusion) | copy-start | bytes 3538948
  45.0 1.5 copy-start.10
  46.5 8.6 %copy-start.2 = (f32[2,128,9,8,128,1]{4,1,3,2,5,0:T(8,128)}, f32[2,128,9,8,128,1]{4,1,3,2,5,0:T(8,128)S(1)}, u32[]{:S(2)}) copy-start(f32[2,128,9,8,128,1]{4,1,3,2,5,0:T(8,128)S(1)} %fusion.7) | copy-start | bytes 28311556
  56.0 1.6 %copy-start.12 = (bf16[32,9,256]{2,0,1:T(8,128)(2,1)S(1)}, bf16[32,9,256]{2,0,1:T(8,128)(2,1)}, u32[]{:S(2)}) copy-start(bf16[32,9,256]{2,0,1:T(8,128)(2,1)} %param.20) | copy-start | bytes 442372
  56.0 2.4 %copy-start.34 = (s32[9]{0:T(128)S(1)}, s32[9]{0:T(128)}, u32[]{:S(2)}) copy-start(s32[9]{0:T(128)} %constant.104) | copy-start | bytes 112
  56.1 15.7 %collective-permute-start.6 = (f32[64,9,256]{2,0,1:T(8,128)S(1)}, f32[64,9,256]{2,0,1:T(8,128)}, u32[]{:S(2)}, u32[]{:S(2)}) collective-permute-start(f32[64,9,256]{2,0,1:T(8,128)S(1)} %constant_dynamic-slice_fusion.2), channel_id=1, source_target_pairs={{0,2},{1,3},{2,0},{3,1},{4,6},{5,7},{6,4},{7,5},{8,10},{9,11},{10,... | collective-permute-start | bytes 1769480 | tf_op jit(solution)/shard_map/ppermute | solution.py:19
  59.0 14.3 %copy-start.27 = (s32[3,128]{1,0:T(4,128)S(1)}, s32[3,128]{1,0:T(4,128)}, u32[]{:S(2)}) copy-start(s32[3,128]{1,0:T(4,128)} %param.15) | copy-start | bytes 4612
  73.2 1.6 %collective-permute-start.7 = (f32[32,9,256]{2,0,1:T(8,128)S(1)}, f32[32,9,256]{2,0,1:T(8,128)S(1)}, u32[]{:S(2)}, u32[]{:S(2)}) collective-permute-start(f32[32,9,256]{2,0,1:T(8,128)S(1)} %constant_dynamic-slice_fusion.1), channel_id=1, source_target_pairs={{0,1},{1,0},{2,3},{3,2},{4,5},{5,4},{6,7},{7,6},{8,9},{9,8},{10,11... | collective-permute-start | bytes 884744 | tf_op jit(solution)/shard_map/ppermute | solution.py:19
  92.2 1.4 copy-start.11
  92.2 1.4 copy-start.26
  103.8 5.4 %copy-start.5 = (f32[2,128,9,128]{3,1,2,0:T(8,128)S(1)}, f32[2,128,9,128]{3,1,2,0:T(8,128)}, u32[]{:S(2)}) copy-start(f32[2,128,9,128]{3,1,2,0:T(8,128)} %copy.281) | copy-start | bytes 3538948
  108.8 7.3 %collective-permute-start.13 = (f32[128,8]{0,1:T(8,128)S(1)}, f32[128,8]{0,1:T(8,128)}, u32[]{:S(2)}, u32[]{:S(2)}) collective-permute-start(f32[128,8]{0,1:T(8,128)S(1)} %fusion), channel_id=1, source_target_pairs={{0,1},{1,0},{2,3},{3,2},{4,5},{5,4},{6,7},{7,6},{8,9},{9,8},{10,11... | collective-permute-start | bytes 12296 | tf_op jit(solution)/shard_map/ppermute | solution.py:19
  109.2 3.4 %copy-start.28 = (f32[2,5]{1,0:T(2,128)S(1)}, f32[2,5]{1,0:T(2,128)}, u32[]{:S(2)}) copy-start(f32[2,5]{1,0:T(2,128)} %copy.280) | copy-start | bytes 124
  112.7 1.2 copy-start.33
  112.9 2.7 %copy-start.7 = (f32[128,128]{0,1:T(8,128)S(1)}, f32[128,128]{0,1:T(8,128)}, u32[]{:S(2)}) copy-start(f32[128,128]{0,1:T(8,128)} %copy-done.6) | copy-start | bytes 196612
  113.0 2.7 %copy-start.24 = (f32[2]{0:T(128)S(1)}, f32[2]{0:T(128)}, u32[]{:S(2)}) copy-start(f32[2]{0:T(128)} %copy-done.23) | copy-start | bytes 28
  113.0 2.7 %copy-start.31 = (f32[2]{0:T(128)S(1)}, f32[2]{0:T(128)}, u32[]{:S(2)}) copy-start(f32[2]{0:T(128)} %copy-done.30) | copy-start | bytes 28
  115.7 2.6 %copy-start.9 = (f32[2,1,128,128]{2,3,0,1:T(8,128)S(1)}, f32[2,1,128,128]{2,3,0,1:T(8,128)}, u32[]{:S(2)}) copy-start(f32[2,1,128,128]{2,3,0,1:T(8,128)} %get-tuple-element.50) | copy-start | bytes 393220
  115.7 2.6 %copy-start.17 = (f32[2,3,128]{2,0,1:T(2,128)S(1)}, f32[2,3,128]{2,0,1:T(2,128)}, u32[]{:S(2)}) copy-start(f32[2,3,128]{2,0,1:T(2,128)} %copy-done.16) | copy-start | bytes 9220
  115.7 2.6 %copy-start.19 = (f32[2,3,128]{2,0,1:T(2,128)S(1)}, f32[2,3,128]{2,0,1:T(2,128)}, u32[]{:S(2)}) copy-start(f32[2,3,128]{2,0,1:T(2,128)} %copy-done.18) | copy-start | bytes 9220
  115.7 6.3 %copy-start.15 = (f32[2,5]{0,1:T(8,128)S(1)}, f32[2,5]{0,1:T(8,128)}, u32[]{:S(2)}) copy-start(f32[2,5]{0,1:T(8,128)} %copy-done.14) | copy-start | bytes 124
  115.7 6.3 %copy-start.21 = (f32[2,5]{0,1:T(8,128)S(1)}, f32[2,5]{0,1:T(8,128)}, u32[]{:S(2)}) copy-start(f32[2,5]{0,1:T(8,128)} %copy-done.20) | copy-start | bytes 124
  115.7 14.4 %copy-start.8 = (bf16[32,8,256]{2,0,1:T(8,128)(2,1)S(1)}, bf16[32,8,256]{2,0,1:T(8,128)(2,1)}, u32[]{:S(2)}) copy-start(bf16[32,8,256]{2,0,1:T(8,128)(2,1)} %get-tuple-element.60) | copy-start | bytes 393220
  116.8 3.6 %collective-permute-start.14 = (f32[128,8]{0,1:T(8,128)S(1)}, f32[128,8]{0,1:T(8,128)S(1)}, u32[]{:S(2)}, u32[]{:S(2)}) collective-permute-start(f32[128,8]{0,1:T(8,128)S(1)} %add.206), channel_id=1, source_target_pairs={{0,2},{1,3},{2,0},{3,1},{4,6},{5,7},{6,4},{7,5},{8,10},{9,11},{10,... | collective-permute-start | bytes 12296 | tf_op jit(solution)/shard_map/ppermute | solution.py:19
  118.3 26.0 %copy-start.25 = (s32[384]{0:T(512)S(1)}, s32[384]{0:T(512)}, u32[]{:S(2)}) copy-start(s32[384]{0:T(512)} %fusion.92) | copy-start | bytes 4612
  120.5 3.6 %collective-permute-start.15 = (f32[32,8]{0,1:T(8,128)S(1)}, f32[32,8]{0,1:T(8,128)S(1)}, u32[]{:S(2)}, u32[]{:S(2)}) collective-permute-start(f32[32,8]{0,1:T(8,128)S(1)} %constant_dynamic-slice_fusion), channel_id=1, source_target_pairs={{0,4},{4,0},{8,12},{12,8},{16,20},{20,16},{24,28},{28,24},{1,5},{5... | collective-permute-start | bytes 3080 | tf_op jit(solution)/shard_map/ppermute | solution.py:19
  122.1 3.6 %collective-permute-start.8 = (f32[3,640]{1,0:T(4,128)S(1)}, f32[3,640]{1,0:T(4,128)S(1)}, u32[]{:S(2)}, u32[]{:S(2)}) collective-permute-start(f32[3,640]{1,0:T(4,128)S(1)} %bitcast.380), channel_id=1, source_target_pairs={{0,1},{1,0},{2,3},{3,2},{4,5},{5,4},{6,7},{7,6},{8,9},{9,8},{10,11... | collective-permute-start | bytes 23048 | tf_op jit(solution)/shard_map/ppermute | solution.py:19
  124.2 3.6 %collective-permute-start.16 = (f32[32,8]{0,1:T(8,128)S(1)}, f32[32,8]{0,1:T(8,128)S(1)}, u32[]{:S(2)}, u32[]{:S(2)}) collective-permute-start(f32[32,8]{0,1:T(8,128)S(1)} %fusion.102), channel_id=1, source_target_pairs={{0,8},{4,12},{8,0},{12,4},{16,24},{20,28},{24,16},{28,20},{1,9},{5... | collective-permute-start | bytes 3080 | tf_op jit(solution)/shard_map/ppermute | solution.py:19
  125.7 7.1 %collective-permute-start.9 = (f32[3,640]{1,0:T(4,128)S(1)}, f32[3,640]{1,0:T(4,128)S(1)}, u32[]{:S(2)}, u32[]{:S(2)}) collective-permute-start(f32[3,640]{1,0:T(4,128)S(1)} %fusion.103), channel_id=1, source_target_pairs={{0,2},{1,3},{2,0},{3,1},{4,6},{5,7},{6,4},{7,5},{8,10},{9,11},{10,... | collective-permute-start | bytes 23048 | tf_op jit(solution)/shard_map/ppermute | solution.py:19
  127.8 4.5 %collective-permute-start.17 = (f32[32,8]{0,1:T(8,128)S(1)}, f32[32,8]{0,1:T(8,128)S(1)}, u32[]{:S(2)}, u32[]{:S(2)}) collective-permute-start(f32[32,8]{0,1:T(8,128)S(1)} %add.209), channel_id=1, source_target_pairs={{0,16},{4,20},{8,24},{12,28},{16,0},{20,4},{24,8},{28,12},{1,17},{... | collective-permute-start | bytes 3080 | tf_op jit(solution)/shard_map/ppermute | solution.py:19
  136.2 6.4 %collective-permute-start.10 = (f32[35,128]{1,0:T(8,128)S(1)}, f32[35,128]{1,0:T(8,128)S(1)}, u32[]{:S(2)}, u32[]{:S(2)}) collective-permute-start(f32[35,128]{1,0:T(8,128)S(1)} %pad_maximum_fusion.4), channel_id=1, source_target_pairs={{0,4},{4,0},{8,12},{12,8},{16,20},{20,16},{24,28},{28,24},{1,5},{5... | collective-permute-start | bytes 53768 | tf_op jit(solution)/shard_map/ppermute | solution.py:19
  137.8 4.9 %collective-permute-start.11 = (f32[35,128]{1,0:T(8,128)S(1)}, f32[35,128]{1,0:T(8,128)S(1)}, u32[]{:S(2)}, u32[]{:S(2)}) collective-permute-start(f32[35,128]{1,0:T(8,128)S(1)} %pad_maximum_fusion.5), channel_id=1, source_target_pairs={{0,8},{4,12},{8,0},{12,4},{16,24},{20,28},{24,16},{28,20},{1,9},{5... | collective-permute-start | bytes 53768 | tf_op jit(solution)/shard_map/ppermute | solution.py:19
  139.3 4.9 %collective-permute-start.12 = (f32[35,128]{1,0:T(8,128)S(1)}, f32[35,128]{1,0:T(8,128)S(1)}, u32[]{:S(2)}, u32[]{:S(2)}) collective-permute-start(f32[35,128]{1,0:T(8,128)S(1)} %pad_maximum_fusion.6), channel_id=1, source_target_pairs={{0,16},{4,20},{8,24},{12,28},{16,0},{20,4},{24,8},{28,12},{1,17},{... | collective-permute-start | bytes 53768 | tf_op jit(solution)/shard_map/ppermute | solution.py:19
Sparse Core Ops, SparseCore 0:
  114.0 21.4 reduce-scatter.3

commit v6 on v5

--- a/solution.py
+++ b/solution.py
@@ -100,21 +100,24 @@
     src_atoms = src_pos.shape[1]
     src_blocks = src_atoms // block_size
     own_blocks = atoms_dev // block_size
-    tiles_here = pair_tiles.shape[0] // chan_count
-    my_tiles = chan_index * tiles_here + jnp.arange(tiles_here, dtype=jnp.int32)
-    my_pairs = jnp.take(pair_tiles, my_tiles, axis=0, mode="clip")
-    target_idx = my_pairs[:, 0]
-    source_idx = my_pairs[:, 1]
-    live = jnp.take(tile_live, my_tiles, mode="clip").astype(jnp.float32)
+    rows = block_size // chan_count
+    row_low = chan_index * rows
+    target_idx = pair_tiles[:, 0]
+    source_idx = pair_tiles[:, 1]
+    live = tile_live.astype(jnp.float32)
     block_ids = jnp.arange(src_blocks, dtype=jnp.int32)
     target_hot = (target_idx[:, None] == block_ids[None]).astype(jnp.float32) * live[:, None]
     source_hot = (source_idx[:, None] == block_ids[None]).astype(jnp.float32) * live[:, None]
     same = (target_idx == source_idx).astype(jnp.float32)
-    eye = jnp.eye(block_size, dtype=jnp.float32)
+    eye = (
+        (row_low + jnp.arange(rows, dtype=jnp.int32))[:, None]
+        == jnp.arange(block_size, dtype=jnp.int32)[None]
+    ).astype(jnp.float32)
     pair_keep = live[:, None, None] * (1.0 - same[:, None, None] * eye[None])
     pos_blocks = jnp.moveaxis(src_pos.reshape(3, src_blocks, block_size), 1, 0)
+    pos_rows = lax.dynamic_slice_in_dim(pos_blocks, row_low, rows, 2)
     feat_blocks = jnp.moveaxis(full_feat.reshape(all_chan, src_blocks, block_size), 1, 0)
-    target_pos = jnp.take(pos_blocks, target_idx, axis=0, mode="clip")
+    target_pos = jnp.take(pos_rows, target_idx, axis=0, mode="clip")
     source_pos = jnp.take(pos_blocks, source_idx, axis=0, mode="clip")
     source_feat = jnp.take(feat_blocks, source_idx, axis=0, mode="clip")
 
@@ -129,40 +132,44 @@
     msg_acc = jnp.einsum(
         "lktij,tbcj->bclki", pair_values, routed_feat, preferred_element_type=jnp.float32
     )
-    moment_part = jnp.einsum("bclki,ck->clbi", msg_acc, full_weight).reshape(
-        all_chan, components, atoms_dev
-    )
-    moments = halving_sum(moment_part, "chan")
+    moments = jnp.einsum("bclki,ck->clbi", msg_acc, full_weight)
     packed = moments.astype(jnp.bfloat16)
     mixing = jnp.take(mix_weight, jnp.array(ORDER_OF, dtype=jnp.int32), axis=0)
     offset = chan_index * chan_dev
-    gathered_piece = lax.all_gather(packed, "chan", axis=0, tiled=True)
-    weight_part = lax.dynamic_slice(
-        mixing, (0, offset, 0), (components, chan_dev, gathered_piece.shape[0])
-    )
     mixed_out = jnp.einsum(
-        "lxc,cli->xli", weight_part, gathered_piece, preferred_element_type=jnp.float32
-    )
-    scalar_part = mixed_out[:, 0, :]
+        "lxc,clbi->xlbi", mixing, packed, preferred_element_type=jnp.float32
+    )
+    scalar_part = mixed_out[:, 0]
     gate_value = jax.nn.sigmoid(scalar_part)
-    result = jnp.concatenate(
-        [(scalar_part * gate_value)[:, None, :], mixed_out[:, 1:, :] * gate_value[:, None, :]],
+    result_rows = jnp.concatenate(
+        [(scalar_part * gate_value)[:, None], mixed_out[:, 1:] * gate_value[:, None]],
         axis=1,
     ).astype(jnp.bfloat16)
-    upstream = out_grad.astype(jnp.float32)
-    scalar_grad = upstream[:, 0, :] * (
+    result = lax.all_to_all(
+        result_rows.reshape(all_chan, components, own_blocks, 1, rows),
+        "chan",
+        0,
+        3,
+        tiled=True,
+    ).reshape(chan_dev, components, atoms_dev)
+    grad_rows = lax.all_to_all(
+        out_grad.reshape(chan_dev, components, own_blocks, chan_count, rows),
+        "chan",
+        3,
+        0,
+        tiled=True,
+    ).reshape(all_chan, components, own_blocks, rows)
+    upstream = grad_rows.astype(jnp.float32)
+    scalar_grad = upstream[:, 0] * (
         gate_value * (1.0 + scalar_part * (1.0 - gate_value))
-    ) + gate_value * (1.0 - gate_value) * jnp.sum(upstream[:, 1:, :] * mixed_out[:, 1:, :], axis=1)
-    rest_grad = upstream[:, 1:, :] * gate_value[:, None, :]
-    dz_packed = jnp.concatenate([scalar_grad[:, None, :], rest_grad], axis=1).astype(jnp.bfloat16)
-    gathered_piece = lax.all_gather(dz_packed, "chan", axis=0, tiled=True)
+    ) + gate_value * (1.0 - gate_value) * jnp.sum(upstream[:, 1:] * mixed_out[:, 1:], axis=1)
+    rest_grad = upstream[:, 1:] * gate_value[:, None]
+    dz_packed = jnp.concatenate([scalar_grad[:, None], rest_grad], axis=1).astype(jnp.bfloat16)
     moment_grad_all = jnp.einsum(
-        "lxc,xli->cli", mixing, gathered_piece, preferred_element_type=jnp.float32
-    )
-    grad_blocks = jnp.moveaxis(
-        moment_grad_all.reshape(all_chan, components, own_blocks, block_size), 2, 0
-    )
-    grad_rad = jnp.einsum("bclki,bcli->ck", msg_acc, grad_blocks)
+        "lxc,xlbi->clbi", mixing, dz_packed, preferred_element_type=jnp.float32
+    )
+    grad_rad = jnp.einsum("bclki,clbi->ck", msg_acc, moment_grad_all)
+    grad_blocks = jnp.moveaxis(moment_grad_all, 2, 0)
     tile_grad = jnp.take(grad_blocks, target_idx, axis=0, mode="clip")
     weighted = (
         live[:, None, None, None, None]
@@ -181,10 +188,13 @@
     grad_part = jnp.sum(
         source_hot[:, None, :, None] * grad_source[:, :, None, :], axis=0
     ).reshape(all_chan, src_atoms)
-    dpos_src = jnp.sum(
-        target_hot[:, None, :, None] * target_grad[:, :, None, :]
-        + source_hot[:, None, :, None] * source_grad_pos[:, :, None, :],
-        axis=0,
+    row_hot = (jnp.arange(chan_count, dtype=jnp.int32) == chan_index).astype(jnp.float32)
+    target_part = jnp.sum(target_hot[:, None, :, None] * target_grad[:, :, None, :], axis=0)
+    dpos_src = (
+        row_hot[None, None, :, None] * target_part[:, :, None, :]
+        + jnp.sum(source_hot[:, None, :, None] * source_grad_pos[:, :, None, :], axis=0).reshape(
+            3, src_blocks, chan_count, rows
+        )
     ).reshape(3, src_atoms)
     grad_src = lax.psum_scatter(grad_part, "chan", scatter_dimension=0, tiled=True)
     for chan_bit in range(chan_count.bit_length() - 1):

time: 156 us -> 133 us (0.85)
  blocking collectives: 26.1 us -> 11.5 us
  matrix products: 21.2 us -> 8.37 us
  local copies, waits for them, and re-layouts: 23.2 us -> 35.9 us
  waiting for transfers between devices: 23.3 us -> 10.9 us
  starting transfers between devices: 24.4 us -> 29.1 us
    all_gather x2 -> x0, blocking collectives: 15.2 us -> none  [the longest x1 7.65 us: body(): gathered_piece = lax.all_gather(dz_packed, 'chan', axis=0, tiled=True)]
    dot_general x4 -> x2, matrix products: 16.3 us -> 1.23 us  [the longest x1 1.02 us: body(): jnp.einsum('lxc,clbi->xlbi', mixing, packed, preferred_element_type=jnp.f...]
    ppermute x18 -> x16, waiting for transfers between devices: 20.8 us -> 6.88 us  [partner(): return lax.ppermute(value, axis, pairs)]
    all_to_all x0 -> x2, starting transfers between devices: none -> 6.67 us  [the longest x1 3.34 us: body(): lax.all_to_all(result_rows.reshape(all_chan, components, own_blocks, 1, r...]
    dot_general x1, other arithmetic: 4.96 us -> 0.32 us  [body(): grad_rad = jnp.einsum('bclki,clbi->ck', msg_acc, moment_grad_all)]
    all_to_all x0 -> x2, waiting for transfers between devices: none -> 4 us  [the longest x1 4 us: body(): lax.all_to_all(result_rows.reshape(all_chan, components, own_blocks, 1, r...]
    reduce_sum x2 -> x4, other arithmetic: 0.13 us -> 3.8 us  [the longest x1 3.58 us: body(): harm_grad = jnp.sum(value_grad * radial[None], axis=1)]
    ppermute x6, local copies, waits for them, and re-layouts: 1.97 us -> 4.54 us  [partner(): return lax.ppermute(value, axis, pairs)]
  transfers between devices with their start and end apart: 19 -> 19, of which waited for: 9 -> 5; matrix products, arithmetic and copies ran while one was open for 17% -> 32% of each run, Pallas kernels for 0% -> 0%
where the time goes in v6:
time: 133 us; the launch traced here: 132 us
  local copies, waits for them, and re-layouts  35.9 us (27%)
  starting transfers between devices  29.1 us (22%)
  other arithmetic  21.3 us (16%)
  between operations  15 us (11%)
  blocking collectives  11.5 us (9%)
  waiting for transfers between devices  10.9 us (8%)
  matrix products  8.37 us (6%)
    ppermute x16, starting transfers between devices, partner(): return lax.ppermute(value, axis, pairs)  22.4 us
    unnamed x92, local copies, waits for them, and re-layouts  8.75 us
    ppermute x16, waiting for transfers between devices, partner(): return lax.ppermute(value, axis, pairs)  6.88 us
    all_gather x1, blocking collectives, body(): full_feat = lax.all_gather(src_feat, 'chan', axis=0, tiled=True)  6.28 us
    all_gather x1, blocking collectives, body(): full_weight = lax.all_gather(radial_weight, 'chan', axis=0, tiled=True)  5.2 us
    ppermute x6, local copies, waits for them, and re-layouts, partner(): return lax.ppermute(value, axis, pairs)  4.54 us
    all_to_all x1, waiting for transfers between devices, body(): lax.all_to_all(result_rows.reshape(all_chan, components, own_blocks, 1, r...  4 us
    dot_general x1, matrix products, body(): jnp.einsum('lktij,tbcj->bclki', pair_values, routed_feat, preferred_eleme...  3.69 us
  transfers between devices with their start and end apart: 19, of which 5 were waited for; matrix products, arithmetic and copies ran while one was open for 32% of the time, Pallas kernels for 0%

profile of v6, /device:TPU:0, one launch (start us, length us, event | category | flops | bytes accessed | tf_op | source)
XLA Modules:
  0.0 132.0 jit_solution(16470889410517442296)
XLA Ops:
  7.2 0.8 compare_and_fusion.2
  8.0 0.8 copy.284
  9.6 3.0 %collective-permute-start.3 = (f32[3,128]{0,1:T(8,128)S(1)}, f32[3,128]{0,1:T(8,128)S(1)}, u32[]{:S(2)}, u32[]{:S(2)}) collective-permute-start(f32[3,128]{0,1:T(8,128)S(1)} %select_bitcast_fusion.2), channel_id=1, source_target_pairs={{0,4},{4,0},{8,12},{12,8},{16,20},{20,16},{24,28},{28,24},{1,5},{5... | collective-permute-start | bytes 4616 | tf_op jit(solution)/shard_map/ppermute | solution.py:19
  13.3 1.6 %collective-permute-start.4 = (f32[3,128]{0,1:T(8,128)S(1)}, f32[3,128]{0,1:T(8,128)S(1)}, u32[]{:S(2)}, u32[]{:S(2)}) collective-permute-start(f32[3,128]{0,1:T(8,128)S(1)} %select_bitcast_fusion.1), channel_id=1, source_target_pairs={{0,8},{4,12},{8,0},{12,4},{16,24},{20,28},{24,16},{28,20},{1,9},{5... | collective-permute-start | bytes 4616 | tf_op jit(solution)/shard_map/ppermute | solution.py:19
  15.7 2.7 %collective-permute-start.5 = (f32[3,128]{0,1:T(8,128)S(1)}, f32[3,128]{0,1:T(8,128)S(1)}, u32[]{:S(2)}, u32[]{:S(2)}) collective-permute-start(f32[3,128]{0,1:T(8,128)S(1)} %select_bitcast_fusion), channel_id=1, source_target_pairs={{0,16},{4,20},{8,24},{12,28},{16,0},{20,4},{24,8},{28,12},{1,17},{... | collective-permute-start | bytes 4616 | tf_op jit(solution)/shard_map/ppermute | solution.py:19
  18.4 0.8 copy.276
  19.2 0.7 gather_fusion.5
  19.9 0.7 select_bitcast_fusion.5
  21.1 0.7 gather_fusion.6
  21.8 0.7 select_bitcast_fusion.4
  23.0 1.3 reshape.513
  24.3 0.7 copy.300
  25.0 1.2 reshape.651
  26.2 3.3 %all-to-all-start.1 = ((bf16[4,2,9216]{2,1,0:T(2,128)(2,1)}), bf16[4,2,9216]{2,1,0:T(2,128)(2,1)S(1)}, u32[]{:S(2)}, u32[]{:S(2)}) async-start(bf16[4,2,9216]{2,1,0:T(2,128)(2,1)} %reshape.651), calls=%async_computation.1 | async-start | bytes 294912 | tf_op jit(solution)/shard_map/all_to_all | solution.py:155
  30.2 0.7 gather_fusion.7
  31.1 0.7 select_bitcast_fusion.3
  32.4 5.2 %all-gather = f32[4,32,8]{1,2,0:T(8,128)S(1)} all-gather(f32[1,32,8]{1,2,0:T(8,128)S(1)} %bitcast.409), channel_id=1, replica_groups=mesh['space'=8,'chan'=4] {'chan'}, dimensions={0}, use_global_device_ids=true | all-gather | bytes 5120 | tf_op jit(solution)/shard_map/all_gather | solution.py:98
  37.7 0.7 broadcast_multiply_fusion
  38.4 0.7 copy.305
  39.7 0.7 copy.313
  40.5 0.7 mul.629
  44.7 1.5 %copy.279 = bf16[32,128]{1,0:T(8,128)(2,1)} copy(bf16[32,128]{0,1:T(8,128)(2,1)} %collective-permute-done) | data formatting | bytes 16384 | tf_op jit(solution)/shard_map/ppermute | solution.py:19
  46.2 1.4 %copy.280 = bf16[32,128]{1,0:T(8,128)(2,1)} copy(bf16[32,128]{0,1:T(8,128)(2,1)} %collective-permute-done.1) | data formatting | bytes 16384 | tf_op jit(solution)/shard_map/ppermute | solution.py:19
  47.6 1.4 %copy.281 = bf16[32,128]{1,0:T(8,128)(2,1)} copy(bf16[32,128]{0,1:T(8,128)(2,1)} %collective-permute-done.2) | data formatting | bytes 16384 | tf_op jit(solution)/shard_map/ppermute | solution.py:19
  49.1 0.8 pad_maximum_fusion.2
  49.8 6.3 %all_gather.6 = bf16[128,640]{1,0:T(8,128)(2,1)} all-gather(bf16[32,640]{1,0:T(8,128)(2,1)S(1)} %pad_maximum_fusion.2), channel_id=1, replica_groups=mesh['space'=8,'chan'=4] {'chan'}, dimensions={0}, use_global_device_ids=true | all-gather | bytes 204800 | tf_op jit(solution)/shard_map/all_gather | solution.py:97
  56.1 1.7 %copy.282 = bf16[128,640]{0,1:T(8,128)(2,1)} copy(bf16[128,640]{1,0:T(8,128)(2,1)} %all_gather.6) | data formatting | bytes 327680 | tf_op jit(solution)/shard_map/all_gather | solution.py:97
  57.8 1.7 %copy.283 = bf16[128,5,128]{2,0,1:T(8,128)(2,1)} copy(bf16[128,5,128]{0,2,1:T(8,128)(2,1)} %bitcast.405) | data formatting | bytes 327680 | tf_op jit(solution)/shard_map/reshape | solution.py:119
  59.6 1.6 %gather_fusion = bf16[8,128,128]{2,1,0:T(8,128)(2,1)S(1)} fusion(bf16[5,128,128]{2,1,0:T(8,128)(2,1)} %bitcast.404, s32[1024]{0:T(1024)} %copy-done.30), kind=kCustom, calls=%fused_computation.6 | custom fusion | bytes 524320 | tf_op jit(solution)/shard_map/jit(_take)/gather | solution.py:122
  61.3 3.7 %fusion.7 = (bf16[128,2,9,32]{0,3,2,1:T(8,128)(2,1)S(1)}, f32[2,128,9,8,32,1]{1,4,5,3,2,0:T(8,128)}) fusion(f32[128,8]{0,1:T(8,128)} %copy-done.25, f32[8,128,128]{2,1,0:T(8,128)S(1)} %convert_element_type.72, f32[8,2]{0,1:T(2,128)} %copy.275, f32[8,8,32,128]{3,2,0,1:T(8,128)S(1)} %fusion.17, f32[9,8,32,128]{3,2,1,0:T(8,128)S(1)} %multiply_dynamic-update-slice_fusion), kind=kOutput, calls=%fused_computation.26 | convolution fusion | flops 1214308352 | bytes 5263424 | tf_op jit(solution)/shard_map/lktij,tbcj->bclki/dot_general | solution.py:132
  65.0 1.0 convolution_bitcast_fusion
  66.4 0.8 copy.301
  68.3 0.7 multiply_convert_fusion.3
  69.2 0.9 gather_fusion.4
  70.2 1.4 %multiply_convert_fusion = bf16[8,128,9,8,32]{1,4,3,2,0:T(8,128)(2,1)S(1)} fusion(f32[8,128,9,32]{1,3,2,0:T(8,128)S(1)} %gather_fusion.4, f32[8,128,8]{1,2,0:T(8,128)S(1)} %copy-done.16), kind=kLoop, calls=%fused_computation.14 | loop fusion | flops 4718592 | bytes 5931008 | tf_op jit(solution)/shard_map/convert_element_type | solution.py:178
  71.7 2.1 %fusion.8 = f32[8,128,128]{2,1,0:T(8,128)S(1)} fusion(bf16[8,128,9,8,32]{1,4,3,2,0:T(8,128)(2,1)S(1)} %multiply_convert_fusion, f32[8,8,32,128]{3,2,0,1:T(8,128)S(1)} %copy-done.2, f32[9,8,32,128]{3,2,1,0:T(8,128)S(1)} %copy-done.7), kind=kOutput, calls=%fused_computation.29 | convolution fusion | flops 608698368 | bytes 7471104 | tf_op jit(solution)/shard_map/tclki,lktij->tcj/dot_general | solution.py:179
  73.8 1.4 %fusion.104 = f32[8,128,2304]{1,2,0:S(1)} fusion(bf16[8,128,2304]{1,2,0:T(8,128)(2,1)S(1)} %bitcast.399, bf16[8,128,128]{2,1,0:T(8,128)(2,1)S(1)} %gather_fusion), kind=kOutput, calls=%fused_computation.227 | convolution fusion | flops 603979776 | bytes 14417920
  75.2 3.6 %multiply_reduce_fusion.1 = (f32[9,8,32,128]{3,2,0,1:T(8,128)S(1)}, f32[8,8,32,128]{3,2,0,1:T(8,128)}) fusion(f32[9,8,8,32,128]{4,3,1,0,2:T(8,128)S(1)} %bitcast.398, f32[8,8,32,128]{3,2,0,1:T(8,128)S(1)} %copy-done.2, f32[9,8,32,128]{3,2,1,0:T(8,128)S(1)} %copy-done.7), kind=kLoop, calls=%fused_computation.13 | loop fusion | flops 8880128 | bytes 13893632 | tf_op jit(solution)/shard_map/reduce_sum | solution.py:185
  78.8 0.8 fusion.39
  79.5 0.9 fusion.72
  81.9 0.9 copy.338
  82.9 1.5 %fusion.18 = (f32[8,32,128]{2,1,0:T(8,128)S(1)}, f32[8,32,128]{2,1,0:T(8,128)S(1)}) fusion(f32[8,8,32,128]{3,2,0,1:T(8,128)S(1)} %copy-done.3, f32[8]{0:T(128)S(1)} %copy-done.36, f32[8,32,128]{2,1,0:T(8,128)} %copy-done.8, f32[8,32,128]{2,1,0:T(8,128)} %copy-done.9), kind=kLoop, calls=%fused_computation.37 | loop fusion | flops 2818048 | bytes 1572896 | tf_op jit(solution)/shard_map/transpose(jvp())/reduce_sum | solution.py:56
  85.9 1.8 %collective-permute-start.12 = (f32[128,8]{0,1:T(8,128)S(1)}, f32[128,8]{0,1:T(8,128)S(1)}, u32[]{:S(2)}, u32[]{:S(2)}) collective-permute-start(f32[128,8]{0,1:T(8,128)S(1)} %add.180), channel_id=1, source_target_pairs={{0,2},{1,3},{2,0},{3,1},{4,6},{5,7},{6,4},{7,5},{8,10},{9,11},{10,... | collective-permute-start | bytes 12296 | tf_op jit(solution)/shard_map/ppermute | solution.py:19
  87.9 1.7 %collective-permute-done.12 = f32[128,8]{0,1:T(8,128)S(1)} collective-permute-done((f32[128,8]{0,1:T(8,128)S(1)}, f32[128,8]{0,1:T(8,128)S(1)}, u32[]{:S(2)}, u32[]{:S(2)}) %collective-permute-start.12) | collective-permute-done | bytes 4128 | tf_op jit(solution)/shard_map/ppermute | solution.py:19
  89.7 1.8 %collective-permute-start.13 = (f32[32,8]{0,1:T(8,128)S(1)}, f32[32,8]{0,1:T(8,128)S(1)}, u32[]{:S(2)}, u32[]{:S(2)}) collective-permute-start(f32[32,8]{0,1:T(8,128)S(1)} %constant_dynamic-slice_fusion), channel_id=1, source_target_pairs={{0,4},{4,0},{8,12},{12,8},{16,20},{20,16},{24,28},{28,24},{1,5},{5... | collective-permute-start | bytes 3080 | tf_op jit(solution)/shard_map/ppermute | solution.py:19
  91.5 1.7 %collective-permute-done.13 = f32[32,8]{0,1:T(8,128)S(1)} collective-permute-done((f32[32,8]{0,1:T(8,128)S(1)}, f32[32,8]{0,1:T(8,128)S(1)}, u32[]{:S(2)}, u32[]{:S(2)}) %collective-permute-start.13) | collective-permute-done | bytes 1056 | tf_op jit(solution)/shard_map/ppermute | solution.py:19
  93.3 1.8 %collective-permute-start.14 = (f32[32,8]{0,1:T(8,128)S(1)}, f32[32,8]{0,1:T(8,128)S(1)}, u32[]{:S(2)}, u32[]{:S(2)}) collective-permute-start(f32[32,8]{0,1:T(8,128)S(1)} %fusion.107), channel_id=1, source_target_pairs={{0,8},{4,12},{8,0},{12,4},{16,24},{20,28},{24,16},{28,20},{1,9},{5... | collective-permute-start | bytes 3080 | tf_op jit(solution)/shard_map/ppermute | solution.py:19
  95.2 1.9 %collective-permute-start.7 = (f32[3,640]{1,0:T(4,128)S(1)}, f32[3,640]{1,0:T(4,128)S(1)}, u32[]{:S(2)}, u32[]{:S(2)}) collective-permute-start(f32[3,640]{1,0:T(4,128)S(1)} %add.176), channel_id=1, source_target_pairs={{0,2},{1,3},{2,0},{3,1},{4,6},{5,7},{6,4},{7,5},{8,10},{9,11},{10,... | collective-permute-start | bytes 23048 | tf_op jit(solution)/shard_map/ppermute | solution.py:19
  97.1 2.7 %collective-permute-start.15 = (f32[32,8]{0,1:T(8,128)S(1)}, f32[32,8]{0,1:T(8,128)S(1)}, u32[]{:S(2)}, u32[]{:S(2)}) collective-permute-start(f32[32,8]{0,1:T(8,128)S(1)} %add.183), channel_id=1, source_target_pairs={{0,16},{4,20},{8,24},{12,28},{16,0},{20,4},{24,8},{28,12},{1,17},{... | collective-permute-start | bytes 3080 | tf_op jit(solution)/shard_map/ppermute | solution.py:19
  99.8 0.8 copy.298
  100.7 1.2 reshape.649
  101.9 3.3 %all-to-all-start = ((bf16[4,2,9216]{2,1,0:T(2,128)(2,1)}), bf16[4,2,9216]{2,1,0:T(2,128)(2,1)S(1)}, u32[]{:S(2)}, u32[]{:S(2)}) async-start(bf16[4,2,9216]{2,1,0:T(2,128)(2,1)} %reshape.649), calls=%async_computation | async-start | bytes 294912 | tf_op jit(solution)/shard_map/all_to_all | solution.py:148
  106.0 4.0 %all-to-all-done = bf16[4,2,9216]{2,1,0:T(2,128)(2,1)S(1)} async-done(((bf16[4,2,9216]{2,1,0:T(2,128)(2,1)}), bf16[4,2,9216]{2,1,0:T(2,128)(2,1)S(1)}, u32[]{:S(2)}, u32[]{:S(2)}) %all-to-all-start) | async-done | bytes 147488 | tf_op jit(solution)/shard_map/all_to_all | solution.py:148
  110.3 0.8 copy.299
  111.1 1.1 reshape.512
  112.1 0.8 fusion.102
  112.9 1.6 %collective-permute-start.8 = (f32[35,128]{1,0:T(8,128)S(1)}, f32[35,128]{1,0:T(8,128)S(1)}, u32[]{:S(2)}, u32[]{:S(2)}) collective-permute-start(f32[35,128]{1,0:T(8,128)S(1)} %pad_maximum_fusion.3), channel_id=1, source_target_pairs={{0,4},{4,0},{8,12},{12,8},{16,20},{20,16},{24,28},{28,24},{1,5},{5... | collective-permute-start | bytes 53768 | tf_op jit(solution)/shard_map/ppermute | solution.py:19
  114.5 1.6 %collective-permute-start.9 = (f32[35,128]{1,0:T(8,128)S(1)}, f32[35,128]{1,0:T(8,128)S(1)}, u32[]{:S(2)}, u32[]{:S(2)}) collective-permute-start(f32[35,128]{1,0:T(8,128)S(1)} %pad_maximum_fusion.4), channel_id=1, source_target_pairs={{0,8},{4,12},{8,0},{12,4},{16,24},{20,28},{24,16},{28,20},{1,9},{5... | collective-permute-start | bytes 53768 | tf_op jit(solution)/shard_map/ppermute | solution.py:19
  116.4 0.8 slice.124
  117.4 0.9 collective-permute-done.9
  118.3 2.6 %collective-permute-done.10 = f32[35,128]{1,0:T(8,128)S(1)} collective-permute-done((f32[35,128]{1,0:T(8,128)S(1)}, f32[35,128]{1,0:T(8,128)S(1)}, u32[]{:S(2)}, u32[]{:S(2)}) %collective-permute-start.10) | collective-permute-done | bytes 17952 | tf_op jit(solution)/shard_map/ppermute | solution.py:19
  121.0 2.7 %scatter_fusion = f32[35,256]{0,1:T(8,128)S(1)} fusion(f32[35,256]{0,1:T(8,128)S(1)} %pad_maximum_fusion.1, s32[384]{0:T(512)S(1)} %fusion.99, f32[384,35]{1,0:T(8,128)S(1)} %copy.318), kind=kCustom, calls=%fused_computation.11 | custom fusion | flops 13440 | bytes 162816 | tf_op jit(solution)/shard_map/scatter-add | solution.py:216
  123.8 0.7 copy.320
  124.5 0.7 copy.319
  (188 shorter events, 15.8 us)
Async XLA Ops:
  7.2 34.0 %copy-start = (bf16[3,128,128]{2,1,0:T(8,128)(2,1)S(1)}, bf16[3,128,128]{2,1,0:T(8,128)(2,1)}, u32[]{:S(2)}) copy-start(bf16[3,128,128]{2,1,0:T(8,128)(2,1)} %param.19) | copy-start | bytes 294916
  9.6 32.2 %collective-permute-start.3 = (f32[3,128]{0,1:T(8,128)S(1)}, f32[3,128]{0,1:T(8,128)S(1)}, u32[]{:S(2)}, u32[]{:S(2)}) collective-permute-start(f32[3,128]{0,1:T(8,128)S(1)} %select_bitcast_fusion.2), channel_id=1, source_target_pairs={{0,4},{4,0},{8,12},{12,8},{16,20},{20,16},{24,28},{28,24},{1,5},{5... | collective-permute-start | bytes 4616 | tf_op jit(solution)/shard_map/ppermute | solution.py:19
  13.3 28.6 %collective-permute-start.4 = (f32[3,128]{0,1:T(8,128)S(1)}, f32[3,128]{0,1:T(8,128)S(1)}, u32[]{:S(2)}, u32[]{:S(2)}) collective-permute-start(f32[3,128]{0,1:T(8,128)S(1)} %select_bitcast_fusion.1), channel_id=1, source_target_pairs={{0,8},{4,12},{8,0},{12,4},{16,24},{20,28},{24,16},{28,20},{1,9},{5... | collective-permute-start | bytes 4616 | tf_op jit(solution)/shard_map/ppermute | solution.py:19
  15.7 26.3 %collective-permute-start.5 = (f32[3,128]{0,1:T(8,128)S(1)}, f32[3,128]{0,1:T(8,128)S(1)}, u32[]{:S(2)}, u32[]{:S(2)}) collective-permute-start(f32[3,128]{0,1:T(8,128)S(1)} %select_bitcast_fusion), channel_id=1, source_target_pairs={{0,16},{4,20},{8,24},{12,28},{16,0},{20,4},{24,8},{28,12},{1,17},{... | collective-permute-start | bytes 4616 | tf_op jit(solution)/shard_map/ppermute | solution.py:19
  20.6 24.1 %collective-permute-start = (bf16[32,128]{0,1:T(8,128)(2,1)}, bf16[32,128]{0,1:T(8,128)(2,1)}, u32[]{:S(2)}, u32[]{:S(2)}) collective-permute-start(bf16[32,128]{0,1:T(8,128)(2,1)} %select_bitcast_fusion.5), channel_id=1, source_target_pairs={{0,4},{4,0},{8,12},{12,8},{16,20},{20,16},{24,28},{28,24},{1,5},{5... | collective-permute-start | bytes 24584 | tf_op jit(solution)/shard_map/ppermute | solution.py:19
  22.5 23.7 %collective-permute-start.1 = (bf16[32,128]{0,1:T(8,128)(2,1)}, bf16[32,128]{0,1:T(8,128)(2,1)}, u32[]{:S(2)}, u32[]{:S(2)}) collective-permute-start(bf16[32,128]{0,1:T(8,128)(2,1)} %select_bitcast_fusion.4), channel_id=1, source_target_pairs={{0,8},{4,12},{8,0},{12,4},{16,24},{20,28},{24,16},{28,20},{1,9},{5... | collective-permute-start | bytes 24584 | tf_op jit(solution)/shard_map/ppermute | solution.py:19
  24.2 5.4 %copy-start.37 = (s32[8,2]{0,1:T(2,128)S(1)}, s32[8,2]{0,1:T(2,128)}, u32[]{:S(2)}) copy-start(s32[8,2]{0,1:T(2,128)} %param.16) | copy-start | bytes 196
  24.2 6.8 %copy-start.39 = (s32[8]{0:T(128)S(1)}, s32[8]{0:T(128)}, u32[]{:S(2)}) copy-start(s32[8]{0:T(128)} %param.17) | copy-start | bytes 100
  24.2 7.5 %copy-start.38 = (s32[9]{0:T(128)S(1)}, s32[9]{0:T(128)}, u32[]{:S(2)}) copy-start(s32[9]{0:T(128)} %constant.99) | copy-start | bytes 112
  24.3 8.2 %copy-start.32 = (f32[32,8]{0,1:T(8,128)S(1)}, f32[32,8]{0,1:T(8,128)}, u32[]{:S(2)}) copy-start(f32[32,8]{0,1:T(8,128)} %param.18) | copy-start | bytes 3076
  25.0 17.1 %copy-start.23 = (f32[3,256]{1,0:T(4,128)S(1)}, f32[3,256]{1,0:T(4,128)}, u32[]{:S(2)}) copy-start(f32[3,256]{1,0:T(4,128)} %param.13) | copy-start | bytes 9220
  26.2 39.8 %all-to-all-start.1 = ((bf16[4,2,9216]{2,1,0:T(2,128)(2,1)}), bf16[4,2,9216]{2,1,0:T(2,128)(2,1)S(1)}, u32[]{:S(2)}, u32[]{:S(2)}) async-start(bf16[4,2,9216]{2,1,0:T(2,128)(2,1)} %reshape.651), calls=%async_computation.1 | async-start | bytes 294912 | tf_op jit(solution)/shard_map/all_to_all | solution.py:155
  29.5 82.6 %reduce-scatter.4.cloned.1.call-start = ((), (), s32[]{:S(2)}) async-start(), calls=%async_computation.3 | async-start | bytes 409600
  29.7 14.4 %copy-start.33 = (f32[8]{0:T(128)}, f32[8]{0:T(128)S(1)}, u32[]{:S(2)}) copy-start(f32[8]{0:T(128)S(1)} %compare_convert_fusion.1) | copy-start | bytes 100
  31.0 12.4 %copy-start.30 = (s32[1024]{0:T(1024)}, s32[1024]{0:T(1024)S(1)}, u32[]{:S(2)}) copy-start(s32[1024]{0:T(1024)S(1)} %pad_clamp_fusion.3) | copy-start | bytes 12292
  31.1 13.0 %copy-start.14 = (f32[32,128]{1,0:T(8,128)}, f32[32,128]{1,0:T(8,128)S(1)}, u32[]{:S(2)}) copy-start(f32[32,128]{1,0:T(8,128)S(1)} %fusion.94) | copy-start | bytes 49156
  31.1 13.0 %copy-start.28 = (f32[8]{0:T(128)}, f32[8]{0:T(128)S(1)}, u32[]{:S(2)}) copy-start(f32[8]{0:T(128)S(1)} %convert_element_type.71) | copy-start | bytes 100
  32.4 7.3 %copy-start.21 = (f32[8,5]{1,0:T(8,128)}, f32[8,5]{1,0:T(8,128)S(1)}, u32[]{:S(2)}) copy-start(f32[8,5]{1,0:T(8,128)S(1)} %get-tuple-element.71) | copy-start | bytes 484
  37.7 5.6 %copy-start.25 = (f32[128,8]{0,1:T(8,128)}, f32[128,8]{0,1:T(8,128)S(1)}, u32[]{:S(2)}) copy-start(f32[128,8]{0,1:T(8,128)S(1)} %reshape.622) | copy-start | bytes 12292
  41.8 5.9 %collective-permute-start.2 = (bf16[32,128]{0,1:T(8,128)(2,1)}, bf16[32,128]{0,1:T(8,128)(2,1)}, u32[]{:S(2)}, u32[]{:S(2)}) collective-permute-start(bf16[32,128]{0,1:T(8,128)(2,1)} %select_bitcast_fusion.3), channel_id=1, source_target_pairs={{0,16},{4,20},{8,24},{12,28},{16,0},{20,4},{24,8},{28,12},{1,17},{... | collective-permute-start | bytes 24584 | tf_op jit(solution)/shard_map/ppermute | solution.py:19
  42.8 1.1 copy-start.17
  43.4 0.6 copy-start.19
  43.7 0.7 copy-start.35
  44.2 13.6 %copy-start.8 = (f32[8,32,128]{2,1,0:T(8,128)}, f32[8,32,128]{2,1,0:T(8,128)S(1)}, u32[]{:S(2)}) copy-start(f32[8,32,128]{2,1,0:T(8,128)S(1)} %get-tuple-element.51) | copy-start | bytes 393220
  44.2 13.6 %copy-start.9 = (f32[8,32,128]{2,1,0:T(8,128)}, f32[8,32,128]{2,1,0:T(8,128)S(1)}, u32[]{:S(2)}) copy-start(f32[8,32,128]{2,1,0:T(8,128)S(1)} %get-tuple-element.52) | copy-start | bytes 393220
  44.6 16.6 %copy-start.1 = (f32[8,8,32,128]{3,2,0,1:T(8,128)}, f32[8,8,32,128]{3,2,0,1:T(8,128)S(1)}, u32[]{:S(2)}) copy-start(f32[8,8,32,128]{3,2,0,1:T(8,128)S(1)} %fusion.17) | copy-start | bytes 3145732
  44.7 16.5 %copy-start.6 = (f32[9,8,32,128]{3,2,1,0:T(8,128)}, f32[9,8,32,128]{3,2,1,0:T(8,128)S(1)}, u32[]{:S(2)}) copy-start(f32[9,8,32,128]{3,2,1,0:T(8,128)S(1)} %multiply_dynamic-update-slice_fusion) | copy-start | bytes 3538948
  67.3 1.0 copy-start.4
  69.2 0.9 copy-start.16
  70.1 1.4 %copy-start.2 = (f32[8,8,32,128]{3,2,0,1:T(8,128)S(1)}, f32[8,8,32,128]{3,2,0,1:T(8,128)}, u32[]{:S(2)}) copy-start(f32[8,8,32,128]{3,2,0,1:T(8,128)} %copy-done.1) | copy-start | bytes 3145732
  70.1 1.6 %copy-start.7 = (f32[9,8,32,128]{3,2,1,0:T(8,128)S(1)}, f32[9,8,32,128]{3,2,1,0:T(8,128)}, u32[]{:S(2)}) copy-start(f32[9,8,32,128]{3,2,1,0:T(8,128)} %copy-done.6) | copy-start | bytes 3538948
  78.8 1.7 %copy-start.5 = (f32[2,128,9,8,32,1]{1,4,5,3,2,0:T(8,128)S(1)}, f32[2,128,9,8,32,1]{1,4,5,3,2,0:T(8,128)}, u32[]{:S(2)}) copy-start(f32[2,128,9,8,32,1]{1,4,5,3,2,0:T(8,128)} %get-tuple-element.76) | copy-start | bytes 7077892
  80.5 0.8 copy-start.22
  80.8 2.1 %copy-start.3 = (f32[8,8,32,128]{3,2,0,1:T(8,128)S(1)}, f32[8,8,32,128]{3,2,0,1:T(8,128)}, u32[]{:S(2)}) copy-start(f32[8,8,32,128]{3,2,0,1:T(8,128)} %get-tuple-element.35) | copy-start | bytes 3145732
  80.8 2.1 %copy-start.36 = (f32[8]{0:T(128)S(1)}, f32[8]{0:T(128)}, u32[]{:S(2)}) copy-start(f32[8]{0:T(128)} %add_multiply_fusion) | copy-start | bytes 100
  80.8 5.1 %collective-permute-start.11 = (f32[128,8]{0,1:T(8,128)S(1)}, f32[128,8]{0,1:T(8,128)S(1)}, u32[]{:S(2)}, u32[]{:S(2)}) collective-permute-start(f32[128,8]{0,1:T(8,128)S(1)} %fusion.6), channel_id=1, source_target_pairs={{0,1},{1,0},{2,3},{3,2},{4,5},{5,4},{6,7},{7,6},{8,9},{9,8},{10,11... | collective-permute-start | bytes 12296 | tf_op jit(solution)/shard_map/ppermute | solution.py:19
  81.9 2.5 %copy-start.15 = (f32[32,128]{1,0:T(8,128)S(1)}, f32[32,128]{1,0:T(8,128)}, u32[]{:S(2)}) copy-start(f32[32,128]{1,0:T(8,128)} %copy-done.14) | copy-start | bytes 49156
  81.9 2.5 %copy-start.29 = (f32[8]{0:T(128)S(1)}, f32[8]{0:T(128)}, u32[]{:S(2)}) copy-start(f32[8]{0:T(128)} %copy-done.28) | copy-start | bytes 100
  81.9 2.5 %copy-start.34 = (f32[8]{0:T(128)S(1)}, f32[8]{0:T(128)}, u32[]{:S(2)}) copy-start(f32[8]{0:T(128)} %copy-done.33) | copy-start | bytes 100
  84.4 0.9 copy-start.11
  84.4 1.0 copy-start.12
  84.4 1.0 copy-start.13
  84.4 1.0 copy-start.18
  84.4 1.0 copy-start.20
  84.5 1.3 copy-start.27
  84.5 3.2 %copy-start.26 = (f32[8,5]{0,1:T(8,128)S(1)}, f32[8,5]{0,1:T(8,128)}, u32[]{:S(2)}) copy-start(f32[8,5]{0,1:T(8,128)} %copy.313) | copy-start | bytes 484
  84.5 7.0 %copy-start.24 = (f32[640]{0:T(1024)S(1)}, f32[640]{0:T(1024)}, u32[]{:S(2)}) copy-start(f32[640]{0:T(1024)} %mul.629) | copy-start | bytes 7684
  84.5 10.7 %copy-start.31 = (s32[3,128]{1,0:T(4,128)S(1)}, s32[3,128]{1,0:T(4,128)}, u32[]{:S(2)}) copy-start(s32[3,128]{1,0:T(4,128)} %param.15) | copy-start | bytes 4612
  84.5 15.3 %copy-start.10 = (bf16[128,8,2,1,32]{0,4,2,1,3:T(8,128)(2,1)S(1)}, bf16[128,8,2,1,32]{0,4,2,1,3:T(8,128)(2,1)}, u32[]{:S(2)}) copy-start(bf16[128,8,2,1,32]{0,4,2,1,3:T(8,128)(2,1)} %get-tuple-element.57) | copy-start | bytes 393220
  85.9 3.7 %collective-permute-start.12 = (f32[128,8]{0,1:T(8,128)S(1)}, f32[128,8]{0,1:T(8,128)S(1)}, u32[]{:S(2)}, u32[]{:S(2)}) collective-permute-start(f32[128,8]{0,1:T(8,128)S(1)} %add.180), channel_id=1, source_target_pairs={{0,2},{1,3},{2,0},{3,1},{4,6},{5,7},{6,4},{7,5},{8,10},{9,11},{10,... | collective-permute-start | bytes 12296 | tf_op jit(solution)/shard_map/ppermute | solution.py:19
  89.7 3.6 %collective-permute-start.13 = (f32[32,8]{0,1:T(8,128)S(1)}, f32[32,8]{0,1:T(8,128)S(1)}, u32[]{:S(2)}, u32[]{:S(2)}) collective-permute-start(f32[32,8]{0,1:T(8,128)S(1)} %constant_dynamic-slice_fusion), channel_id=1, source_target_pairs={{0,4},{4,0},{8,12},{12,8},{16,20},{20,16},{24,28},{28,24},{1,5},{5... | collective-permute-start | bytes 3080 | tf_op jit(solution)/shard_map/ppermute | solution.py:19
  91.5 3.8 %collective-permute-start.6 = (f32[3,640]{1,0:T(4,128)S(1)}, f32[3,640]{1,0:T(4,128)S(1)}, u32[]{:S(2)}, u32[]{:S(2)}) collective-permute-start(f32[3,640]{1,0:T(4,128)S(1)} %bitcast_add_fusion.2), channel_id=1, source_target_pairs={{0,1},{1,0},{2,3},{3,2},{4,5},{5,4},{6,7},{7,6},{8,9},{9,8},{10,11... | collective-permute-start | bytes 23048 | tf_op jit(solution)/shard_map/ppermute | solution.py:19
  93.3 3.8 %collective-permute-start.14 = (f32[32,8]{0,1:T(8,128)S(1)}, f32[32,8]{0,1:T(8,128)S(1)}, u32[]{:S(2)}, u32[]{:S(2)}) collective-permute-start(f32[32,8]{0,1:T(8,128)S(1)} %fusion.107), channel_id=1, source_target_pairs={{0,8},{4,12},{8,0},{12,4},{16,24},{20,28},{24,16},{28,20},{1,9},{5... | collective-permute-start | bytes 3080 | tf_op jit(solution)/shard_map/ppermute | solution.py:19
  95.2 10.6 %collective-permute-start.7 = (f32[3,640]{1,0:T(4,128)S(1)}, f32[3,640]{1,0:T(4,128)S(1)}, u32[]{:S(2)}, u32[]{:S(2)}) collective-permute-start(f32[3,640]{1,0:T(4,128)S(1)} %add.176), channel_id=1, source_target_pairs={{0,2},{1,3},{2,0},{3,1},{4,6},{5,7},{6,4},{7,5},{8,10},{9,11},{10,... | collective-permute-start | bytes 23048 | tf_op jit(solution)/shard_map/ppermute | solution.py:19
  97.1 8.1 %collective-permute-start.15 = (f32[32,8]{0,1:T(8,128)S(1)}, f32[32,8]{0,1:T(8,128)S(1)}, u32[]{:S(2)}, u32[]{:S(2)}) collective-permute-start(f32[32,8]{0,1:T(8,128)S(1)} %add.183), channel_id=1, source_target_pairs={{0,16},{4,20},{8,24},{12,28},{16,0},{20,4},{24,8},{28,12},{1,17},{... | collective-permute-start | bytes 3080 | tf_op jit(solution)/shard_map/ppermute | solution.py:19
  101.9 8.1 %all-to-all-start = ((bf16[4,2,9216]{2,1,0:T(2,128)(2,1)}), bf16[4,2,9216]{2,1,0:T(2,128)(2,1)S(1)}, u32[]{:S(2)}, u32[]{:S(2)}) async-start(bf16[4,2,9216]{2,1,0:T(2,128)(2,1)} %reshape.649), calls=%async_computation | async-start | bytes 294912 | tf_op jit(solution)/shard_map/all_to_all | solution.py:148
  112.9 4.5 %collective-permute-start.8 = (f32[35,128]{1,0:T(8,128)S(1)}, f32[35,128]{1,0:T(8,128)S(1)}, u32[]{:S(2)}, u32[]{:S(2)}) collective-permute-start(f32[35,128]{1,0:T(8,128)S(1)} %pad_maximum_fusion.3), channel_id=1, source_target_pairs={{0,4},{4,0},{8,12},{12,8},{16,20},{20,16},{24,28},{28,24},{1,5},{5... | collective-permute-start | bytes 53768 | tf_op jit(solution)/shard_map/ppermute | solution.py:19
  114.5 3.8 %collective-permute-start.9 = (f32[35,128]{1,0:T(8,128)S(1)}, f32[35,128]{1,0:T(8,128)S(1)}, u32[]{:S(2)}, u32[]{:S(2)}) collective-permute-start(f32[35,128]{1,0:T(8,128)S(1)} %pad_maximum_fusion.4), channel_id=1, source_target_pairs={{0,8},{4,12},{8,0},{12,4},{16,24},{20,28},{24,16},{28,20},{1,9},{5... | collective-permute-start | bytes 53768 | tf_op jit(solution)/shard_map/ppermute | solution.py:19
  116.1 4.8 %collective-permute-start.10 = (f32[35,128]{1,0:T(8,128)S(1)}, f32[35,128]{1,0:T(8,128)S(1)}, u32[]{:S(2)}, u32[]{:S(2)}) collective-permute-start(f32[35,128]{1,0:T(8,128)S(1)} %pad_maximum_fusion.5), channel_id=1, source_target_pairs={{0,16},{4,20},{8,24},{12,28},{16,0},{20,4},{24,8},{28,12},{1,17},{... | collective-permute-start | bytes 53768 | tf_op jit(solution)/shard_map/ppermute | solution.py:19
Sparse Core Ops, SparseCore 0:
  83.0 22.2 reduce-scatter.3

commit v7 on v6

--- a/solution.py
+++ b/solution.py
@@ -94,10 +94,23 @@
         pos_list.append(got_pos)
     src_pos = jnp.concatenate(pos_list, axis=1)
     src_feat = jnp.concatenate(feat_list, axis=1)
-    full_feat = lax.all_gather(src_feat, "chan", axis=0, tiled=True)
-    full_weight = lax.all_gather(radial_weight, "chan", axis=0, tiled=True)
+    src_atoms = src_pos.shape[1]
+    weight_high = radial_weight.astype(jnp.bfloat16)
+    weight_rest = radial_weight - weight_high.astype(jnp.float32)
+    weight_mid = weight_rest.astype(jnp.bfloat16)
+    weight_low = (weight_rest - weight_mid.astype(jnp.float32)).astype(jnp.bfloat16)
+    full_both = lax.all_gather(
+        jnp.concatenate([src_feat, weight_high, weight_mid, weight_low], axis=1),
+        "chan",
+        axis=0,
+        tiled=True,
+    )
+    full_feat = full_both[:, :src_atoms]
+    pieces = full_both[:, src_atoms:].astype(jnp.float32)
+    full_weight = (
+        pieces[:, :radial_count] + pieces[:, radial_count : 2 * radial_count]
+    ) + pieces[:, 2 * radial_count :]
     all_chan = full_feat.shape[0]
-    src_atoms = src_pos.shape[1]
     src_blocks = src_atoms // block_size
     own_blocks = atoms_dev // block_size
     rows = block_size // chan_count

time: 133 us -> 127 us (0.955)
  blocking collectives: 11.5 us -> 6.35 us
  local copies, waits for them, and re-layouts: 35.9 us -> 33.8 us
    all_gather x2 -> x1, blocking collectives: 11.5 us -> 6.35 us  [body(): lax.all_gather(jnp.concatenate([src_feat, weight_high, weight_mid, weight...]
    ppermute x6, local copies, waits for them, and re-layouts: 4.54 us -> 1.98 us  [partner(): return lax.ppermute(value, axis, pairs)]
    unnamed x92 -> x91, local copies, waits for them, and re-layouts: 8.75 us -> 10.7 us
    all_gather x2 -> x0, local copies, waits for them, and re-layouts: 1.73 us -> none  [the longest x1 1.72 us: body(): full_feat = lax.all_gather(src_feat, 'chan', axis=0, tiled=True)]
    ppermute x16, starting transfers between devices: 22.4 us -> 21 us  [partner(): return lax.ppermute(value, axis, pairs)]
  transfers between devices with their start and end apart: 19 -> 19, of which waited for: 5 -> 6; matrix products, arithmetic and copies ran while one was open for 32% -> 32% of each run, Pallas kernels for 0% -> 0%
where the time goes in v7:
time: 127 us; the launch traced here: 126 us
  local copies, waits for them, and re-layouts  33.8 us (27%)
  starting transfers between devices  28.4 us (22%)
  other arithmetic  21.3 us (17%)
  between operations  15 us (12%)
  waiting for transfers between devices  12.1 us (10%)
  matrix products  8.74 us (7%)
  blocking collectives  6.35 us (5%)
    ppermute x16, starting transfers between devices, partner(): return lax.ppermute(value, axis, pairs)  21 us
    unnamed x91, local copies, waits for them, and re-layouts  10.7 us
    ppermute x16, waiting for transfers between devices, partner(): return lax.ppermute(value, axis, pairs)  8.1 us
    all_gather x1, blocking collectives, body(): lax.all_gather(jnp.concatenate([src_feat, weight_high, weight_mid, weight...  6.35 us
    dot_general x1, matrix products, body(): jnp.einsum('lktij,tbcj->bclki', pair_values, routed_feat, preferred_eleme...  4.07 us
    all_to_all x1, waiting for transfers between devices, body(): lax.all_to_all(result_rows.reshape(all_chan, components, own_blocks, 1, r...  4 us
    all_to_all x1, starting transfers between devices, body(): lax.all_to_all(out_grad.reshape(chan_dev, components, own_blocks, chan_co...  3.96 us
    reduce_sum x1, other arithmetic, body(): harm_grad = jnp.sum(value_grad * radial[None], axis=1)  3.58 us
  transfers between devices with their start and end apart: 19, of which 6 were waited for; matrix products, arithmetic and copies ran while one was open for 32% of the time, Pallas kernels for 0%

profile of v7, /device:TPU:0, one launch (start us, length us, event | category | flops | bytes accessed | tf_op | source)
XLA Modules:
  0.0 125.6 jit_solution(2749540580717777190)
XLA Ops:
  7.2 0.8 compare_and_fusion.2
  8.0 0.8 copy.298
  9.6 3.0 %collective-permute-start.3 = (f32[3,128]{0,1:T(8,128)S(1)}, f32[3,128]{0,1:T(8,128)S(1)}, u32[]{:S(2)}, u32[]{:S(2)}) collective-permute-start(f32[3,128]{0,1:T(8,128)S(1)} %select_bitcast_fusion.2), channel_id=1, source_target_pairs={{0,4},{4,0},{8,12},{12,8},{16,20},{20,16},{24,28},{28,24},{1,5},{5... | collective-permute-start | bytes 4616 | tf_op jit(solution)/shard_map/ppermute | solution.py:19
  13.3 1.6 %collective-permute-start.4 = (f32[3,128]{0,1:T(8,128)S(1)}, f32[3,128]{0,1:T(8,128)S(1)}, u32[]{:S(2)}, u32[]{:S(2)}) collective-permute-start(f32[3,128]{0,1:T(8,128)S(1)} %select_bitcast_fusion.1), channel_id=1, source_target_pairs={{0,8},{4,12},{8,0},{12,4},{16,24},{20,28},{24,16},{28,20},{1,9},{5... | collective-permute-start | bytes 4616 | tf_op jit(solution)/shard_map/ppermute | solution.py:19
  15.7 2.7 %collective-permute-start.5 = (f32[3,128]{0,1:T(8,128)S(1)}, f32[3,128]{0,1:T(8,128)S(1)}, u32[]{:S(2)}, u32[]{:S(2)}) collective-permute-start(f32[3,128]{0,1:T(8,128)S(1)} %select_bitcast_fusion), channel_id=1, source_target_pairs={{0,16},{4,20},{8,24},{12,28},{16,0},{20,4},{24,8},{28,12},{1,17},{... | collective-permute-start | bytes 4616 | tf_op jit(solution)/shard_map/ppermute | solution.py:19
  18.4 0.8 copy.286
  19.2 0.7 gather_fusion.5
  19.9 0.7 select_bitcast_fusion.5
  21.1 0.7 gather_fusion.6
  21.8 0.7 select_bitcast_fusion.4
  23.0 1.3 reshape.513
  24.3 0.7 copy.314
  25.0 1.2 reshape.649
  26.2 4.0 %all-to-all-start.1 = ((bf16[4,2,9216]{2,1,0:T(2,128)(2,1)}), bf16[4,2,9216]{2,1,0:T(2,128)(2,1)}, u32[]{:S(2)}, u32[]{:S(2)}) async-start(bf16[4,2,9216]{2,1,0:T(2,128)(2,1)} %reshape.649), calls=%async_computation.1 | async-start | bytes 294912 | tf_op jit(solution)/shard_map/all_to_all | solution.py:168
  30.3 0.7 gather_fusion.7
  31.1 0.7 select_bitcast_fusion.3
  32.8 0.7 copy.319
  39.1 0.9 copy.290
  40.0 1.4 %collective-permute-done.2 = bf16[32,128]{0,1:T(8,128)(2,1)} collective-permute-done((bf16[32,128]{0,1:T(8,128)(2,1)}, bf16[32,128]{0,1:T(8,128)(2,1)}, u32[]{:S(2)}, u32[]{:S(2)}) %collective-permute-start.2) | collective-permute-done | bytes 8224 | tf_op jit(solution)/shard_map/ppermute | solution.py:19
  41.4 0.8 copy.291
  42.3 6.4 %all_gather.3 = bf16[128,664]{1,0:T(8,128)(2,1)S(1)} all-gather(bf16[32,664]{1,0:T(8,128)(2,1)S(1)} %concatenate.40), channel_id=1, replica_groups=mesh['space'=8,'chan'=4] {'chan'}, dimensions={0}, use_global_device_ids=true | all-gather | bytes 212480 | tf_op jit(solution)/shard_map/all_gather | solution.py:102
  48.6 0.7 slice.141
  49.3 1.1 copy.355
  50.4 0.8 copy.297
  51.2 1.6 %gather_fusion = bf16[8,128,128]{2,1,0:T(8,128)(2,1)S(1)} fusion(bf16[5,128,128]{2,1,0:T(8,128)(2,1)} %bitcast.401, s32[1024]{0:T(1024)} %copy-done.29), kind=kCustom, calls=%fused_computation.6 | custom fusion | bytes 524320 | tf_op jit(solution)/shard_map/jit(_take)/gather | solution.py:135
  52.9 0.8 convert_element_type.96
  53.9 4.1 %fusion.7 = (bf16[128,2,9,32]{0,3,2,1:T(8,128)(2,1)S(1)}, f32[2,128,9,8,32,1]{1,4,5,3,2,0:T(8,128)}) fusion(f32[128,8]{0,1:T(8,128)S(1)} %copy.367, f32[8,128,128]{2,1,0:T(8,128)} %convert_element_type.96, f32[8,2]{0,1:T(2,128)} %copy.295, f32[8,8,32,128]{3,2,0,1:T(8,128)S(1)} %fusion.17, f32[9,8,32,128]{3,2,1,0:T(8,128)S(1)} %multiply_dynamic-update-slice_fusion), kind=kOutput, calls=%fused_computation.26 | convolution fusion | flops 1214308352 | bytes 5263424 | tf_op jit(solution)/shard_map/lktij,tbcj->bclki/dot_general | solution.py:145
  57.9 1.0 convolution_bitcast_fusion
  59.0 0.7 broadcast_multiply_fusion
  59.6 1.3 %reshape.650 = bf16[4,9,2,32,32]{4,3,2,1,0:T(8,128)(2,1)S(1)} reshape(bf16[4,2,9216]{2,1,0:T(2,128)(2,1)} %all-to-all-done.1) | data formatting | bytes 294912
  61.1 0.8 copy.315
  62.9 0.7 multiply_convert_fusion.3
  63.9 0.9 gather_fusion.4
  64.8 1.4 %multiply_convert_fusion = bf16[8,128,9,8,32]{1,4,3,2,0:T(8,128)(2,1)S(1)} fusion(f32[8,128,9,32]{1,3,2,0:T(8,128)S(1)} %gather_fusion.4, f32[8,128,8]{1,2,0:T(8,128)S(1)} %copy-done.14), kind=kLoop, calls=%fused_computation.14 | loop fusion | flops 4718592 | bytes 5931008 | tf_op jit(solution)/shard_map/convert_element_type | solution.py:191
  66.4 2.1 %fusion.8 = f32[8,128,128]{2,1,0:T(8,128)S(1)} fusion(bf16[8,128,9,8,32]{1,4,3,2,0:T(8,128)(2,1)S(1)} %multiply_convert_fusion, f32[8,8,32,128]{3,2,0,1:T(8,128)S(1)} %copy-done.2, f32[9,8,32,128]{3,2,1,0:T(8,128)S(1)} %copy-done.7), kind=kOutput, calls=%fused_computation.29 | convolution fusion | flops 608698368 | bytes 7471104 | tf_op jit(solution)/shard_map/tclki,lktij->tcj/dot_general | solution.py:192
  68.5 1.4 %fusion.105 = f32[8,128,2304]{1,2,0:S(1)} fusion(bf16[8,128,2304]{1,2,0:T(8,128)(2,1)S(1)} %bitcast.396, bf16[8,128,128]{2,1,0:T(8,128)(2,1)S(1)} %gather_fusion), kind=kOutput, calls=%fused_computation.232 | convolution fusion | flops 603979776 | bytes 14417920
  69.8 3.6 %multiply_reduce_fusion.1 = (f32[9,8,32,128]{3,2,0,1:T(8,128)S(1)}, f32[8,8,32,128]{3,2,0,1:T(8,128)}) fusion(f32[9,8,8,32,128]{4,3,1,0,2:T(8,128)S(1)} %bitcast.395, f32[8,8,32,128]{3,2,0,1:T(8,128)S(1)} %copy-done.2, f32[9,8,32,128]{3,2,1,0:T(8,128)S(1)} %copy-done.7), kind=kLoop, calls=%fused_computation.13 | loop fusion | flops 8880128 | bytes 13893632 | tf_op jit(solution)/shard_map/reduce_sum | solution.py:198
  73.4 0.8 fusion.39
  74.2 0.9 fusion.72
  76.6 0.9 copy.353
  77.5 1.5 %fusion.18 = (f32[8,32,128]{2,1,0:T(8,128)S(1)}, f32[8,32,128]{2,1,0:T(8,128)S(1)}) fusion(f32[8,8,32,128]{3,2,0,1:T(8,128)S(1)} %copy-done.3, f32[8]{0:T(128)S(1)} %copy-done.35, f32[8,32,128]{2,1,0:T(8,128)} %copy-done.8, f32[8,32,128]{2,1,0:T(8,128)} %copy-done.9), kind=kLoop, calls=%fused_computation.37 | loop fusion | flops 2818048 | bytes 1572896 | tf_op jit(solution)/shard_map/transpose(jvp())/reduce_sum | solution.py:56
  80.5 0.7 add.188
  81.2 1.7 %collective-permute-start.12 = (f32[128,8]{0,1:T(8,128)S(1)}, f32[128,8]{0,1:T(8,128)S(1)}, u32[]{:S(2)}, u32[]{:S(2)}) collective-permute-start(f32[128,8]{0,1:T(8,128)S(1)} %add.188), channel_id=1, source_target_pairs={{0,2},{1,3},{2,0},{3,1},{4,6},{5,7},{6,4},{7,5},{8,10},{9,11},{10,... | collective-permute-start | bytes 12296 | tf_op jit(solution)/shard_map/ppermute | solution.py:19
  83.1 1.7 %collective-permute-done.12 = f32[128,8]{0,1:T(8,128)S(1)} collective-permute-done((f32[128,8]{0,1:T(8,128)S(1)}, f32[128,8]{0,1:T(8,128)S(1)}, u32[]{:S(2)}, u32[]{:S(2)}) %collective-permute-start.12) | collective-permute-done | bytes 4128 | tf_op jit(solution)/shard_map/ppermute | solution.py:19
  84.9 1.5 %collective-permute-start.13 = (f32[32,8]{0,1:T(8,128)S(1)}, f32[32,8]{0,1:T(8,128)S(1)}, u32[]{:S(2)}, u32[]{:S(2)}) collective-permute-start(f32[32,8]{0,1:T(8,128)S(1)} %constant_dynamic-slice_fusion), channel_id=1, source_target_pairs={{0,4},{4,0},{8,12},{12,8},{16,20},{20,16},{24,28},{28,24},{1,5},{5... | collective-permute-start | bytes 3080 | tf_op jit(solution)/shard_map/ppermute | solution.py:19
  86.5 2.0 %collective-permute-done.13 = f32[32,8]{0,1:T(8,128)S(1)} collective-permute-done((f32[32,8]{0,1:T(8,128)S(1)}, f32[32,8]{0,1:T(8,128)S(1)}, u32[]{:S(2)}, u32[]{:S(2)}) %collective-permute-start.13) | collective-permute-done | bytes 1056 | tf_op jit(solution)/shard_map/ppermute | solution.py:19
  88.6 1.2 collective-permute-start.14
  89.9 1.8 %collective-permute-start.7 = (f32[3,640]{1,0:T(4,128)S(1)}, f32[3,640]{1,0:T(4,128)S(1)}, u32[]{:S(2)}, u32[]{:S(2)}) collective-permute-start(f32[3,640]{1,0:T(4,128)S(1)} %add.184), channel_id=1, source_target_pairs={{0,2},{1,3},{2,0},{3,1},{4,6},{5,7},{6,4},{7,5},{8,10},{9,11},{10,... | collective-permute-start | bytes 23048 | tf_op jit(solution)/shard_map/ppermute | solution.py:19
  92.2 1.2 collective-permute-start.15
  93.5 0.8 copy.311
  94.3 1.2 reshape.647
  95.5 3.3 %all-to-all-start = ((bf16[4,2,9216]{2,1,0:T(2,128)(2,1)}), bf16[4,2,9216]{2,1,0:T(2,128)(2,1)S(1)}, u32[]{:S(2)}, u32[]{:S(2)}) async-start(bf16[4,2,9216]{2,1,0:T(2,128)(2,1)} %reshape.647), calls=%async_computation | async-start | bytes 294912 | tf_op jit(solution)/shard_map/all_to_all | solution.py:161
  99.6 4.0 %all-to-all-done = bf16[4,2,9216]{2,1,0:T(2,128)(2,1)S(1)} async-done(((bf16[4,2,9216]{2,1,0:T(2,128)(2,1)}), bf16[4,2,9216]{2,1,0:T(2,128)(2,1)S(1)}, u32[]{:S(2)}, u32[]{:S(2)}) %all-to-all-start) | async-done | bytes 147488 | tf_op jit(solution)/shard_map/all_to_all | solution.py:161
  103.9 0.8 copy.312
  104.7 1.1 reshape.512
  105.7 0.8 fusion.103
  106.5 1.6 %collective-permute-start.8 = (f32[35,128]{1,0:T(8,128)S(1)}, f32[35,128]{1,0:T(8,128)S(1)}, u32[]{:S(2)}, u32[]{:S(2)}) collective-permute-start(f32[35,128]{1,0:T(8,128)S(1)} %pad_maximum_fusion.2), channel_id=1, source_target_pairs={{0,4},{4,0},{8,12},{12,8},{16,20},{20,16},{24,28},{28,24},{1,5},{5... | collective-permute-start | bytes 53768 | tf_op jit(solution)/shard_map/ppermute | solution.py:19
  108.1 1.6 %collective-permute-start.9 = (f32[35,128]{1,0:T(8,128)S(1)}, f32[35,128]{1,0:T(8,128)S(1)}, u32[]{:S(2)}, u32[]{:S(2)}) collective-permute-start(f32[35,128]{1,0:T(8,128)S(1)} %pad_maximum_fusion.3), channel_id=1, source_target_pairs={{0,8},{4,12},{8,0},{12,4},{16,24},{20,28},{24,16},{28,20},{1,9},{5... | collective-permute-start | bytes 53768 | tf_op jit(solution)/shard_map/ppermute | solution.py:19
  109.7 1.4 %collective-permute-start.10 = (f32[35,128]{1,0:T(8,128)S(1)}, f32[35,128]{1,0:T(8,128)S(1)}, u32[]{:S(2)}, u32[]{:S(2)}) collective-permute-start(f32[35,128]{1,0:T(8,128)S(1)} %pad_maximum_fusion.4), channel_id=1, source_target_pairs={{0,16},{4,20},{8,24},{12,28},{16,0},{20,4},{24,8},{28,12},{1,17},{... | collective-permute-start | bytes 53768 | tf_op jit(solution)/shard_map/ppermute | solution.py:19
  111.0 0.8 slice.149
  112.0 2.4 %collective-permute-done.10 = f32[35,128]{1,0:T(8,128)S(1)} collective-permute-done((f32[35,128]{1,0:T(8,128)S(1)}, f32[35,128]{1,0:T(8,128)S(1)}, u32[]{:S(2)}, u32[]{:S(2)}) %collective-permute-start.10) | collective-permute-done | bytes 17952 | tf_op jit(solution)/shard_map/ppermute | solution.py:19
  114.6 2.7 %scatter_fusion = f32[35,256]{0,1:T(8,128)S(1)} fusion(f32[35,256]{0,1:T(8,128)S(1)} %pad_maximum_fusion.1, s32[384]{0:T(512)S(1)} %fusion.100, f32[384,35]{1,0:T(8,128)S(1)} %copy.332), kind=kCustom, calls=%fused_computation.11 | custom fusion | flops 13440 | bytes 162816 | tf_op jit(solution)/shard_map/scatter-add | solution.py:229
  117.4 0.7 copy.334
  118.1 0.7 copy.333
  (191 shorter events, 17.0 us)
Async XLA Ops:
  7.2 28.4 %copy-start = (bf16[3,128,128]{2,1,0:T(8,128)(2,1)S(1)}, bf16[3,128,128]{2,1,0:T(8,128)(2,1)}, u32[]{:S(2)}) copy-start(bf16[3,128,128]{2,1,0:T(8,128)(2,1)} %param.19) | copy-start | bytes 294916
  9.6 26.6 %collective-permute-start.3 = (f32[3,128]{0,1:T(8,128)S(1)}, f32[3,128]{0,1:T(8,128)S(1)}, u32[]{:S(2)}, u32[]{:S(2)}) collective-permute-start(f32[3,128]{0,1:T(8,128)S(1)} %select_bitcast_fusion.2), channel_id=1, source_target_pairs={{0,4},{4,0},{8,12},{12,8},{16,20},{20,16},{24,28},{28,24},{1,5},{5... | collective-permute-start | bytes 4616 | tf_op jit(solution)/shard_map/ppermute | solution.py:19
  13.3 23.0 %collective-permute-start.4 = (f32[3,128]{0,1:T(8,128)S(1)}, f32[3,128]{0,1:T(8,128)S(1)}, u32[]{:S(2)}, u32[]{:S(2)}) collective-permute-start(f32[3,128]{0,1:T(8,128)S(1)} %select_bitcast_fusion.1), channel_id=1, source_target_pairs={{0,8},{4,12},{8,0},{12,4},{16,24},{20,28},{24,16},{28,20},{1,9},{5... | collective-permute-start | bytes 4616 | tf_op jit(solution)/shard_map/ppermute | solution.py:19
  15.7 20.7 %collective-permute-start.5 = (f32[3,128]{0,1:T(8,128)S(1)}, f32[3,128]{0,1:T(8,128)S(1)}, u32[]{:S(2)}, u32[]{:S(2)}) collective-permute-start(f32[3,128]{0,1:T(8,128)S(1)} %select_bitcast_fusion), channel_id=1, source_target_pairs={{0,16},{4,20},{8,24},{12,28},{16,0},{20,4},{24,8},{28,12},{1,17},{... | collective-permute-start | bytes 4616 | tf_op jit(solution)/shard_map/ppermute | solution.py:19
  20.6 18.4 %collective-permute-start = (bf16[32,128]{0,1:T(8,128)(2,1)}, bf16[32,128]{0,1:T(8,128)(2,1)S(1)}, u32[]{:S(2)}, u32[]{:S(2)}) collective-permute-start(bf16[32,128]{0,1:T(8,128)(2,1)} %select_bitcast_fusion.5), channel_id=1, source_target_pairs={{0,4},{4,0},{8,12},{12,8},{16,20},{20,16},{24,28},{28,24},{1,5},{5... | collective-permute-start | bytes 24584 | tf_op jit(solution)/shard_map/ppermute | solution.py:19
  22.5 16.6 %collective-permute-start.1 = (bf16[32,128]{0,1:T(8,128)(2,1)}, bf16[32,128]{0,1:T(8,128)(2,1)}, u32[]{:S(2)}, u32[]{:S(2)}) collective-permute-start(bf16[32,128]{0,1:T(8,128)(2,1)} %select_bitcast_fusion.4), channel_id=1, source_target_pairs={{0,8},{4,12},{8,0},{12,4},{16,24},{20,28},{24,16},{28,20},{1,9},{5... | collective-permute-start | bytes 24584 | tf_op jit(solution)/shard_map/ppermute | solution.py:19
  24.2 6.0 %copy-start.36 = (s32[8,2]{0,1:T(2,128)S(1)}, s32[8,2]{0,1:T(2,128)}, u32[]{:S(2)}) copy-start(s32[8,2]{0,1:T(2,128)} %param.16) | copy-start | bytes 196
  24.2 6.9 %copy-start.38 = (s32[8]{0:T(128)S(1)}, s32[8]{0:T(128)}, u32[]{:S(2)}) copy-start(s32[8]{0:T(128)} %param.17) | copy-start | bytes 100
  24.2 7.6 %copy-start.31 = (f32[32,8]{0,1:T(8,128)S(1)}, f32[32,8]{0,1:T(8,128)}, u32[]{:S(2)}) copy-start(f32[32,8]{0,1:T(8,128)} %param.18) | copy-start | bytes 3076
  24.3 7.6 %copy-start.37 = (s32[9]{0:T(128)S(1)}, s32[9]{0:T(128)}, u32[]{:S(2)}) copy-start(s32[9]{0:T(128)} %constant.99) | copy-start | bytes 112
  25.0 11.5 %copy-start.22 = (f32[3,256]{1,0:T(4,128)S(1)}, f32[3,256]{1,0:T(4,128)}, u32[]{:S(2)}) copy-start(f32[3,256]{1,0:T(4,128)} %param.13) | copy-start | bytes 9220
  26.2 33.4 %all-to-all-start.1 = ((bf16[4,2,9216]{2,1,0:T(2,128)(2,1)}), bf16[4,2,9216]{2,1,0:T(2,128)(2,1)}, u32[]{:S(2)}, u32[]{:S(2)}) async-start(bf16[4,2,9216]{2,1,0:T(2,128)(2,1)} %reshape.649), calls=%async_computation.1 | async-start | bytes 294912 | tf_op jit(solution)/shard_map/all_to_all | solution.py:168
  30.2 75.6 %reduce-scatter.4.cloned.1.call-start = ((), (), s32[]{:S(2)}) async-start(), calls=%async_computation.3 | async-start | bytes 409600
  30.3 8.2 %copy-start.32 = (f32[8]{0:T(128)}, f32[8]{0:T(128)S(1)}, u32[]{:S(2)}) copy-start(f32[8]{0:T(128)S(1)} %compare_convert_fusion.1) | copy-start | bytes 100
  30.3 8.3 %copy-start.34 = (f32[8]{0:T(128)}, f32[8]{0:T(128)S(1)}, u32[]{:S(2)}) copy-start(f32[8]{0:T(128)S(1)} %add_multiply_fusion) | copy-start | bytes 100
  31.0 6.7 %copy-start.29 = (s32[1024]{0:T(1024)}, s32[1024]{0:T(1024)S(1)}, u32[]{:S(2)}) copy-start(s32[1024]{0:T(1024)S(1)} %pad_clamp_fusion.3) | copy-start | bytes 12292
  31.1 7.4 %copy-start.26 = (f32[8]{0:T(128)}, f32[8]{0:T(128)S(1)}, u32[]{:S(2)}) copy-start(f32[8]{0:T(128)S(1)} %convert_element_type.95) | copy-start | bytes 100
  32.5 1.6 %copy-start.20 = (f32[8,5]{1,0:T(8,128)}, f32[8,5]{1,0:T(8,128)S(1)}, u32[]{:S(2)}) copy-start(f32[8,5]{1,0:T(8,128)S(1)} %get-tuple-element.74) | copy-start | bytes 484
  36.2 5.2 %collective-permute-start.2 = (bf16[32,128]{0,1:T(8,128)(2,1)}, bf16[32,128]{0,1:T(8,128)(2,1)}, u32[]{:S(2)}, u32[]{:S(2)}) collective-permute-start(bf16[32,128]{0,1:T(8,128)(2,1)} %select_bitcast_fusion.3), channel_id=1, source_target_pairs={{0,16},{4,20},{8,24},{12,28},{16,0},{20,4},{24,8},{28,12},{1,17},{... | collective-permute-start | bytes 24584 | tf_op jit(solution)/shard_map/ppermute | solution.py:19
  37.2 1.0 copy-start.15
  37.8 0.6 copy-start.17
  38.5 3.7 %copy-start.19 = (bf16[32,256]{1,0:T(8,128)(2,1)S(1)}, bf16[32,256]{1,0:T(8,128)(2,1)}, u32[]{:S(2)}) copy-start(bf16[32,256]{1,0:T(8,128)(2,1)} %param.14) | copy-start | bytes 49156
  38.6 10.7 %copy-start.8 = (f32[8,32,128]{2,1,0:T(8,128)}, f32[8,32,128]{2,1,0:T(8,128)S(1)}, u32[]{:S(2)}) copy-start(f32[8,32,128]{2,1,0:T(8,128)S(1)} %get-tuple-element.51) | copy-start | bytes 393220
  38.6 10.7 %copy-start.9 = (f32[8,32,128]{2,1,0:T(8,128)}, f32[8,32,128]{2,1,0:T(8,128)S(1)}, u32[]{:S(2)}) copy-start(f32[8,32,128]{2,1,0:T(8,128)S(1)} %get-tuple-element.52) | copy-start | bytes 393220
  38.9 14.9 %copy-start.1 = (f32[8,8,32,128]{3,2,0,1:T(8,128)}, f32[8,8,32,128]{3,2,0,1:T(8,128)S(1)}, u32[]{:S(2)}) copy-start(f32[8,8,32,128]{3,2,0,1:T(8,128)S(1)} %fusion.17) | copy-start | bytes 3145732
  39.0 14.8 %copy-start.6 = (f32[9,8,32,128]{3,2,1,0:T(8,128)}, f32[9,8,32,128]{3,2,1,0:T(8,128)S(1)}, u32[]{:S(2)}) copy-start(f32[9,8,32,128]{3,2,1,0:T(8,128)S(1)} %multiply_dynamic-update-slice_fusion) | copy-start | bytes 3538948
  53.9 5.1 %copy-start.27 = (f32[8]{0:T(128)S(1)}, f32[8]{0:T(128)}, u32[]{:S(2)}) copy-start(f32[8]{0:T(128)} %copy-done.26) | copy-start | bytes 100
  61.9 1.0 copy-start.4
  63.9 0.9 copy-start.14
  64.8 1.4 %copy-start.2 = (f32[8,8,32,128]{3,2,0,1:T(8,128)S(1)}, f32[8,8,32,128]{3,2,0,1:T(8,128)}, u32[]{:S(2)}) copy-start(f32[8,8,32,128]{3,2,0,1:T(8,128)} %copy-done.1) | copy-start | bytes 3145732
  64.8 1.6 %copy-start.7 = (f32[9,8,32,128]{3,2,1,0:T(8,128)S(1)}, f32[9,8,32,128]{3,2,1,0:T(8,128)}, u32[]{:S(2)}) copy-start(f32[9,8,32,128]{3,2,1,0:T(8,128)} %copy-done.6) | copy-start | bytes 3538948
  73.4 1.7 %copy-start.5 = (f32[2,128,9,8,32,1]{1,4,5,3,2,0:T(8,128)S(1)}, f32[2,128,9,8,32,1]{1,4,5,3,2,0:T(8,128)}, u32[]{:S(2)}) copy-start(f32[2,128,9,8,32,1]{1,4,5,3,2,0:T(8,128)} %get-tuple-element.79) | copy-start | bytes 7077892
  75.1 1.0 copy-start.21
  75.4 2.1 %copy-start.3 = (f32[8,8,32,128]{3,2,0,1:T(8,128)S(1)}, f32[8,8,32,128]{3,2,0,1:T(8,128)}, u32[]{:S(2)}) copy-start(f32[8,8,32,128]{3,2,0,1:T(8,128)} %get-tuple-element.35) | copy-start | bytes 3145732
  75.5 2.1 %copy-start.35 = (f32[8]{0:T(128)S(1)}, f32[8]{0:T(128)}, u32[]{:S(2)}) copy-start(f32[8]{0:T(128)} %copy-done.34) | copy-start | bytes 100
  75.5 5.1 %collective-permute-start.11 = (f32[128,8]{0,1:T(8,128)S(1)}, f32[128,8]{0,1:T(8,128)}, u32[]{:S(2)}, u32[]{:S(2)}) collective-permute-start(f32[128,8]{0,1:T(8,128)S(1)} %fusion.6), channel_id=1, source_target_pairs={{0,1},{1,0},{2,3},{3,2},{4,5},{5,4},{6,7},{7,6},{8,9},{9,8},{10,11... | collective-permute-start | bytes 12296 | tf_op jit(solution)/shard_map/ppermute | solution.py:19
  76.6 2.5 %copy-start.28 = (f32[8]{0:T(128)S(1)}, f32[8]{0:T(128)}, u32[]{:S(2)}) copy-start(f32[8]{0:T(128)} %copy-done.26) | copy-start | bytes 100
  76.6 2.5 %copy-start.33 = (f32[8]{0:T(128)S(1)}, f32[8]{0:T(128)}, u32[]{:S(2)}) copy-start(f32[8]{0:T(128)} %copy-done.32) | copy-start | bytes 100
  79.0 0.9 copy-start.11
  79.0 1.0 copy-start.12
  79.1 1.0 copy-start.13
  79.1 1.0 copy-start.16
  79.1 1.0 copy-start.18
  79.1 1.3 %copy-start.25 = (f32[8,5]{0,1:T(8,128)S(1)}, f32[8,5]{0,1:T(8,128)}, u32[]{:S(2)}) copy-start(f32[8,5]{0,1:T(8,128)} %copy.319) | copy-start | bytes 484
  79.1 3.8 %copy-start.24 = (f32[8,5]{0,1:T(8,128)S(1)}, f32[8,5]{0,1:T(8,128)}, u32[]{:S(2)}) copy-start(f32[8,5]{0,1:T(8,128)} %copy.327) | copy-start | bytes 484
  79.1 7.3 %copy-start.23 = (f32[640]{0:T(1024)S(1)}, f32[640]{0:T(1024)}, u32[]{:S(2)}) copy-start(f32[640]{0:T(1024)} %mul.629) | copy-start | bytes 7684
  79.1 10.7 %copy-start.30 = (s32[3,128]{1,0:T(4,128)S(1)}, s32[3,128]{1,0:T(4,128)}, u32[]{:S(2)}) copy-start(s32[3,128]{1,0:T(4,128)} %param.15) | copy-start | bytes 4612
  79.2 14.3 %copy-start.10 = (bf16[128,8,2,1,32]{0,4,2,1,3:T(8,128)(2,1)S(1)}, bf16[128,8,2,1,32]{0,4,2,1,3:T(8,128)(2,1)}, u32[]{:S(2)}) copy-start(bf16[128,8,2,1,32]{0,4,2,1,3:T(8,128)(2,1)} %get-tuple-element.57) | copy-start | bytes 393220
  81.2 3.6 %collective-permute-start.12 = (f32[128,8]{0,1:T(8,128)S(1)}, f32[128,8]{0,1:T(8,128)S(1)}, u32[]{:S(2)}, u32[]{:S(2)}) collective-permute-start(f32[128,8]{0,1:T(8,128)S(1)} %add.188), channel_id=1, source_target_pairs={{0,2},{1,3},{2,0},{3,1},{4,6},{5,7},{6,4},{7,5},{8,10},{9,11},{10,... | collective-permute-start | bytes 12296 | tf_op jit(solution)/shard_map/ppermute | solution.py:19
  84.9 3.6 %collective-permute-start.13 = (f32[32,8]{0,1:T(8,128)S(1)}, f32[32,8]{0,1:T(8,128)S(1)}, u32[]{:S(2)}, u32[]{:S(2)}) collective-permute-start(f32[32,8]{0,1:T(8,128)S(1)} %constant_dynamic-slice_fusion), channel_id=1, source_target_pairs={{0,4},{4,0},{8,12},{12,8},{16,20},{20,16},{24,28},{28,24},{1,5},{5... | collective-permute-start | bytes 3080 | tf_op jit(solution)/shard_map/ppermute | solution.py:19
  86.4 3.4 %collective-permute-start.6 = (f32[3,640]{1,0:T(4,128)S(1)}, f32[3,640]{1,0:T(4,128)S(1)}, u32[]{:S(2)}, u32[]{:S(2)}) collective-permute-start(f32[3,640]{1,0:T(4,128)S(1)} %bitcast_add_fusion.2), channel_id=1, source_target_pairs={{0,1},{1,0},{2,3},{3,2},{4,5},{5,4},{6,7},{7,6},{8,9},{9,8},{10,11... | collective-permute-start | bytes 23048 | tf_op jit(solution)/shard_map/ppermute | solution.py:19
  88.6 3.6 %collective-permute-start.14 = (f32[32,8]{0,1:T(8,128)S(1)}, f32[32,8]{0,1:T(8,128)S(1)}, u32[]{:S(2)}, u32[]{:S(2)}) collective-permute-start(f32[32,8]{0,1:T(8,128)S(1)} %fusion.108), channel_id=1, source_target_pairs={{0,8},{4,12},{8,0},{12,4},{16,24},{20,28},{24,16},{28,20},{1,9},{5... | collective-permute-start | bytes 3080 | tf_op jit(solution)/shard_map/ppermute | solution.py:19
  89.9 9.6 %collective-permute-start.7 = (f32[3,640]{1,0:T(4,128)S(1)}, f32[3,640]{1,0:T(4,128)S(1)}, u32[]{:S(2)}, u32[]{:S(2)}) collective-permute-start(f32[3,640]{1,0:T(4,128)S(1)} %add.184), channel_id=1, source_target_pairs={{0,2},{1,3},{2,0},{3,1},{4,6},{5,7},{6,4},{7,5},{8,10},{9,11},{10,... | collective-permute-start | bytes 23048 | tf_op jit(solution)/shard_map/ppermute | solution.py:19
  92.2 6.6 %collective-permute-start.15 = (f32[32,8]{0,1:T(8,128)S(1)}, f32[32,8]{0,1:T(8,128)S(1)}, u32[]{:S(2)}, u32[]{:S(2)}) collective-permute-start(f32[32,8]{0,1:T(8,128)S(1)} %add.191), channel_id=1, source_target_pairs={{0,16},{4,20},{8,24},{12,28},{16,0},{20,4},{24,8},{28,12},{1,17},{... | collective-permute-start | bytes 3080 | tf_op jit(solution)/shard_map/ppermute | solution.py:19
  95.5 8.1 %all-to-all-start = ((bf16[4,2,9216]{2,1,0:T(2,128)(2,1)}), bf16[4,2,9216]{2,1,0:T(2,128)(2,1)S(1)}, u32[]{:S(2)}, u32[]{:S(2)}) async-start(bf16[4,2,9216]{2,1,0:T(2,128)(2,1)} %reshape.647), calls=%async_computation | async-start | bytes 294912 | tf_op jit(solution)/shard_map/all_to_all | solution.py:161
  106.5 5.5 %collective-permute-start.8 = (f32[35,128]{1,0:T(8,128)S(1)}, f32[35,128]{1,0:T(8,128)S(1)}, u32[]{:S(2)}, u32[]{:S(2)}) collective-permute-start(f32[35,128]{1,0:T(8,128)S(1)} %pad_maximum_fusion.2), channel_id=1, source_target_pairs={{0,4},{4,0},{8,12},{12,8},{16,20},{20,16},{24,28},{28,24},{1,5},{5... | collective-permute-start | bytes 53768 | tf_op jit(solution)/shard_map/ppermute | solution.py:19
  108.1 3.9 %collective-permute-start.9 = (f32[35,128]{1,0:T(8,128)S(1)}, f32[35,128]{1,0:T(8,128)S(1)}, u32[]{:S(2)}, u32[]{:S(2)}) collective-permute-start(f32[35,128]{1,0:T(8,128)S(1)} %pad_maximum_fusion.3), channel_id=1, source_target_pairs={{0,8},{4,12},{8,0},{12,4},{16,24},{20,28},{24,16},{28,20},{1,9},{5... | collective-permute-start | bytes 53768 | tf_op jit(solution)/shard_map/ppermute | solution.py:19
  109.7 4.8 %collective-permute-start.10 = (f32[35,128]{1,0:T(8,128)S(1)}, f32[35,128]{1,0:T(8,128)S(1)}, u32[]{:S(2)}, u32[]{:S(2)}) collective-permute-start(f32[35,128]{1,0:T(8,128)S(1)} %pad_maximum_fusion.4), channel_id=1, source_target_pairs={{0,16},{4,20},{8,24},{12,28},{16,0},{20,4},{24,8},{28,12},{1,17},{... | collective-permute-start | bytes 53768 | tf_op jit(solution)/shard_map/ppermute | solution.py:19
Sparse Core Ops, SparseCore 0:
  77.6 20.5 reduce-scatter.3

commit v8 on v7

--- a/solution.py
+++ b/solution.py
@@ -83,15 +83,20 @@
     chan_index = lax.axis_index("chan")
     pos_list = [positions]
     feat_list = [features]
+    both_rows = jnp.take(
+        jnp.concatenate([features.astype(jnp.float32), positions], axis=0),
+        send_rows[:levels].reshape(-1),
+        axis=1,
+        mode="clip",
+    )
     for level_bit in range(levels):
-        sent_rows = send_rows[level_bit]
-        got_feat, got_pos = partner(
-            (jnp.take(features, sent_rows, axis=1), jnp.take(positions, sent_rows, axis=1)),
+        got_both = partner(
+            both_rows[:, level_bit * block_size : (level_bit + 1) * block_size],
             "space",
             level_bit,
         )
-        feat_list.append(got_feat)
-        pos_list.append(got_pos)
+        feat_list.append(got_both[:chan_dev].astype(jnp.bfloat16))
+        pos_list.append(got_both[chan_dev:])
     src_pos = jnp.concatenate(pos_list, axis=1)
     src_feat = jnp.concatenate(feat_list, axis=1)
     src_atoms = src_pos.shape[1]

time: 127 us -> 107 us (0.84)
  local copies, waits for them, and re-layouts: 33.8 us -> 24.1 us
  starting transfers between devices: 28.4 us -> 22.8 us
  other arithmetic: 21.3 us -> 19.7 us
    ppermute x16 -> x13, starting transfers between devices: 21 us -> 16.1 us  [partner(): return lax.ppermute(value, axis, pairs)]
    gather x6 -> x1, local copies, waits for them, and re-layouts: 4.07 us -> 1.12 us  [body(): jnp.take(jnp.concatenate([features.astype(jnp.float32), positions], axis=...]
    unnamed x91 -> x89, local copies, waits for them, and re-layouts: 10.7 us -> 7.81 us
    select_n x6 -> x0, other arithmetic: 2.31 us -> none  [the longest x3 2.06 us: body(): jnp.take(features, sent_rows, axis=1)]
    ppermute x6 -> x0, local copies, waits for them, and re-layouts: 1.98 us -> none  [partner(): return lax.ppermute(value, axis, pairs)]
    ppermute x16 -> x13, waiting for transfers between devices: 8.1 us -> 6.96 us  [partner(): return lax.ppermute(value, axis, pairs)]
  transfers between devices with their start and end apart: 19 -> 16, of which waited for: 6 -> 5; matrix products, arithmetic and copies ran while one was open for 32% -> 24% of each run, Pallas kernels for 0% -> 0%
where the time goes in v8:
time: 107 us; the launch traced here: 106 us
  local copies, waits for them, and re-layouts  24.1 us (23%)
  starting transfers between devices  22.8 us (21%)
  other arithmetic  19.7 us (18%)
  between operations  15 us (14%)
  waiting for transfers between devices  11 us (10%)
  matrix products  7.67 us (7%)
  blocking collectives  6.01 us (6%)
    ppermute x13, starting transfers between devices, partner(): return lax.ppermute(value, axis, pairs)  16.1 us
    unnamed x89, local copies, waits for them, and re-layouts  7.81 us
    ppermute x13, waiting for transfers between devices, partner(): return lax.ppermute(value, axis, pairs)  6.96 us
    all_gather x1, blocking collectives, body(): lax.all_gather(jnp.concatenate([src_feat, weight_high, weight_mid, weight...  6.01 us
    all_to_all x1, waiting for transfers between devices, body(): lax.all_to_all(result_rows.reshape(all_chan, components, own_blocks, 1, r...  4 us
    reduce_sum x1, other arithmetic, body(): harm_grad = jnp.sum(value_grad * radial[None], axis=1)  3.8 us
    all_to_all x1, starting transfers between devices, body(): lax.all_to_all(out_grad.reshape(chan_dev, components, own_blocks, chan_co...  3.34 us
    all_to_all x1, starting transfers between devices, body(): lax.all_to_all(result_rows.reshape(all_chan, components, own_blocks, 1, r...  3.34 us
  transfers between devices with their start and end apart: 16, of which 5 were waited for; matrix products, arithmetic and copies ran while one was open for 24% of the time, Pallas kernels for 0%

profile of v8, /device:TPU:0, one launch (start us, length us, event | category | flops | bytes accessed | tf_op | source)
XLA Modules:
  0.0 106.2 jit_solution(5519545173009802851)
XLA Ops:
  7.2 0.8 slice_bitcast_fusion.2
  8.0 0.7 convert_element_type.95
  8.7 0.7 pad_maximum_fusion.2
  9.5 0.7 pad_clamp_fusion.3
  10.2 1.1 %gather_fusion = f32[384,35]{1,0:T(8,128)S(1)} fusion(f32[35,256]{0,1:T(8,128)S(1)} %copy.258, s32[1024]{0:T(1024)S(1)} %get-tuple-element.73), kind=kCustom, calls=%fused_computation | custom fusion | bytes 109056 | tf_op jit(solution)/shard_map/jit(_take)/gather | solution.py:86
  11.3 3.0 %collective-permute-start = (f32[35,128]{0,1:T(8,128)S(1)}, f32[35,128]{0,1:T(8,128)S(1)}, u32[]{:S(2)}, u32[]{:S(2)}) collective-permute-start(f32[35,128]{0,1:T(8,128)S(1)} %get-tuple-element.43), channel_id=1, source_target_pairs={{0,4},{4,0},{8,12},{12,8},{16,20},{20,16},{24,28},{28,24},{1,5},{5... | collective-permute-start | bytes 53768 | tf_op jit(solution)/shard_map/ppermute | solution.py:19
  14.3 1.6 %collective-permute-start.1 = (f32[35,128]{0,1:T(8,128)S(1)}, f32[35,128]{0,1:T(8,128)S(1)}, u32[]{:S(2)}, u32[]{:S(2)}) collective-permute-start(f32[35,128]{0,1:T(8,128)S(1)} %get-tuple-element.44), channel_id=1, source_target_pairs={{0,8},{4,12},{8,0},{12,4},{16,24},{20,28},{24,16},{28,20},{1,9},{5... | collective-permute-start | bytes 53768 | tf_op jit(solution)/shard_map/ppermute | solution.py:19
  15.9 2.6 %collective-permute-start.2 = (f32[35,128]{0,1:T(8,128)S(1)}, f32[35,128]{0,1:T(8,128)S(1)}, u32[]{:S(2)}, u32[]{:S(2)}) collective-permute-start(f32[35,128]{0,1:T(8,128)S(1)} %get-tuple-element.45), channel_id=1, source_target_pairs={{0,16},{4,20},{8,24},{12,28},{16,0},{20,4},{24,8},{28,12},{1,17},{... | collective-permute-start | bytes 53768 | tf_op jit(solution)/shard_map/ppermute | solution.py:19
  18.8 0.7 copy.281
  19.5 1.2 %reshape.581 = bf16[4,2,9216]{2,1,0:T(2,128)(2,1)} reshape(bf16[4,9,2,32,32]{4,3,2,1,0:T(8,128)(2,1)S(1)} %bitcast.378) | data formatting | bytes 294912
  20.7 3.3 %all-to-all-start.1 = ((bf16[4,2,9216]{2,1,0:T(2,128)(2,1)}), bf16[4,2,9216]{2,1,0:T(2,128)(2,1)S(1)}, u32[]{:S(2)}, u32[]{:S(2)}) async-start(bf16[4,2,9216]{2,1,0:T(2,128)(2,1)} %reshape.581), calls=%async_computation.1 | async-start | bytes 294912 | tf_op jit(solution)/shard_map/all_to_all | solution.py:173
  24.4 0.6 pad_clamp_fusion
  25.3 0.7 copy.286
  26.1 0.7 copy.294
  26.8 0.7 mul.629
  27.5 0.6 gather_fusion.4
  28.5 6.0 %all_gather.3 = bf16[128,664]{1,0:T(8,128)(2,1)S(1)} all-gather(bf16[32,664]{1,0:T(8,128)(2,1)S(1)} %concatenate.44), channel_id=1, replica_groups=mesh['space'=8,'chan'=4] {'chan'}, dimensions={0}, use_global_device_ids=true | all-gather | bytes 212480 | tf_op jit(solution)/shard_map/all_gather | solution.py:107
  35.1 0.6 gather_fusion.3
  35.7 0.6 gather_fusion.2
  37.1 0.4 slice-done
  37.9 0.6 gather_fusion.1
  38.8 0.6 copy-done.8
  39.8 3.0 %fusion.7 = (bf16[128,2,9,32]{0,3,2,1:T(8,128)(2,1)S(1)}, f32[2,128,9,8,32,1]{1,4,5,3,2,0:T(8,128)}) fusion(f32[128,8]{0,1:T(8,128)S(1)} %copy.334, f32[8,128,128]{2,1,0:T(8,128)S(1)} %convert_element_type.103, f32[8,2]{0,1:T(2,128)S(1)} %copy.265, f32[8,8,32,128]{3,2,0,1:T(8,128)S(1)} %fusion.17, f32[9,8,32,128]{3,2,1,0:T(8,128)S(1)} %multiply_dynamic-update-slice_fusion), kind=kOutput, calls=%fused_computation.21 | convolution fusion | flops 1214308352 | bytes 5263424 | tf_op jit(solution)/shard_map/lktij,tbcj->bclki/dot_general | solution.py:150
  42.8 1.0 convolution_bitcast_fusion
  43.8 0.7 broadcast_multiply_fusion
  44.9 0.8 copy.282
  45.8 0.5 reshape.506
  46.3 0.4 copy-done.4
  46.8 0.7 multiply_convert_fusion.3
  47.8 0.9 gather_fusion.5
  48.7 1.4 %multiply_convert_fusion = bf16[8,128,9,8,32]{1,4,3,2,0:T(8,128)(2,1)S(1)} fusion(f32[8,128,9,32]{1,3,2,0:T(8,128)S(1)} %gather_fusion.5, f32[8,128,8]{1,2,0:T(8,128)S(1)} %copy-done.16), kind=kLoop, calls=%fused_computation.9 | loop fusion | flops 4718592 | bytes 5931008 | tf_op jit(solution)/shard_map/convert_element_type | solution.py:196
  50.2 2.1 %fusion.8 = f32[8,128,128]{2,1,0:T(8,128)S(1)} fusion(bf16[8,128,9,8,32]{1,4,3,2,0:T(8,128)(2,1)S(1)} %multiply_convert_fusion, f32[8,8,32,128]{3,2,0,1:T(8,128)S(1)} %copy-done.2, f32[9,8,32,128]{3,2,1,0:T(8,128)S(1)} %copy-done.7), kind=kOutput, calls=%fused_computation.24 | convolution fusion | flops 608698368 | bytes 7471104 | tf_op jit(solution)/shard_map/tclki,lktij->tcj/dot_general | solution.py:197
  52.3 1.4 %fusion.106 = f32[8,128,2304]{1,2,0:S(1)} fusion(bf16[8,128,2304]{1,2,0:T(8,128)(2,1)S(1)} %bitcast.377, bf16[8,128,128]{2,1,0:T(8,128)(2,1)S(1)} %gather_fusion.1), kind=kOutput, calls=%fused_computation.218 | convolution fusion | flops 603979776 | bytes 14417920
  53.7 3.8 %multiply_reduce_fusion.1 = (f32[9,8,32,128]{3,2,0,1:T(8,128)S(1)}, f32[8,8,32,128]{3,2,0,1:T(8,128)}) fusion(f32[9,8,8,32,128]{4,3,1,0,2:T(8,128)S(1)} %bitcast.376, f32[8,8,32,128]{3,2,0,1:T(8,128)S(1)} %copy-done.2, f32[9,8,32,128]{3,2,1,0:T(8,128)S(1)} %copy-done.7), kind=kLoop, calls=%fused_computation.8 | loop fusion | flops 8880128 | bytes 13893632 | tf_op jit(solution)/shard_map/reduce_sum | solution.py:203
  57.5 0.8 fusion.39
  58.3 0.9 fusion.72
  59.6 0.4 collective-permute-start.8
  60.5 0.9 copy.320
  61.4 1.5 %fusion.18 = (f32[8,32,128]{2,1,0:T(8,128)S(1)}, f32[8,32,128]{2,1,0:T(8,128)S(1)}) fusion(f32[8,8,32,128]{3,2,0,1:T(8,128)S(1)} %copy-done.3, f32[8]{0:T(128)S(1)} %copy-done.35, f32[8,32,128]{2,1,0:T(8,128)} %copy-done.8, f32[8,32,128]{2,1,0:T(8,128)} %copy-done.9), kind=kLoop, calls=%fused_computation.32 | loop fusion | flops 2818048 | bytes 1572896 | tf_op jit(solution)/shard_map/transpose(jvp())/reduce_sum | solution.py:56
  63.0 0.3 fusion.51
  63.4 0.4 copy-done.12
  64.4 0.7 add.176
  65.1 1.7 %collective-permute-start.9 = (f32[128,8]{0,1:T(8,128)S(1)}, f32[128,8]{0,1:T(8,128)S(1)}, u32[]{:S(2)}, u32[]{:S(2)}) collective-permute-start(f32[128,8]{0,1:T(8,128)S(1)} %add.176), channel_id=1, source_target_pairs={{0,2},{1,3},{2,0},{3,1},{4,6},{5,7},{6,4},{7,5},{8,10},{9,11},{10,... | collective-permute-start | bytes 12296 | tf_op jit(solution)/shard_map/ppermute | solution.py:19
  67.0 1.7 %collective-permute-done.9 = f32[128,8]{0,1:T(8,128)S(1)} collective-permute-done((f32[128,8]{0,1:T(8,128)S(1)}, f32[128,8]{0,1:T(8,128)S(1)}, u32[]{:S(2)}, u32[]{:S(2)}) %collective-permute-start.9) | collective-permute-done | bytes 4128 | tf_op jit(solution)/shard_map/ppermute | solution.py:19
  68.8 0.5 collective-permute-start.10
  69.4 3.0 %collective-permute-done.10 = f32[32,8]{0,1:T(8,128)S(1)} collective-permute-done((f32[32,8]{0,1:T(8,128)S(1)}, f32[32,8]{0,1:T(8,128)S(1)}, u32[]{:S(2)}, u32[]{:S(2)}) %collective-permute-start.10) | collective-permute-done | bytes 1056 | tf_op jit(solution)/shard_map/ppermute | solution.py:19
  72.5 0.4 collective-permute-start.11
  73.0 1.8 %collective-permute-start.4 = (f32[3,640]{1,0:T(4,128)S(1)}, f32[3,640]{1,0:T(4,128)S(1)}, u32[]{:S(2)}, u32[]{:S(2)}) collective-permute-start(f32[3,640]{1,0:T(4,128)S(1)} %add.172), channel_id=1, source_target_pairs={{0,2},{1,3},{2,0},{3,1},{4,6},{5,7},{6,4},{7,5},{8,10},{9,11},{10,... | collective-permute-start | bytes 23048 | tf_op jit(solution)/shard_map/ppermute | solution.py:19
  74.7 1.3 %collective-permute-done.11 = f32[32,8]{0,1:T(8,128)S(1)} collective-permute-done((f32[32,8]{0,1:T(8,128)S(1)}, f32[32,8]{0,1:T(8,128)S(1)}, u32[]{:S(2)}, u32[]{:S(2)}) %collective-permute-start.11) | collective-permute-done | bytes 1056 | tf_op jit(solution)/shard_map/ppermute | solution.py:19
  76.4 0.8 copy.278
  77.3 1.2 %reshape.579 = bf16[4,2,9216]{2,1,0:T(2,128)(2,1)} reshape(bf16[128,1,9,2,32]{4,3,2,1,0:T(2,128)(2,1)S(1)} %bitcast.379) | data formatting | bytes 294912
  78.5 3.3 %all-to-all-start = ((bf16[4,2,9216]{2,1,0:T(2,128)(2,1)}), bf16[4,2,9216]{2,1,0:T(2,128)(2,1)S(1)}, u32[]{:S(2)}, u32[]{:S(2)}) async-start(bf16[4,2,9216]{2,1,0:T(2,128)(2,1)} %reshape.579), calls=%async_computation | async-start | bytes 294912 | tf_op jit(solution)/shard_map/all_to_all | solution.py:166
  81.8 0.6 add.180
  82.6 4.0 %all-to-all-done = bf16[4,2,9216]{2,1,0:T(2,128)(2,1)S(1)} async-done(((bf16[4,2,9216]{2,1,0:T(2,128)(2,1)}), bf16[4,2,9216]{2,1,0:T(2,128)(2,1)S(1)}, u32[]{:S(2)}, u32[]{:S(2)}) %all-to-all-start) | async-done | bytes 147488 | tf_op jit(solution)/shard_map/all_to_all | solution.py:166
  86.9 0.8 copy.279
  87.6 1.1 %reshape.502 = bf16[32,9,256]{2,0,1:T(8,128)(2,1)} reshape(bf16[32,9,2,4,1,32]{5,3,2,0,1,4:T(4,128)(2,1)S(1)} %copy.279) | data formatting | bytes 294912 | tf_op jit(solution)/shard_map/reshape | solution.py:172
  88.7 0.8 fusion.104
  89.5 0.6 collective-permute-start.5
  90.3 2.8 %collective-permute-start.7 = (f32[35,128]{1,0:T(8,128)S(1)}, f32[35,128]{1,0:T(8,128)S(1)}, u32[]{:S(2)}, u32[]{:S(2)}) collective-permute-start(f32[35,128]{1,0:T(8,128)S(1)} %pad_maximum_fusion.5), channel_id=1, source_target_pairs={{0,16},{4,20},{8,24},{12,28},{16,0},{20,4},{24,8},{28,12},{1,17},{... | collective-permute-start | bytes 53768 | tf_op jit(solution)/shard_map/ppermute | solution.py:19
  93.1 0.8 slice.175
  94.1 0.9 collective-permute-done.7
  95.1 2.7 %scatter_fusion = f32[35,256]{0,1:T(8,128)S(1)} fusion(f32[35,256]{0,1:T(8,128)S(1)} %pad_maximum_fusion.1, s32[384]{0:T(512)S(1)} %fusion.100, f32[384,35]{1,0:T(8,128)S(1)} %copy.299), kind=kCustom, calls=%fused_computation.6 | custom fusion | flops 13440 | bytes 162816 | tf_op jit(solution)/shard_map/scatter-add | solution.py:234
  97.9 0.7 copy.301
  98.6 0.7 copy.300
  (179 shorter events, 8.1 us)
Async XLA Ops:
  7.2 20.3 %copy-start = (bf16[3,128,128]{2,1,0:T(8,128)(2,1)S(1)}, bf16[3,128,128]{2,1,0:T(8,128)(2,1)}, u32[]{:S(2)}) copy-start(bf16[3,128,128]{2,1,0:T(8,128)(2,1)} %param.15) | copy-start | bytes 294916
  7.2 11.3 %copy-start.15 = (bf16[32,9,256]{2,0,1:T(8,128)(2,1)S(1)}, bf16[32,9,256]{2,0,1:T(8,128)(2,1)}, u32[]{:S(2)}) copy-start(bf16[32,9,256]{2,0,1:T(8,128)(2,1)} %param.16) | copy-start | bytes 442372
  11.3 16.8 %collective-permute-start = (f32[35,128]{0,1:T(8,128)S(1)}, f32[35,128]{0,1:T(8,128)S(1)}, u32[]{:S(2)}, u32[]{:S(2)}) collective-permute-start(f32[35,128]{0,1:T(8,128)S(1)} %get-tuple-element.43), channel_id=1, source_target_pairs={{0,4},{4,0},{8,12},{12,8},{16,20},{20,16},{24,28},{28,24},{1,5},{5... | collective-permute-start | bytes 53768 | tf_op jit(solution)/shard_map/ppermute | solution.py:19
  14.3 13.8 %collective-permute-start.1 = (f32[35,128]{0,1:T(8,128)S(1)}, f32[35,128]{0,1:T(8,128)S(1)}, u32[]{:S(2)}, u32[]{:S(2)}) collective-permute-start(f32[35,128]{0,1:T(8,128)S(1)} %get-tuple-element.44), channel_id=1, source_target_pairs={{0,8},{4,12},{8,0},{12,4},{16,24},{20,28},{24,16},{28,20},{1,9},{5... | collective-permute-start | bytes 53768 | tf_op jit(solution)/shard_map/ppermute | solution.py:19
  15.9 12.3 %collective-permute-start.2 = (f32[35,128]{0,1:T(8,128)S(1)}, f32[35,128]{0,1:T(8,128)S(1)}, u32[]{:S(2)}, u32[]{:S(2)}) collective-permute-start(f32[35,128]{0,1:T(8,128)S(1)} %get-tuple-element.45), channel_id=1, source_target_pairs={{0,16},{4,20},{8,24},{12,28},{16,0},{20,4},{24,8},{28,12},{1,17},{... | collective-permute-start | bytes 53768 | tf_op jit(solution)/shard_map/ppermute | solution.py:19
  18.8 5.4 %copy-start.36 = (s32[8,2]{0,1:T(2,128)S(1)}, s32[8,2]{0,1:T(2,128)}, u32[]{:S(2)}) copy-start(s32[8,2]{0,1:T(2,128)} %param.12) | copy-start | bytes 196
  18.8 5.5 %copy-start.38 = (s32[8]{0:T(128)S(1)}, s32[8]{0:T(128)}, u32[]{:S(2)}) copy-start(s32[8]{0:T(128)} %param.13) | copy-start | bytes 100
  18.8 5.5 %copy-start.31 = (f32[32,8]{0,1:T(8,128)S(1)}, f32[32,8]{0,1:T(8,128)}, u32[]{:S(2)}) copy-start(f32[32,8]{0,1:T(8,128)} %param.14) | copy-start | bytes 3076
  18.8 5.5 %copy-start.37 = (s32[9]{0:T(128)S(1)}, s32[9]{0:T(128)}, u32[]{:S(2)}) copy-start(s32[9]{0:T(128)} %constant.79) | copy-start | bytes 112
  19.5 8.9 %copy-start.21 = (bf16[32,256]{1,0:T(8,128)(2,1)S(1)}, bf16[32,256]{1,0:T(8,128)(2,1)}, u32[]{:S(2)}) copy-start(bf16[32,256]{1,0:T(8,128)(2,1)} %param.10) | copy-start | bytes 49156
  20.7 23.8 %all-to-all-start.1 = ((bf16[4,2,9216]{2,1,0:T(2,128)(2,1)}), bf16[4,2,9216]{2,1,0:T(2,128)(2,1)S(1)}, u32[]{:S(2)}, u32[]{:S(2)}) async-start(bf16[4,2,9216]{2,1,0:T(2,128)(2,1)} %reshape.581), calls=%async_computation.1 | async-start | bytes 294912 | tf_op jit(solution)/shard_map/all_to_all | solution.py:173
  24.1 64.6 %reduce-scatter.4.cloned.1.call-start = ((), (), s32[]{:S(2)}) async-start(), calls=%async_computation.3 | async-start | bytes 409600
  24.2 14.5 %copy-start.32 = (f32[8]{0:T(128)}, f32[8]{0:T(128)S(1)}, u32[]{:S(2)}) copy-start(f32[8]{0:T(128)S(1)} %compare_convert_fusion.1) | copy-start | bytes 100
  24.2 14.6 %copy-start.34 = (f32[8]{0:T(128)}, f32[8]{0:T(128)S(1)}, u32[]{:S(2)}) copy-start(f32[8]{0:T(128)S(1)} %add_multiply_fusion) | copy-start | bytes 100
  24.3 19.5 %copy-start.28 = (f32[8]{0:T(128)}, f32[8]{0:T(128)S(1)}, u32[]{:S(2)}) copy-start(f32[8]{0:T(128)S(1)} %convert_element_type.102) | copy-start | bytes 100
  25.0 1.0 copy-start.22
  25.2 9.8 %copy-start.24 = (f32[3,256]{1,0:T(4,128)S(1)}, f32[3,256]{1,0:T(4,128)}, u32[]{:S(2)}) copy-start(f32[3,256]{1,0:T(4,128)} %param.9) | copy-start | bytes 9220
  34.5 2.1 %copy-start.10 = (bf16[128,664]{1,0:T(8,128)(2,1)}, bf16[128,664]{1,0:T(8,128)(2,1)S(1)}, u32[]{:S(2)}) copy-start(bf16[128,664]{1,0:T(8,128)(2,1)S(1)} %all_gather.3) | copy-start | bytes 509956
  35.7 1.1 copy-start.17
  36.3 0.6 copy-start.19
  36.6 0.9 slice-start
  37.5 2.3 %copy-start.6 = (f32[9,8,32,128]{3,2,1,0:T(8,128)}, f32[9,8,32,128]{3,2,1,0:T(8,128)S(1)}, u32[]{:S(2)}) copy-start(f32[9,8,32,128]{3,2,1,0:T(8,128)S(1)} %multiply_dynamic-update-slice_fusion) | copy-start | bytes 3538948
  38.8 0.7 copy-start.8
  38.8 0.7 copy-start.9
  39.8 3.0 %copy-start.1 = (f32[8,8,32,128]{3,2,0,1:T(8,128)}, f32[8,8,32,128]{3,2,0,1:T(8,128)S(1)}, u32[]{:S(2)}) copy-start(f32[8,8,32,128]{3,2,0,1:T(8,128)S(1)} %fusion.17) | copy-start | bytes 3145732
  45.8 1.0 copy-start.4
  47.8 0.9 copy-start.16
  48.7 1.4 %copy-start.2 = (f32[8,8,32,128]{3,2,0,1:T(8,128)S(1)}, f32[8,8,32,128]{3,2,0,1:T(8,128)}, u32[]{:S(2)}) copy-start(f32[8,8,32,128]{3,2,0,1:T(8,128)} %copy-done.1) | copy-start | bytes 3145732
  48.7 1.6 %copy-start.7 = (f32[9,8,32,128]{3,2,1,0:T(8,128)S(1)}, f32[9,8,32,128]{3,2,1,0:T(8,128)}, u32[]{:S(2)}) copy-start(f32[9,8,32,128]{3,2,1,0:T(8,128)} %copy-done.6) | copy-start | bytes 3538948
  57.5 1.7 %copy-start.5 = (f32[2,128,9,8,32,1]{1,4,5,3,2,0:T(8,128)S(1)}, f32[2,128,9,8,32,1]{1,4,5,3,2,0:T(8,128)}, u32[]{:S(2)}) copy-start(f32[2,128,9,8,32,1]{1,4,5,3,2,0:T(8,128)} %get-tuple-element.70) | copy-start | bytes 7077892
  59.2 0.8 copy-start.23
  59.5 1.8 %copy-start.3 = (f32[8,8,32,128]{3,2,0,1:T(8,128)S(1)}, f32[8,8,32,128]{3,2,0,1:T(8,128)}, u32[]{:S(2)}) copy-start(f32[8,8,32,128]{3,2,0,1:T(8,128)} %get-tuple-element.33) | copy-start | bytes 3145732
  59.5 1.8 %copy-start.35 = (f32[8]{0:T(128)S(1)}, f32[8]{0:T(128)}, u32[]{:S(2)}) copy-start(f32[8]{0:T(128)} %copy-done.34) | copy-start | bytes 100
  59.6 4.8 %collective-permute-start.8 = (f32[128,8]{0,1:T(8,128)S(1)}, f32[128,8]{0,1:T(8,128)}, u32[]{:S(2)}, u32[]{:S(2)}) collective-permute-start(f32[128,8]{0,1:T(8,128)S(1)} %fusion.6), channel_id=1, source_target_pairs={{0,1},{1,0},{2,3},{3,2},{4,5},{5,4},{6,7},{7,6},{8,9},{9,8},{10,11... | collective-permute-start | bytes 12296 | tf_op jit(solution)/shard_map/ppermute | solution.py:19
  60.4 2.5 %copy-start.29 = (f32[8]{0:T(128)S(1)}, f32[8]{0:T(128)}, u32[]{:S(2)}) copy-start(f32[8]{0:T(128)} %copy-done.28) | copy-start | bytes 100
  60.5 2.5 %copy-start.33 = (f32[8]{0:T(128)S(1)}, f32[8]{0:T(128)}, u32[]{:S(2)}) copy-start(f32[8]{0:T(128)} %copy-done.32) | copy-start | bytes 100
  62.9 0.9 copy-start.12
  62.9 1.0 copy-start.13
  62.9 1.0 copy-start.14
  62.9 1.0 copy-start.18
  63.0 1.0 copy-start.20
  63.0 1.3 %copy-start.27 = (f32[8,5]{0,1:T(8,128)S(1)}, f32[8,5]{0,1:T(8,128)}, u32[]{:S(2)}) copy-start(f32[8,5]{0,1:T(8,128)} %copy.286) | copy-start | bytes 484
  63.0 3.8 %copy-start.26 = (f32[8,5]{0,1:T(8,128)S(1)}, f32[8,5]{0,1:T(8,128)}, u32[]{:S(2)}) copy-start(f32[8,5]{0,1:T(8,128)} %copy.294) | copy-start | bytes 484
  63.0 6.3 %copy-start.25 = (f32[640]{0:T(1024)S(1)}, f32[640]{0:T(1024)}, u32[]{:S(2)}) copy-start(f32[640]{0:T(1024)} %mul.629) | copy-start | bytes 7684
  63.0 9.9 %copy-start.30 = (s32[3,128]{1,0:T(4,128)S(1)}, s32[3,128]{1,0:T(4,128)}, u32[]{:S(2)}) copy-start(s32[3,128]{1,0:T(4,128)} %param.11) | copy-start | bytes 4612
  63.0 13.4 %copy-start.11 = (bf16[128,8,2,1,32]{0,4,2,1,3:T(8,128)(2,1)S(1)}, bf16[128,8,2,1,32]{0,4,2,1,3:T(8,128)(2,1)}, u32[]{:S(2)}) copy-start(bf16[128,8,2,1,32]{0,4,2,1,3:T(8,128)(2,1)} %get-tuple-element.52) | copy-start | bytes 393220
  65.1 3.6 %collective-permute-start.9 = (f32[128,8]{0,1:T(8,128)S(1)}, f32[128,8]{0,1:T(8,128)S(1)}, u32[]{:S(2)}, u32[]{:S(2)}) collective-permute-start(f32[128,8]{0,1:T(8,128)S(1)} %add.176), channel_id=1, source_target_pairs={{0,2},{1,3},{2,0},{3,1},{4,6},{5,7},{6,4},{7,5},{8,10},{9,11},{10,... | collective-permute-start | bytes 12296 | tf_op jit(solution)/shard_map/ppermute | solution.py:19
  68.8 3.6 %collective-permute-start.10 = (f32[32,8]{0,1:T(8,128)S(1)}, f32[32,8]{0,1:T(8,128)S(1)}, u32[]{:S(2)}, u32[]{:S(2)}) collective-permute-start(f32[32,8]{0,1:T(8,128)S(1)} %constant_dynamic-slice_fusion), channel_id=1, source_target_pairs={{0,4},{4,0},{8,12},{12,8},{16,20},{20,16},{24,28},{28,24},{1,5},{5... | collective-permute-start | bytes 3080 | tf_op jit(solution)/shard_map/ppermute | solution.py:19
  69.3 3.6 %collective-permute-start.3 = (f32[3,640]{1,0:T(4,128)S(1)}, f32[3,640]{1,0:T(4,128)S(1)}, u32[]{:S(2)}, u32[]{:S(2)}) collective-permute-start(f32[3,640]{1,0:T(4,128)S(1)} %bitcast_add_fusion.2), channel_id=1, source_target_pairs={{0,1},{1,0},{2,3},{3,2},{4,5},{5,4},{6,7},{7,6},{8,9},{9,8},{10,11... | collective-permute-start | bytes 23048 | tf_op jit(solution)/shard_map/ppermute | solution.py:19
  72.5 3.6 %collective-permute-start.11 = (f32[32,8]{0,1:T(8,128)S(1)}, f32[32,8]{0,1:T(8,128)S(1)}, u32[]{:S(2)}, u32[]{:S(2)}) collective-permute-start(f32[32,8]{0,1:T(8,128)S(1)} %fusion.109), channel_id=1, source_target_pairs={{0,8},{4,12},{8,0},{12,4},{16,24},{20,28},{24,16},{28,20},{1,9},{5... | collective-permute-start | bytes 3080 | tf_op jit(solution)/shard_map/ppermute | solution.py:19
  73.0 9.5 %collective-permute-start.4 = (f32[3,640]{1,0:T(4,128)S(1)}, f32[3,640]{1,0:T(4,128)S(1)}, u32[]{:S(2)}, u32[]{:S(2)}) collective-permute-start(f32[3,640]{1,0:T(4,128)S(1)} %add.172), channel_id=1, source_target_pairs={{0,2},{1,3},{2,0},{3,1},{4,6},{5,7},{6,4},{7,5},{8,10},{9,11},{10,... | collective-permute-start | bytes 23048 | tf_op jit(solution)/shard_map/ppermute | solution.py:19
  76.1 5.8 %collective-permute-start.12 = (f32[32,8]{0,1:T(8,128)S(1)}, f32[32,8]{0,1:T(8,128)S(1)}, u32[]{:S(2)}, u32[]{:S(2)}) collective-permute-start(f32[32,8]{0,1:T(8,128)S(1)} %add.179), channel_id=1, source_target_pairs={{0,16},{4,20},{8,24},{12,28},{16,0},{20,4},{24,8},{28,12},{1,17},{... | collective-permute-start | bytes 3080 | tf_op jit(solution)/shard_map/ppermute | solution.py:19
  78.5 8.1 %all-to-all-start = ((bf16[4,2,9216]{2,1,0:T(2,128)(2,1)}), bf16[4,2,9216]{2,1,0:T(2,128)(2,1)S(1)}, u32[]{:S(2)}, u32[]{:S(2)}) async-start(bf16[4,2,9216]{2,1,0:T(2,128)(2,1)} %reshape.579), calls=%async_computation | async-start | bytes 294912 | tf_op jit(solution)/shard_map/all_to_all | solution.py:166
  89.5 4.6 %collective-permute-start.5 = (f32[35,128]{1,0:T(8,128)S(1)}, f32[35,128]{1,0:T(8,128)S(1)}, u32[]{:S(2)}, u32[]{:S(2)}) collective-permute-start(f32[35,128]{1,0:T(8,128)S(1)} %pad_maximum_fusion.3), channel_id=1, source_target_pairs={{0,4},{4,0},{8,12},{12,8},{16,20},{20,16},{24,28},{28,24},{1,5},{5... | collective-permute-start | bytes 53768 | tf_op jit(solution)/shard_map/ppermute | solution.py:19
  90.1 4.0 %collective-permute-start.6 = (f32[35,128]{1,0:T(8,128)S(1)}, f32[35,128]{1,0:T(8,128)S(1)}, u32[]{:S(2)}, u32[]{:S(2)}) collective-permute-start(f32[35,128]{1,0:T(8,128)S(1)} %pad_maximum_fusion.4), channel_id=1, source_target_pairs={{0,8},{4,12},{8,0},{12,4},{16,24},{20,28},{24,16},{28,20},{1,9},{5... | collective-permute-start | bytes 53768 | tf_op jit(solution)/shard_map/ppermute | solution.py:19
  90.3 4.7 %collective-permute-start.7 = (f32[35,128]{1,0:T(8,128)S(1)}, f32[35,128]{1,0:T(8,128)S(1)}, u32[]{:S(2)}, u32[]{:S(2)}) collective-permute-start(f32[35,128]{1,0:T(8,128)S(1)} %pad_maximum_fusion.5), channel_id=1, source_target_pairs={{0,16},{4,20},{8,24},{12,28},{16,0},{20,4},{24,8},{28,12},{1,17},{... | collective-permute-start | bytes 53768 | tf_op jit(solution)/shard_map/ppermute | solution.py:19
Sparse Core Ops, SparseCore 0:
  61.5 17.9 reduce-scatter.3

commit v9 on v8

--- a/solution.py
+++ b/solution.py
@@ -28,6 +28,33 @@
         give = lax.dynamic_slice_in_dim(value, (1 - mine) * half, half, 0)
         value = keep + partner(give, axis, bit)
     return value
+
+
+def as_rows(value, width):
+    flat = value.reshape(-1)
+    count = -(-flat.shape[0] // width)
+    return jnp.pad(flat, (0, count * width - flat.shape[0])).reshape(count, width)
+
+
+def halving_with(value, extras, axis):
+    index = lax.axis_index(axis)
+    width = value.shape[1]
+    extra_rows = as_rows(jnp.concatenate([extra.reshape(-1) for extra in extras]), width)
+    for bit in reversed(range(lax.axis_size(axis).bit_length() - 1)):
+        half = value.shape[0] // 2
+        mine = (index >> bit) & 1
+        keep = lax.dynamic_slice_in_dim(value, mine * half, half, 0)
+        give = lax.dynamic_slice_in_dim(value, (1 - mine) * half, half, 0)
+        got = partner(jnp.concatenate([give, extra_rows], axis=0), axis, bit)
+        value = keep + got[:half]
+        extra_rows = extra_rows + got[half:]
+    flat = extra_rows.reshape(-1)
+    sums = []
+    start = 0
+    for extra in extras:
+        sums.append(flat[start : start + extra.size].reshape(extra.shape))
+        start += extra.size
+    return value, sums
 
 
 def geometry(target_pos, source_pos, pair_keep, radial_count):
@@ -214,22 +241,26 @@
             3, src_blocks, chan_count, rows
         )
     ).reshape(3, src_atoms)
-    grad_src = lax.psum_scatter(grad_part, "chan", scatter_dimension=0, tiled=True)
-    for chan_bit in range(chan_count.bit_length() - 1):
-        other_pos, other_rad = partner((dpos_src, grad_rad), "chan", chan_bit)
-        dpos_src = dpos_src + other_pos
-        grad_rad = grad_rad + other_rad
+    grad_src, (dpos_src, grad_rad) = halving_with(grad_part, (dpos_src, grad_rad), "chan")
     grad_rad = lax.dynamic_slice_in_dim(grad_rad, offset, chan_dev, 0)
     own_both = jnp.concatenate([grad_src[:, :atoms_dev], dpos_src[:, :atoms_dev]], axis=0)
+    ghost_rows = chan_dev + 3
     back_list = []
     for level_bit in range(levels):
         low = atoms_dev + level_bit * block_size
         ghost_both = jnp.concatenate(
-            [grad_src[:, low : low + block_size], dpos_src[:, low : low + block_size]], axis=0
-        )
-        back_both, other_rad = partner((ghost_both, grad_rad), "space", level_bit)
-        grad_rad = grad_rad + other_rad
-        back_list.append(back_both)
+            [
+                grad_src[:, low : low + block_size],
+                dpos_src[:, low : low + block_size],
+                as_rows(grad_rad, block_size),
+            ],
+            axis=0,
+        )
+        back_both = partner(ghost_both, "space", level_bit)
+        grad_rad = grad_rad + back_both[ghost_rows:].reshape(-1)[: grad_rad.size].reshape(
+            grad_rad.shape
+        )
+        back_list.append(back_both[:ghost_rows])
     all_rows = send_rows[:levels].reshape(-1)
     own_both = own_both.at[:, all_rows].add(jnp.concatenate(back_list, axis=1))
     own_grad = own_both[:chan_dev]

time: 107 us -> 94.1 us (0.88)
  between operations: 15 us -> 1.53 us
  waiting for transfers between devices: 11 us -> 18.1 us
  starting transfers between devices: 22.8 us -> 17.2 us
  local copies, waits for them, and re-layouts: 24.1 us -> 22.5 us
    ppermute x13 -> x8, waiting for transfers between devices: 6.96 us -> 14.2 us  [partner(): return lax.ppermute(value, axis, pairs)]
    ppermute x13 -> x8, starting transfers between devices: 16.1 us -> 10.5 us  [partner(): return lax.ppermute(value, axis, pairs)]
    reduce_sum x1, other arithmetic: 0.3 us -> 2.23 us  [body(): jnp.sum(source_hot[:, None, :, None] * grad_source[:, :, None, :], axis=0)]
    unnamed x89 -> x60, local copies, waits for them, and re-layouts: 7.81 us -> 7.55 us
  transfers between devices with their start and end apart: 16 -> 10, of which waited for: 5 -> 4; matrix products, arithmetic and copies ran while one was open for 24% -> 18% of each run, Pallas kernels for 0% -> 0%
where the time goes in v9:
time: 94.1 us; the launch traced here: 93.4 us
  local copies, waits for them, and re-layouts  22.5 us (24%)
  other arithmetic  19.6 us (21%)
  waiting for transfers between devices  18.1 us (19%)
  starting transfers between devices  17.2 us (18%)
  matrix products  8.5 us (9%)
  blocking collectives  6.05 us (6%)
  between operations  1.53 us (2%)
    ppermute x8, waiting for transfers between devices, partner(): return lax.ppermute(value, axis, pairs)  14.2 us
    ppermute x8, starting transfers between devices, partner(): return lax.ppermute(value, axis, pairs)  10.5 us
    unnamed x60, local copies, waits for them, and re-layouts  7.55 us
    all_gather x1, blocking collectives, body(): lax.all_gather(jnp.concatenate([src_feat, weight_high, weight_mid, weight...  6.05 us
    all_to_all x1, waiting for transfers between devices, body(): lax.all_to_all(result_rows.reshape(all_chan, components, own_blocks, 1, r...  3.86 us
    reduce_sum x1, other arithmetic, body(): harm_grad = jnp.sum(value_grad * radial[None], axis=1)  3.81 us
    all_to_all x1, starting transfers between devices, body(): lax.all_to_all(out_grad.reshape(chan_dev, components, own_blocks, chan_co...  3.34 us
    all_to_all x1, starting transfers between devices, body(): lax.all_to_all(result_rows.reshape(all_chan, components, own_blocks, 1, r...  3.34 us
  transfers between devices with their start and end apart: 10, of which 4 were waited for; matrix products, arithmetic and copies ran while one was open for 18% of the time, Pallas kernels for 0%

profile of v9, /device:TPU:0, one launch (start us, length us, event | category | flops | bytes accessed | tf_op | source)
XLA Modules:
  0.0 93.4 jit_solution(9609816358222938226)
XLA Ops:
  0.7 0.8 slice_bitcast_fusion.2
  1.4 0.7 convert_element_type.97
  2.1 0.7 pad_maximum_fusion.4
  2.9 0.7 pad_clamp_fusion.3
  3.6 1.1 %gather_fusion = f32[384,35]{1,0:T(8,128)S(1)} fusion(f32[35,256]{0,1:T(8,128)S(1)} %copy.232, s32[1024]{0:T(1024)S(1)} %get-tuple-element.69), kind=kCustom, calls=%fused_computation | custom fusion | bytes 109056 | tf_op jit(solution)/shard_map/jit(_take)/gather | solution.py:113
  4.8 3.0 %collective-permute-start = (f32[35,128]{0,1:T(8,128)S(1)}, f32[35,128]{0,1:T(8,128)S(1)}, u32[]{:S(2)}, u32[]{:S(2)}) collective-permute-start(f32[35,128]{0,1:T(8,128)S(1)} %get-tuple-element.45), channel_id=1, source_target_pairs={{0,4},{4,0},{8,12},{12,8},{16,20},{20,16},{24,28},{28,24},{1,5},{5... | collective-permute-start | bytes 53768 | tf_op jit(solution)/shard_map/ppermute | solution.py:19
  7.8 1.6 %collective-permute-start.1 = (f32[35,128]{0,1:T(8,128)S(1)}, f32[35,128]{0,1:T(8,128)S(1)}, u32[]{:S(2)}, u32[]{:S(2)}) collective-permute-start(f32[35,128]{0,1:T(8,128)S(1)} %get-tuple-element.46), channel_id=1, source_target_pairs={{0,8},{4,12},{8,0},{12,4},{16,24},{20,28},{24,16},{28,20},{1,9},{5... | collective-permute-start | bytes 53768 | tf_op jit(solution)/shard_map/ppermute | solution.py:19
  9.4 2.6 %collective-permute-start.2 = (f32[35,128]{0,1:T(8,128)S(1)}, f32[35,128]{0,1:T(8,128)S(1)}, u32[]{:S(2)}, u32[]{:S(2)}) collective-permute-start(f32[35,128]{0,1:T(8,128)S(1)} %get-tuple-element.47), channel_id=1, source_target_pairs={{0,16},{4,20},{8,24},{12,28},{16,0},{20,4},{24,8},{28,12},{1,17},{... | collective-permute-start | bytes 53768 | tf_op jit(solution)/shard_map/ppermute | solution.py:19
  12.0 0.2 reshape.531
  12.3 0.7 copy.255
  13.0 1.2 %reshape.612 = bf16[4,2,9216]{2,1,0:T(2,128)(2,1)} reshape(bf16[4,9,2,32,32]{4,3,2,1,0:T(8,128)(2,1)S(1)} %bitcast.379) | data formatting | bytes 294912
  14.2 3.3 %all-to-all-start.1 = ((bf16[4,2,9216]{2,1,0:T(2,128)(2,1)}), bf16[4,2,9216]{2,1,0:T(2,128)(2,1)S(1)}, u32[]{:S(2)}, u32[]{:S(2)}) async-start(bf16[4,2,9216]{2,1,0:T(2,128)(2,1)} %reshape.612), calls=%async_computation.1 | async-start | bytes 294912 | tf_op jit(solution)/shard_map/all_to_all | solution.py:200
  17.6 0.5 compare_convert_fusion
  18.8 0.6 gather_fusion.4
  19.9 6.1 %all_gather.3 = bf16[128,664]{1,0:T(8,128)(2,1)S(1)} all-gather(bf16[32,664]{1,0:T(8,128)(2,1)S(1)} %concatenate.53), channel_id=1, replica_groups=mesh['space'=8,'chan'=4] {'chan'}, dimensions={0}, use_global_device_ids=true | all-gather | bytes 212480 | tf_op jit(solution)/shard_map/all_gather | solution.py:134
  26.5 0.6 gather_fusion.2
  27.1 0.6 gather_fusion.3
  27.9 0.2 copy.241
  28.2 0.6 gather_fusion.1
  29.7 0.8 copy-done.8
  30.5 0.3 fusion.17
  30.8 3.0 %fusion.7 = (bf16[128,2,9,32]{0,3,2,1:T(8,128)(2,1)S(1)}, f32[2,128,9,8,32,1]{1,4,5,3,2,0:T(8,128)}) fusion(f32[128,8]{0,1:T(8,128)S(1)} %copy.309, f32[8,128,128]{2,1,0:T(8,128)S(1)} %convert_element_type.105, f32[8,2]{0,1:T(2,128)S(1)} %copy.239, f32[8,8,32,128]{3,2,0,1:T(8,128)S(1)} %fusion.17, f32[9,8,32,128]{3,2,1,0:T(8,128)S(1)} %multiply_dynamic-update-slice_fusion), kind=kOutput, calls=%fused_computation.21 | convolution fusion | flops 1214308352 | bytes 5263424 | tf_op jit(solution)/shard_map/lktij,tbcj->bclki/dot_general | solution.py:177
  33.8 1.1 %convolution_bitcast_fusion = f32[128,9,2,32]{0,3,2,1:T(8,128)} fusion(bf16[9,128,128]{2,1,0:T(8,128)(2,1)S(1)} %gather_fusion.4, bf16[128,2,9,32]{0,3,2,1:T(8,128)(2,1)S(1)} %get-tuple-element.65), kind=kOutput, calls=%fused_computation.26 | convolution fusion | flops 18874368 | bytes 737280 | tf_op jit(solution)/shard_map/lxc,clbi->xlbi/dot_general | solution.py:184
  34.9 0.3 reshape.613
  35.3 0.8 copy.256
  36.2 0.5 reshape.539
  36.7 0.4 copy-done.4
  37.2 0.7 multiply_convert_fusion.3
  37.9 0.2 fusion.26
  38.2 0.6 gather_fusion.5
  38.8 1.4 %multiply_convert_fusion = bf16[8,128,9,8,32]{1,4,3,2,0:T(8,128)(2,1)S(1)} fusion(f32[8,128,9,32]{1,3,2,0:T(8,128)S(1)} %gather_fusion.5, f32[8,128,8]{1,2,0:T(8,128)S(1)} %broadcast_multiply_fusion), kind=kLoop, calls=%fused_computation.9 | loop fusion | flops 4718592 | bytes 5931008 | tf_op jit(solution)/shard_map/convert_element_type | solution.py:223
  40.2 0.2 copy-done.7
  40.4 2.9 %fusion.8 = f32[8,128,128]{2,1,0:T(8,128)} fusion(bf16[8,128,9,8,32]{1,4,3,2,0:T(8,128)(2,1)S(1)} %multiply_convert_fusion, f32[8,8,32,128]{3,2,0,1:T(8,128)S(1)} %copy-done.2, f32[9,8,32,128]{3,2,1,0:T(8,128)S(1)} %copy-done.7), kind=kOutput, calls=%fused_computation.24 | convolution fusion | flops 608698368 | bytes 7471104 | tf_op jit(solution)/shard_map/tclki,lktij->tcj/dot_general | solution.py:224
  43.3 1.4 %fusion.106 = f32[8,128,2304]{1,2,0:S(1)} fusion(bf16[8,128,2304]{1,2,0:T(8,128)(2,1)S(1)} %bitcast.376, bf16[8,128,128]{2,1,0:T(8,128)(2,1)S(1)} %gather_fusion.1), kind=kOutput, calls=%fused_computation.228 | convolution fusion | flops 603979776 | bytes 14417920
  44.6 3.8 %multiply_reduce_fusion.1 = (f32[9,8,32,128]{3,2,0,1:T(8,128)S(1)}, f32[8,8,32,128]{3,2,0,1:T(8,128)}) fusion(f32[9,8,8,32,128]{4,3,1,0,2:T(8,128)S(1)} %bitcast.375, f32[8,8,32,128]{3,2,0,1:T(8,128)S(1)} %copy-done.2, f32[9,8,32,128]{3,2,1,0:T(8,128)S(1)} %copy-done.7), kind=kLoop, calls=%fused_computation.8 | loop fusion | flops 8880128 | bytes 13893632 | tf_op jit(solution)/shard_map/reduce_sum | solution.py:230
  48.5 0.8 fusion.39
  49.2 0.9 fusion.72
  50.2 0.3 fusion.6
  50.7 2.2 %multiply_reduce_fusion.2 = f32[128,5,128]{2,0,1:T(8,128)} fusion(f32[8,128,128]{2,1,0:T(8,128)} %fusion.8, f32[8,5]{1,0:T(8,128)S(1)} %get-tuple-element.61), kind=kLoop, calls=%fused_computation.17 | loop fusion | flops 1228800 | bytes 852128 | tf_op jit(solution)/shard_map/reduce_sum | solution.py:233
  52.9 1.1 %copy.259 = f32[128,5,128]{0,2,1:T(8,128)S(1)} copy(f32[128,5,128]{2,0,1:T(8,128)} %multiply_reduce_fusion.2) | data formatting | bytes 655360 | tf_op jit(solution)/shard_map/reduce_sum | solution.py:233
  54.1 0.5 fusion.18
  54.7 0.3 fusion.51
  55.0 0.5 copy-done.13
  55.7 0.3 fusion.84
  56.4 0.2 copy.269
  56.9 1.8 %collective-permute-start.3 = (f32[69,640]{0,1:T(8,128)S(1)}, f32[69,640]{0,1:T(8,128)S(1)}, u32[]{:S(2)}, u32[]{:S(2)}) collective-permute-start(f32[69,640]{0,1:T(8,128)S(1)} %pad_maximum_fusion), channel_id=1, source_target_pairs={{0,2},{1,3},{2,0},{3,1},{4,6},{5,7},{6,4},{7,5},{8,10},{9,11},{10,... | collective-permute-start | bytes 529928 | tf_op jit(solution)/shard_map/ppermute | solution.py:19
  58.7 8.2 %collective-permute-done.3 = f32[69,640]{0,1:T(8,128)S(1)} collective-permute-done((f32[69,640]{0,1:T(8,128)S(1)}, f32[69,640]{0,1:T(8,128)S(1)}, u32[]{:S(2)}, u32[]{:S(2)}) %collective-permute-start.3) | collective-permute-done | bytes 176672 | tf_op jit(solution)/shard_map/ppermute | solution.py:19
  67.6 1.6 %collective-permute-done.4 = f32[37,640]{0,1:T(8,128)S(1)} collective-permute-done((f32[37,640]{0,1:T(8,128)S(1)}, f32[37,640]{0,1:T(8,128)S(1)}, u32[]{:S(2)}, u32[]{:S(2)}) %collective-permute-start.4) | collective-permute-done | bytes 94752 | tf_op jit(solution)/shard_map/ppermute | solution.py:19
  69.6 0.2 slice_add_fusion.1
  70.2 0.6 collective-permute-start.5
  70.8 0.8 copy.252
  71.6 1.2 %reshape.610 = bf16[4,2,9216]{2,1,0:T(2,128)(2,1)} reshape(bf16[128,1,9,2,32]{4,3,2,1,0:T(2,128)(2,1)S(1)} %bitcast.380) | data formatting | bytes 294912
  72.9 3.3 %all-to-all-start = ((bf16[4,2,9216]{2,1,0:T(2,128)(2,1)}), bf16[4,2,9216]{2,1,0:T(2,128)(2,1)S(1)}, u32[]{:S(2)}, u32[]{:S(2)}) async-start(bf16[4,2,9216]{2,1,0:T(2,128)(2,1)} %reshape.610), calls=%async_computation | async-start | bytes 294912 | tf_op jit(solution)/shard_map/all_to_all | solution.py:193
  76.6 0.5 collective-permute-start.6
  77.1 3.9 %all-to-all-done = bf16[4,2,9216]{2,1,0:T(2,128)(2,1)S(1)} async-done(((bf16[4,2,9216]{2,1,0:T(2,128)(2,1)}), bf16[4,2,9216]{2,1,0:T(2,128)(2,1)S(1)}, u32[]{:S(2)}, u32[]{:S(2)}) %all-to-all-start) | async-done | bytes 147488 | tf_op jit(solution)/shard_map/all_to_all | solution.py:193
  81.0 0.3 reshape.611
  81.3 0.8 copy.253
  82.0 1.1 %reshape.530 = bf16[32,9,256]{2,0,1:T(8,128)(2,1)} reshape(bf16[32,9,2,4,1,32]{5,3,2,0,1,4:T(4,128)(2,1)S(1)} %copy.253) | data formatting | bytes 294912 | tf_op jit(solution)/shard_map/reshape | solution.py:199
  83.5 0.4 collective-permute-start.7
  84.0 4.3 %collective-permute-done.7 = f32[37,128]{1,0:T(8,128)S(1)} collective-permute-done((f32[37,128]{1,0:T(8,128)S(1)}, f32[37,128]{1,0:T(8,128)S(1)}, u32[]{:S(2)}, u32[]{:S(2)}) %collective-permute-start.7) | collective-permute-done | bytes 18976 | tf_op jit(solution)/shard_map/ppermute | solution.py:19
  88.5 2.7 %scatter_fusion = f32[35,256]{0,1:T(8,128)S(1)} fusion(f32[35,256]{0,1:T(8,128)S(1)} %pad_maximum_fusion.3, s32[384]{0:T(512)S(1)} %fusion.100, f32[384,35]{1,0:T(8,128)S(1)} %copy.278), kind=kCustom, calls=%fused_computation.6 | custom fusion | flops 13440 | bytes 162816 | tf_op jit(solution)/shard_map/scatter-add | solution.py:265
  91.4 0.7 copy.281
  92.1 0.7 copy.279
  92.8 0.7 copy.280
  (161 shorter events, 7.0 us)
Async XLA Ops:
  0.6 18.2 %copy-start = (bf16[3,128,128]{2,1,0:T(8,128)(2,1)S(1)}, bf16[3,128,128]{2,1,0:T(8,128)(2,1)}, u32[]{:S(2)}) copy-start(bf16[3,128,128]{2,1,0:T(8,128)(2,1)} %param.15) | copy-start | bytes 294916
  0.6 11.3 %copy-start.16 = (bf16[32,9,256]{2,0,1:T(8,128)(2,1)S(1)}, bf16[32,9,256]{2,0,1:T(8,128)(2,1)}, u32[]{:S(2)}) copy-start(bf16[32,9,256]{2,0,1:T(8,128)(2,1)} %param.16) | copy-start | bytes 442372
  4.8 14.7 %collective-permute-start = (f32[35,128]{0,1:T(8,128)S(1)}, f32[35,128]{0,1:T(8,128)S(1)}, u32[]{:S(2)}, u32[]{:S(2)}) collective-permute-start(f32[35,128]{0,1:T(8,128)S(1)} %get-tuple-element.45), channel_id=1, source_target_pairs={{0,4},{4,0},{8,12},{12,8},{16,20},{20,16},{24,28},{28,24},{1,5},{5... | collective-permute-start | bytes 53768 | tf_op jit(solution)/shard_map/ppermute | solution.py:19
  7.8 11.7 %collective-permute-start.1 = (f32[35,128]{0,1:T(8,128)S(1)}, f32[35,128]{0,1:T(8,128)S(1)}, u32[]{:S(2)}, u32[]{:S(2)}) collective-permute-start(f32[35,128]{0,1:T(8,128)S(1)} %get-tuple-element.46), channel_id=1, source_target_pairs={{0,8},{4,12},{8,0},{12,4},{16,24},{20,28},{24,16},{28,20},{1,9},{5... | collective-permute-start | bytes 53768 | tf_op jit(solution)/shard_map/ppermute | solution.py:19
  9.4 10.3 %collective-permute-start.2 = (f32[35,128]{0,1:T(8,128)S(1)}, f32[35,128]{0,1:T(8,128)S(1)}, u32[]{:S(2)}, u32[]{:S(2)}) collective-permute-start(f32[35,128]{0,1:T(8,128)S(1)} %get-tuple-element.47), channel_id=1, source_target_pairs={{0,16},{4,20},{8,24},{12,28},{16,0},{20,4},{24,8},{28,12},{1,17},{... | collective-permute-start | bytes 53768 | tf_op jit(solution)/shard_map/ppermute | solution.py:19
  12.2 5.3 %copy-start.21 = (s32[8,2]{0,1:T(2,128)S(1)}, s32[8,2]{0,1:T(2,128)}, u32[]{:S(2)}) copy-start(s32[8,2]{0,1:T(2,128)} %param.12) | copy-start | bytes 196
  12.2 5.9 %copy-start.24 = (s32[8]{0:T(128)S(1)}, s32[8]{0:T(128)}, u32[]{:S(2)}) copy-start(s32[8]{0:T(128)} %param.13) | copy-start | bytes 100
  12.3 5.9 %copy-start.20 = (f32[32,8]{0,1:T(8,128)S(1)}, f32[32,8]{0,1:T(8,128)}, u32[]{:S(2)}) copy-start(f32[32,8]{0,1:T(8,128)} %param.14) | copy-start | bytes 3076
  12.3 6.0 %copy-start.23 = (s32[9]{0:T(128)S(1)}, s32[9]{0:T(128)}, u32[]{:S(2)}) copy-start(s32[9]{0:T(128)} %constant.86) | copy-start | bytes 112
  13.0 6.8 %copy-start.17 = (bf16[32,256]{1,0:T(8,128)(2,1)S(1)}, bf16[32,256]{1,0:T(8,128)(2,1)}, u32[]{:S(2)}) copy-start(bf16[32,256]{1,0:T(8,128)(2,1)} %param.10) | copy-start | bytes 49156
  14.2 20.7 %all-to-all-start.1 = ((bf16[4,2,9216]{2,1,0:T(2,128)(2,1)}), bf16[4,2,9216]{2,1,0:T(2,128)(2,1)S(1)}, u32[]{:S(2)}, u32[]{:S(2)}) async-start(bf16[4,2,9216]{2,1,0:T(2,128)(2,1)} %reshape.612), calls=%async_computation.1 | async-start | bytes 294912 | tf_op jit(solution)/shard_map/all_to_all | solution.py:200
  18.3 8.1 %copy-start.18 = (f32[3,256]{1,0:T(4,128)S(1)}, f32[3,256]{1,0:T(4,128)}, u32[]{:S(2)}) copy-start(f32[3,256]{1,0:T(4,128)} %param.9) | copy-start | bytes 9220
  29.5 4.2 %copy-start.6 = (f32[9,8,32,128]{3,2,1,0:T(8,128)}, f32[9,8,32,128]{3,2,1,0:T(8,128)S(1)}, u32[]{:S(2)}) copy-start(f32[9,8,32,128]{3,2,1,0:T(8,128)S(1)} %multiply_dynamic-update-slice_fusion) | copy-start | bytes 3538948
  29.6 0.8 copy-start.8
  29.6 0.8 copy-start.10
  30.8 3.0 %copy-start.1 = (f32[8,8,32,128]{3,2,0,1:T(8,128)}, f32[8,8,32,128]{3,2,0,1:T(8,128)S(1)}, u32[]{:S(2)}) copy-start(f32[8,8,32,128]{3,2,0,1:T(8,128)S(1)} %fusion.17) | copy-start | bytes 3145732
  36.2 1.0 %copy-start.4 = (f32[128,9,2,32]{0,3,2,1:T(8,128)S(1)}, f32[128,9,2,32]{0,3,2,1:T(8,128)}, u32[]{:S(2)}) copy-start(f32[128,9,2,32]{0,3,2,1:T(8,128)} %convolution_bitcast_fusion) | copy-start | bytes 884740
  38.8 1.4 %copy-start.2 = (f32[8,8,32,128]{3,2,0,1:T(8,128)S(1)}, f32[8,8,32,128]{3,2,0,1:T(8,128)}, u32[]{:S(2)}) copy-start(f32[8,8,32,128]{3,2,0,1:T(8,128)} %copy-done.1) | copy-start | bytes 3145732
  38.8 1.6 %copy-start.7 = (f32[9,8,32,128]{3,2,1,0:T(8,128)S(1)}, f32[9,8,32,128]{3,2,1,0:T(8,128)}, u32[]{:S(2)}) copy-start(f32[9,8,32,128]{3,2,1,0:T(8,128)} %copy-done.6) | copy-start | bytes 3538948
  48.5 1.7 %copy-start.5 = (f32[2,128,9,8,32,1]{1,4,5,3,2,0:T(8,128)S(1)}, f32[2,128,9,8,32,1]{1,4,5,3,2,0:T(8,128)}, u32[]{:S(2)}) copy-start(f32[2,128,9,8,32,1]{1,4,5,3,2,0:T(8,128)} %get-tuple-element.66) | copy-start | bytes 7077892
  50.5 3.6 %copy-start.3 = (f32[8,8,32,128]{3,2,0,1:T(8,128)S(1)}, f32[8,8,32,128]{3,2,0,1:T(8,128)}, u32[]{:S(2)}) copy-start(f32[8,8,32,128]{3,2,0,1:T(8,128)} %get-tuple-element.29) | copy-start | bytes 3145732
  50.5 3.6 %copy-start.9 = (f32[8,32,128]{2,1,0:T(8,128)S(1)}, f32[8,32,128]{2,1,0:T(8,128)}, u32[]{:S(2)}) copy-start(f32[8,32,128]{2,1,0:T(8,128)} %copy-done.8) | copy-start | bytes 393220
  50.5 3.6 %copy-start.11 = (f32[8,32,128]{2,1,0:T(8,128)S(1)}, f32[8,32,128]{2,1,0:T(8,128)}, u32[]{:S(2)}) copy-start(f32[8,32,128]{2,1,0:T(8,128)} %copy-done.10) | copy-start | bytes 393220
  54.6 0.9 copy-start.13
  54.6 1.0 %copy-start.14 = (f32[8,1,32,128]{3,2,0,1:T(8,128)S(1)}, f32[8,1,32,128]{3,2,0,1:T(8,128)}, u32[]{:S(2)}) copy-start(f32[8,1,32,128]{3,2,0,1:T(8,128)} %get-tuple-element.34) | copy-start | bytes 393220
  54.6 1.0 %copy-start.15 = (f32[8,1,32,128]{3,2,0,1:T(8,128)S(1)}, f32[8,1,32,128]{3,2,0,1:T(8,128)}, u32[]{:S(2)}) copy-start(f32[8,1,32,128]{3,2,0,1:T(8,128)} %get-tuple-element.35) | copy-start | bytes 393220
  54.6 1.5 %copy-start.22 = (f32[4]{0:T(128)S(1)}, f32[4]{0:T(128)}, u32[]{:S(2)}) copy-start(f32[4]{0:T(128)} %compare_convert_fusion) | copy-start | bytes 52
  56.9 10.0 %collective-permute-start.3 = (f32[69,640]{0,1:T(8,128)S(1)}, f32[69,640]{0,1:T(8,128)S(1)}, u32[]{:S(2)}, u32[]{:S(2)}) collective-permute-start(f32[69,640]{0,1:T(8,128)S(1)} %pad_maximum_fusion), channel_id=1, source_target_pairs={{0,2},{1,3},{2,0},{3,1},{4,6},{5,7},{6,4},{7,5},{8,10},{9,11},{10,... | collective-permute-start | bytes 529928 | tf_op jit(solution)/shard_map/ppermute | solution.py:19
  67.5 1.7 %collective-permute-start.4 = (f32[37,640]{0,1:T(8,128)S(1)}, f32[37,640]{0,1:T(8,128)S(1)}, u32[]{:S(2)}, u32[]{:S(2)}) collective-permute-start(f32[37,640]{0,1:T(8,128)S(1)} %pad_maximum_fusion.1), channel_id=1, source_target_pairs={{0,1},{1,0},{2,3},{3,2},{4,5},{5,4},{6,7},{7,6},{8,9},{9,8},{10,11... | collective-permute-start | bytes 284168 | tf_op jit(solution)/shard_map/ppermute | solution.py:19
  69.5 1.3 %copy-start.12 = (bf16[128,8,2,1,32]{0,4,2,1,3:T(8,128)(2,1)S(1)}, bf16[128,8,2,1,32]{0,4,2,1,3:T(8,128)(2,1)}, u32[]{:S(2)}) copy-start(bf16[128,8,2,1,32]{0,4,2,1,3:T(8,128)(2,1)} %get-tuple-element.51) | copy-start | bytes 393220
  70.2 6.9 %copy-start.19 = (s32[3,128]{1,0:T(4,128)S(1)}, s32[3,128]{1,0:T(4,128)}, u32[]{:S(2)}) copy-start(s32[3,128]{1,0:T(4,128)} %param.11) | copy-start | bytes 4612
  70.2 6.1 %collective-permute-start.5 = (f32[37,128]{1,0:T(8,128)S(1)}, f32[37,128]{1,0:T(8,128)S(1)}, u32[]{:S(2)}, u32[]{:S(2)}) collective-permute-start(f32[37,128]{1,0:T(8,128)S(1)} %pad_maximum_fusion.5), channel_id=1, source_target_pairs={{0,4},{4,0},{8,12},{12,8},{16,20},{20,16},{24,28},{28,24},{1,5},{5... | collective-permute-start | bytes 56840 | tf_op jit(solution)/shard_map/ppermute | solution.py:19
  72.9 8.1 %all-to-all-start = ((bf16[4,2,9216]{2,1,0:T(2,128)(2,1)}), bf16[4,2,9216]{2,1,0:T(2,128)(2,1)S(1)}, u32[]{:S(2)}, u32[]{:S(2)}) async-start(bf16[4,2,9216]{2,1,0:T(2,128)(2,1)} %reshape.610), calls=%async_computation | async-start | bytes 294912 | tf_op jit(solution)/shard_map/all_to_all | solution.py:193
  76.6 6.7 %collective-permute-start.6 = (f32[37,128]{1,0:T(8,128)S(1)}, f32[37,128]{1,0:T(8,128)S(1)}, u32[]{:S(2)}, u32[]{:S(2)}) collective-permute-start(f32[37,128]{1,0:T(8,128)S(1)} %pad_maximum_fusion.6), channel_id=1, source_target_pairs={{0,8},{4,12},{8,0},{12,4},{16,24},{20,28},{24,16},{28,20},{1,9},{5... | collective-permute-start | bytes 56840 | tf_op jit(solution)/shard_map/ppermute | solution.py:19
  83.5 4.9 %collective-permute-start.7 = (f32[37,128]{1,0:T(8,128)S(1)}, f32[37,128]{1,0:T(8,128)S(1)}, u32[]{:S(2)}, u32[]{:S(2)}) collective-permute-start(f32[37,128]{1,0:T(8,128)S(1)} %pad_maximum_fusion.7), channel_id=1, source_target_pairs={{0,16},{4,20},{8,24},{12,28},{16,0},{20,4},{24,8},{28,12},{1,17},{... | collective-permute-start | bytes 56840 | tf_op jit(solution)/shard_map/ppermute | solution.py:19

commit v10 on v9

--- a/solution.py
+++ b/solution.py
@@ -40,11 +40,14 @@
     index = lax.axis_index(axis)
     width = value.shape[1]
     extra_rows = as_rows(jnp.concatenate([extra.reshape(-1) for extra in extras]), width)
-    for bit in reversed(range(lax.axis_size(axis).bit_length() - 1)):
-        half = value.shape[0] // 2
+    count = lax.axis_size(axis)
+    chunk = value.shape[0] // count
+    for bit in range(count.bit_length() - 1):
+        groups = value.reshape(-1, 2, chunk, width)
         mine = (index >> bit) & 1
-        keep = lax.dynamic_slice_in_dim(value, mine * half, half, 0)
-        give = lax.dynamic_slice_in_dim(value, (1 - mine) * half, half, 0)
+        keep = lax.dynamic_index_in_dim(groups, mine, 1, keepdims=False).reshape(-1, width)
+        give = lax.dynamic_index_in_dim(groups, 1 - mine, 1, keepdims=False).reshape(-1, width)
+        half = give.shape[0]
         got = partner(jnp.concatenate([give, extra_rows], axis=0), axis, bit)
         value = keep + got[:half]
         extra_rows = extra_rows + got[half:]

time: 94.1 us -> 94.3 us (level)
  waiting for transfers between devices: 18.1 us -> 12.9 us
  local copies, waits for them, and re-layouts: 22.5 us -> 25.1 us
  other arithmetic: 19.6 us -> 21.3 us
    ppermute x8, waiting for transfers between devices: 14.2 us -> 8.85 us  [partner(): return lax.ppermute(value, axis, pairs)]
    reduce_sum x1, other arithmetic: 3.81 us -> 5.29 us  [body(): harm_grad = jnp.sum(value_grad * radial[None], axis=1)]
    another operation x0 -> x1, local copies, waits for them, and re-layouts: none -> 1.13 us  [halving_with(): groups = value.reshape(-1, 2, chunk, width)]
    unnamed x60 -> x92, local copies, waits for them, and re-layouts: 7.55 us -> 8.61 us
  transfers between devices with their start and end apart: 10 -> 10, of which waited for: 4 -> 4; matrix products, arithmetic and copies ran while one was open for 18% -> 21% of each run, Pallas kernels for 0% -> 0%
where the time goes in v10:
time: 94.3 us; the launch traced here: 93.6 us
  local copies, waits for them, and re-layouts  25.1 us (27%)
  other arithmetic  21.3 us (23%)
  starting transfers between devices  18.1 us (19%)
  waiting for transfers between devices  12.9 us (14%)
  matrix products  8.5 us (9%)
  blocking collectives  6.04 us (6%)
  between operations  1.66 us (2%)
    ppermute x8, starting transfers between devices, partner(): return lax.ppermute(value, axis, pairs)  10.9 us
    ppermute x8, waiting for transfers between devices, partner(): return lax.ppermute(value, axis, pairs)  8.85 us
    unnamed x92, local copies, waits for them, and re-layouts  8.61 us
    all_gather x1, blocking collectives, body(): lax.all_gather(jnp.concatenate([src_feat, weight_high, weight_mid, weight...  6.04 us
    reduce_sum x1, other arithmetic, body(): harm_grad = jnp.sum(value_grad * radial[None], axis=1)  5.29 us
    all_to_all x1, waiting for transfers between devices, body(): lax.all_to_all(result_rows.reshape(all_chan, components, own_blocks, 1, r...  4.01 us
    all_to_all x1, starting transfers between devices, body(): lax.all_to_all(out_grad.reshape(chan_dev, components, own_blocks, chan_co...  3.95 us
    all_to_all x1, starting transfers between devices, body(): lax.all_to_all(result_rows.reshape(all_chan, components, own_blocks, 1, r...  3.34 us
  transfers between devices with their start and end apart: 10, of which 4 were waited for; matrix products, arithmetic and copies ran while one was open for 21% of the time, Pallas kernels for 0%

profile of v10, /device:TPU:0, one launch (start us, length us, event | category | flops | bytes accessed | tf_op | source)
XLA Modules:
  0.0 93.6 jit_solution(4172741723407576543)
XLA Ops:
  0.7 0.8 slice_bitcast_fusion.2
  1.4 0.7 convert_element_type.97
  2.1 0.7 pad_maximum_fusion.3
  2.9 0.7 pad_clamp_fusion.3
  3.6 1.1 %gather_fusion = f32[384,35]{1,0:T(8,128)S(1)} fusion(f32[35,256]{0,1:T(8,128)S(1)} %copy.216, s32[1024]{0:T(1024)S(1)} %get-tuple-element.71), kind=kCustom, calls=%fused_computation | custom fusion | bytes 109056 | tf_op jit(solution)/shard_map/jit(_take)/gather | solution.py:116
  4.8 3.0 %collective-permute-start = (f32[35,128]{0,1:T(8,128)S(1)}, f32[35,128]{0,1:T(8,128)S(1)}, u32[]{:S(2)}, u32[]{:S(2)}) collective-permute-start(f32[35,128]{0,1:T(8,128)S(1)} %get-tuple-element.41), channel_id=1, source_target_pairs={{0,4},{4,0},{8,12},{12,8},{16,20},{20,16},{24,28},{28,24},{1,5},{5... | collective-permute-start | bytes 53768 | tf_op jit(solution)/shard_map/ppermute | solution.py:19
  7.8 1.6 %collective-permute-start.1 = (f32[35,128]{0,1:T(8,128)S(1)}, f32[35,128]{0,1:T(8,128)S(1)}, u32[]{:S(2)}, u32[]{:S(2)}) collective-permute-start(f32[35,128]{0,1:T(8,128)S(1)} %get-tuple-element.42), channel_id=1, source_target_pairs={{0,8},{4,12},{8,0},{12,4},{16,24},{20,28},{24,16},{28,20},{1,9},{5... | collective-permute-start | bytes 53768 | tf_op jit(solution)/shard_map/ppermute | solution.py:19
  9.4 2.6 %collective-permute-start.2 = (f32[35,128]{0,1:T(8,128)S(1)}, f32[35,128]{0,1:T(8,128)S(1)}, u32[]{:S(2)}, u32[]{:S(2)}) collective-permute-start(f32[35,128]{0,1:T(8,128)S(1)} %get-tuple-element.43), channel_id=1, source_target_pairs={{0,16},{4,20},{8,24},{12,28},{16,0},{20,4},{24,8},{28,12},{1,17},{... | collective-permute-start | bytes 53768 | tf_op jit(solution)/shard_map/ppermute | solution.py:19
  12.3 0.7 copy.239
  13.0 1.2 %reshape.632 = bf16[4,2,9216]{2,1,0:T(2,128)(2,1)} reshape(bf16[4,9,2,32,32]{4,3,2,1,0:T(8,128)(2,1)S(1)} %bitcast.384) | data formatting | bytes 294912
  14.2 4.0 %all-to-all-start.1 = ((bf16[4,2,9216]{2,1,0:T(2,128)(2,1)}), bf16[4,2,9216]{2,1,0:T(2,128)(2,1)}, u32[]{:S(2)}, u32[]{:S(2)}) async-start(bf16[4,2,9216]{2,1,0:T(2,128)(2,1)} %reshape.632), calls=%async_computation.1 | async-start | bytes 294912 | tf_op jit(solution)/shard_map/all_to_all | solution.py:203
  18.2 0.6 compare_convert_fusion
  18.9 0.6 pad_clamp_fusion
  19.9 0.7 copy.244
  20.7 0.7 copy.252
  21.3 0.6 gather_fusion.4
  22.4 6.0 %all_gather.3 = bf16[128,664]{1,0:T(8,128)(2,1)S(1)} all-gather(bf16[32,664]{1,0:T(8,128)(2,1)S(1)} %concatenate.53), channel_id=1, replica_groups=mesh['space'=8,'chan'=4] {'chan'}, dimensions={0}, use_global_device_ids=true | all-gather | bytes 212480 | tf_op jit(solution)/shard_map/all_gather | solution.py:137
  29.0 0.6 gather_fusion.2
  29.6 0.6 gather_fusion.3
  30.7 0.6 gather_fusion.1
  32.2 0.8 copy-done.10
  33.0 0.3 fusion.17
  33.2 3.0 %fusion.7 = (bf16[128,2,9,32]{0,3,2,1:T(8,128)(2,1)S(1)}, f32[2,128,9,8,32,1]{1,4,5,3,2,0:T(8,128)}) fusion(f32[128,8]{0,1:T(8,128)S(1)} %copy.285, f32[8,128,128]{2,1,0:T(8,128)S(1)} %convert_element_type.105, f32[8,2]{0,1:T(2,128)S(1)} %copy.223, f32[8,8,32,128]{3,2,0,1:T(8,128)S(1)} %fusion.17, f32[9,8,32,128]{3,2,1,0:T(8,128)S(1)} %multiply_dynamic-update-slice_fusion), kind=kOutput, calls=%fused_computation.21 | convolution fusion | flops 1214308352 | bytes 5263424 | tf_op jit(solution)/shard_map/lktij,tbcj->bclki/dot_general | solution.py:180
  36.3 1.1 %convolution_bitcast_fusion = f32[128,9,2,32]{0,3,2,1:T(8,128)} fusion(bf16[9,128,128]{2,1,0:T(8,128)(2,1)S(1)} %gather_fusion.4, bf16[128,2,9,32]{0,3,2,1:T(8,128)(2,1)S(1)} %get-tuple-element.67), kind=kOutput, calls=%fused_computation.26 | convolution fusion | flops 18874368 | bytes 737280 | tf_op jit(solution)/shard_map/lxc,clbi->xlbi/dot_general | solution.py:187
  37.3 0.7 broadcast_multiply_fusion
  38.0 1.3 %reshape.633 = bf16[4,9,2,32,32]{4,3,2,1,0:T(8,128)(2,1)S(1)} reshape(bf16[4,2,9216]{2,1,0:T(2,128)(2,1)} %all-to-all-done.1) | data formatting | bytes 294912
  39.5 0.8 copy.240
  40.3 0.5 reshape.559
  40.8 0.4 copy-done.4
  41.3 0.6 fusion.91
  41.9 0.7 multiply_convert_fusion.3
  42.9 0.9 gather_fusion.5
  43.8 1.4 %multiply_convert_fusion = bf16[8,128,9,8,32]{1,4,3,2,0:T(8,128)(2,1)S(1)} fusion(f32[8,128,9,32]{1,3,2,0:T(8,128)S(1)} %gather_fusion.5, f32[8,128,8]{1,2,0:T(8,128)S(1)} %copy-done.17), kind=kLoop, calls=%fused_computation.9 | loop fusion | flops 4718592 | bytes 5931008 | tf_op jit(solution)/shard_map/convert_element_type | solution.py:226
  45.4 2.9 %fusion.8 = f32[8,128,128]{2,1,0:T(8,128)} fusion(bf16[8,128,9,8,32]{1,4,3,2,0:T(8,128)(2,1)S(1)} %multiply_convert_fusion, f32[8,8,32,128]{3,2,0,1:T(8,128)S(1)} %copy-done.2, f32[9,8,32,128]{3,2,1,0:T(8,128)S(1)} %copy-done.7), kind=kOutput, calls=%fused_computation.24 | convolution fusion | flops 608698368 | bytes 7471104 | tf_op jit(solution)/shard_map/tclki,lktij->tcj/dot_general | solution.py:227
  48.2 1.4 %fusion.106 = f32[8,128,2304]{1,2,0:S(1)} fusion(bf16[8,128,2304]{1,2,0:T(8,128)(2,1)S(1)} %bitcast.383, bf16[8,128,128]{2,1,0:T(8,128)(2,1)S(1)} %gather_fusion.1), kind=kOutput, calls=%fused_computation.229 | convolution fusion | flops 603979776 | bytes 14417920
  49.6 5.3 %multiply_reduce_fusion.1 = (f32[9,8,32,128]{3,2,0,1:T(8,128)S(1)}, f32[8,8,32,128]{3,2,0,1:T(8,128)}) fusion(f32[9,8,8,32,128]{4,3,1,0,2:T(8,128)S(1)} %bitcast.382, f32[8,8,32,128]{3,2,0,1:T(8,128)S(1)} %copy-done.2, f32[9,8,32,128]{3,2,1,0:T(8,128)} %copy-done.6), kind=kLoop, calls=%fused_computation.8 | loop fusion | flops 8880128 | bytes 13893632 | tf_op jit(solution)/shard_map/reduce_sum | solution.py:233
  54.9 0.8 fusion.39
  55.7 0.9 fusion.72
  56.6 0.3 fusion.6
  57.3 1.5 %multiply_reduce_fusion.2 = f32[128,5,128]{2,0,1:T(8,128)S(1)} fusion(f32[8,128,128]{2,1,0:T(8,128)} %fusion.8, f32[8,5]{1,0:T(8,128)S(1)} %copy-done.25), kind=kLoop, calls=%fused_computation.17 | loop fusion | flops 1228800 | bytes 852128 | tf_op jit(solution)/shard_map/reduce_sum | solution.py:236
  58.8 1.0 %copy.243 = f32[128,5,128]{2,1,0:T(8,128)} copy(f32[128,5,128]{2,0,1:T(8,128)S(1)} %multiply_reduce_fusion.2) | data formatting | bytes 655360 | tf_op jit(solution)/shard_map/reduce_sum | solution.py:236
  59.8 1.1 %reshape_reshape.13 = f32[2,2,32,640]{3,2,1,0:T(8,128)S(1)} reshape(f32[128,5,128]{2,1,0:T(8,128)} %copy.243) | data formatting | bytes 655360 | tf_op jit(solution)/shard_map/reshape;reshape | solution.py:46
  61.0 0.5 fusion.18
  61.6 0.3 fusion.51
  61.9 0.5 copy-done.13
  62.5 0.3 fusion.84
  63.4 0.4 collective-permute-start.3
  63.8 1.1 %collective-permute-done.3 = f32[69,640]{1,0:T(8,128)S(1)} collective-permute-done((f32[69,640]{1,0:T(8,128)S(1)}, f32[69,640]{1,0:T(8,128)S(1)}, u32[]{:S(2)}, u32[]{:S(2)}) %collective-permute-start.3) | collective-permute-done | bytes 176672 | tf_op jit(solution)/shard_map/ppermute | solution.py:19
  64.9 1.8 %collective-permute-start.4 = (f32[37,640]{1,0:T(8,128)S(1)}, f32[37,640]{1,0:T(8,128)S(1)}, u32[]{:S(2)}, u32[]{:S(2)}) collective-permute-start(f32[37,640]{1,0:T(8,128)S(1)} %pad_maximum_fusion.2), channel_id=1, source_target_pairs={{0,2},{1,3},{2,0},{3,1},{4,6},{5,7},{6,4},{7,5},{8,10},{9,11},{10,... | collective-permute-start | bytes 284168 | tf_op jit(solution)/shard_map/ppermute | solution.py:19
  66.7 3.4 %collective-permute-done.4 = f32[37,640]{1,0:T(8,128)S(1)} collective-permute-done((f32[37,640]{1,0:T(8,128)S(1)}, f32[37,640]{1,0:T(8,128)S(1)}, u32[]{:S(2)}, u32[]{:S(2)}) %collective-permute-start.4) | collective-permute-done | bytes 94752 | tf_op jit(solution)/shard_map/ppermute | solution.py:19
  70.5 0.6 collective-permute-start.5
  71.1 0.8 copy.236
  71.9 1.2 %reshape.630 = bf16[4,2,9216]{2,1,0:T(2,128)(2,1)} reshape(bf16[128,1,9,2,32]{4,3,2,1,0:T(2,128)(2,1)S(1)} %bitcast.385) | data formatting | bytes 294912
  73.1 3.3 %all-to-all-start = ((bf16[4,2,9216]{2,1,0:T(2,128)(2,1)}), bf16[4,2,9216]{2,1,0:T(2,128)(2,1)S(1)}, u32[]{:S(2)}, u32[]{:S(2)}) async-start(bf16[4,2,9216]{2,1,0:T(2,128)(2,1)} %reshape.630), calls=%async_computation | async-start | bytes 294912 | tf_op jit(solution)/shard_map/all_to_all | solution.py:196
  76.7 0.5 collective-permute-start.6
  77.3 4.0 %all-to-all-done = bf16[4,2,9216]{2,1,0:T(2,128)(2,1)S(1)} async-done(((bf16[4,2,9216]{2,1,0:T(2,128)(2,1)}), bf16[4,2,9216]{2,1,0:T(2,128)(2,1)S(1)}, u32[]{:S(2)}, u32[]{:S(2)}) %all-to-all-start) | async-done | bytes 147488 | tf_op jit(solution)/shard_map/all_to_all | solution.py:196
  81.5 0.8 copy.237
  82.3 1.1 %reshape.546 = bf16[32,9,256]{2,0,1:T(8,128)(2,1)} reshape(bf16[32,9,2,4,1,32]{5,3,2,0,1,4:T(4,128)(2,1)S(1)} %copy.237) | data formatting | bytes 294912 | tf_op jit(solution)/shard_map/reshape | solution.py:202
  83.6 0.4 collective-permute-start.7
  84.1 4.3 %collective-permute-done.7 = f32[37,128]{1,0:T(8,128)S(1)} collective-permute-done((f32[37,128]{1,0:T(8,128)S(1)}, f32[37,128]{1,0:T(8,128)S(1)}, u32[]{:S(2)}, u32[]{:S(2)}) %collective-permute-start.7) | collective-permute-done | bytes 18976 | tf_op jit(solution)/shard_map/ppermute | solution.py:19
  88.6 2.7 %scatter_fusion = f32[35,256]{0,1:T(8,128)S(1)} fusion(f32[35,256]{0,1:T(8,128)S(1)} %copy.253, s32[384]{0:T(512)S(1)} %fusion.100, f32[384,35]{1,0:T(8,128)S(1)} %copy.254), kind=kCustom, calls=%fused_computation.6 | custom fusion | flops 13440 | bytes 162816 | tf_op jit(solution)/shard_map/scatter-add | solution.py:268
  91.5 0.7 copy.257
  92.2 0.7 copy.255
  92.9 0.7 copy.256
  (187 shorter events, 6.3 us)
Async XLA Ops:
  0.6 20.7 %copy-start = (bf16[3,128,128]{2,1,0:T(8,128)(2,1)S(1)}, bf16[3,128,128]{2,1,0:T(8,128)(2,1)}, u32[]{:S(2)}) copy-start(bf16[3,128,128]{2,1,0:T(8,128)(2,1)} %param.15) | copy-start | bytes 294916
  0.6 11.3 %copy-start.16 = (bf16[32,9,256]{2,0,1:T(8,128)(2,1)S(1)}, bf16[32,9,256]{2,0,1:T(8,128)(2,1)}, u32[]{:S(2)}) copy-start(bf16[32,9,256]{2,0,1:T(8,128)(2,1)} %param.16) | copy-start | bytes 442372
  4.8 17.2 %collective-permute-start = (f32[35,128]{0,1:T(8,128)S(1)}, f32[35,128]{0,1:T(8,128)S(1)}, u32[]{:S(2)}, u32[]{:S(2)}) collective-permute-start(f32[35,128]{0,1:T(8,128)S(1)} %get-tuple-element.41), channel_id=1, source_target_pairs={{0,4},{4,0},{8,12},{12,8},{16,20},{20,16},{24,28},{28,24},{1,5},{5... | collective-permute-start | bytes 53768 | tf_op jit(solution)/shard_map/ppermute | solution.py:19
  7.8 14.2 %collective-permute-start.1 = (f32[35,128]{0,1:T(8,128)S(1)}, f32[35,128]{0,1:T(8,128)S(1)}, u32[]{:S(2)}, u32[]{:S(2)}) collective-permute-start(f32[35,128]{0,1:T(8,128)S(1)} %get-tuple-element.42), channel_id=1, source_target_pairs={{0,8},{4,12},{8,0},{12,4},{16,24},{20,28},{24,16},{28,20},{1,9},{5... | collective-permute-start | bytes 53768 | tf_op jit(solution)/shard_map/ppermute | solution.py:19
  9.4 12.8 %collective-permute-start.2 = (f32[35,128]{0,1:T(8,128)S(1)}, f32[35,128]{0,1:T(8,128)S(1)}, u32[]{:S(2)}, u32[]{:S(2)}) collective-permute-start(f32[35,128]{0,1:T(8,128)S(1)} %get-tuple-element.43), channel_id=1, source_target_pairs={{0,16},{4,20},{8,24},{12,28},{16,0},{20,4},{24,8},{28,12},{1,17},{... | collective-permute-start | bytes 53768 | tf_op jit(solution)/shard_map/ppermute | solution.py:19
  12.2 5.9 %copy-start.37 = (s32[8,2]{0,1:T(2,128)S(1)}, s32[8,2]{0,1:T(2,128)}, u32[]{:S(2)}) copy-start(s32[8,2]{0,1:T(2,128)} %param.12) | copy-start | bytes 196
  12.2 6.6 %copy-start.40 = (s32[8]{0:T(128)S(1)}, s32[8]{0:T(128)}, u32[]{:S(2)}) copy-start(s32[8]{0:T(128)} %param.13) | copy-start | bytes 100
  12.3 6.6 %copy-start.32 = (f32[32,8]{0,1:T(8,128)S(1)}, f32[32,8]{0,1:T(8,128)}, u32[]{:S(2)}) copy-start(f32[32,8]{0,1:T(8,128)} %param.14) | copy-start | bytes 3076
  12.3 6.7 %copy-start.39 = (s32[9]{0:T(128)S(1)}, s32[9]{0:T(128)}, u32[]{:S(2)}) copy-start(s32[9]{0:T(128)} %constant.98) | copy-start | bytes 112
  13.0 9.3 %copy-start.22 = (bf16[32,256]{1,0:T(8,128)(2,1)S(1)}, bf16[32,256]{1,0:T(8,128)(2,1)}, u32[]{:S(2)}) copy-start(bf16[32,256]{1,0:T(8,128)(2,1)} %param.10) | copy-start | bytes 49156
  14.2 23.8 %all-to-all-start.1 = ((bf16[4,2,9216]{2,1,0:T(2,128)(2,1)}), bf16[4,2,9216]{2,1,0:T(2,128)(2,1)}, u32[]{:S(2)}, u32[]{:S(2)}) async-start(bf16[4,2,9216]{2,1,0:T(2,128)(2,1)} %reshape.632), calls=%async_computation.1 | async-start | bytes 294912 | tf_op jit(solution)/shard_map/all_to_all | solution.py:203
  18.2 13.9 %copy-start.33 = (f32[8]{0:T(128)}, f32[8]{0:T(128)S(1)}, u32[]{:S(2)}) copy-start(f32[8]{0:T(128)S(1)} %compare_convert_fusion.1) | copy-start | bytes 100
  18.8 18.5 %copy-start.29 = (f32[8]{0:T(128)}, f32[8]{0:T(128)S(1)}, u32[]{:S(2)}) copy-start(f32[8]{0:T(128)S(1)} %convert_element_type.104) | copy-start | bytes 100
  18.9 9.5 %copy-start.24 = (f32[8,5]{1,0:T(8,128)}, f32[8,5]{1,0:T(8,128)S(1)}, u32[]{:S(2)}) copy-start(f32[8,5]{1,0:T(8,128)S(1)} %get-tuple-element.63) | copy-start | bytes 484
  19.6 12.6 %copy-start.35 = (f32[8]{0:T(128)}, f32[8]{0:T(128)S(1)}, u32[]{:S(2)}) copy-start(f32[8]{0:T(128)S(1)} %add_multiply_fusion) | copy-start | bytes 100
  19.6 9.3 %copy-start.26 = (f32[3,256]{1,0:T(4,128)S(1)}, f32[3,256]{1,0:T(4,128)}, u32[]{:S(2)}) copy-start(f32[3,256]{1,0:T(4,128)} %param.9) | copy-start | bytes 9220
  29.5 1.9 %copy-start.18 = (f32[8,3,128]{2,0,1:T(8,128)}, f32[8,3,128]{2,0,1:T(8,128)S(1)}, u32[]{:S(2)}) copy-start(f32[8,3,128]{2,0,1:T(8,128)S(1)} %copy.230) | copy-start | bytes 36868
  30.2 1.4 %copy-start.20 = (f32[8,3,32]{2,0,1:T(8,128)}, f32[8,3,32]{2,0,1:T(8,128)S(1)}, u32[]{:S(2)}) copy-start(f32[8,3,32]{2,0,1:T(8,128)S(1)} %copy.232) | copy-start | bytes 9220
  32.1 4.2 %copy-start.6 = (f32[9,8,32,128]{3,2,1,0:T(8,128)}, f32[9,8,32,128]{3,2,1,0:T(8,128)S(1)}, u32[]{:S(2)}) copy-start(f32[9,8,32,128]{3,2,1,0:T(8,128)S(1)} %multiply_dynamic-update-slice_fusion) | copy-start | bytes 3538948
  32.2 0.8 copy-start.10
  32.2 4.1 %copy-start.8 = (f32[8,32,128]{2,1,0:T(8,128)}, f32[8,32,128]{2,1,0:T(8,128)S(1)}, u32[]{:S(2)}) copy-start(f32[8,32,128]{2,1,0:T(8,128)S(1)} %get-tuple-element.44) | copy-start | bytes 393220
  33.2 3.0 %copy-start.1 = (f32[8,8,32,128]{3,2,0,1:T(8,128)}, f32[8,8,32,128]{3,2,0,1:T(8,128)S(1)}, u32[]{:S(2)}) copy-start(f32[8,8,32,128]{3,2,0,1:T(8,128)S(1)} %fusion.17) | copy-start | bytes 3145732
  40.3 1.0 %copy-start.4 = (f32[128,9,2,32]{0,3,2,1:T(8,128)S(1)}, f32[128,9,2,32]{0,3,2,1:T(8,128)}, u32[]{:S(2)}) copy-start(f32[128,9,2,32]{0,3,2,1:T(8,128)} %convolution_bitcast_fusion) | copy-start | bytes 884740
  42.9 0.9 copy-start.17
  43.8 1.4 %copy-start.2 = (f32[8,8,32,128]{3,2,0,1:T(8,128)S(1)}, f32[8,8,32,128]{3,2,0,1:T(8,128)}, u32[]{:S(2)}) copy-start(f32[8,8,32,128]{3,2,0,1:T(8,128)} %copy-done.1) | copy-start | bytes 3145732
  43.8 1.6 %copy-start.7 = (f32[9,8,32,128]{3,2,1,0:T(8,128)S(1)}, f32[9,8,32,128]{3,2,1,0:T(8,128)}, u32[]{:S(2)}) copy-start(f32[9,8,32,128]{3,2,1,0:T(8,128)} %copy-done.6) | copy-start | bytes 3538948
  54.9 1.7 %copy-start.5 = (f32[2,128,9,8,32,1]{1,4,5,3,2,0:T(8,128)S(1)}, f32[2,128,9,8,32,1]{1,4,5,3,2,0:T(8,128)}, u32[]{:S(2)}) copy-start(f32[2,128,9,8,32,1]{1,4,5,3,2,0:T(8,128)} %get-tuple-element.68) | copy-start | bytes 7077892
  56.6 0.7 copy-start.25
  57.3 3.7 %copy-start.3 = (f32[8,8,32,128]{3,2,0,1:T(8,128)S(1)}, f32[8,8,32,128]{3,2,0,1:T(8,128)}, u32[]{:S(2)}) copy-start(f32[8,8,32,128]{3,2,0,1:T(8,128)} %get-tuple-element.29) | copy-start | bytes 3145732
  57.3 3.7 %copy-start.9 = (f32[8,32,128]{2,1,0:T(8,128)S(1)}, f32[8,32,128]{2,1,0:T(8,128)}, u32[]{:S(2)}) copy-start(f32[8,32,128]{2,1,0:T(8,128)} %copy-done.8) | copy-start | bytes 393220
  57.3 3.7 %copy-start.11 = (f32[8,32,128]{2,1,0:T(8,128)S(1)}, f32[8,32,128]{2,1,0:T(8,128)}, u32[]{:S(2)}) copy-start(f32[8,32,128]{2,1,0:T(8,128)} %copy-done.10) | copy-start | bytes 393220
  57.3 3.7 %copy-start.36 = (f32[8]{0:T(128)S(1)}, f32[8]{0:T(128)}, u32[]{:S(2)}) copy-start(f32[8]{0:T(128)} %copy-done.35) | copy-start | bytes 100
  59.8 1.7 %copy-start.30 = (f32[8]{0:T(128)S(1)}, f32[8]{0:T(128)}, u32[]{:S(2)}) copy-start(f32[8]{0:T(128)} %copy-done.29) | copy-start | bytes 100
  59.8 1.8 %copy-start.34 = (f32[8]{0:T(128)S(1)}, f32[8]{0:T(128)}, u32[]{:S(2)}) copy-start(f32[8]{0:T(128)} %copy-done.33) | copy-start | bytes 100
  61.5 0.9 copy-start.13
  61.5 1.0 %copy-start.14 = (f32[8,1,32,128]{3,2,0,1:T(8,128)S(1)}, f32[8,1,32,128]{3,2,0,1:T(8,128)}, u32[]{:S(2)}) copy-start(f32[8,1,32,128]{3,2,0,1:T(8,128)} %get-tuple-element.34) | copy-start | bytes 393220
  61.5 1.0 %copy-start.15 = (f32[8,1,32,128]{3,2,0,1:T(8,128)S(1)}, f32[8,1,32,128]{3,2,0,1:T(8,128)}, u32[]{:S(2)}) copy-start(f32[8,1,32,128]{3,2,0,1:T(8,128)} %get-tuple-element.35) | copy-start | bytes 393220
  61.5 1.0 %copy-start.19 = (f32[8,3,128]{2,0,1:T(8,128)S(1)}, f32[8,3,128]{2,0,1:T(8,128)}, u32[]{:S(2)}) copy-start(f32[8,3,128]{2,0,1:T(8,128)} %copy-done.18) | copy-start | bytes 36868
  61.5 1.0 %copy-start.21 = (f32[8,3,32]{2,0,1:T(8,128)S(1)}, f32[8,3,32]{2,0,1:T(8,128)}, u32[]{:S(2)}) copy-start(f32[8,3,32]{2,0,1:T(8,128)} %copy-done.20) | copy-start | bytes 9220
  61.6 1.3 %copy-start.28 = (f32[8,5]{0,1:T(8,128)S(1)}, f32[8,5]{0,1:T(8,128)}, u32[]{:S(2)}) copy-start(f32[8,5]{0,1:T(8,128)} %copy.252) | copy-start | bytes 484
  61.6 1.4 %copy-start.27 = (f32[8,5]{0,1:T(8,128)S(1)}, f32[8,5]{0,1:T(8,128)}, u32[]{:S(2)}) copy-start(f32[8,5]{0,1:T(8,128)} %copy.244) | copy-start | bytes 484
  61.6 1.5 %copy-start.38 = (f32[4]{0:T(128)S(1)}, f32[4]{0:T(128)}, u32[]{:S(2)}) copy-start(f32[4]{0:T(128)} %compare_convert_fusion) | copy-start | bytes 52
  63.3 7.7 %copy-start.12 = (bf16[128,8,2,1,32]{0,4,2,1,3:T(8,128)(2,1)S(1)}, bf16[128,8,2,1,32]{0,4,2,1,3:T(8,128)(2,1)}, u32[]{:S(2)}) copy-start(bf16[128,8,2,1,32]{0,4,2,1,3:T(8,128)(2,1)} %get-tuple-element.50) | copy-start | bytes 393220
  63.3 7.7 %copy-start.23 = (bf16[128,1,2,1,32]{0,4,2,1,3:T(8,128)(2,1)S(1)}, bf16[128,1,2,1,32]{0,4,2,1,3:T(8,128)(2,1)}, u32[]{:S(2)}) copy-start(bf16[128,1,2,1,32]{0,4,2,1,3:T(8,128)(2,1)} %get-tuple-element.39) | copy-start | bytes 49156
  63.4 1.5 %collective-permute-start.3 = (f32[69,640]{1,0:T(8,128)S(1)}, f32[69,640]{1,0:T(8,128)S(1)}, u32[]{:S(2)}, u32[]{:S(2)}) collective-permute-start(f32[69,640]{1,0:T(8,128)S(1)} %pad_maximum_fusion), channel_id=1, source_target_pairs={{0,1},{1,0},{2,3},{3,2},{4,5},{5,4},{6,7},{7,6},{8,9},{9,8},{10,11... | collective-permute-start | bytes 529928 | tf_op jit(solution)/shard_map/ppermute | solution.py:19
  64.9 5.2 %collective-permute-start.4 = (f32[37,640]{1,0:T(8,128)S(1)}, f32[37,640]{1,0:T(8,128)S(1)}, u32[]{:S(2)}, u32[]{:S(2)}) collective-permute-start(f32[37,640]{1,0:T(8,128)S(1)} %pad_maximum_fusion.2), channel_id=1, source_target_pairs={{0,2},{1,3},{2,0},{3,1},{4,6},{5,7},{6,4},{7,5},{8,10},{9,11},{10,... | collective-permute-start | bytes 284168 | tf_op jit(solution)/shard_map/ppermute | solution.py:19
  70.4 6.9 %copy-start.31 = (s32[3,128]{1,0:T(4,128)S(1)}, s32[3,128]{1,0:T(4,128)}, u32[]{:S(2)}) copy-start(s32[3,128]{1,0:T(4,128)} %param.11) | copy-start | bytes 4612
  70.5 6.0 %collective-permute-start.5 = (f32[37,128]{1,0:T(8,128)S(1)}, f32[37,128]{1,0:T(8,128)S(1)}, u32[]{:S(2)}, u32[]{:S(2)}) collective-permute-start(f32[37,128]{1,0:T(8,128)S(1)} %pad_maximum_fusion.5), channel_id=1, source_target_pairs={{0,4},{4,0},{8,12},{12,8},{16,20},{20,16},{24,28},{28,24},{1,5},{5... | collective-permute-start | bytes 56840 | tf_op jit(solution)/shard_map/ppermute | solution.py:19
  73.1 8.1 %all-to-all-start = ((bf16[4,2,9216]{2,1,0:T(2,128)(2,1)}), bf16[4,2,9216]{2,1,0:T(2,128)(2,1)S(1)}, u32[]{:S(2)}, u32[]{:S(2)}) async-start(bf16[4,2,9216]{2,1,0:T(2,128)(2,1)} %reshape.630), calls=%async_computation | async-start | bytes 294912 | tf_op jit(solution)/shard_map/all_to_all | solution.py:196
  76.7 6.7 %collective-permute-start.6 = (f32[37,128]{1,0:T(8,128)S(1)}, f32[37,128]{1,0:T(8,128)S(1)}, u32[]{:S(2)}, u32[]{:S(2)}) collective-permute-start(f32[37,128]{1,0:T(8,128)S(1)} %pad_maximum_fusion.6), channel_id=1, source_target_pairs={{0,8},{4,12},{8,0},{12,4},{16,24},{20,28},{24,16},{28,20},{1,9},{5... | collective-permute-start | bytes 56840 | tf_op jit(solution)/shard_map/ppermute | solution.py:19
  83.6 4.9 %collective-permute-start.7 = (f32[37,128]{1,0:T(8,128)S(1)}, f32[37,128]{1,0:T(8,128)S(1)}, u32[]{:S(2)}, u32[]{:S(2)}) collective-permute-start(f32[37,128]{1,0:T(8,128)S(1)} %pad_maximum_fusion.7), channel_id=1, source_target_pairs={{0,16},{4,20},{8,24},{12,28},{16,0},{20,4},{24,8},{28,12},{1,17},{... | collective-permute-start | bytes 56840 | tf_op jit(solution)/shard_map/ppermute | solution.py:19

commit v11 on v10

--- a/solution.py
+++ b/solution.py
@@ -265,7 +265,12 @@
         )
         back_list.append(back_both[:ghost_rows])
     all_rows = send_rows[:levels].reshape(-1)
-    own_both = own_both.at[:, all_rows].add(jnp.concatenate(back_list, axis=1))
+    ghost_hot = (all_rows[:, None] == jnp.arange(atoms_dev, dtype=jnp.int32)[None]).astype(
+        jnp.float32
+    )
+    own_both = own_both + jnp.dot(
+        jnp.concatenate(back_list, axis=1), ghost_hot, precision=lax.Precision.HIGHEST
+    )
     own_grad = own_both[:chan_dev]
     own_dpos = own_both[chan_dev:]
     return (result, own_grad.astype(jnp.bfloat16), -own_dpos, grad_rad)

time: 94.3 us -> 90.3 us (0.958)
  other arithmetic: 21.3 us -> 19 us
  local copies, waits for them, and re-layouts: 25.1 us -> 24 us
  waiting for transfers between devices: 12.9 us -> 11.9 us
    scatter-add x1 -> x0, other arithmetic: 2.68 us -> none  [body(): own_both = own_both.at[:, all_rows].add(jnp.concatenate(back_list, axis=1))]
    unnamed x92 -> x90, local copies, waits for them, and re-layouts: 8.61 us -> 7.24 us
    ppermute x8, waiting for transfers between devices: 8.85 us -> 7.79 us  [partner(): return lax.ppermute(value, axis, pairs)]
where the time goes in v11:
time: 90.3 us; the launch traced here: 89.6 us
  local copies, waits for them, and re-layouts  24 us (27%)
  other arithmetic  19 us (21%)
  starting transfers between devices  18.2 us (20%)
  waiting for transfers between devices  11.9 us (13%)
  matrix products  8.75 us (10%)
  blocking collectives  6.04 us (7%)
  between operations  1.62 us (2%)
    ppermute x8, starting transfers between devices, partner(): return lax.ppermute(value, axis, pairs)  10.9 us
    ppermute x8, waiting for transfers between devices, partner(): return lax.ppermute(value, axis, pairs)  7.79 us
    unnamed x90, local copies, waits for them, and re-layouts  7.24 us
    all_gather x1, blocking collectives, body(): lax.all_gather(jnp.concatenate([src_feat, weight_high, weight_mid, weight...  6.04 us
    reduce_sum x1, other arithmetic, body(): harm_grad = jnp.sum(value_grad * radial[None], axis=1)  5.28 us
    all_to_all x1, waiting for transfers between devices, body(): lax.all_to_all(result_rows.reshape(all_chan, components, own_blocks, 1, r...  4.15 us
    all_to_all x1, starting transfers between devices, body(): lax.all_to_all(out_grad.reshape(chan_dev, components, own_blocks, chan_co...  3.96 us
    all_to_all x1, starting transfers between devices, body(): lax.all_to_all(result_rows.reshape(all_chan, components, own_blocks, 1, r...  3.34 us
  transfers between devices with their start and end apart: 10, of which 4 were waited for; matrix products, arithmetic and copies ran while one was open for 21% of the time, Pallas kernels for 0%

profile of v11, /device:TPU:0, one launch (start us, length us, event | category | flops | bytes accessed | tf_op | source)
XLA Modules:
  0.0 89.6 jit_solution(16250259485113360106)
XLA Ops:
  0.7 0.8 slice_bitcast_fusion.2
  1.4 0.7 convert_element_type.98
  2.1 0.7 pad_maximum_fusion.3
  2.9 0.7 pad_clamp_fusion.3
  3.6 1.1 %gather_fusion = f32[384,35]{1,0:T(8,128)S(1)} fusion(f32[35,256]{0,1:T(8,128)S(1)} %copy.192, s32[1024]{0:T(1024)S(1)} %get-tuple-element.67), kind=kCustom, calls=%fused_computation | custom fusion | bytes 109056 | tf_op jit(solution)/shard_map/jit(_take)/gather | solution.py:116
  4.8 3.0 %collective-permute-start = (f32[35,128]{0,1:T(8,128)S(1)}, f32[35,128]{0,1:T(8,128)S(1)}, u32[]{:S(2)}, u32[]{:S(2)}) collective-permute-start(f32[35,128]{0,1:T(8,128)S(1)} %get-tuple-element.37), channel_id=1, source_target_pairs={{0,4},{4,0},{8,12},{12,8},{16,20},{20,16},{24,28},{28,24},{1,5},{5... | collective-permute-start | bytes 53768 | tf_op jit(solution)/shard_map/ppermute | solution.py:19
  7.8 1.6 %collective-permute-start.1 = (f32[35,128]{0,1:T(8,128)S(1)}, f32[35,128]{0,1:T(8,128)S(1)}, u32[]{:S(2)}, u32[]{:S(2)}) collective-permute-start(f32[35,128]{0,1:T(8,128)S(1)} %get-tuple-element.38), channel_id=1, source_target_pairs={{0,8},{4,12},{8,0},{12,4},{16,24},{20,28},{24,16},{28,20},{1,9},{5... | collective-permute-start | bytes 53768 | tf_op jit(solution)/shard_map/ppermute | solution.py:19
  9.4 2.6 %collective-permute-start.2 = (f32[35,128]{0,1:T(8,128)S(1)}, f32[35,128]{0,1:T(8,128)S(1)}, u32[]{:S(2)}, u32[]{:S(2)}) collective-permute-start(f32[35,128]{0,1:T(8,128)S(1)} %get-tuple-element.39), channel_id=1, source_target_pairs={{0,16},{4,20},{8,24},{12,28},{16,0},{20,4},{24,8},{28,12},{1,17},{... | collective-permute-start | bytes 53768 | tf_op jit(solution)/shard_map/ppermute | solution.py:19
  12.3 0.7 copy.215
  13.0 1.2 %reshape.595 = bf16[4,2,9216]{2,1,0:T(2,128)(2,1)} reshape(bf16[4,9,2,32,32]{4,3,2,1,0:T(8,128)(2,1)S(1)} %bitcast.377) | data formatting | bytes 294912
  14.2 4.0 %all-to-all-start.1 = ((bf16[4,2,9216]{2,1,0:T(2,128)(2,1)}), bf16[4,2,9216]{2,1,0:T(2,128)(2,1)}, u32[]{:S(2)}, u32[]{:S(2)}) async-start(bf16[4,2,9216]{2,1,0:T(2,128)(2,1)} %reshape.595), calls=%async_computation.1 | async-start | bytes 294912 | tf_op jit(solution)/shard_map/all_to_all | solution.py:203
  18.2 0.5 compare_convert_fusion
  18.9 0.6 pad_clamp_fusion
  19.9 0.7 copy.220
  20.6 0.7 copy.228
  21.3 0.6 gather_fusion.4
  22.3 6.0 %all_gather.3 = bf16[128,664]{1,0:T(8,128)(2,1)S(1)} all-gather(bf16[32,664]{1,0:T(8,128)(2,1)S(1)} %concatenate.53), channel_id=1, replica_groups=mesh['space'=8,'chan'=4] {'chan'}, dimensions={0}, use_global_device_ids=true | all-gather | bytes 212480 | tf_op jit(solution)/shard_map/all_gather | solution.py:137
  28.9 0.6 gather_fusion.2
  29.6 0.6 gather_fusion.3
  30.7 0.6 gather_fusion.1
  32.1 0.8 copy-done.10
  32.9 0.3 fusion.17
  33.2 3.0 %fusion.7 = (bf16[128,2,9,32]{0,3,2,1:T(8,128)(2,1)S(1)}, f32[2,128,9,8,32,1]{1,4,5,3,2,0:T(8,128)}) fusion(f32[128,8]{0,1:T(8,128)S(1)} %copy.257, f32[8,128,128]{2,1,0:T(8,128)S(1)} %convert_element_type.106, f32[8,2]{0,1:T(2,128)S(1)} %copy.199, f32[8,8,32,128]{3,2,0,1:T(8,128)S(1)} %fusion.17, f32[9,8,32,128]{3,2,1,0:T(8,128)S(1)} %multiply_dynamic-update-slice_fusion), kind=kOutput, calls=%fused_computation.20 | convolution fusion | flops 1214308352 | bytes 5263424 | tf_op jit(solution)/shard_map/lktij,tbcj->bclki/dot_general | solution.py:180
  36.2 1.0 %convolution_bitcast_fusion = f32[128,9,2,32]{0,3,2,1:T(8,128)} fusion(bf16[9,128,128]{2,1,0:T(8,128)(2,1)S(1)} %gather_fusion.4, bf16[128,2,9,32]{0,3,2,1:T(8,128)(2,1)S(1)} %get-tuple-element.63), kind=kOutput, calls=%fused_computation.25 | convolution fusion | flops 18874368 | bytes 737280 | tf_op jit(solution)/shard_map/lxc,clbi->xlbi/dot_general | solution.py:187
  37.2 0.7 broadcast_multiply_fusion
  37.9 1.3 %reshape.596 = bf16[4,9,2,32,32]{4,3,2,1,0:T(8,128)(2,1)S(1)} reshape(bf16[4,2,9216]{2,1,0:T(2,128)(2,1)} %all-to-all-done.1) | data formatting | bytes 294912
  39.4 0.8 copy.216
  40.2 0.5 reshape.531
  40.8 0.4 copy-done.4
  41.2 0.6 fusion.98
  41.9 0.7 multiply_convert_fusion.3
  42.8 0.9 gather_fusion.5
  43.7 1.4 %multiply_convert_fusion = bf16[8,128,9,8,32]{1,4,3,2,0:T(8,128)(2,1)S(1)} fusion(f32[8,128,9,32]{1,3,2,0:T(8,128)S(1)} %gather_fusion.5, f32[8,128,8]{1,2,0:T(8,128)S(1)} %copy-done.17), kind=kLoop, calls=%fused_computation.8 | loop fusion | flops 4718592 | bytes 5931008 | tf_op jit(solution)/shard_map/convert_element_type | solution.py:226
  45.3 2.9 %fusion.8 = f32[8,128,128]{2,1,0:T(8,128)} fusion(bf16[8,128,9,8,32]{1,4,3,2,0:T(8,128)(2,1)S(1)} %multiply_convert_fusion, f32[8,8,32,128]{3,2,0,1:T(8,128)S(1)} %copy-done.2, f32[9,8,32,128]{3,2,1,0:T(8,128)S(1)} %copy-done.7), kind=kOutput, calls=%fused_computation.23 | convolution fusion | flops 608698368 | bytes 7471104 | tf_op jit(solution)/shard_map/tclki,lktij->tcj/dot_general | solution.py:227
  48.1 1.4 %fusion.115 = f32[8,128,2304]{1,2,0:S(1)} fusion(bf16[8,128,2304]{1,2,0:T(8,128)(2,1)S(1)} %bitcast.376, bf16[8,128,128]{2,1,0:T(8,128)(2,1)S(1)} %gather_fusion.1), kind=kOutput, calls=%fused_computation.234 | convolution fusion | flops 603979776 | bytes 14417920
  49.5 5.3 %multiply_reduce_fusion.1 = (f32[9,8,32,128]{3,2,0,1:T(8,128)S(1)}, f32[8,8,32,128]{3,2,0,1:T(8,128)}) fusion(f32[9,8,8,32,128]{4,3,1,0,2:T(8,128)S(1)} %bitcast.375, f32[8,8,32,128]{3,2,0,1:T(8,128)S(1)} %copy-done.2, f32[9,8,32,128]{3,2,1,0:T(8,128)} %copy-done.6), kind=kLoop, calls=%fused_computation.7 | loop fusion | flops 8880128 | bytes 13893632 | tf_op jit(solution)/shard_map/reduce_sum | solution.py:233
  54.8 0.8 fusion.41
  55.5 0.9 %fusion.74 = (f32[8,1,32,128]{3,2,0,1:T(8,128)}, f32[8,1,32,128]{3,2,0,1:T(8,128)}) fusion(f32[9,8,32,128]{3,2,0,1:T(8,128)S(1)} %get-tuple-element.24, f32[8,3,32,128]{3,2,0,1:T(8,128)S(1)} %get-tuple-element.47, f32[8,32,128]{2,1,0:T(8,128)S(1)} %get-tuple-element.48), kind=kLoop, calls=%fused_computation.115 | loop fusion | flops 950272 | bytes 1703936 | tf_op jit(solution)/shard_map/transpose(jvp())/div | solution.py:69
  56.5 0.3 fusion.6
  57.2 1.5 %multiply_reduce_fusion.2 = f32[128,5,128]{2,0,1:T(8,128)S(1)} fusion(f32[8,128,128]{2,1,0:T(8,128)} %fusion.8, f32[8,5]{1,0:T(8,128)S(1)} %copy-done.25), kind=kLoop, calls=%fused_computation.16 | loop fusion | flops 1228800 | bytes 852128 | tf_op jit(solution)/shard_map/reduce_sum | solution.py:236
  58.7 1.0 %copy.219 = f32[128,5,128]{2,1,0:T(8,128)} copy(f32[128,5,128]{2,0,1:T(8,128)S(1)} %multiply_reduce_fusion.2) | data formatting | bytes 655360 | tf_op jit(solution)/shard_map/reduce_sum | solution.py:236
  59.7 1.1 %reshape_reshape.13 = f32[2,2,32,640]{3,2,1,0:T(8,128)S(1)} reshape(f32[128,5,128]{2,1,0:T(8,128)} %copy.219) | data formatting | bytes 655360 | tf_op jit(solution)/shard_map/reshape;reshape | solution.py:46
  60.8 0.5 fusion.18
  61.4 0.3 fusion.53
  61.8 0.5 copy-done.13
  62.4 0.3 fusion.86
  63.2 0.4 collective-permute-start.3
  63.6 1.1 %collective-permute-done.3 = f32[69,640]{1,0:T(8,128)S(1)} collective-permute-done((f32[69,640]{1,0:T(8,128)S(1)}, f32[69,640]{1,0:T(8,128)S(1)}, u32[]{:S(2)}, u32[]{:S(2)}) %collective-permute-start.3) | collective-permute-done | bytes 176672 | tf_op jit(solution)/shard_map/ppermute | solution.py:19
  64.8 1.8 %collective-permute-start.4 = (f32[37,640]{1,0:T(8,128)S(1)}, f32[37,640]{1,0:T(8,128)S(1)}, u32[]{:S(2)}, u32[]{:S(2)}) collective-permute-start(f32[37,640]{1,0:T(8,128)S(1)} %pad_maximum_fusion.2), channel_id=1, source_target_pairs={{0,2},{1,3},{2,0},{3,1},{4,6},{5,7},{6,4},{7,5},{8,10},{9,11},{10,... | collective-permute-start | bytes 284168 | tf_op jit(solution)/shard_map/ppermute | solution.py:19
  66.6 3.4 %collective-permute-done.4 = f32[37,640]{1,0:T(8,128)S(1)} collective-permute-done((f32[37,640]{1,0:T(8,128)S(1)}, f32[37,640]{1,0:T(8,128)S(1)}, u32[]{:S(2)}, u32[]{:S(2)}) %collective-permute-start.4) | collective-permute-done | bytes 94752 | tf_op jit(solution)/shard_map/ppermute | solution.py:19
  70.3 0.6 collective-permute-start.5
  70.9 3.3 %collective-permute-done.5 = f32[37,128]{1,0:T(8,128)S(1)} collective-permute-done((f32[37,128]{1,0:T(8,128)S(1)}, f32[37,128]{1,0:T(8,128)S(1)}, u32[]{:S(2)}, u32[]{:S(2)}) %collective-permute-start.5) | collective-permute-done | bytes 18976 | tf_op jit(solution)/shard_map/ppermute | solution.py:19
  74.4 0.5 collective-permute-start.6
  74.9 0.8 copy.212
  75.8 1.2 %reshape.593 = bf16[4,2,9216]{2,1,0:T(2,128)(2,1)} reshape(bf16[128,1,9,2,32]{4,3,2,1,0:T(2,128)(2,1)S(1)} %bitcast.378) | data formatting | bytes 294912
  77.0 3.3 %all-to-all-start = ((bf16[4,2,9216]{2,1,0:T(2,128)(2,1)}), bf16[4,2,9216]{2,1,0:T(2,128)(2,1)S(1)}, u32[]{:S(2)}, u32[]{:S(2)}) async-start(bf16[4,2,9216]{2,1,0:T(2,128)(2,1)} %reshape.593), calls=%async_computation | async-start | bytes 294912 | tf_op jit(solution)/shard_map/all_to_all | solution.py:196
  80.6 0.4 collective-permute-start.7
  81.0 4.1 %all-to-all-done = bf16[4,2,9216]{2,1,0:T(2,128)(2,1)S(1)} async-done(((bf16[4,2,9216]{2,1,0:T(2,128)(2,1)}), bf16[4,2,9216]{2,1,0:T(2,128)(2,1)S(1)}, u32[]{:S(2)}, u32[]{:S(2)}) %all-to-all-start) | async-done | bytes 147488 | tf_op jit(solution)/shard_map/all_to_all | solution.py:196
  85.4 0.8 copy.213
  86.2 1.1 %reshape.518 = bf16[32,9,256]{2,0,1:T(8,128)(2,1)} reshape(bf16[32,9,2,4,1,32]{5,3,2,0,1,4:T(4,128)(2,1)S(1)} %copy.213) | data formatting | bytes 294912 | tf_op jit(solution)/shard_map/reshape | solution.py:202
  87.3 0.3 maximum_add_fusion
  87.6 0.6 slice_negate_fusion
  88.2 0.6 slice.342
  88.9 0.7 copy.229
  (180 shorter events, 5.9 us)
Async XLA Ops:
  0.6 20.6 %copy-start = (bf16[3,128,128]{2,1,0:T(8,128)(2,1)S(1)}, bf16[3,128,128]{2,1,0:T(8,128)(2,1)}, u32[]{:S(2)}) copy-start(bf16[3,128,128]{2,1,0:T(8,128)(2,1)} %param.15) | copy-start | bytes 294916
  0.6 11.3 %copy-start.16 = (bf16[32,9,256]{2,0,1:T(8,128)(2,1)S(1)}, bf16[32,9,256]{2,0,1:T(8,128)(2,1)}, u32[]{:S(2)}) copy-start(bf16[32,9,256]{2,0,1:T(8,128)(2,1)} %param.16) | copy-start | bytes 442372
  4.8 17.1 %collective-permute-start = (f32[35,128]{0,1:T(8,128)S(1)}, f32[35,128]{0,1:T(8,128)S(1)}, u32[]{:S(2)}, u32[]{:S(2)}) collective-permute-start(f32[35,128]{0,1:T(8,128)S(1)} %get-tuple-element.37), channel_id=1, source_target_pairs={{0,4},{4,0},{8,12},{12,8},{16,20},{20,16},{24,28},{28,24},{1,5},{5... | collective-permute-start | bytes 53768 | tf_op jit(solution)/shard_map/ppermute | solution.py:19
  7.8 14.2 %collective-permute-start.1 = (f32[35,128]{0,1:T(8,128)S(1)}, f32[35,128]{0,1:T(8,128)S(1)}, u32[]{:S(2)}, u32[]{:S(2)}) collective-permute-start(f32[35,128]{0,1:T(8,128)S(1)} %get-tuple-element.38), channel_id=1, source_target_pairs={{0,8},{4,12},{8,0},{12,4},{16,24},{20,28},{24,16},{28,20},{1,9},{5... | collective-permute-start | bytes 53768 | tf_op jit(solution)/shard_map/ppermute | solution.py:19
  9.4 12.7 %collective-permute-start.2 = (f32[35,128]{0,1:T(8,128)S(1)}, f32[35,128]{0,1:T(8,128)S(1)}, u32[]{:S(2)}, u32[]{:S(2)}) collective-permute-start(f32[35,128]{0,1:T(8,128)S(1)} %get-tuple-element.39), channel_id=1, source_target_pairs={{0,16},{4,20},{8,24},{12,28},{16,0},{20,4},{24,8},{28,12},{1,17},{... | collective-permute-start | bytes 53768 | tf_op jit(solution)/shard_map/ppermute | solution.py:19
  12.2 6.0 %copy-start.37 = (s32[8,2]{0,1:T(2,128)S(1)}, s32[8,2]{0,1:T(2,128)}, u32[]{:S(2)}) copy-start(s32[8,2]{0,1:T(2,128)} %param.12) | copy-start | bytes 196
  12.2 6.5 %copy-start.40 = (s32[8]{0:T(128)S(1)}, s32[8]{0:T(128)}, u32[]{:S(2)}) copy-start(s32[8]{0:T(128)} %param.13) | copy-start | bytes 100
  12.3 6.5 %copy-start.31 = (f32[32,8]{0,1:T(8,128)S(1)}, f32[32,8]{0,1:T(8,128)}, u32[]{:S(2)}) copy-start(f32[32,8]{0,1:T(8,128)} %param.14) | copy-start | bytes 3076
  12.3 6.6 %copy-start.39 = (s32[9]{0:T(128)S(1)}, s32[9]{0:T(128)}, u32[]{:S(2)}) copy-start(s32[9]{0:T(128)} %constant.95) | copy-start | bytes 112
  13.0 9.2 %copy-start.22 = (bf16[32,256]{1,0:T(8,128)(2,1)S(1)}, bf16[32,256]{1,0:T(8,128)(2,1)}, u32[]{:S(2)}) copy-start(bf16[32,256]{1,0:T(8,128)(2,1)} %param.10) | copy-start | bytes 49156
  14.2 23.7 %all-to-all-start.1 = ((bf16[4,2,9216]{2,1,0:T(2,128)(2,1)}), bf16[4,2,9216]{2,1,0:T(2,128)(2,1)}, u32[]{:S(2)}, u32[]{:S(2)}) async-start(bf16[4,2,9216]{2,1,0:T(2,128)(2,1)} %reshape.595), calls=%async_computation.1 | async-start | bytes 294912 | tf_op jit(solution)/shard_map/all_to_all | solution.py:203
  18.2 13.8 %copy-start.32 = (f32[8]{0:T(128)}, f32[8]{0:T(128)S(1)}, u32[]{:S(2)}) copy-start(f32[8]{0:T(128)S(1)} %compare_convert_fusion.1) | copy-start | bytes 100
  18.8 18.5 %copy-start.29 = (f32[8]{0:T(128)}, f32[8]{0:T(128)S(1)}, u32[]{:S(2)}) copy-start(f32[8]{0:T(128)S(1)} %convert_element_type.105) | copy-start | bytes 100
  18.9 9.5 %copy-start.24 = (f32[8,5]{1,0:T(8,128)}, f32[8,5]{1,0:T(8,128)S(1)}, u32[]{:S(2)}) copy-start(f32[8,5]{1,0:T(8,128)S(1)} %get-tuple-element.59) | copy-start | bytes 484
  19.6 12.6 %copy-start.34 = (f32[8]{0:T(128)}, f32[8]{0:T(128)S(1)}, u32[]{:S(2)}) copy-start(f32[8]{0:T(128)S(1)} %add_multiply_fusion) | copy-start | bytes 100
  19.6 9.3 %copy-start.26 = (f32[3,256]{1,0:T(4,128)S(1)}, f32[3,256]{1,0:T(4,128)}, u32[]{:S(2)}) copy-start(f32[3,256]{1,0:T(4,128)} %param.9) | copy-start | bytes 9220
  29.5 1.9 %copy-start.18 = (f32[8,3,128]{2,0,1:T(8,128)}, f32[8,3,128]{2,0,1:T(8,128)S(1)}, u32[]{:S(2)}) copy-start(f32[8,3,128]{2,0,1:T(8,128)S(1)} %copy.206) | copy-start | bytes 36868
  30.2 1.4 %copy-start.20 = (f32[8,3,32]{2,0,1:T(8,128)}, f32[8,3,32]{2,0,1:T(8,128)S(1)}, u32[]{:S(2)}) copy-start(f32[8,3,32]{2,0,1:T(8,128)S(1)} %copy.208) | copy-start | bytes 9220
  32.0 4.2 %copy-start.6 = (f32[9,8,32,128]{3,2,1,0:T(8,128)}, f32[9,8,32,128]{3,2,1,0:T(8,128)S(1)}, u32[]{:S(2)}) copy-start(f32[9,8,32,128]{3,2,1,0:T(8,128)S(1)} %multiply_dynamic-update-slice_fusion) | copy-start | bytes 3538948
  32.1 0.8 copy-start.10
  32.1 4.1 %copy-start.8 = (f32[8,32,128]{2,1,0:T(8,128)}, f32[8,32,128]{2,1,0:T(8,128)S(1)}, u32[]{:S(2)}) copy-start(f32[8,32,128]{2,1,0:T(8,128)S(1)} %get-tuple-element.40) | copy-start | bytes 393220
  33.2 3.0 %copy-start.1 = (f32[8,8,32,128]{3,2,0,1:T(8,128)}, f32[8,8,32,128]{3,2,0,1:T(8,128)S(1)}, u32[]{:S(2)}) copy-start(f32[8,8,32,128]{3,2,0,1:T(8,128)S(1)} %fusion.17) | copy-start | bytes 3145732
  40.2 1.0 %copy-start.4 = (f32[128,9,2,32]{0,3,2,1:T(8,128)S(1)}, f32[128,9,2,32]{0,3,2,1:T(8,128)}, u32[]{:S(2)}) copy-start(f32[128,9,2,32]{0,3,2,1:T(8,128)} %convolution_bitcast_fusion) | copy-start | bytes 884740
  42.8 0.9 copy-start.17
  43.7 1.4 %copy-start.2 = (f32[8,8,32,128]{3,2,0,1:T(8,128)S(1)}, f32[8,8,32,128]{3,2,0,1:T(8,128)}, u32[]{:S(2)}) copy-start(f32[8,8,32,128]{3,2,0,1:T(8,128)} %copy-done.1) | copy-start | bytes 3145732
  43.7 1.6 %copy-start.7 = (f32[9,8,32,128]{3,2,1,0:T(8,128)S(1)}, f32[9,8,32,128]{3,2,1,0:T(8,128)}, u32[]{:S(2)}) copy-start(f32[9,8,32,128]{3,2,1,0:T(8,128)} %copy-done.6) | copy-start | bytes 3538948
  54.8 1.7 %copy-start.5 = (f32[2,128,9,8,32,1]{1,4,5,3,2,0:T(8,128)S(1)}, f32[2,128,9,8,32,1]{1,4,5,3,2,0:T(8,128)}, u32[]{:S(2)}) copy-start(f32[2,128,9,8,32,1]{1,4,5,3,2,0:T(8,128)} %get-tuple-element.64) | copy-start | bytes 7077892
  56.5 0.7 copy-start.25
  57.2 3.6 %copy-start.3 = (f32[8,8,32,128]{3,2,0,1:T(8,128)S(1)}, f32[8,8,32,128]{3,2,0,1:T(8,128)}, u32[]{:S(2)}) copy-start(f32[8,8,32,128]{3,2,0,1:T(8,128)} %get-tuple-element.25) | copy-start | bytes 3145732
  57.2 3.6 %copy-start.9 = (f32[8,32,128]{2,1,0:T(8,128)S(1)}, f32[8,32,128]{2,1,0:T(8,128)}, u32[]{:S(2)}) copy-start(f32[8,32,128]{2,1,0:T(8,128)} %copy-done.8) | copy-start | bytes 393220
  57.2 3.6 %copy-start.11 = (f32[8,32,128]{2,1,0:T(8,128)S(1)}, f32[8,32,128]{2,1,0:T(8,128)}, u32[]{:S(2)}) copy-start(f32[8,32,128]{2,1,0:T(8,128)} %copy-done.10) | copy-start | bytes 393220
  57.2 3.7 %copy-start.35 = (f32[8]{0:T(128)S(1)}, f32[8]{0:T(128)}, u32[]{:S(2)}) copy-start(f32[8]{0:T(128)} %copy-done.34) | copy-start | bytes 100
  59.6 1.7 %copy-start.30 = (f32[8]{0:T(128)S(1)}, f32[8]{0:T(128)}, u32[]{:S(2)}) copy-start(f32[8]{0:T(128)} %copy-done.29) | copy-start | bytes 100
  59.6 1.8 %copy-start.33 = (f32[8]{0:T(128)S(1)}, f32[8]{0:T(128)}, u32[]{:S(2)}) copy-start(f32[8]{0:T(128)} %copy-done.32) | copy-start | bytes 100
  61.3 0.9 %copy-start.13 = (f32[8,1,32,128]{3,2,0,1:T(8,128)S(1)}, f32[8,1,32,128]{3,2,0,1:T(8,128)}, u32[]{:S(2)}) copy-start(f32[8,1,32,128]{3,2,0,1:T(8,128)} %fusion.41) | copy-start | bytes 393220
  61.4 1.0 %copy-start.14 = (f32[8,1,32,128]{3,2,0,1:T(8,128)S(1)}, f32[8,1,32,128]{3,2,0,1:T(8,128)}, u32[]{:S(2)}) copy-start(f32[8,1,32,128]{3,2,0,1:T(8,128)} %get-tuple-element.30) | copy-start | bytes 393220
  61.4 1.0 %copy-start.15 = (f32[8,1,32,128]{3,2,0,1:T(8,128)S(1)}, f32[8,1,32,128]{3,2,0,1:T(8,128)}, u32[]{:S(2)}) copy-start(f32[8,1,32,128]{3,2,0,1:T(8,128)} %get-tuple-element.31) | copy-start | bytes 393220
  61.4 1.0 %copy-start.19 = (f32[8,3,128]{2,0,1:T(8,128)S(1)}, f32[8,3,128]{2,0,1:T(8,128)}, u32[]{:S(2)}) copy-start(f32[8,3,128]{2,0,1:T(8,128)} %copy-done.18) | copy-start | bytes 36868
  61.4 1.0 %copy-start.21 = (f32[8,3,32]{2,0,1:T(8,128)S(1)}, f32[8,3,32]{2,0,1:T(8,128)}, u32[]{:S(2)}) copy-start(f32[8,3,32]{2,0,1:T(8,128)} %copy-done.20) | copy-start | bytes 9220
  61.4 1.3 %copy-start.28 = (f32[8,5]{0,1:T(8,128)S(1)}, f32[8,5]{0,1:T(8,128)}, u32[]{:S(2)}) copy-start(f32[8,5]{0,1:T(8,128)} %copy.228) | copy-start | bytes 484
  61.4 1.4 %copy-start.27 = (f32[8,5]{0,1:T(8,128)S(1)}, f32[8,5]{0,1:T(8,128)}, u32[]{:S(2)}) copy-start(f32[8,5]{0,1:T(8,128)} %copy.220) | copy-start | bytes 484
  61.4 1.5 %copy-start.38 = (f32[4]{0:T(128)S(1)}, f32[4]{0:T(128)}, u32[]{:S(2)}) copy-start(f32[4]{0:T(128)} %compare_convert_fusion) | copy-start | bytes 52
  63.2 11.7 %copy-start.12 = (bf16[128,8,2,1,32]{0,4,2,1,3:T(8,128)(2,1)S(1)}, bf16[128,8,2,1,32]{0,4,2,1,3:T(8,128)(2,1)}, u32[]{:S(2)}) copy-start(bf16[128,8,2,1,32]{0,4,2,1,3:T(8,128)(2,1)} %get-tuple-element.46) | copy-start | bytes 393220
  63.2 11.7 %copy-start.23 = (bf16[128,1,2,1,32]{0,4,2,1,3:T(8,128)(2,1)S(1)}, bf16[128,1,2,1,32]{0,4,2,1,3:T(8,128)(2,1)}, u32[]{:S(2)}) copy-start(bf16[128,1,2,1,32]{0,4,2,1,3:T(8,128)(2,1)} %get-tuple-element.35) | copy-start | bytes 49156
  63.2 1.5 %collective-permute-start.3 = (f32[69,640]{1,0:T(8,128)S(1)}, f32[69,640]{1,0:T(8,128)S(1)}, u32[]{:S(2)}, u32[]{:S(2)}) collective-permute-start(f32[69,640]{1,0:T(8,128)S(1)} %pad_maximum_fusion), channel_id=1, source_target_pairs={{0,1},{1,0},{2,3},{3,2},{4,5},{5,4},{6,7},{7,6},{8,9},{9,8},{10,11... | collective-permute-start | bytes 529928 | tf_op jit(solution)/shard_map/ppermute | solution.py:19
  64.8 5.2 %collective-permute-start.4 = (f32[37,640]{1,0:T(8,128)S(1)}, f32[37,640]{1,0:T(8,128)S(1)}, u32[]{:S(2)}, u32[]{:S(2)}) collective-permute-start(f32[37,640]{1,0:T(8,128)S(1)} %pad_maximum_fusion.2), channel_id=1, source_target_pairs={{0,2},{1,3},{2,0},{3,1},{4,6},{5,7},{6,4},{7,5},{8,10},{9,11},{10,... | collective-permute-start | bytes 284168 | tf_op jit(solution)/shard_map/ppermute | solution.py:19
  70.3 3.8 %collective-permute-start.5 = (f32[37,128]{1,0:T(8,128)S(1)}, f32[37,128]{1,0:T(8,128)S(1)}, u32[]{:S(2)}, u32[]{:S(2)}) collective-permute-start(f32[37,128]{1,0:T(8,128)S(1)} %pad_maximum_fusion.4), channel_id=1, source_target_pairs={{0,4},{4,0},{8,12},{12,8},{16,20},{20,16},{24,28},{28,24},{1,5},{5... | collective-permute-start | bytes 56840 | tf_op jit(solution)/shard_map/ppermute | solution.py:19
  74.4 5.9 %collective-permute-start.6 = (f32[37,128]{1,0:T(8,128)S(1)}, f32[37,128]{1,0:T(8,128)S(1)}, u32[]{:S(2)}, u32[]{:S(2)}) collective-permute-start(f32[37,128]{1,0:T(8,128)S(1)} %pad_maximum_fusion.5), channel_id=1, source_target_pairs={{0,8},{4,12},{8,0},{12,4},{16,24},{20,28},{24,16},{28,20},{1,9},{5... | collective-permute-start | bytes 56840 | tf_op jit(solution)/shard_map/ppermute | solution.py:19
  77.0 8.1 %all-to-all-start = ((bf16[4,2,9216]{2,1,0:T(2,128)(2,1)}), bf16[4,2,9216]{2,1,0:T(2,128)(2,1)S(1)}, u32[]{:S(2)}, u32[]{:S(2)}) async-start(bf16[4,2,9216]{2,1,0:T(2,128)(2,1)} %reshape.593), calls=%async_computation | async-start | bytes 294912 | tf_op jit(solution)/shard_map/all_to_all | solution.py:196
  80.6 6.7 %collective-permute-start.7 = (f32[37,128]{1,0:T(8,128)S(1)}, f32[37,128]{1,0:T(8,128)S(1)}, u32[]{:S(2)}, u32[]{:S(2)}) collective-permute-start(f32[37,128]{1,0:T(8,128)S(1)} %pad_maximum_fusion.6), channel_id=1, source_target_pairs={{0,16},{4,20},{8,24},{12,28},{16,0},{20,4},{24,8},{28,12},{1,17},{... | collective-permute-start | bytes 56840 | tf_op jit(solution)/shard_map/ppermute | solution.py:19
  85.4 1.9 %copy-start.36 = (s32[3,128]{1,0:T(4,128)S(1)}, s32[3,128]{1,0:T(4,128)}, u32[]{:S(2)}) copy-start(s32[3,128]{1,0:T(4,128)} %param.11) | copy-start | bytes 4612

commit v12 on v11

--- a/solution.py
+++ b/solution.py
@@ -3,6 +3,7 @@
 import jax
 import jax.numpy as jnp
 from jax import lax
+from jax.experimental import pallas as pl
 from jax.sharding import PartitionSpec as P
 
 SOFTENING = 0.25
@@ -58,6 +59,46 @@
         sums.append(flat[start : start + extra.size].reshape(extra.shape))
         start += extra.size
     return value, sums
+
+
+def value_grad_kernel(weight_ref, feat_ref, radial_ref, harm_ref, harm_out, radial_out):
+    value_grad = lax.dot_general(
+        weight_ref[0],
+        feat_ref[0],
+        (((0,), (0,)), ((), ())),
+        preferred_element_type=jnp.float32,
+    )
+    radial = radial_ref[:, 0]
+    harmonics = harm_ref[:, 0]
+    value_grad = value_grad.reshape(harmonics.shape[0], radial.shape[0], *radial.shape[1:])
+    harm_out[:, 0] = jnp.sum(value_grad * radial[None], axis=1)
+    radial_out[:, 0] = jnp.sum(value_grad * harmonics[:, None], axis=0)
+
+
+def value_grad_sums(weighted, source_feat, radial, harmonics):
+    tiles, chans = weighted.shape[:2]
+    flat = weighted.reshape(tiles, chans, -1)
+    lanes = source_feat.shape[2]
+    radial_count, _, rows, _ = radial.shape
+    components = harmonics.shape[0]
+    return pl.pallas_call(
+        value_grad_kernel,
+        grid=(tiles,),
+        in_specs=[
+            pl.BlockSpec((1, chans, flat.shape[2]), lambda t: (t, 0, 0)),
+            pl.BlockSpec((1, chans, lanes), lambda t: (t, 0, 0)),
+            pl.BlockSpec((radial_count, 1, rows, lanes), lambda t: (0, t, 0, 0)),
+            pl.BlockSpec((components, 1, rows, lanes), lambda t: (0, t, 0, 0)),
+        ],
+        out_specs=[
+            pl.BlockSpec((components, 1, rows, lanes), lambda t: (0, t, 0, 0)),
+            pl.BlockSpec((radial_count, 1, rows, lanes), lambda t: (0, t, 0, 0)),
+        ],
+        out_shape=[
+            jax.ShapeDtypeStruct(harmonics.shape, jnp.float32),
+            jax.ShapeDtypeStruct(radial.shape, jnp.float32),
+        ],
+    )(flat, source_feat, radial, harmonics)
 
 
 def geometry(target_pos, source_pos, pair_keep, radial_count):
@@ -227,11 +268,7 @@
     grad_source = jnp.einsum(
         "tclki,lktij->tcj", weighted, pair_values, preferred_element_type=jnp.float32
     )
-    value_grad = jnp.einsum(
-        "tclki,tcj->lktij", weighted, source_feat, preferred_element_type=jnp.float32
-    )
-    harm_grad = jnp.sum(value_grad * radial[None], axis=1)
-    rad_grad = jnp.sum(value_grad * harmonics[:, None], axis=0)
+    harm_grad, rad_grad = value_grad_sums(weighted, source_feat, radial, harmonics)
     target_grad, source_grad_pos = pullback((harm_grad, rad_grad))
     grad_part = jnp.sum(
         source_hot[:, None, :, None] * grad_source[:, :, None, :], axis=0

time: 90.3 us -> 101 us (1.12)
  Pallas kernels: 0 us -> 8.03 us
  local copies, waits for them, and re-layouts: 24 us -> 26.7 us
  waiting for transfers between devices: 11.9 us -> 10 us
  starting transfers between devices: 18.2 us -> 19.5 us
    pallas_call x0 -> x1, Pallas kernels: none -> 8.03 us  [value_grad_sums(): pl.pallas_call(value_grad_kernel, grid=(tiles,), in_specs=[pl.BlockSpec((...]
    convert_element_type x0 -> x1, local copies, waits for them, and re-layouts: none -> 6.72 us  [body(): weighted = (live[:, None, None, None, None] * full_weight[None, :, None,...]
    reduce_sum x1 -> x0, other arithmetic: 5.28 us -> none  [body(): harm_grad = jnp.sum(value_grad * radial[None], axis=1)]
    convert_element_type x0 -> x1, other arithmetic: none -> 3.75 us  [body(): pair_values = (harmonics[:, None] * radial[None]).astype(jnp.bfloat16)]
    unnamed x90 -> x84, local copies, waits for them, and re-layouts: 7.24 us -> 4.33 us
    dot_general x1, matrix products: 2.98 us -> 5.26 us  [body(): jnp.einsum('lktij,tbcj->bclki', pair_values, routed_feat, preferred_eleme...]
    convert_element_type x1, other arithmetic: 1.36 us -> 3.52 us  [body(): weighted = (live[:, None, None, None, None] * full_weight[None, :, None,...]
    all_to_all x1, waiting for transfers between devices: 4.15 us -> 2.23 us  [body(): lax.all_to_all(result_rows.reshape(all_chan, components, own_blocks, 1, r...]
  transfers between devices with their start and end apart: 10 -> 10, of which waited for: 4 -> 4; matrix products, arithmetic and copies ran while one was open for 21% -> 24% of each run, Pallas kernels for 0% -> 0%
where the time goes in v12:
time: 101 us
  local copies, waits for them, and re-layouts  26.7 us (26%)
  other arithmetic  19.7 us (20%)
  starting transfers between devices  19.5 us (19%)
  waiting for transfers between devices  10 us (10%)
  matrix products  9.09 us (9%)
  Pallas kernels  8.03 us (8%)
  blocking collectives  5.87 us (6%)
  between operations  1.67 us (2%)
    ppermute x8, starting transfers between devices, partner(): return lax.ppermute(value, axis, pairs)  11.9 us
    pallas_call x1, Pallas kernels, value_grad_sums(): pl.pallas_call(value_grad_kernel, grid=(tiles,), in_specs=[pl.BlockSpec((...  8.03 us
    ppermute x8, waiting for transfers between devices, partner(): return lax.ppermute(value, axis, pairs)  7.79 us
    convert_element_type x1, local copies, waits for them, and re-layouts, body(): weighted = (live[:, None, None, None, None] * full_weight[None, :, None,...  6.72 us
    all_gather x1, blocking collectives, body(): lax.all_gather(jnp.concatenate([src_feat, weight_high, weight_mid, weight...  5.87 us
    dot_general x1, matrix products, body(): jnp.einsum('lktij,tbcj->bclki', pair_values, routed_feat, preferred_eleme...  5.26 us
    unnamed x84, local copies, waits for them, and re-layouts  4.33 us
    all_to_all x1, starting transfers between devices, body(): lax.all_to_all(out_grad.reshape(chan_dev, components, own_blocks, chan_co...  4.21 us
  transfers between devices with their start and end apart: 10, of which 4 were waited for; matrix products, arithmetic and copies ran while one was open for 24% of the time, Pallas kernels for 0%

profile of v12, /device:TPU:0, one launch (start us, length us, event | category | flops | bytes accessed | tf_op | source)
XLA Modules:
  0.0 100.6 jit_solution(14075440875311449755)
XLA Ops:
  0.6 1.3 %reshape.524 = bf16[32,9,2,4,32]{4,3,2,0,1:T(4,128)(2,1)S(1)} reshape(bf16[32,9,256]{2,0,1:T(8,128)(2,1)} %param.16) | data formatting | bytes 294912 | tf_op jit(solution)/shard_map/reshape | solution.py:245
  2.0 0.7 copy.179
  2.7 1.2 %reshape.598 = bf16[4,2,9216]{2,1,0:T(2,128)(2,1)} reshape(bf16[4,9,2,32,32]{4,3,2,1,0:T(8,128)(2,1)S(1)} %bitcast.335) | data formatting | bytes 294912
  3.9 4.2 %all-to-all-start.1 = ((bf16[4,2,9216]{2,1,0:T(2,128)(2,1)}), bf16[4,2,9216]{2,1,0:T(2,128)(2,1)S(1)}, u32[]{:S(2)}, u32[]{:S(2)}) async-start(bf16[4,2,9216]{2,1,0:T(2,128)(2,1)} %reshape.598), calls=%async_computation.1 | async-start | bytes 294912 | tf_op jit(solution)/shard_map/all_to_all | solution.py:244
  8.3 1.1 %gather_fusion = f32[384,35]{1,0:T(8,128)S(1)} fusion(f32[35,256]{0,1:T(8,128)S(1)} %copy.156, s32[1024]{0:T(1024)S(1)} %get-tuple-element.69), kind=kCustom, calls=%fused_computation | custom fusion | bytes 109056 | tf_op jit(solution)/shard_map/jit(_take)/gather | solution.py:157
  9.5 2.2 %collective-permute-start = (f32[35,128]{0,1:T(8,128)S(1)}, f32[35,128]{0,1:T(8,128)S(1)}, u32[]{:S(2)}, u32[]{:S(2)}) collective-permute-start(f32[35,128]{0,1:T(8,128)S(1)} %get-tuple-element.39), channel_id=1, source_target_pairs={{0,4},{4,0},{8,12},{12,8},{16,20},{20,16},{24,28},{28,24},{1,5},{5... | collective-permute-start | bytes 53768 | tf_op jit(solution)/shard_map/ppermute | solution.py:20
  11.7 1.6 %collective-permute-start.1 = (f32[35,128]{0,1:T(8,128)S(1)}, f32[35,128]{0,1:T(8,128)S(1)}, u32[]{:S(2)}, u32[]{:S(2)}) collective-permute-start(f32[35,128]{0,1:T(8,128)S(1)} %get-tuple-element.40), channel_id=1, source_target_pairs={{0,8},{4,12},{8,0},{12,4},{16,24},{20,28},{24,16},{28,20},{1,9},{5... | collective-permute-start | bytes 53768 | tf_op jit(solution)/shard_map/ppermute | solution.py:20
  13.3 2.6 %collective-permute-start.2 = (f32[35,128]{0,1:T(8,128)S(1)}, f32[35,128]{0,1:T(8,128)S(1)}, u32[]{:S(2)}, u32[]{:S(2)}) collective-permute-start(f32[35,128]{0,1:T(8,128)S(1)} %get-tuple-element.41), channel_id=1, source_target_pairs={{0,16},{4,20},{8,24},{12,28},{16,0},{20,4},{24,8},{28,12},{1,17},{... | collective-permute-start | bytes 53768 | tf_op jit(solution)/shard_map/ppermute | solution.py:20
  16.0 0.6 pad_clamp_fusion
  16.7 0.6 compare_convert_fusion
  17.6 0.7 copy.183
  18.3 0.7 copy.185
  19.0 0.6 gather_fusion.4
  20.0 5.9 %all_gather.3 = bf16[128,664]{1,0:T(8,128)(2,1)S(1)} all-gather(bf16[32,664]{1,0:T(8,128)(2,1)S(1)} %concatenate.53), channel_id=1, replica_groups=mesh['space'=8,'chan'=4] {'chan'}, dimensions={0}, use_global_device_ids=true | all-gather | bytes 212480 | tf_op jit(solution)/shard_map/all_gather | solution.py:178
  26.7 0.6 gather_fusion.3
  27.3 0.6 gather_fusion.2
  27.9 0.2 broadcast_subtract_fusion
  28.8 1.3 %fusion.14.radial_ref = f32[8,8,32,128]{3,2,1,0:T(8,128)} fusion(f32[8,32,128]{2,1,0:T(8,128)S(1)} %get-tuple-element.43, f32[8]{0:T(128)S(1)} %add_multiply_fusion, f32[8,32,128]{2,1,0:T(8,128)S(1)} %get-tuple-element.42), kind=kLoop, calls=%fused_computation.27 | loop fusion | flops 1048576 | bytes 1310752 | tf_op jit(solution)/shard_map/jvp()/mul | solution.py:127
  30.1 3.7 %multiply_convert_fusion.1 = bf16[9,8,8,32,128]{4,3,1,2,0:T(8,128)(2,1)} fusion(f32[9,8,32,128]{3,2,1,0:T(8,128)S(1)} %multiply_dynamic-update-slice_fusion.harm_ref, f32[8,32,128]{2,1,0:T(8,128)S(1)} %get-tuple-element.43, f32[8]{0:T(128)S(1)} %add_multiply_fusion, f32[8,32,128]{2,1,0:T(8,128)S(1)} %get-tuple-element.42), kind=kLoop, calls=%fused_computation.7 | loop fusion | flops 5767168 | bytes 6160416 | tf_op jit(solution)/shard_map/convert_element_type | solution.py:217
  33.8 0.2 copy.206
  34.0 0.2 copy.165
  34.2 0.6 gather_fusion.1
  34.8 5.3 %fusion.6 = (bf16[128,2,9,32]{0,3,2,1:T(8,128)(2,1)S(1)}, f32[2,128,9,8,32,1]{1,4,5,3,2,0:T(8,128)}) fusion(f32[128,8]{0,1:T(8,128)S(1)} %copy.207, bf16[9,8,8,32,128]{4,3,1,2,0:T(8,128)(2,1)} %multiply_convert_fusion.1, f32[8,128,128]{2,1,0:T(8,128)S(1)} %convert_element_type.110, f32[8,2]{0,1:T(2,128)S(1)} %copy.163), kind=kOutput, calls=%fused_computation.17 | convolution fusion | flops 1209589760 | bytes 7753792 | tf_op jit(solution)/shard_map/lktij,tbcj->bclki/dot_general | solution.py:221
  40.1 0.3 convolution_bitcast_fusion
  40.5 0.3 reshape.599
  40.9 0.8 copy.180
  41.8 0.5 reshape.536
  42.4 0.6 fusion.95
  43.0 0.7 multiply_convert_fusion.3
  43.7 0.2 fusion.24
  43.9 0.8 gather_fusion.5
  44.7 3.5 %multiply_convert_fusion = bf16[8,128,9,8,32]{1,4,3,2,0:T(8,128)(2,1)} fusion(f32[8,128,9,32]{1,3,2,0:T(8,128)S(1)} %gather_fusion.5, f32[8,128,8]{1,2,0:T(8,128)S(1)} %broadcast_multiply_fusion), kind=kLoop, calls=%fused_computation.6 | loop fusion | flops 4718592 | bytes 5931008 | tf_op jit(solution)/shard_map/convert_element_type | solution.py:267
  48.2 6.7 %copy.184.weight_ref = bf16[8,128,2304]{2,1,0:T(8,128)(2,1)} copy(bf16[8,128,2304]{1,2,0:T(8,128)(2,1)} %bitcast.334) | data formatting | bytes 9437184 | tf_op jit(solution)/shard_map/convert_element_type | solution.py:267
  54.9 8.0 %shard_map.120 = (f32[9,8,32,128]{3,2,1,0:T(8,128)}, f32[8,8,32,128]{3,2,1,0:T(8,128)}) custom-call(bf16[8,128,2304]{2,1,0:T(8,128)(2,1)} %copy.184.weight_ref, bf16[8,128,128]{2,1,0:T(8,128)(2,1)} %copy-done.4, f32[8,8,32,128]{3,2,1,0:T(8,128)} %fusion.14.radial_ref, f32[9,8,32,128]{3,2,1,0:T(8,128)} %copy-done.1), custom_call_target="tpu_custom_call" | custom-call | tf_op jit(solution)/shard_map/pallas_call | solution.py:84
  63.0 2.3 %fusion.73 = (f32[8,1,32,128]{3,2,0,1:T(8,128)}, f32[8,1,32,128]{3,2,0,1:T(8,128)}) fusion(f32[9,8,32,128]{3,2,1,0:T(8,128)} %get-tuple-element.6, f32[8,3,32,128]{3,2,0,1:T(8,128)S(1)} %get-tuple-element.49, f32[8,32,128]{2,1,0:T(8,128)S(1)} %get-tuple-element.50), kind=kLoop, calls=%fused_computation.119 | loop fusion | flops 950272 | bytes 1703936 | tf_op jit(solution)/shard_map/transpose(jvp())/div | solution.py:110
  65.3 0.8 fusion.38
  66.1 3.0 %fusion.7 = f32[8,128,128]{2,1,0:T(8,128)} fusion(f32[9,8,32,128]{3,2,1,0:T(8,128)S(1)} %copy-done.2, f32[8,128,9,32]{1,3,2,0:T(8,128)S(1)} %gather_fusion.5, f32[8,128,8]{1,2,0:T(8,128)S(1)} %copy-done.14, f32[8,32,128]{2,1,0:T(8,128)S(1)} %get-tuple-element.43, f32[8]{0:T(128)S(1)} %copy-done.29, f32[8,32,128]{2,1,0:T(8,128)S(1)} %get-tuple-element.42), kind=kOutput, calls=%fused_computation.20 | convolution fusion | flops 614465536 | bytes 3178528 | tf_op jit(solution)/shard_map/tclki,lktij->tcj/dot_general | solution.py:268
  69.1 0.3 fusion.5
  69.5 0.7 reshape.528
  70.3 1.1 %fusion.15 = (f32[8,32,128]{2,1,0:T(8,128)S(1)}, f32[8,32,128]{2,1,0:T(8,128)S(1)}) fusion(f32[8,8,32,128]{3,2,1,0:T(8,128)S(1)} %copy-done.6, f32[8]{0:T(128)} %copy-done.28, f32[8,32,128]{2,1,0:T(8,128)S(1)} %get-tuple-element.42, f32[8,32,128]{2,1,0:T(8,128)S(1)} %get-tuple-element.43), kind=kLoop, calls=%fused_computation.28 | loop fusion | flops 2818048 | bytes 1572896 | tf_op jit(solution)/shard_map/transpose(jvp())/reduce_sum | solution.py:127
  71.6 1.1 %fusion.50 = f32[8,32,128]{2,1,0:T(8,128)S(1)} fusion(f32[8,32,128]{2,1,0:T(8,128)S(1)} %get-tuple-element.29, f32[8,32,128]{2,1,0:T(8,128)S(1)} %get-tuple-element.28, f32[9,8,32,128]{3,2,1,0:T(8,128)S(1)} %copy-done.3, f32[8,3,32,128]{3,2,0,1:T(8,128)S(1)} %get-tuple-element.49, f32[8,32,128]{2,1,0:T(8,128)S(1)} %get-tuple-element.50, ...), kind=kLoop, calls=%fused_computation.78 | loop fusion | flops 2260992 | bytes 1982528 | tf_op jit(solution)/shard_map/transpose(jvp())/add_any | solution.py:107
  72.7 0.3 fusion.83
  73.5 0.3 multiply_reduce_fusion
  73.8 0.2 copy.182
  74.2 0.4 collective-permute-start.3
  74.7 1.1 %collective-permute-done.3 = f32[69,640]{1,0:T(8,128)S(1)} collective-permute-done((f32[69,640]{1,0:T(8,128)S(1)}, f32[69,640]{1,0:T(8,128)S(1)}, u32[]{:S(2)}, u32[]{:S(2)}) %collective-permute-start.3) | collective-permute-done | bytes 176672 | tf_op jit(solution)/shard_map/ppermute | solution.py:20
  75.8 1.8 %collective-permute-start.4 = (f32[37,640]{1,0:T(8,128)S(1)}, f32[37,640]{1,0:T(8,128)S(1)}, u32[]{:S(2)}, u32[]{:S(2)}) collective-permute-start(f32[37,640]{1,0:T(8,128)S(1)} %pad_maximum_fusion.2), channel_id=1, source_target_pairs={{0,2},{1,3},{2,0},{3,1},{4,6},{5,7},{6,4},{7,5},{8,10},{9,11},{10,... | collective-permute-start | bytes 284168 | tf_op jit(solution)/shard_map/ppermute | solution.py:20
  77.6 3.4 %collective-permute-done.4 = f32[37,640]{1,0:T(8,128)S(1)} collective-permute-done((f32[37,640]{1,0:T(8,128)S(1)}, f32[37,640]{1,0:T(8,128)S(1)}, u32[]{:S(2)}, u32[]{:S(2)}) %collective-permute-start.4) | collective-permute-done | bytes 94752 | tf_op jit(solution)/shard_map/ppermute | solution.py:20
  81.0 0.1 slice.182
  81.4 0.6 collective-permute-start.5
  81.9 3.3 %collective-permute-done.5 = f32[37,128]{1,0:T(8,128)S(1)} collective-permute-done((f32[37,128]{1,0:T(8,128)S(1)}, f32[37,128]{1,0:T(8,128)S(1)}, u32[]{:S(2)}, u32[]{:S(2)}) %collective-permute-start.5) | collective-permute-done | bytes 18976 | tf_op jit(solution)/shard_map/ppermute | solution.py:20
  85.4 0.5 collective-permute-start.6
  86.0 0.8 copy.176
  86.8 1.2 %reshape.596 = bf16[4,2,9216]{2,1,0:T(2,128)(2,1)} reshape(bf16[128,1,9,2,32]{4,3,2,1,0:T(2,128)(2,1)S(1)} %bitcast.336) | data formatting | bytes 294912
  88.0 3.3 %all-to-all-start = ((bf16[4,2,9216]{2,1,0:T(2,128)(2,1)}), bf16[4,2,9216]{2,1,0:T(2,128)(2,1)S(1)}, u32[]{:S(2)}, u32[]{:S(2)}) async-start(bf16[4,2,9216]{2,1,0:T(2,128)(2,1)} %reshape.596), calls=%async_computation | async-start | bytes 294912 | tf_op jit(solution)/shard_map/all_to_all | solution.py:237
  91.6 2.3 %collective-permute-start.7 = (f32[37,128]{1,0:T(8,128)S(1)}, f32[37,128]{1,0:T(8,128)S(1)}, u32[]{:S(2)}, u32[]{:S(2)}) collective-permute-start(f32[37,128]{1,0:T(8,128)S(1)} %pad_maximum_fusion.6), channel_id=1, source_target_pairs={{0,16},{4,20},{8,24},{12,28},{16,0},{20,4},{24,8},{28,12},{1,17},{... | collective-permute-start | bytes 56840 | tf_op jit(solution)/shard_map/ppermute | solution.py:20
  93.9 2.2 %all-to-all-done = bf16[4,2,9216]{2,1,0:T(2,128)(2,1)S(1)} async-done(((bf16[4,2,9216]{2,1,0:T(2,128)(2,1)}), bf16[4,2,9216]{2,1,0:T(2,128)(2,1)S(1)}, u32[]{:S(2)}, u32[]{:S(2)}) %all-to-all-start) | async-done | bytes 147488 | tf_op jit(solution)/shard_map/all_to_all | solution.py:237
  96.1 0.3 reshape.597
  96.4 0.8 copy.177
  97.2 1.1 %reshape.523 = bf16[32,9,256]{2,0,1:T(8,128)(2,1)} reshape(bf16[32,9,2,4,1,32]{5,3,2,0,1,4:T(4,128)(2,1)S(1)} %copy.177) | data formatting | bytes 294912 | tf_op jit(solution)/shard_map/reshape | solution.py:243
  98.3 0.3 maximum_add_fusion
  98.6 0.6 slice.342
  99.2 0.6 slice_negate_fusion
  99.9 0.7 copy.186
  (176 shorter events, 4.3 us)
Async XLA Ops:
  0.6 18.4 %copy-start = (bf16[3,128,128]{2,1,0:T(8,128)(2,1)S(1)}, bf16[3,128,128]{2,1,0:T(8,128)(2,1)}, u32[]{:S(2)}) copy-start(bf16[3,128,128]{2,1,0:T(8,128)(2,1)} %param.15) | copy-start | bytes 294916
  1.9 6.2 %copy-start.34 = (s32[8,2]{0,1:T(2,128)S(1)}, s32[8,2]{0,1:T(2,128)}, u32[]{:S(2)}) copy-start(s32[8,2]{0,1:T(2,128)} %param.12) | copy-start | bytes 196
  2.0 6.2 %copy-start.19 = (bf16[32,256]{1,0:T(8,128)(2,1)S(1)}, bf16[32,256]{1,0:T(8,128)(2,1)}, u32[]{:S(2)}) copy-start(bf16[32,256]{1,0:T(8,128)(2,1)} %param.10) | copy-start | bytes 49156
  2.0 6.2 %copy-start.23 = (f32[3,256]{1,0:T(4,128)S(1)}, f32[3,256]{1,0:T(4,128)}, u32[]{:S(2)}) copy-start(f32[3,256]{1,0:T(4,128)} %param.9) | copy-start | bytes 9220
  2.0 6.3 %copy-start.32 = (s32[3,128]{1,0:T(4,128)S(1)}, s32[3,128]{1,0:T(4,128)}, u32[]{:S(2)}) copy-start(s32[3,128]{1,0:T(4,128)} %param.11) | copy-start | bytes 4612
  2.7 13.2 %copy-start.30 = (f32[32,8]{0,1:T(8,128)S(1)}, f32[32,8]{0,1:T(8,128)}, u32[]{:S(2)}) copy-start(f32[32,8]{0,1:T(8,128)} %param.14) | copy-start | bytes 3076
  2.7 13.3 %copy-start.37 = (s32[8]{0:T(128)S(1)}, s32[8]{0:T(128)}, u32[]{:S(2)}) copy-start(s32[8]{0:T(128)} %param.13) | copy-start | bytes 100
  2.7 13.3 %copy-start.36 = (s32[9]{0:T(128)S(1)}, s32[9]{0:T(128)}, u32[]{:S(2)}) copy-start(s32[9]{0:T(128)} %constant.95) | copy-start | bytes 112
  3.9 36.6 %all-to-all-start.1 = ((bf16[4,2,9216]{2,1,0:T(2,128)(2,1)}), bf16[4,2,9216]{2,1,0:T(2,128)(2,1)S(1)}, u32[]{:S(2)}, u32[]{:S(2)}) async-start(bf16[4,2,9216]{2,1,0:T(2,128)(2,1)} %reshape.598), calls=%async_computation.1 | async-start | bytes 294912 | tf_op jit(solution)/shard_map/all_to_all | solution.py:244
  9.5 10.1 %collective-permute-start = (f32[35,128]{0,1:T(8,128)S(1)}, f32[35,128]{0,1:T(8,128)S(1)}, u32[]{:S(2)}, u32[]{:S(2)}) collective-permute-start(f32[35,128]{0,1:T(8,128)S(1)} %get-tuple-element.39), channel_id=1, source_target_pairs={{0,4},{4,0},{8,12},{12,8},{16,20},{20,16},{24,28},{28,24},{1,5},{5... | collective-permute-start | bytes 53768 | tf_op jit(solution)/shard_map/ppermute | solution.py:20
  11.7 8.0 %collective-permute-start.1 = (f32[35,128]{0,1:T(8,128)S(1)}, f32[35,128]{0,1:T(8,128)S(1)}, u32[]{:S(2)}, u32[]{:S(2)}) collective-permute-start(f32[35,128]{0,1:T(8,128)S(1)} %get-tuple-element.40), channel_id=1, source_target_pairs={{0,8},{4,12},{8,0},{12,4},{16,24},{20,28},{24,16},{28,20},{1,9},{5... | collective-permute-start | bytes 53768 | tf_op jit(solution)/shard_map/ppermute | solution.py:20
  13.3 6.6 %collective-permute-start.2 = (f32[35,128]{0,1:T(8,128)S(1)}, f32[35,128]{0,1:T(8,128)S(1)}, u32[]{:S(2)}, u32[]{:S(2)}) collective-permute-start(f32[35,128]{0,1:T(8,128)S(1)} %get-tuple-element.41), channel_id=1, source_target_pairs={{0,16},{4,20},{8,24},{12,28},{16,0},{20,4},{24,8},{28,12},{1,17},{... | collective-permute-start | bytes 53768 | tf_op jit(solution)/shard_map/ppermute | solution.py:20
  15.9 12.8 %copy-start.31 = (f32[8]{0:T(128)}, f32[8]{0:T(128)S(1)}, u32[]{:S(2)}) copy-start(f32[8]{0:T(128)S(1)} %compare_convert_fusion.1) | copy-start | bytes 100
  15.9 14.2 %copy-start.28 = (f32[8]{0:T(128)}, f32[8]{0:T(128)S(1)}, u32[]{:S(2)}) copy-start(f32[8]{0:T(128)S(1)} %add_multiply_fusion) | copy-start | bytes 100
  16.0 24.4 %copy-start.27 = (f32[8]{0:T(128)}, f32[8]{0:T(128)S(1)}, u32[]{:S(2)}) copy-start(f32[8]{0:T(128)S(1)} %convert_element_type.109) | copy-start | bytes 100
  16.7 9.6 %copy-start.21 = (f32[8,5]{1,0:T(8,128)}, f32[8,5]{1,0:T(8,128)S(1)}, u32[]{:S(2)}) copy-start(f32[8,5]{1,0:T(8,128)S(1)} %get-tuple-element.61) | copy-start | bytes 484
  25.9 2.2 %copy-start.7 = (bf16[128,664]{1,0:T(8,128)(2,1)}, bf16[128,664]{1,0:T(8,128)(2,1)S(1)}, u32[]{:S(2)}) copy-start(bf16[128,664]{1,0:T(8,128)(2,1)S(1)} %all_gather.3) | copy-start | bytes 509956
  27.3 1.0 %copy-start.15 = (f32[8,3,32]{2,0,1:T(8,128)}, f32[8,3,32]{2,0,1:T(8,128)S(1)}, u32[]{:S(2)}) copy-start(f32[8,3,32]{2,0,1:T(8,128)S(1)} %copy.172) | copy-start | bytes 9220
  27.9 0.6 copy-start.17
  28.7 5.2 %copy-start.1 = (f32[9,8,32,128]{3,2,1,0:T(8,128)}, f32[9,8,32,128]{3,2,1,0:T(8,128)S(1)}, u32[]{:S(2)}) copy-start(f32[9,8,32,128]{3,2,1,0:T(8,128)S(1)} %multiply_dynamic-update-slice_fusion.harm_ref) | copy-start | bytes 3538948
  30.1 3.8 %slice-start = ((bf16[128,664]{1,0:T(8,128)(2,1)}), bf16[128,640]{1,0:T(8,128)(2,1)S(1)}, s32[]{:S(2)}) async-start(bf16[128,664]{1,0:T(8,128)(2,1)} %copy-done.7), calls=%async_computation.2 | async-start | bytes 327680 | tf_op jit(solution)/shard_map/slice | solution.py:184
  34.8 5.3 %copy-start.4 = (bf16[8,128,128]{2,1,0:T(8,128)(2,1)}, bf16[8,128,128]{2,1,0:T(8,128)(2,1)S(1)}, u32[]{:S(2)}) copy-start(bf16[8,128,128]{2,1,0:T(8,128)(2,1)S(1)} %gather_fusion.1) | copy-start | bytes 786436
  40.5 4.2 %copy-start.13 = (f32[8,128,8]{1,2,0:T(8,128)}, f32[8,128,8]{1,2,0:T(8,128)S(1)}, u32[]{:S(2)}) copy-start(f32[8,128,8]{1,2,0:T(8,128)S(1)} %broadcast_multiply_fusion) | copy-start | bytes 98308
  63.0 2.3 %copy-start.3 = (f32[9,8,32,128]{3,2,1,0:T(8,128)S(1)}, f32[9,8,32,128]{3,2,1,0:T(8,128)}, u32[]{:S(2)}) copy-start(f32[9,8,32,128]{3,2,1,0:T(8,128)} %get-tuple-element.6) | copy-start | bytes 3538948
  63.0 3.1 %copy-start.2 = (f32[9,8,32,128]{3,2,1,0:T(8,128)S(1)}, f32[9,8,32,128]{3,2,1,0:T(8,128)}, u32[]{:S(2)}) copy-start(f32[9,8,32,128]{3,2,1,0:T(8,128)} %copy-done.1) | copy-start | bytes 3538948
  63.0 3.1 %copy-start.14 = (f32[8,128,8]{1,2,0:T(8,128)S(1)}, f32[8,128,8]{1,2,0:T(8,128)}, u32[]{:S(2)}) copy-start(f32[8,128,8]{1,2,0:T(8,128)} %copy-done.13) | copy-start | bytes 98308
  63.0 3.1 %copy-start.29 = (f32[8]{0:T(128)S(1)}, f32[8]{0:T(128)}, u32[]{:S(2)}) copy-start(f32[8]{0:T(128)} %copy-done.28) | copy-start | bytes 100
  66.1 3.0 %copy-start.5 = (f32[2,128,9,8,32,1]{1,4,5,3,2,0:T(8,128)S(1)}, f32[2,128,9,8,32,1]{1,4,5,3,2,0:T(8,128)}, u32[]{:S(2)}) copy-start(f32[2,128,9,8,32,1]{1,4,5,3,2,0:T(8,128)} %get-tuple-element.66) | copy-start | bytes 7077892
  69.1 1.2 %copy-start.6 = (f32[8,8,32,128]{3,2,1,0:T(8,128)S(1)}, f32[8,8,32,128]{3,2,1,0:T(8,128)}, u32[]{:S(2)}) copy-start(f32[8,8,32,128]{3,2,1,0:T(8,128)} %get-tuple-element.7) | copy-start | bytes 3145732
  71.4 1.3 %copy-start.10 = (f32[8,1,32,128]{3,2,0,1:T(8,128)S(1)}, f32[8,1,32,128]{3,2,0,1:T(8,128)}, u32[]{:S(2)}) copy-start(f32[8,1,32,128]{3,2,0,1:T(8,128)} %fusion.38) | copy-start | bytes 393220
  71.4 1.3 %copy-start.11 = (f32[8,1,32,128]{3,2,0,1:T(8,128)S(1)}, f32[8,1,32,128]{3,2,0,1:T(8,128)}, u32[]{:S(2)}) copy-start(f32[8,1,32,128]{3,2,0,1:T(8,128)} %get-tuple-element.32) | copy-start | bytes 393220
  71.5 1.3 %copy-start.12 = (f32[8,1,32,128]{3,2,0,1:T(8,128)S(1)}, f32[8,1,32,128]{3,2,0,1:T(8,128)}, u32[]{:S(2)}) copy-start(f32[8,1,32,128]{3,2,0,1:T(8,128)} %get-tuple-element.33) | copy-start | bytes 393220
  71.5 1.3 %copy-start.16 = (f32[8,3,32]{2,0,1:T(8,128)S(1)}, f32[8,3,32]{2,0,1:T(8,128)}, u32[]{:S(2)}) copy-start(f32[8,3,32]{2,0,1:T(8,128)} %copy-done.15) | copy-start | bytes 9220
  71.5 1.3 %copy-start.18 = (f32[8,3,128]{2,0,1:T(8,128)S(1)}, f32[8,3,128]{2,0,1:T(8,128)}, u32[]{:S(2)}) copy-start(f32[8,3,128]{2,0,1:T(8,128)} %copy-done.17) | copy-start | bytes 36868
  71.5 1.6 %copy-start.26 = (f32[8,5]{0,1:T(8,128)S(1)}, f32[8,5]{0,1:T(8,128)}, u32[]{:S(2)}) copy-start(f32[8,5]{0,1:T(8,128)} %copy.183) | copy-start | bytes 484
  71.5 1.7 %copy-start.35 = (f32[4]{0:T(128)S(1)}, f32[4]{0:T(128)}, u32[]{:S(2)}) copy-start(f32[4]{0:T(128)} %compare_convert_fusion) | copy-start | bytes 52
  71.5 1.9 %copy-start.25 = (f32[8,5]{0,1:T(8,128)S(1)}, f32[8,5]{0,1:T(8,128)}, u32[]{:S(2)}) copy-start(f32[8,5]{0,1:T(8,128)} %copy.185) | copy-start | bytes 484
  71.5 2.0 %copy-start.24 = (f32[1024]{0:T(1024)S(1)}, f32[1024]{0:T(1024)}, u32[]{:S(2)}) copy-start(f32[1024]{0:T(1024)} %reshape.528) | copy-start | bytes 12292
  71.5 2.0 %copy-start.9 = (f32[8,128,128]{2,1,0:T(8,128)S(1)}, f32[8,128,128]{2,1,0:T(8,128)}, u32[]{:S(2)}) copy-start(f32[8,128,128]{2,1,0:T(8,128)} %fusion.7) | copy-start | bytes 1572868
  71.5 2.0 %copy-start.22 = (f32[8,5]{1,0:T(8,128)S(1)}, f32[8,5]{1,0:T(8,128)}, u32[]{:S(2)}) copy-start(f32[8,5]{1,0:T(8,128)} %copy-done.21) | copy-start | bytes 484
  74.2 11.7 %copy-start.8 = (bf16[128,8,2,1,32]{0,4,2,1,3:T(8,128)(2,1)S(1)}, bf16[128,8,2,1,32]{0,4,2,1,3:T(8,128)(2,1)}, u32[]{:S(2)}) copy-start(bf16[128,8,2,1,32]{0,4,2,1,3:T(8,128)(2,1)} %get-tuple-element.48) | copy-start | bytes 393220
  74.2 11.7 %copy-start.20 = (bf16[128,1,2,1,32]{0,4,2,1,3:T(8,128)(2,1)S(1)}, bf16[128,1,2,1,32]{0,4,2,1,3:T(8,128)(2,1)}, u32[]{:S(2)}) copy-start(bf16[128,1,2,1,32]{0,4,2,1,3:T(8,128)(2,1)} %get-tuple-element.37) | copy-start | bytes 49156
  74.2 1.5 %collective-permute-start.3 = (f32[69,640]{1,0:T(8,128)S(1)}, f32[69,640]{1,0:T(8,128)S(1)}, u32[]{:S(2)}, u32[]{:S(2)}) collective-permute-start(f32[69,640]{1,0:T(8,128)S(1)} %pad_maximum_fusion), channel_id=1, source_target_pairs={{0,1},{1,0},{2,3},{3,2},{4,5},{5,4},{6,7},{7,6},{8,9},{9,8},{10,11... | collective-permute-start | bytes 529928 | tf_op jit(solution)/shard_map/ppermute | solution.py:20
  75.8 5.2 %collective-permute-start.4 = (f32[37,640]{1,0:T(8,128)S(1)}, f32[37,640]{1,0:T(8,128)S(1)}, u32[]{:S(2)}, u32[]{:S(2)}) collective-permute-start(f32[37,640]{1,0:T(8,128)S(1)} %pad_maximum_fusion.2), channel_id=1, source_target_pairs={{0,2},{1,3},{2,0},{3,1},{4,6},{5,7},{6,4},{7,5},{8,10},{9,11},{10,... | collective-permute-start | bytes 284168 | tf_op jit(solution)/shard_map/ppermute | solution.py:20
  81.4 3.8 %collective-permute-start.5 = (f32[37,128]{1,0:T(8,128)S(1)}, f32[37,128]{1,0:T(8,128)S(1)}, u32[]{:S(2)}, u32[]{:S(2)}) collective-permute-start(f32[37,128]{1,0:T(8,128)S(1)} %pad_maximum_fusion.4), channel_id=1, source_target_pairs={{0,4},{4,0},{8,12},{12,8},{16,20},{20,16},{24,28},{28,24},{1,5},{5... | collective-permute-start | bytes 56840 | tf_op jit(solution)/shard_map/ppermute | solution.py:20
  85.4 5.9 %collective-permute-start.6 = (f32[37,128]{1,0:T(8,128)S(1)}, f32[37,128]{1,0:T(8,128)S(1)}, u32[]{:S(2)}, u32[]{:S(2)}) collective-permute-start(f32[37,128]{1,0:T(8,128)S(1)} %pad_maximum_fusion.5), channel_id=1, source_target_pairs={{0,8},{4,12},{8,0},{12,4},{16,24},{20,28},{24,16},{28,20},{1,9},{5... | collective-permute-start | bytes 56840 | tf_op jit(solution)/shard_map/ppermute | solution.py:20
  88.0 8.1 %all-to-all-start = ((bf16[4,2,9216]{2,1,0:T(2,128)(2,1)}), bf16[4,2,9216]{2,1,0:T(2,128)(2,1)S(1)}, u32[]{:S(2)}, u32[]{:S(2)}) async-start(bf16[4,2,9216]{2,1,0:T(2,128)(2,1)} %reshape.596), calls=%async_computation | async-start | bytes 294912 | tf_op jit(solution)/shard_map/all_to_all | solution.py:237
  91.6 6.7 %collective-permute-start.7 = (f32[37,128]{1,0:T(8,128)S(1)}, f32[37,128]{1,0:T(8,128)S(1)}, u32[]{:S(2)}, u32[]{:S(2)}) collective-permute-start(f32[37,128]{1,0:T(8,128)S(1)} %pad_maximum_fusion.6), channel_id=1, source_target_pairs={{0,16},{4,20},{8,24},{12,28},{16,0},{20,4},{24,8},{28,12},{1,17},{... | collective-permute-start | bytes 56840 | tf_op jit(solution)/shard_map/ppermute | solution.py:20
  96.4 1.9 %copy-start.33 = (s32[3,128]{1,0:T(4,128)S(1)}, s32[3,128]{1,0:T(4,128)}, u32[]{:S(2)}) copy-start(s32[3,128]{1,0:T(4,128)} %param.11) | copy-start | bytes 4612

commit v13 on v11

--- a/solution.py
+++ b/solution.py
@@ -113,11 +113,13 @@
     chan_index = lax.axis_index("chan")
     pos_list = [positions]
     feat_list = [features]
-    both_rows = jnp.take(
+    send_hot = (
+        jnp.arange(atoms_dev, dtype=jnp.int32)[:, None] == send_rows[:levels].reshape(1, -1)
+    ).astype(jnp.float32)
+    both_rows = jnp.dot(
         jnp.concatenate([features.astype(jnp.float32), positions], axis=0),
-        send_rows[:levels].reshape(-1),
-        axis=1,
-        mode="clip",
+        send_hot,
+        precision=lax.Precision.HIGHEST,
     )
     for level_bit in range(levels):
         got_both = partner(

time: 90.3 us -> 88.2 us (0.977)
  local copies, waits for them, and re-layouts: 24 us -> 22.3 us
  other arithmetic: 19 us -> 17.7 us
  matrix products: 8.75 us -> 9.7 us
    gather x1 -> x0, local copies, waits for them, and re-layouts: 1.12 us -> none  [body(): jnp.take(jnp.concatenate([features.astype(jnp.float32), positions], axis=...]
    reshape x2, local copies, waits for them, and re-layouts: 0.93 us -> 1.93 us  [body(): out_grad.reshape(chan_dev, components, own_blocks, chan_count, rows)]
    dot_general x0 -> x1, matrix products: none -> 0.95 us  [body(): jnp.dot(jnp.concatenate([features.astype(jnp.float32), positions], axis=0...]
    unnamed x90 -> x88, local copies, waits for them, and re-layouts: 7.24 us -> 7.25 us
  transfers between devices with their start and end apart: 10 -> 10, of which waited for: 4 -> 4; matrix products, arithmetic and copies ran while one was open for 21% -> 22% of each run, Pallas kernels for 0% -> 0%
where the time goes in v13:
time: 88.2 us; the launch traced here: 87.5 us
  local copies, waits for them, and re-layouts  22.3 us (25%)
  starting transfers between devices  18.3 us (21%)
  other arithmetic  17.7 us (20%)
  waiting for transfers between devices  11.9 us (13%)
  matrix products  9.7 us (11%)
  blocking collectives  5.85 us (7%)
  between operations  1.65 us (2%)
    ppermute x8, starting transfers between devices, partner(): return lax.ppermute(value, axis, pairs)  10.9 us
    ppermute x8, waiting for transfers between devices, partner(): return lax.ppermute(value, axis, pairs)  7.8 us
    unnamed x88, local copies, waits for them, and re-layouts  7.25 us
    all_gather x1, blocking collectives, body(): lax.all_gather(jnp.concatenate([src_feat, weight_high, weight_mid, weight...  5.85 us
    reduce_sum x1, other arithmetic, body(): harm_grad = jnp.sum(value_grad * radial[None], axis=1)  5.25 us
    all_to_all x1, waiting for transfers between devices, body(): lax.all_to_all(result_rows.reshape(all_chan, components, own_blocks, 1, r...  4.15 us
    all_to_all x1, starting transfers between devices, body(): lax.all_to_all(out_grad.reshape(chan_dev, components, own_blocks, chan_co...  4.09 us
    all_to_all x1, starting transfers between devices, body(): lax.all_to_all(result_rows.reshape(all_chan, components, own_blocks, 1, r...  3.34 us
  transfers between devices with their start and end apart: 10, of which 4 were waited for; matrix products, arithmetic and copies ran while one was open for 22% of the time, Pallas kernels for 0%

profile of v13, /device:TPU:0, one launch (start us, length us, event | category | flops | bytes accessed | tf_op | source)
XLA Modules:
  0.0 87.5 jit_solution(10216764653302740388)
XLA Ops:
  0.6 0.8 convert_element_type.99
  1.4 1.0 %fusion.26 = f32[35,384]{1,0:T(8,128)S(1)} fusion(s32[384]{0:T(512)} %bitcast.388, f32[3,256]{1,0:T(4,128)} %param.9, f32[32,256]{1,0:T(8,128)S(1)} %convert_element_type.99), kind=kOutput, calls=%fused_computation.42 | convolution fusion | flops 41394944 | bytes 91136 | tf_op jit(solution)/shard_map/dot_general | solution.py:119
  2.4 3.0 %collective-permute-start = (f32[35,128]{1,0:T(8,128)S(1)}, f32[35,128]{1,0:T(8,128)S(1)}, u32[]{:S(2)}, u32[]{:S(2)}) collective-permute-start(f32[35,128]{1,0:T(8,128)S(1)} %get-tuple-element.42), channel_id=1, source_target_pairs={{0,4},{4,0},{8,12},{12,8},{16,20},{20,16},{24,28},{28,24},{1,5},{5... | collective-permute-start | bytes 53768 | tf_op jit(solution)/shard_map/ppermute | solution.py:19
  5.4 2.6 %collective-permute-start.2 = (f32[35,128]{1,0:T(8,128)S(1)}, f32[35,128]{1,0:T(8,128)S(1)}, u32[]{:S(2)}, u32[]{:S(2)}) collective-permute-start(f32[35,128]{1,0:T(8,128)S(1)} %get-tuple-element.43), channel_id=1, source_target_pairs={{0,16},{4,20},{8,24},{12,28},{16,0},{20,4},{24,8},{28,12},{1,17},{... | collective-permute-start | bytes 53768 | tf_op jit(solution)/shard_map/ppermute | solution.py:19
  8.0 1.6 %collective-permute-start.1 = (f32[35,128]{1,0:T(8,128)S(1)}, f32[35,128]{1,0:T(8,128)S(1)}, u32[]{:S(2)}, u32[]{:S(2)}) collective-permute-start(f32[35,128]{1,0:T(8,128)S(1)} %get-tuple-element.44), channel_id=1, source_target_pairs={{0,8},{4,12},{8,0},{12,4},{16,24},{20,28},{24,16},{28,20},{1,9},{5... | collective-permute-start | bytes 53768 | tf_op jit(solution)/shard_map/ppermute | solution.py:19
  9.6 1.3 %reshape.519 = bf16[32,9,2,4,32]{4,3,2,0,1:T(4,128)(2,1)S(1)} reshape(bf16[32,9,256]{2,0,1:T(8,128)(2,1)} %param.16) | data formatting | bytes 294912 | tf_op jit(solution)/shard_map/reshape | solution.py:206
  10.9 0.7 copy.177
  11.6 1.2 %reshape.586 = bf16[4,2,9216]{2,1,0:T(2,128)(2,1)} reshape(bf16[4,9,2,32,32]{4,3,2,1,0:T(8,128)(2,1)S(1)} %bitcast.376) | data formatting | bytes 294912
  12.8 4.1 %all-to-all-start.1 = ((bf16[4,2,9216]{2,1,0:T(2,128)(2,1)}), bf16[4,2,9216]{2,1,0:T(2,128)(2,1)}, u32[]{:S(2)}, u32[]{:S(2)}) async-start(bf16[4,2,9216]{2,1,0:T(2,128)(2,1)} %reshape.586), calls=%async_computation.1 | async-start | bytes 294912 | tf_op jit(solution)/shard_map/all_to_all | solution.py:205
  17.0 0.6 compare_convert_fusion
  17.7 0.6 pad_clamp_fusion
  18.5 0.7 copy.182
  19.2 0.7 copy.190
  20.1 0.6 gather_fusion.3
  20.9 5.9 %all_gather.3 = bf16[128,664]{1,0:T(8,128)(2,1)S(1)} all-gather(bf16[32,664]{1,0:T(8,128)(2,1)S(1)} %concatenate.53), channel_id=1, replica_groups=mesh['space'=8,'chan'=4] {'chan'}, dimensions={0}, use_global_device_ids=true | all-gather | bytes 212480 | tf_op jit(solution)/shard_map/all_gather | solution.py:139
  26.8 0.6 gather_fusion.1
  27.5 0.6 gather_fusion.2
  28.6 0.6 gather_fusion
  30.1 0.8 copy-done.10
  30.8 0.3 fusion.17
  31.1 3.0 %fusion.7 = (bf16[128,2,9,32]{0,3,2,1:T(8,128)(2,1)S(1)}, f32[2,128,9,8,32,1]{1,4,5,3,2,0:T(8,128)}) fusion(f32[128,8]{0,1:T(8,128)S(1)} %copy.219, f32[8,128,128]{2,1,0:T(8,128)S(1)} %convert_element_type.107, f32[8,2]{0,1:T(2,128)S(1)} %copy.164, f32[8,8,32,128]{3,2,0,1:T(8,128)S(1)} %fusion.17, f32[9,8,32,128]{3,2,1,0:T(8,128)S(1)} %multiply_dynamic-update-slice_fusion), kind=kOutput, calls=%fused_computation.19 | convolution fusion | flops 1214308352 | bytes 5263424 | tf_op jit(solution)/shard_map/lktij,tbcj->bclki/dot_general | solution.py:182
  34.1 1.0 %convolution_bitcast_fusion = f32[128,9,2,32]{0,3,2,1:T(8,128)} fusion(bf16[9,128,128]{2,1,0:T(8,128)(2,1)S(1)} %gather_fusion.3, bf16[128,2,9,32]{0,3,2,1:T(8,128)(2,1)S(1)} %get-tuple-element.63), kind=kOutput, calls=%fused_computation.24 | convolution fusion | flops 18874368 | bytes 737280 | tf_op jit(solution)/shard_map/lxc,clbi->xlbi/dot_general | solution.py:189
  35.2 0.7 broadcast_multiply_fusion
  35.9 1.3 %reshape.587 = bf16[4,9,2,32,32]{4,3,2,1,0:T(8,128)(2,1)S(1)} reshape(bf16[4,2,9216]{2,1,0:T(2,128)(2,1)} %all-to-all-done.1) | data formatting | bytes 294912
  37.3 0.8 copy.178
  38.1 0.5 reshape.531
  38.7 0.4 copy-done.4
  39.1 0.6 fusion.103
  39.8 0.7 multiply_convert_fusion.3
  40.5 0.2 fusion.28
  40.7 0.9 %gather_fusion.4 = f32[8,128,9,32]{1,3,2,0:T(8,128)S(1)} fusion(f32[2,128,9,32]{1,3,0,2:T(8,128)S(1)} %bitcast.373, s32[1024]{0:T(1024)} %get-tuple-element.61), kind=kCustom, calls=%fused_computation.4 | custom fusion | bytes 2359328 | tf_op jit(solution)/shard_map/jit(_take)/gather | solution.py:223
  41.6 1.4 %multiply_convert_fusion = bf16[8,128,9,8,32]{1,4,3,2,0:T(8,128)(2,1)S(1)} fusion(f32[8,128,9,32]{1,3,2,0:T(8,128)S(1)} %gather_fusion.4, f32[8,128,8]{1,2,0:T(8,128)S(1)} %copy-done.16), kind=kLoop, calls=%fused_computation.7 | loop fusion | flops 4718592 | bytes 5931008 | tf_op jit(solution)/shard_map/convert_element_type | solution.py:228
  43.2 2.8 %fusion.8 = f32[8,128,128]{2,1,0:T(8,128)} fusion(bf16[8,128,9,8,32]{1,4,3,2,0:T(8,128)(2,1)S(1)} %multiply_convert_fusion, f32[8,8,32,128]{3,2,0,1:T(8,128)S(1)} %copy-done.2, f32[9,8,32,128]{3,2,1,0:T(8,128)S(1)} %copy-done.7), kind=kOutput, calls=%fused_computation.22 | convolution fusion | flops 608698368 | bytes 7471104 | tf_op jit(solution)/shard_map/tclki,lktij->tcj/dot_general | solution.py:229
  46.0 1.4 %fusion.121 = f32[8,128,2304]{1,2,0:S(1)} fusion(bf16[8,128,2304]{1,2,0:T(8,128)(2,1)S(1)} %bitcast.375, bf16[8,128,128]{2,1,0:T(8,128)(2,1)S(1)} %gather_fusion), kind=kOutput, calls=%fused_computation.238 | convolution fusion | flops 603979776 | bytes 14417920
  47.4 5.3 %multiply_reduce_fusion.1 = (f32[9,8,32,128]{3,2,0,1:T(8,128)S(1)}, f32[8,8,32,128]{3,2,0,1:T(8,128)}) fusion(f32[9,8,8,32,128]{4,3,1,0,2:T(8,128)S(1)} %bitcast.374, f32[8,8,32,128]{3,2,0,1:T(8,128)S(1)} %copy-done.2, f32[9,8,32,128]{3,2,1,0:T(8,128)} %copy-done.6), kind=kLoop, calls=%fused_computation.6 | loop fusion | flops 8880128 | bytes 13893632 | tf_op jit(solution)/shard_map/reduce_sum | solution.py:235
  52.7 0.8 fusion.43
  53.4 0.9 %fusion.76 = (f32[8,1,32,128]{3,2,0,1:T(8,128)}, f32[8,1,32,128]{3,2,0,1:T(8,128)}) fusion(f32[9,8,32,128]{3,2,0,1:T(8,128)S(1)} %get-tuple-element.24, f32[8,3,32,128]{3,2,0,1:T(8,128)S(1)} %get-tuple-element.47, f32[8,32,128]{2,1,0:T(8,128)S(1)} %get-tuple-element.48), kind=kLoop, calls=%fused_computation.117 | loop fusion | flops 950272 | bytes 1703936 | tf_op jit(solution)/shard_map/transpose(jvp())/div | solution.py:69
  54.4 0.3 fusion.6
  55.1 1.5 %multiply_reduce_fusion.2 = f32[128,5,128]{2,0,1:T(8,128)S(1)} fusion(f32[8,128,128]{2,1,0:T(8,128)} %fusion.8, f32[8,5]{1,0:T(8,128)S(1)} %copy-done.24), kind=kLoop, calls=%fused_computation.15 | loop fusion | flops 1228800 | bytes 852128 | tf_op jit(solution)/shard_map/reduce_sum | solution.py:238
  56.5 1.0 %copy.181 = f32[128,5,128]{2,1,0:T(8,128)} copy(f32[128,5,128]{2,0,1:T(8,128)S(1)} %multiply_reduce_fusion.2) | data formatting | bytes 655360 | tf_op jit(solution)/shard_map/reduce_sum | solution.py:238
  57.6 1.1 %reshape_reshape.13 = f32[2,2,32,640]{3,2,1,0:T(8,128)S(1)} reshape(f32[128,5,128]{2,1,0:T(8,128)} %copy.181) | data formatting | bytes 655360 | tf_op jit(solution)/shard_map/reshape;reshape | solution.py:46
  58.7 0.5 fusion.18
  59.4 0.3 fusion.55
  59.7 0.5 copy-done.13
  60.3 0.3 fusion.88
  61.1 0.4 collective-permute-start.3
  61.5 1.1 %collective-permute-done.3 = f32[69,640]{1,0:T(8,128)S(1)} collective-permute-done((f32[69,640]{1,0:T(8,128)S(1)}, f32[69,640]{1,0:T(8,128)S(1)}, u32[]{:S(2)}, u32[]{:S(2)}) %collective-permute-start.3) | collective-permute-done | bytes 176672 | tf_op jit(solution)/shard_map/ppermute | solution.py:19
  62.7 1.8 %collective-permute-start.4 = (f32[37,640]{1,0:T(8,128)S(1)}, f32[37,640]{1,0:T(8,128)S(1)}, u32[]{:S(2)}, u32[]{:S(2)}) collective-permute-start(f32[37,640]{1,0:T(8,128)S(1)} %pad_maximum_fusion.2), channel_id=1, source_target_pairs={{0,2},{1,3},{2,0},{3,1},{4,6},{5,7},{6,4},{7,5},{8,10},{9,11},{10,... | collective-permute-start | bytes 284168 | tf_op jit(solution)/shard_map/ppermute | solution.py:19
  64.5 3.4 %collective-permute-done.4 = f32[37,640]{1,0:T(8,128)S(1)} collective-permute-done((f32[37,640]{1,0:T(8,128)S(1)}, f32[37,640]{1,0:T(8,128)S(1)}, u32[]{:S(2)}, u32[]{:S(2)}) %collective-permute-start.4) | collective-permute-done | bytes 94752 | tf_op jit(solution)/shard_map/ppermute | solution.py:19
  68.2 0.6 collective-permute-start.5
  68.8 3.3 %collective-permute-done.5 = f32[37,128]{1,0:T(8,128)S(1)} collective-permute-done((f32[37,128]{1,0:T(8,128)S(1)}, f32[37,128]{1,0:T(8,128)S(1)}, u32[]{:S(2)}, u32[]{:S(2)}) %collective-permute-start.5) | collective-permute-done | bytes 18976 | tf_op jit(solution)/shard_map/ppermute | solution.py:19
  72.3 0.5 collective-permute-start.6
  72.8 0.8 copy.174
  73.7 1.2 %reshape.584 = bf16[4,2,9216]{2,1,0:T(2,128)(2,1)} reshape(bf16[128,1,9,2,32]{4,3,2,1,0:T(2,128)(2,1)S(1)} %bitcast.377) | data formatting | bytes 294912
  74.9 3.3 %all-to-all-start = ((bf16[4,2,9216]{2,1,0:T(2,128)(2,1)}), bf16[4,2,9216]{2,1,0:T(2,128)(2,1)S(1)}, u32[]{:S(2)}, u32[]{:S(2)}) async-start(bf16[4,2,9216]{2,1,0:T(2,128)(2,1)} %reshape.584), calls=%async_computation | async-start | bytes 294912 | tf_op jit(solution)/shard_map/all_to_all | solution.py:198
  78.5 0.4 collective-permute-start.7
  78.9 4.1 %all-to-all-done = bf16[4,2,9216]{2,1,0:T(2,128)(2,1)S(1)} async-done(((bf16[4,2,9216]{2,1,0:T(2,128)(2,1)}), bf16[4,2,9216]{2,1,0:T(2,128)(2,1)S(1)}, u32[]{:S(2)}, u32[]{:S(2)}) %all-to-all-start) | async-done | bytes 147488 | tf_op jit(solution)/shard_map/all_to_all | solution.py:198
  83.0 0.3 reshape.585
  83.3 0.8 copy.175
  84.1 1.1 %reshape.518 = bf16[32,9,256]{2,0,1:T(8,128)(2,1)} reshape(bf16[32,9,2,4,1,32]{5,3,2,0,1,4:T(4,128)(2,1)S(1)} %copy.175) | data formatting | bytes 294912 | tf_op jit(solution)/shard_map/reshape | solution.py:204
  85.2 0.3 maximum_add_fusion
  85.5 0.6 slice_negate_fusion
  86.1 0.6 slice.337
  86.8 0.7 copy.191
  (170 shorter events, 4.3 us)
Async XLA Ops:
  0.6 19.5 %copy-start = (bf16[3,128,128]{2,1,0:T(8,128)(2,1)S(1)}, bf16[3,128,128]{2,1,0:T(8,128)(2,1)}, u32[]{:S(2)}) copy-start(bf16[3,128,128]{2,1,0:T(8,128)(2,1)} %param.15) | copy-start | bytes 294916
  2.4 18.3 %collective-permute-start = (f32[35,128]{1,0:T(8,128)S(1)}, f32[35,128]{1,0:T(8,128)S(1)}, u32[]{:S(2)}, u32[]{:S(2)}) collective-permute-start(f32[35,128]{1,0:T(8,128)S(1)} %get-tuple-element.42), channel_id=1, source_target_pairs={{0,4},{4,0},{8,12},{12,8},{16,20},{20,16},{24,28},{28,24},{1,5},{5... | collective-permute-start | bytes 53768 | tf_op jit(solution)/shard_map/ppermute | solution.py:19
  5.4 15.3 %collective-permute-start.2 = (f32[35,128]{1,0:T(8,128)S(1)}, f32[35,128]{1,0:T(8,128)S(1)}, u32[]{:S(2)}, u32[]{:S(2)}) collective-permute-start(f32[35,128]{1,0:T(8,128)S(1)} %get-tuple-element.43), channel_id=1, source_target_pairs={{0,16},{4,20},{8,24},{12,28},{16,0},{20,4},{24,8},{28,12},{1,17},{... | collective-permute-start | bytes 53768 | tf_op jit(solution)/shard_map/ppermute | solution.py:19
  8.0 12.8 %collective-permute-start.1 = (f32[35,128]{1,0:T(8,128)S(1)}, f32[35,128]{1,0:T(8,128)S(1)}, u32[]{:S(2)}, u32[]{:S(2)}) collective-permute-start(f32[35,128]{1,0:T(8,128)S(1)} %get-tuple-element.44), channel_id=1, source_target_pairs={{0,8},{4,12},{8,0},{12,4},{16,24},{20,28},{24,16},{28,20},{1,9},{5... | collective-permute-start | bytes 53768 | tf_op jit(solution)/shard_map/ppermute | solution.py:19
  10.8 6.1 %copy-start.35 = (s32[8,2]{0,1:T(2,128)S(1)}, s32[8,2]{0,1:T(2,128)}, u32[]{:S(2)}) copy-start(s32[8,2]{0,1:T(2,128)} %param.12) | copy-start | bytes 196
  10.8 6.7 %copy-start.39 = (s32[8]{0:T(128)S(1)}, s32[8]{0:T(128)}, u32[]{:S(2)}) copy-start(s32[8]{0:T(128)} %param.13) | copy-start | bytes 100
  10.9 6.8 %copy-start.30 = (f32[32,8]{0,1:T(8,128)S(1)}, f32[32,8]{0,1:T(8,128)}, u32[]{:S(2)}) copy-start(f32[32,8]{0,1:T(8,128)} %param.14) | copy-start | bytes 3076
  10.9 6.8 %copy-start.37 = (s32[9]{0:T(128)S(1)}, s32[9]{0:T(128)}, u32[]{:S(2)}) copy-start(s32[9]{0:T(128)} %constant.95) | copy-start | bytes 112
  11.6 9.2 %copy-start.21 = (bf16[32,256]{1,0:T(8,128)(2,1)S(1)}, bf16[32,256]{1,0:T(8,128)(2,1)}, u32[]{:S(2)}) copy-start(bf16[32,256]{1,0:T(8,128)(2,1)} %param.10) | copy-start | bytes 49156
  12.8 14.0 %copy-start.29 = (f32[3,256]{1,0:T(4,128)S(1)}, f32[3,256]{1,0:T(4,128)}, u32[]{:S(2)}) copy-start(f32[3,256]{1,0:T(4,128)} %param.9) | copy-start | bytes 9220
  12.8 23.0 %all-to-all-start.1 = ((bf16[4,2,9216]{2,1,0:T(2,128)(2,1)}), bf16[4,2,9216]{2,1,0:T(2,128)(2,1)}, u32[]{:S(2)}, u32[]{:S(2)}) async-start(bf16[4,2,9216]{2,1,0:T(2,128)(2,1)} %reshape.586), calls=%async_computation.1 | async-start | bytes 294912 | tf_op jit(solution)/shard_map/all_to_all | solution.py:205
  16.9 13.0 %copy-start.31 = (f32[8]{0:T(128)}, f32[8]{0:T(128)S(1)}, u32[]{:S(2)}) copy-start(f32[8]{0:T(128)S(1)} %compare_convert_fusion.1) | copy-start | bytes 100
  17.6 17.6 %copy-start.27 = (f32[8]{0:T(128)}, f32[8]{0:T(128)S(1)}, u32[]{:S(2)}) copy-start(f32[8]{0:T(128)S(1)} %convert_element_type.106) | copy-start | bytes 100
  17.7 2.4 %copy-start.23 = (f32[8,5]{1,0:T(8,128)}, f32[8,5]{1,0:T(8,128)S(1)}, u32[]{:S(2)}) copy-start(f32[8,5]{1,0:T(8,128)S(1)} %get-tuple-element.59) | copy-start | bytes 484
  18.4 11.7 %copy-start.33 = (f32[8]{0:T(128)}, f32[8]{0:T(128)S(1)}, u32[]{:S(2)}) copy-start(f32[8]{0:T(128)S(1)} %add_multiply_fusion) | copy-start | bytes 100
  27.4 1.9 %copy-start.17 = (f32[8,3,128]{2,0,1:T(8,128)}, f32[8,3,128]{2,0,1:T(8,128)S(1)}, u32[]{:S(2)}) copy-start(f32[8,3,128]{2,0,1:T(8,128)S(1)} %copy.168) | copy-start | bytes 36868
  28.1 1.4 %copy-start.19 = (f32[8,3,32]{2,0,1:T(8,128)}, f32[8,3,32]{2,0,1:T(8,128)S(1)}, u32[]{:S(2)}) copy-start(f32[8,3,32]{2,0,1:T(8,128)S(1)} %copy.170) | copy-start | bytes 9220
  29.9 4.2 %copy-start.6 = (f32[9,8,32,128]{3,2,1,0:T(8,128)}, f32[9,8,32,128]{3,2,1,0:T(8,128)S(1)}, u32[]{:S(2)}) copy-start(f32[9,8,32,128]{3,2,1,0:T(8,128)S(1)} %multiply_dynamic-update-slice_fusion) | copy-start | bytes 3538948
  30.0 0.8 copy-start.10
  30.0 4.1 %copy-start.8 = (f32[8,32,128]{2,1,0:T(8,128)}, f32[8,32,128]{2,1,0:T(8,128)S(1)}, u32[]{:S(2)}) copy-start(f32[8,32,128]{2,1,0:T(8,128)S(1)} %get-tuple-element.37) | copy-start | bytes 393220
  31.1 3.0 %copy-start.1 = (f32[8,8,32,128]{3,2,0,1:T(8,128)}, f32[8,8,32,128]{3,2,0,1:T(8,128)S(1)}, u32[]{:S(2)}) copy-start(f32[8,8,32,128]{3,2,0,1:T(8,128)S(1)} %fusion.17) | copy-start | bytes 3145732
  38.1 1.0 %copy-start.4 = (f32[128,9,2,32]{0,3,2,1:T(8,128)S(1)}, f32[128,9,2,32]{0,3,2,1:T(8,128)}, u32[]{:S(2)}) copy-start(f32[128,9,2,32]{0,3,2,1:T(8,128)} %convolution_bitcast_fusion) | copy-start | bytes 884740
  40.7 0.9 %copy-start.16 = (f32[8,128,8]{1,2,0:T(8,128)S(1)}, f32[8,128,8]{1,2,0:T(8,128)}, u32[]{:S(2)}) copy-start(f32[8,128,8]{1,2,0:T(8,128)} %broadcast_multiply_fusion) | copy-start | bytes 98308
  41.6 1.4 %copy-start.2 = (f32[8,8,32,128]{3,2,0,1:T(8,128)S(1)}, f32[8,8,32,128]{3,2,0,1:T(8,128)}, u32[]{:S(2)}) copy-start(f32[8,8,32,128]{3,2,0,1:T(8,128)} %copy-done.1) | copy-start | bytes 3145732
  41.6 1.6 %copy-start.7 = (f32[9,8,32,128]{3,2,1,0:T(8,128)S(1)}, f32[9,8,32,128]{3,2,1,0:T(8,128)}, u32[]{:S(2)}) copy-start(f32[9,8,32,128]{3,2,1,0:T(8,128)} %copy-done.6) | copy-start | bytes 3538948
  52.7 1.7 %copy-start.5 = (f32[2,128,9,8,32,1]{1,4,5,3,2,0:T(8,128)S(1)}, f32[2,128,9,8,32,1]{1,4,5,3,2,0:T(8,128)}, u32[]{:S(2)}) copy-start(f32[2,128,9,8,32,1]{1,4,5,3,2,0:T(8,128)} %get-tuple-element.64) | copy-start | bytes 7077892
  54.4 0.7 copy-start.24
  55.1 3.7 %copy-start.3 = (f32[8,8,32,128]{3,2,0,1:T(8,128)S(1)}, f32[8,8,32,128]{3,2,0,1:T(8,128)}, u32[]{:S(2)}) copy-start(f32[8,8,32,128]{3,2,0,1:T(8,128)} %get-tuple-element.25) | copy-start | bytes 3145732
  55.1 3.7 %copy-start.9 = (f32[8,32,128]{2,1,0:T(8,128)S(1)}, f32[8,32,128]{2,1,0:T(8,128)}, u32[]{:S(2)}) copy-start(f32[8,32,128]{2,1,0:T(8,128)} %copy-done.8) | copy-start | bytes 393220
  55.1 3.7 %copy-start.11 = (f32[8,32,128]{2,1,0:T(8,128)S(1)}, f32[8,32,128]{2,1,0:T(8,128)}, u32[]{:S(2)}) copy-start(f32[8,32,128]{2,1,0:T(8,128)} %copy-done.10) | copy-start | bytes 393220
  55.1 3.7 %copy-start.34 = (f32[8]{0:T(128)S(1)}, f32[8]{0:T(128)}, u32[]{:S(2)}) copy-start(f32[8]{0:T(128)} %copy-done.33) | copy-start | bytes 100
  57.6 1.7 %copy-start.28 = (f32[8]{0:T(128)S(1)}, f32[8]{0:T(128)}, u32[]{:S(2)}) copy-start(f32[8]{0:T(128)} %copy-done.27) | copy-start | bytes 100
  57.6 1.8 %copy-start.32 = (f32[8]{0:T(128)S(1)}, f32[8]{0:T(128)}, u32[]{:S(2)}) copy-start(f32[8]{0:T(128)} %copy-done.31) | copy-start | bytes 100
  59.3 0.9 %copy-start.13 = (f32[8,1,32,128]{3,2,0,1:T(8,128)S(1)}, f32[8,1,32,128]{3,2,0,1:T(8,128)}, u32[]{:S(2)}) copy-start(f32[8,1,32,128]{3,2,0,1:T(8,128)} %fusion.43) | copy-start | bytes 393220
  59.3 1.0 %copy-start.14 = (f32[8,1,32,128]{3,2,0,1:T(8,128)S(1)}, f32[8,1,32,128]{3,2,0,1:T(8,128)}, u32[]{:S(2)}) copy-start(f32[8,1,32,128]{3,2,0,1:T(8,128)} %get-tuple-element.30) | copy-start | bytes 393220
  59.3 1.0 %copy-start.15 = (f32[8,1,32,128]{3,2,0,1:T(8,128)S(1)}, f32[8,1,32,128]{3,2,0,1:T(8,128)}, u32[]{:S(2)}) copy-start(f32[8,1,32,128]{3,2,0,1:T(8,128)} %get-tuple-element.31) | copy-start | bytes 393220
  59.3 1.0 %copy-start.18 = (f32[8,3,128]{2,0,1:T(8,128)S(1)}, f32[8,3,128]{2,0,1:T(8,128)}, u32[]{:S(2)}) copy-start(f32[8,3,128]{2,0,1:T(8,128)} %copy-done.17) | copy-start | bytes 36868
  59.3 1.0 %copy-start.20 = (f32[8,3,32]{2,0,1:T(8,128)S(1)}, f32[8,3,32]{2,0,1:T(8,128)}, u32[]{:S(2)}) copy-start(f32[8,3,32]{2,0,1:T(8,128)} %copy-done.19) | copy-start | bytes 9220
  59.3 1.3 %copy-start.26 = (f32[8,5]{0,1:T(8,128)S(1)}, f32[8,5]{0,1:T(8,128)}, u32[]{:S(2)}) copy-start(f32[8,5]{0,1:T(8,128)} %copy.190) | copy-start | bytes 484
  59.3 1.4 %copy-start.25 = (f32[8,5]{0,1:T(8,128)S(1)}, f32[8,5]{0,1:T(8,128)}, u32[]{:S(2)}) copy-start(f32[8,5]{0,1:T(8,128)} %copy.182) | copy-start | bytes 484
  59.3 1.5 %copy-start.36 = (f32[4]{0:T(128)S(1)}, f32[4]{0:T(128)}, u32[]{:S(2)}) copy-start(f32[4]{0:T(128)} %compare_convert_fusion) | copy-start | bytes 52
  61.1 11.7 %copy-start.12 = (bf16[128,8,2,1,32]{0,4,2,1,3:T(8,128)(2,1)S(1)}, bf16[128,8,2,1,32]{0,4,2,1,3:T(8,128)(2,1)}, u32[]{:S(2)}) copy-start(bf16[128,8,2,1,32]{0,4,2,1,3:T(8,128)(2,1)} %get-tuple-element.46) | copy-start | bytes 393220
  61.1 11.7 %copy-start.22 = (bf16[128,1,2,1,32]{0,4,2,1,3:T(8,128)(2,1)S(1)}, bf16[128,1,2,1,32]{0,4,2,1,3:T(8,128)(2,1)}, u32[]{:S(2)}) copy-start(bf16[128,1,2,1,32]{0,4,2,1,3:T(8,128)(2,1)} %get-tuple-element.35) | copy-start | bytes 49156
  61.1 1.5 %collective-permute-start.3 = (f32[69,640]{1,0:T(8,128)S(1)}, f32[69,640]{1,0:T(8,128)S(1)}, u32[]{:S(2)}, u32[]{:S(2)}) collective-permute-start(f32[69,640]{1,0:T(8,128)S(1)} %pad_maximum_fusion), channel_id=1, source_target_pairs={{0,1},{1,0},{2,3},{3,2},{4,5},{5,4},{6,7},{7,6},{8,9},{9,8},{10,11... | collective-permute-start | bytes 529928 | tf_op jit(solution)/shard_map/ppermute | solution.py:19
  62.7 5.2 %collective-permute-start.4 = (f32[37,640]{1,0:T(8,128)S(1)}, f32[37,640]{1,0:T(8,128)S(1)}, u32[]{:S(2)}, u32[]{:S(2)}) collective-permute-start(f32[37,640]{1,0:T(8,128)S(1)} %pad_maximum_fusion.2), channel_id=1, source_target_pairs={{0,2},{1,3},{2,0},{3,1},{4,6},{5,7},{6,4},{7,5},{8,10},{9,11},{10,... | collective-permute-start | bytes 284168 | tf_op jit(solution)/shard_map/ppermute | solution.py:19
  68.2 3.8 %collective-permute-start.5 = (f32[37,128]{1,0:T(8,128)S(1)}, f32[37,128]{1,0:T(8,128)S(1)}, u32[]{:S(2)}, u32[]{:S(2)}) collective-permute-start(f32[37,128]{1,0:T(8,128)S(1)} %pad_maximum_fusion.3), channel_id=1, source_target_pairs={{0,4},{4,0},{8,12},{12,8},{16,20},{20,16},{24,28},{28,24},{1,5},{5... | collective-permute-start | bytes 56840 | tf_op jit(solution)/shard_map/ppermute | solution.py:19
  72.3 5.9 %collective-permute-start.6 = (f32[37,128]{1,0:T(8,128)S(1)}, f32[37,128]{1,0:T(8,128)S(1)}, u32[]{:S(2)}, u32[]{:S(2)}) collective-permute-start(f32[37,128]{1,0:T(8,128)S(1)} %pad_maximum_fusion.4), channel_id=1, source_target_pairs={{0,8},{4,12},{8,0},{12,4},{16,24},{20,28},{24,16},{28,20},{1,9},{5... | collective-permute-start | bytes 56840 | tf_op jit(solution)/shard_map/ppermute | solution.py:19
  74.9 8.1 %all-to-all-start = ((bf16[4,2,9216]{2,1,0:T(2,128)(2,1)}), bf16[4,2,9216]{2,1,0:T(2,128)(2,1)S(1)}, u32[]{:S(2)}, u32[]{:S(2)}) async-start(bf16[4,2,9216]{2,1,0:T(2,128)(2,1)} %reshape.584), calls=%async_computation | async-start | bytes 294912 | tf_op jit(solution)/shard_map/all_to_all | solution.py:198
  78.5 6.7 %collective-permute-start.7 = (f32[37,128]{1,0:T(8,128)S(1)}, f32[37,128]{1,0:T(8,128)S(1)}, u32[]{:S(2)}, u32[]{:S(2)}) collective-permute-start(f32[37,128]{1,0:T(8,128)S(1)} %pad_maximum_fusion.5), channel_id=1, source_target_pairs={{0,16},{4,20},{8,24},{12,28},{16,0},{20,4},{24,8},{28,12},{1,17},{... | collective-permute-start | bytes 56840 | tf_op jit(solution)/shard_map/ppermute | solution.py:19
  83.3 1.9 %copy-start.38 = (s32[3,128]{1,0:T(4,128)S(1)}, s32[3,128]{1,0:T(4,128)}, u32[]{:S(2)}) copy-start(s32[3,128]{1,0:T(4,128)} %param.11) | copy-start | bytes 4612

commit v14 on v13

--- a/solution.py
+++ b/solution.py
@@ -167,9 +167,17 @@
     pos_blocks = jnp.moveaxis(src_pos.reshape(3, src_blocks, block_size), 1, 0)
     pos_rows = lax.dynamic_slice_in_dim(pos_blocks, row_low, rows, 2)
     feat_blocks = jnp.moveaxis(full_feat.reshape(all_chan, src_blocks, block_size), 1, 0)
-    target_pos = jnp.take(pos_rows, target_idx, axis=0, mode="clip")
-    source_pos = jnp.take(pos_blocks, source_idx, axis=0, mode="clip")
-    source_feat = jnp.take(feat_blocks, source_idx, axis=0, mode="clip")
+    target_pick = (target_idx[:, None] == block_ids[None]).astype(jnp.float32)
+    source_pick = (source_idx[:, None] == block_ids[None]).astype(jnp.float32)
+    exact = lax.Precision.HIGHEST
+    target_pos = jnp.einsum("ts,sdr->tdr", target_pick, pos_rows, precision=exact)
+    source_pos = jnp.einsum("ts,sdb->tdb", source_pick, pos_blocks, precision=exact)
+    source_feat = jnp.einsum(
+        "ts,scb->tcb",
+        source_pick.astype(jnp.bfloat16),
+        feat_blocks,
+        preferred_element_type=jnp.float32,
+    ).astype(jnp.bfloat16)
 
     def geo_fn(first_pos, second_pos):
         return geometry(first_pos, second_pos, pair_keep, radial_count)
@@ -220,7 +228,9 @@
     )
     grad_rad = jnp.einsum("bclki,clbi->ck", msg_acc, moment_grad_all)
     grad_blocks = jnp.moveaxis(moment_grad_all, 2, 0)
-    tile_grad = jnp.take(grad_blocks, target_idx, axis=0, mode="clip")
+    tile_grad = jnp.einsum(
+        "tb,bcli->tcli", target_pick[:, :own_blocks], grad_blocks, precision=exact
+    )
     weighted = (
         live[:, None, None, None, None]
         * full_weight[None, :, None, :, None]

time: 88.2 us -> 94.8 us (1.075)
  other arithmetic: 17.7 us -> 26.3 us
  local copies, waits for them, and re-layouts: 22.3 us -> 17.5 us
  matrix products: 9.7 us -> 13.1 us
    unnamed x8, other arithmetic: 0.64 us -> 5.21 us
    gather x6 -> x0, local copies, waits for them, and re-layouts: 2.66 us -> none  [the longest x1 0.88 us: body(): tile_grad = jnp.take(grad_blocks, target_idx, axis=0, mode='clip')]
    another operation x2, other arithmetic: 1.35 us -> 3.05 us
    dot_general x0 -> x4, matrix products: none -> 1.57 us  [the longest x1 0.89 us: body(): jnp.einsum('tb,bcli->tcli', target_pick[:, :own_blocks], grad_blocks, pre...]
    dot_general x1, matrix products: 2.99 us -> 4.29 us  [body(): jnp.einsum('lktij,tbcj->bclki', pair_values, routed_feat, preferred_eleme...]
    dot_general x1, matrix products: 2.84 us -> 4.09 us  [body(): jnp.einsum('tclki,lktij->tcj', weighted, pair_values, preferred_element_t...]
    unnamed x88 -> x82, local copies, waits for them, and re-layouts: 7.25 us -> 6.02 us
    reduce_sum x1, other arithmetic: 0.03 us -> 1.03 us  [body(): jnp.sum(upstream[:, 1:] * mixed_out[:, 1:], axis=1)]
  transfers between devices with their start and end apart: 10 -> 10, of which waited for: 4 -> 4; matrix products, arithmetic and copies ran while one was open for 22% -> 25% of each run, Pallas kernels for 0% -> 0%
where the time goes in v14:
time: 94.8 us; the launch traced here: 93.9 us
  other arithmetic  26.3 us (28%)
  starting transfers between devices  17.7 us (19%)
  local copies, waits for them, and re-layouts  17.5 us (18%)
  matrix products  13.1 us (14%)
  waiting for transfers between devices  11.9 us (13%)
  blocking collectives  5.86 us (6%)
  between operations  1.54 us (2%)
    ppermute x8, starting transfers between devices, partner(): return lax.ppermute(value, axis, pairs)  10.9 us
    ppermute x8, waiting for transfers between devices, partner(): return lax.ppermute(value, axis, pairs)  7.79 us
    unnamed x82, local copies, waits for them, and re-layouts  6.02 us
    all_gather x1, blocking collectives, body(): lax.all_gather(jnp.concatenate([src_feat, weight_high, weight_mid, weight...  5.86 us
    reduce_sum x1, other arithmetic, body(): harm_grad = jnp.sum(value_grad * radial[None], axis=1)  5.25 us
    unnamed x8, other arithmetic  5.21 us
    dot_general x1, matrix products, body(): jnp.einsum('lktij,tbcj->bclki', pair_values, routed_feat, preferred_eleme...  4.29 us
    all_to_all x1, waiting for transfers between devices, body(): lax.all_to_all(result_rows.reshape(all_chan, components, own_blocks, 1, r...  4.15 us
  transfers between devices with their start and end apart: 10, of which 4 were waited for; matrix products, arithmetic and copies ran while one was open for 25% of the time, Pallas kernels for 0%

profile of v14, /device:TPU:0, one launch (start us, length us, event | category | flops | bytes accessed | tf_op | source)
XLA Modules:
  0.0 93.9 jit_solution(14100899154001232072)
XLA Ops:
  0.6 0.8 convert_element_type.105
  1.4 1.0 %fusion.26 = f32[35,384]{1,0:T(8,128)S(1)} fusion(s32[384]{0:T(512)} %bitcast.398, f32[3,256]{1,0:T(4,128)} %param.9, f32[32,256]{1,0:T(8,128)S(1)} %convert_element_type.105), kind=kOutput, calls=%fused_computation.39 | convolution fusion | flops 41394944 | bytes 91136 | tf_op jit(solution)/shard_map/dot_general | solution.py:119
  2.4 3.0 %collective-permute-start = (f32[35,128]{1,0:T(8,128)S(1)}, f32[35,128]{1,0:T(8,128)S(1)}, u32[]{:S(2)}, u32[]{:S(2)}) collective-permute-start(f32[35,128]{1,0:T(8,128)S(1)} %get-tuple-element.42), channel_id=1, source_target_pairs={{0,4},{4,0},{8,12},{12,8},{16,20},{20,16},{24,28},{28,24},{1,5},{5... | collective-permute-start | bytes 53768 | tf_op jit(solution)/shard_map/ppermute | solution.py:19
  5.4 2.6 %collective-permute-start.2 = (f32[35,128]{1,0:T(8,128)S(1)}, f32[35,128]{1,0:T(8,128)S(1)}, u32[]{:S(2)}, u32[]{:S(2)}) collective-permute-start(f32[35,128]{1,0:T(8,128)S(1)} %get-tuple-element.43), channel_id=1, source_target_pairs={{0,16},{4,20},{8,24},{12,28},{16,0},{20,4},{24,8},{28,12},{1,17},{... | collective-permute-start | bytes 53768 | tf_op jit(solution)/shard_map/ppermute | solution.py:19
  8.0 1.6 %collective-permute-start.1 = (f32[35,128]{1,0:T(8,128)S(1)}, f32[35,128]{1,0:T(8,128)S(1)}, u32[]{:S(2)}, u32[]{:S(2)}) collective-permute-start(f32[35,128]{1,0:T(8,128)S(1)} %get-tuple-element.44), channel_id=1, source_target_pairs={{0,8},{4,12},{8,0},{12,4},{16,24},{20,28},{24,16},{28,20},{1,9},{5... | collective-permute-start | bytes 53768 | tf_op jit(solution)/shard_map/ppermute | solution.py:19
  9.6 1.3 %reshape.517 = bf16[32,9,2,4,32]{4,3,2,0,1:T(4,128)(2,1)S(1)} reshape(bf16[32,9,256]{2,0,1:T(8,128)(2,1)} %param.16) | data formatting | bytes 294912 | tf_op jit(solution)/shard_map/reshape | solution.py:214
  10.9 0.7 copy.194
  11.6 1.2 %reshape.556 = bf16[4,2,9216]{2,1,0:T(2,128)(2,1)} reshape(bf16[4,9,2,32,32]{4,3,2,1,0:T(8,128)(2,1)S(1)} %bitcast.388) | data formatting | bytes 294912
  12.8 3.5 %all-to-all-start.1 = ((bf16[4,2,9216]{2,1,0:T(2,128)(2,1)}), bf16[4,2,9216]{2,1,0:T(2,128)(2,1)S(1)}, u32[]{:S(2)}, u32[]{:S(2)}) async-start(bf16[4,2,9216]{2,1,0:T(2,128)(2,1)} %reshape.556), calls=%async_computation.1 | async-start | bytes 294912 | tf_op jit(solution)/shard_map/all_to_all | solution.py:213
  16.3 0.7 broadcast_dynamic-update-slice_fusion
  17.0 0.5 compare_convert_fusion
  17.5 0.6 iota_compare_fusion.7
  18.6 0.7 copy.192
  19.2 0.6 gather_fusion
  20.0 5.9 %all_gather.3 = bf16[128,664]{1,0:T(8,128)(2,1)S(1)} all-gather(bf16[32,664]{1,0:T(8,128)(2,1)S(1)} %concatenate.53), channel_id=1, replica_groups=mesh['space'=8,'chan'=4] {'chan'}, dimensions={0}, use_global_device_ids=true | all-gather | bytes 212480 | tf_op jit(solution)/shard_map/all_gather | solution.py:139
  27.5 0.7 fusion.91
  28.2 0.7 fusion.90
  28.8 0.7 fusion.103
  29.5 0.7 multiply_dynamic-update-slice_fusion.3
  30.2 0.7 multiply_dynamic-update-slice_fusion.2
  31.0 0.7 multiply_dynamic-update-slice_fusion.1
  31.7 0.7 fusion.45
  32.4 0.7 multiply_dynamic-update-slice_fusion
  33.5 4.3 %fusion.7 = (bf16[128,2,9,32]{0,3,2,1:T(8,128)(2,1)S(1)}, f32[2,128,9,8,32,1]{1,4,5,3,2,0:T(8,128)}) fusion(f32[128,8]{0,1:T(8,128)S(1)} %copy.244, f32[8,128,128]{2,1,0:T(8,128)S(1)} %copy.184, f32[8,2]{0,1:T(2,128)S(1)} %slice.164, f32[8,8,32,128]{3,2,0,1:T(8,128)S(1)} %fusion.17, f32[9,8,32,128]{3,2,1,0:T(8,128)} %multiply_dynamic-update-slice_fusion), kind=kOutput, calls=%fused_computation.15 | convolution fusion | flops 1214308352 | bytes 5263424 | tf_op jit(solution)/shard_map/lktij,tbcj->bclki/dot_general | solution.py:190
  37.8 0.3 convolution_bitcast_fusion
  38.1 0.7 broadcast_multiply_fusion
  39.2 0.8 copy.195
  40.1 1.2 %reshape.529 = f32[128,9,2,32]{0,3,2,1:T(8,128)} reshape(f32[4,32,9,2,1,32]{1,0,5,3,2,4:T(4,128)S(1)} %copy.195) | data formatting | bytes 589824 | tf_op jit(solution)/shard_map/convert_element_type | solution.py:220
  41.3 1.0 %multiply_reduce_fusion.4 = f32[128,2,32]{0,2,1:T(8,128)S(1)} fusion(f32[128,9,2,32]{0,3,2,1:T(8,128)} %reshape.529, f32[128,9,2,32]{0,3,2,1:T(8,128)S(1)} %convolution_bitcast_fusion), kind=kLoop, calls=%fused_computation.51 | loop fusion | flops 122880 | bytes 557056 | tf_op jit(solution)/shard_map/reduce_sum | solution.py:223
  42.4 1.4 %fusion.108 = (bf16[128,1,2,32]{0,3,2,1:T(8,128)(2,1)S(1)}, bf16[128,1,2,1,32]{0,4,2,1,3:T(8,128)(2,1)}, f32[128,2,32]{0,2,1:T(8,128)S(1)}) fusion(f32[128,9,2,32]{0,3,2,1:T(8,128)} %reshape.529, f32[128,2,32]{0,2,1:T(8,128)S(1)} %multiply_reduce_fusion.4, f32[128,9,2,32]{0,3,2,1:T(8,128)S(1)} %convolution_bitcast_fusion), kind=kLoop, calls=%fused_computation.187 | loop fusion | flops 114688 | bytes 163840 | tf_op jit(solution)/shard_map/convert.4
  43.8 1.7 %multiply_convert_fusion.3 = (bf16[128,8,2,32]{0,3,2,1:T(8,128)(2,1)S(1)}, bf16[128,8,2,1,32]{0,4,2,1,3:T(8,128)(2,1)}) fusion(f32[128,9,2,32]{0,3,2,1:T(8,128)} %reshape.529, f32[128,2,32]{0,2,1:T(8,128)S(1)} %get-tuple-element.36, f32[128,9,2,32]{0,3,2,1:T(8,128)S(1)} %convolution_bitcast_fusion), kind=kLoop, calls=%fused_computation.50 | loop fusion | flops 262144 | bytes 819200 | tf_op jit(solution)/shard_map/convert.5
  45.6 0.9 fusion.31
  46.8 0.5 copy-done.11
  47.3 1.3 %multiply_convert_fusion = bf16[8,128,9,8,32]{1,4,3,2,0:T(8,128)(2,1)S(1)} fusion(f32[8,128,9,32]{1,3,2,0:T(8,128)S(1)} %copy.197, f32[8,128,8]{1,2,0:T(8,128)S(1)} %copy-done.11), kind=kLoop, calls=%fused_computation.3 | loop fusion | flops 4718592 | bytes 5931008 | tf_op jit(solution)/shard_map/convert_element_type | solution.py:238
  48.6 4.1 %fusion.8 = f32[8,128,128]{2,1,0:T(8,128)} fusion(bf16[8,128,9,8,32]{1,4,3,2,0:T(8,128)(2,1)S(1)} %multiply_convert_fusion, f32[8,8,32,128]{3,2,0,1:T(8,128)S(1)} %fusion.17, f32[9,8,32,128]{3,2,1,0:T(8,128)} %multiply_dynamic-update-slice_fusion), kind=kOutput, calls=%fused_computation.18 | convolution fusion | flops 608698368 | bytes 7471104 | tf_op jit(solution)/shard_map/tclki,lktij->tcj/dot_general | solution.py:239
  52.7 1.4 %fusion.34 = f32[8,128,2304]{1,2,0:S(1)} fusion(bf16[8,128,2304]{1,2,0:T(8,128)(2,1)S(1)} %bitcast.386, bf16[8,128,128]{2,0,1:T(8,128)(2,1)S(1)} %convolution_convert_fusion), kind=kOutput, calls=%fused_computation.48 | convolution fusion | flops 603979776 | bytes 14417920
  54.1 5.3 %multiply_reduce_fusion.1 = (f32[9,8,32,128]{3,2,0,1:T(8,128)S(1)}, f32[8,8,32,128]{3,2,0,1:T(8,128)}) fusion(f32[9,8,8,32,128]{4,3,1,0,2:T(8,128)S(1)} %bitcast.385, f32[8,8,32,128]{3,2,0,1:T(8,128)S(1)} %fusion.17, f32[9,8,32,128]{3,2,1,0:T(8,128)} %multiply_dynamic-update-slice_fusion), kind=kLoop, calls=%fused_computation.2 | loop fusion | flops 8880128 | bytes 13893632 | tf_op jit(solution)/shard_map/reduce_sum | solution.py:245
  59.4 0.8 fusion.48
  60.1 0.9 fusion.81
  61.1 0.3 fusion.6
  61.8 1.5 %multiply_reduce_fusion.2 = f32[128,5,128]{2,0,1:T(8,128)S(1)} fusion(f32[8,128,128]{2,1,0:T(8,128)} %fusion.8, f32[8,5]{1,0:T(8,128)S(1)} %copy-done.22), kind=kLoop, calls=%fused_computation.11 | loop fusion | flops 1228800 | bytes 852128 | tf_op jit(solution)/shard_map/reduce_sum | solution.py:248
  63.5 0.8 reshape_reshape.13
  64.3 1.4 %fusion.18 = (f32[8,32,128]{2,1,0:T(8,128)S(1)}, f32[8,32,128]{2,1,0:T(8,128)S(1)}) fusion(f32[8,8,32,128]{3,2,0,1:T(8,128)S(1)} %copy-done.1, f32[8]{0:T(128)S(1)} %copy-done.30, f32[8,32,128]{2,1,0:T(8,128)S(1)} %get-tuple-element.37, f32[8,32,128]{2,1,0:T(8,128)} %copy-done.6), kind=kLoop, calls=%fused_computation.27 | loop fusion | flops 2818048 | bytes 1572896 | tf_op jit(solution)/shard_map/transpose(jvp())/reduce_sum | solution.py:86
  65.8 0.3 fusion.60
  66.2 0.4 copy-done.8
  66.8 0.3 fusion.93
  67.6 0.4 collective-permute-start.3
  68.0 1.1 %collective-permute-done.3 = f32[69,640]{1,0:T(8,128)S(1)} collective-permute-done((f32[69,640]{1,0:T(8,128)S(1)}, f32[69,640]{1,0:T(8,128)S(1)}, u32[]{:S(2)}, u32[]{:S(2)}) %collective-permute-start.3) | collective-permute-done | bytes 176672 | tf_op jit(solution)/shard_map/ppermute | solution.py:19
  69.2 1.8 %collective-permute-start.4 = (f32[37,640]{1,0:T(8,128)S(1)}, f32[37,640]{1,0:T(8,128)S(1)}, u32[]{:S(2)}, u32[]{:S(2)}) collective-permute-start(f32[37,640]{1,0:T(8,128)S(1)} %pad_maximum_fusion.2), channel_id=1, source_target_pairs={{0,2},{1,3},{2,0},{3,1},{4,6},{5,7},{6,4},{7,5},{8,10},{9,11},{10,... | collective-permute-start | bytes 284168 | tf_op jit(solution)/shard_map/ppermute | solution.py:19
  71.0 3.4 %collective-permute-done.4 = f32[37,640]{1,0:T(8,128)S(1)} collective-permute-done((f32[37,640]{1,0:T(8,128)S(1)}, f32[37,640]{1,0:T(8,128)S(1)}, u32[]{:S(2)}, u32[]{:S(2)}) %collective-permute-start.4) | collective-permute-done | bytes 94752 | tf_op jit(solution)/shard_map/ppermute | solution.py:19
  74.7 0.6 collective-permute-start.5
  75.3 3.3 %collective-permute-done.5 = f32[37,128]{1,0:T(8,128)S(1)} collective-permute-done((f32[37,128]{1,0:T(8,128)S(1)}, f32[37,128]{1,0:T(8,128)S(1)}, u32[]{:S(2)}, u32[]{:S(2)}) %collective-permute-start.5) | collective-permute-done | bytes 18976 | tf_op jit(solution)/shard_map/ppermute | solution.py:19
  78.8 0.5 collective-permute-start.6
  79.3 0.8 copy.190
  80.2 1.2 %reshape.554 = bf16[4,2,9216]{2,1,0:T(2,128)(2,1)} reshape(bf16[128,1,9,2,32]{4,3,2,1,0:T(2,128)(2,1)S(1)} %bitcast.389) | data formatting | bytes 294912
  81.4 3.3 %all-to-all-start = ((bf16[4,2,9216]{2,1,0:T(2,128)(2,1)}), bf16[4,2,9216]{2,1,0:T(2,128)(2,1)S(1)}, u32[]{:S(2)}, u32[]{:S(2)}) async-start(bf16[4,2,9216]{2,1,0:T(2,128)(2,1)} %reshape.554), calls=%async_computation | async-start | bytes 294912 | tf_op jit(solution)/shard_map/all_to_all | solution.py:206
  85.0 0.4 collective-permute-start.7
  85.4 4.1 %all-to-all-done = bf16[4,2,9216]{2,1,0:T(2,128)(2,1)S(1)} async-done(((bf16[4,2,9216]{2,1,0:T(2,128)(2,1)}), bf16[4,2,9216]{2,1,0:T(2,128)(2,1)S(1)}, u32[]{:S(2)}, u32[]{:S(2)}) %all-to-all-start) | async-done | bytes 147488 | tf_op jit(solution)/shard_map/all_to_all | solution.py:206
  89.8 0.8 copy.191
  90.6 1.1 %reshape.516 = bf16[32,9,256]{2,0,1:T(8,128)(2,1)} reshape(bf16[32,9,2,4,1,32]{5,3,2,0,1,4:T(4,128)(2,1)S(1)} %copy.191) | data formatting | bytes 294912 | tf_op jit(solution)/shard_map/reshape | solution.py:212
  91.7 0.3 maximum_add_fusion
  92.0 0.6 slice_negate_fusion
  92.6 0.6 slice.337
  93.3 0.7 copy.209
  (162 shorter events, 5.6 us)
Async XLA Ops:
  0.6 18.6 %copy-start = (bf16[3,128,128]{2,1,0:T(8,128)(2,1)S(1)}, bf16[3,128,128]{2,1,0:T(8,128)(2,1)}, u32[]{:S(2)}) copy-start(bf16[3,128,128]{2,1,0:T(8,128)(2,1)} %param.15) | copy-start | bytes 294916
  2.4 17.5 %collective-permute-start = (f32[35,128]{1,0:T(8,128)S(1)}, f32[35,128]{1,0:T(8,128)S(1)}, u32[]{:S(2)}, u32[]{:S(2)}) collective-permute-start(f32[35,128]{1,0:T(8,128)S(1)} %get-tuple-element.42), channel_id=1, source_target_pairs={{0,4},{4,0},{8,12},{12,8},{16,20},{20,16},{24,28},{28,24},{1,5},{5... | collective-permute-start | bytes 53768 | tf_op jit(solution)/shard_map/ppermute | solution.py:19
  5.4 14.5 %collective-permute-start.2 = (f32[35,128]{1,0:T(8,128)S(1)}, f32[35,128]{1,0:T(8,128)S(1)}, u32[]{:S(2)}, u32[]{:S(2)}) collective-permute-start(f32[35,128]{1,0:T(8,128)S(1)} %get-tuple-element.43), channel_id=1, source_target_pairs={{0,16},{4,20},{8,24},{12,28},{16,0},{20,4},{24,8},{28,12},{1,17},{... | collective-permute-start | bytes 53768 | tf_op jit(solution)/shard_map/ppermute | solution.py:19
  8.0 11.9 %collective-permute-start.1 = (f32[35,128]{1,0:T(8,128)S(1)}, f32[35,128]{1,0:T(8,128)S(1)}, u32[]{:S(2)}, u32[]{:S(2)}) collective-permute-start(f32[35,128]{1,0:T(8,128)S(1)} %get-tuple-element.44), channel_id=1, source_target_pairs={{0,8},{4,12},{8,0},{12,4},{16,24},{20,28},{24,16},{28,20},{1,9},{5... | collective-permute-start | bytes 53768 | tf_op jit(solution)/shard_map/ppermute | solution.py:19
  10.8 5.5 %copy-start.32 = (s32[8,2]{0,1:T(2,128)S(1)}, s32[8,2]{0,1:T(2,128)}, u32[]{:S(2)}) copy-start(s32[8,2]{0,1:T(2,128)} %param.12) | copy-start | bytes 196
  10.8 6.7 %copy-start.36 = (s32[8]{0:T(128)S(1)}, s32[8]{0:T(128)}, u32[]{:S(2)}) copy-start(s32[8]{0:T(128)} %param.13) | copy-start | bytes 100
  10.9 7.3 %copy-start.34 = (s32[9]{0:T(128)S(1)}, s32[9]{0:T(128)}, u32[]{:S(2)}) copy-start(s32[9]{0:T(128)} %constant.95) | copy-start | bytes 112
  10.9 7.3 %copy-start.26 = (f32[32,8]{0,1:T(8,128)S(1)}, f32[32,8]{0,1:T(8,128)}, u32[]{:S(2)}) copy-start(f32[32,8]{0,1:T(8,128)} %param.14) | copy-start | bytes 3076
  11.6 8.4 %copy-start.16 = (bf16[32,256]{1,0:T(8,128)(2,1)S(1)}, bf16[32,256]{1,0:T(8,128)(2,1)}, u32[]{:S(2)}) copy-start(bf16[32,256]{1,0:T(8,128)(2,1)} %param.10) | copy-start | bytes 49156
  12.8 13.1 %copy-start.25 = (f32[3,256]{1,0:T(4,128)S(1)}, f32[3,256]{1,0:T(4,128)}, u32[]{:S(2)}) copy-start(f32[3,256]{1,0:T(4,128)} %param.9) | copy-start | bytes 9220
  12.8 26.0 %all-to-all-start.1 = ((bf16[4,2,9216]{2,1,0:T(2,128)(2,1)}), bf16[4,2,9216]{2,1,0:T(2,128)(2,1)S(1)}, u32[]{:S(2)}, u32[]{:S(2)}) async-start(bf16[4,2,9216]{2,1,0:T(2,128)(2,1)} %reshape.556), calls=%async_computation.1 | async-start | bytes 294912 | tf_op jit(solution)/shard_map/all_to_all | solution.py:213
  16.3 16.8 %copy-start.27 = (f32[8]{0:T(128)}, f32[8]{0:T(128)S(1)}, u32[]{:S(2)}) copy-start(f32[8]{0:T(128)S(1)} %compare_convert_fusion.1) | copy-start | bytes 100
  17.5 20.6 %copy-start.23 = (f32[8]{0:T(128)}, f32[8]{0:T(128)S(1)}, u32[]{:S(2)}) copy-start(f32[8]{0:T(128)S(1)} %convert_element_type.112) | copy-start | bytes 100
  18.2 1.6 %copy-start.20 = (f32[8,5]{0,1:T(8,128)}, f32[8,5]{0,1:T(8,128)S(1)}, u32[]{:S(2)}) copy-start(f32[8,5]{0,1:T(8,128)S(1)} %get-tuple-element.58) | copy-start | bytes 484
  18.2 7.9 %copy-start.18 = (f32[8,5]{0,1:T(8,128)}, f32[8,5]{0,1:T(8,128)S(1)}, u32[]{:S(2)}) copy-start(f32[8,5]{0,1:T(8,128)S(1)} %get-tuple-element.57) | copy-start | bytes 484
  18.3 14.9 %copy-start.29 = (f32[8]{0:T(128)}, f32[8]{0:T(128)S(1)}, u32[]{:S(2)}) copy-start(f32[8]{0:T(128)S(1)} %add_multiply_fusion) | copy-start | bytes 100
  19.8 18.0 %copy-start.2 = (bf16[9,128,128]{2,1,0:T(8,128)(2,1)}, bf16[9,128,128]{2,1,0:T(8,128)(2,1)S(1)}, u32[]{:S(2)}) copy-start(bf16[9,128,128]{2,1,0:T(8,128)(2,1)S(1)} %gather_fusion) | copy-start | bytes 884740
  26.2 1.1 %copy-start.12 = (f32[8,3,128]{2,0,1:T(8,128)}, f32[8,3,128]{2,0,1:T(8,128)S(1)}, u32[]{:S(2)}) copy-start(f32[8,3,128]{2,0,1:T(8,128)S(1)} %fusion.114) | copy-start | bytes 36868
  26.4 0.9 copy-start.14
  33.2 4.6 %copy-start.6 = (f32[8,32,128]{2,1,0:T(8,128)}, f32[8,32,128]{2,1,0:T(8,128)S(1)}, u32[]{:S(2)}) copy-start(f32[8,32,128]{2,1,0:T(8,128)S(1)} %get-tuple-element.38) | copy-start | bytes 393220
  41.3 4.1 %copy-start.3 = (bf16[9,128,128]{2,1,0:T(8,128)(2,1)S(1)}, bf16[9,128,128]{2,1,0:T(8,128)(2,1)}, u32[]{:S(2)}) copy-start(bf16[9,128,128]{2,1,0:T(8,128)(2,1)} %copy-done.2) | copy-start | bytes 884740
  41.3 4.3 %copy-start.31 = (pred[8,5]{0,1:T(8,128)(4,1)S(1)}, pred[8,5]{0,1:T(8,128)(4,1)}, u32[]{:S(2)}) copy-start(pred[8,5]{0,1:T(8,128)(4,1)} %iota_compare_fusion.7) | copy-start | bytes 124
  46.5 0.8 copy-start.11
  59.4 1.7 %copy-start.4 = (f32[2,128,9,8,32,1]{1,4,5,3,2,0:T(8,128)S(1)}, f32[2,128,9,8,32,1]{1,4,5,3,2,0:T(8,128)}, u32[]{:S(2)}) copy-start(f32[2,128,9,8,32,1]{1,4,5,3,2,0:T(8,128)} %get-tuple-element.60) | copy-start | bytes 7077892
  61.1 0.7 copy-start.22
  61.8 2.5 %copy-start.1 = (f32[8,8,32,128]{3,2,0,1:T(8,128)S(1)}, f32[8,8,32,128]{3,2,0,1:T(8,128)}, u32[]{:S(2)}) copy-start(f32[8,8,32,128]{3,2,0,1:T(8,128)} %get-tuple-element.25) | copy-start | bytes 3145732
  61.8 2.5 %copy-start.30 = (f32[8]{0:T(128)S(1)}, f32[8]{0:T(128)}, u32[]{:S(2)}) copy-start(f32[8]{0:T(128)} %copy-done.29) | copy-start | bytes 100
  63.4 2.3 %copy-start.24 = (f32[8]{0:T(128)S(1)}, f32[8]{0:T(128)}, u32[]{:S(2)}) copy-start(f32[8]{0:T(128)} %copy-done.23) | copy-start | bytes 100
  63.4 2.3 %copy-start.28 = (f32[8]{0:T(128)S(1)}, f32[8]{0:T(128)}, u32[]{:S(2)}) copy-start(f32[8]{0:T(128)} %copy-done.27) | copy-start | bytes 100
  65.7 0.9 copy-start.8
  65.7 1.0 %copy-start.9 = (f32[8,1,32,128]{3,2,0,1:T(8,128)S(1)}, f32[8,1,32,128]{3,2,0,1:T(8,128)}, u32[]{:S(2)}) copy-start(f32[8,1,32,128]{3,2,0,1:T(8,128)} %get-tuple-element.30) | copy-start | bytes 393220
  65.7 1.0 %copy-start.10 = (f32[8,1,32,128]{3,2,0,1:T(8,128)S(1)}, f32[8,1,32,128]{3,2,0,1:T(8,128)}, u32[]{:S(2)}) copy-start(f32[8,1,32,128]{3,2,0,1:T(8,128)} %get-tuple-element.31) | copy-start | bytes 393220
  65.8 1.0 %copy-start.13 = (f32[8,3,128]{2,0,1:T(8,128)S(1)}, f32[8,3,128]{2,0,1:T(8,128)}, u32[]{:S(2)}) copy-start(f32[8,3,128]{2,0,1:T(8,128)} %copy-done.12) | copy-start | bytes 36868
  65.8 1.0 %copy-start.15 = (f32[8,3,32]{2,0,1:T(8,128)S(1)}, f32[8,3,32]{2,0,1:T(8,128)}, u32[]{:S(2)}) copy-start(f32[8,3,32]{2,0,1:T(8,128)} %copy-done.14) | copy-start | bytes 9220
  65.8 1.3 %copy-start.19 = (f32[8,5]{0,1:T(8,128)S(1)}, f32[8,5]{0,1:T(8,128)}, u32[]{:S(2)}) copy-start(f32[8,5]{0,1:T(8,128)} %copy-done.18) | copy-start | bytes 484
  65.8 1.4 %copy-start.21 = (f32[8,5]{0,1:T(8,128)S(1)}, f32[8,5]{0,1:T(8,128)}, u32[]{:S(2)}) copy-start(f32[8,5]{0,1:T(8,128)} %copy-done.20) | copy-start | bytes 484
  65.8 1.5 %copy-start.33 = (f32[4]{0:T(128)S(1)}, f32[4]{0:T(128)}, u32[]{:S(2)}) copy-start(f32[4]{0:T(128)} %compare_convert_fusion) | copy-start | bytes 52
  65.8 1.7 %copy-start.5 = (f32[2,2,32,640]{3,2,1,0:T(8,128)S(1)}, f32[2,2,32,640]{3,2,1,0:T(8,128)}, u32[]{:S(2)}) copy-start(f32[2,2,32,640]{3,2,1,0:T(8,128)} %reshape_reshape.13) | copy-start | bytes 983044
  67.6 11.7 %copy-start.7 = (bf16[128,8,2,1,32]{0,4,2,1,3:T(8,128)(2,1)S(1)}, bf16[128,8,2,1,32]{0,4,2,1,3:T(8,128)(2,1)}, u32[]{:S(2)}) copy-start(bf16[128,8,2,1,32]{0,4,2,1,3:T(8,128)(2,1)} %get-tuple-element.46) | copy-start | bytes 393220
  67.6 11.7 %copy-start.17 = (bf16[128,1,2,1,32]{0,4,2,1,3:T(8,128)(2,1)S(1)}, bf16[128,1,2,1,32]{0,4,2,1,3:T(8,128)(2,1)}, u32[]{:S(2)}) copy-start(bf16[128,1,2,1,32]{0,4,2,1,3:T(8,128)(2,1)} %get-tuple-element.35) | copy-start | bytes 49156
  67.6 1.5 %collective-permute-start.3 = (f32[69,640]{1,0:T(8,128)S(1)}, f32[69,640]{1,0:T(8,128)S(1)}, u32[]{:S(2)}, u32[]{:S(2)}) collective-permute-start(f32[69,640]{1,0:T(8,128)S(1)} %pad_maximum_fusion), channel_id=1, source_target_pairs={{0,1},{1,0},{2,3},{3,2},{4,5},{5,4},{6,7},{7,6},{8,9},{9,8},{10,11... | collective-permute-start | bytes 529928 | tf_op jit(solution)/shard_map/ppermute | solution.py:19
  69.2 5.2 %collective-permute-start.4 = (f32[37,640]{1,0:T(8,128)S(1)}, f32[37,640]{1,0:T(8,128)S(1)}, u32[]{:S(2)}, u32[]{:S(2)}) collective-permute-start(f32[37,640]{1,0:T(8,128)S(1)} %pad_maximum_fusion.2), channel_id=1, source_target_pairs={{0,2},{1,3},{2,0},{3,1},{4,6},{5,7},{6,4},{7,5},{8,10},{9,11},{10,... | collective-permute-start | bytes 284168 | tf_op jit(solution)/shard_map/ppermute | solution.py:19
  74.7 3.8 %collective-permute-start.5 = (f32[37,128]{1,0:T(8,128)S(1)}, f32[37,128]{1,0:T(8,128)S(1)}, u32[]{:S(2)}, u32[]{:S(2)}) collective-permute-start(f32[37,128]{1,0:T(8,128)S(1)} %pad_maximum_fusion.3), channel_id=1, source_target_pairs={{0,4},{4,0},{8,12},{12,8},{16,20},{20,16},{24,28},{28,24},{1,5},{5... | collective-permute-start | bytes 56840 | tf_op jit(solution)/shard_map/ppermute | solution.py:19
  78.8 5.9 %collective-permute-start.6 = (f32[37,128]{1,0:T(8,128)S(1)}, f32[37,128]{1,0:T(8,128)S(1)}, u32[]{:S(2)}, u32[]{:S(2)}) collective-permute-start(f32[37,128]{1,0:T(8,128)S(1)} %pad_maximum_fusion.4), channel_id=1, source_target_pairs={{0,8},{4,12},{8,0},{12,4},{16,24},{20,28},{24,16},{28,20},{1,9},{5... | collective-permute-start | bytes 56840 | tf_op jit(solution)/shard_map/ppermute | solution.py:19
  81.4 8.1 %all-to-all-start = ((bf16[4,2,9216]{2,1,0:T(2,128)(2,1)}), bf16[4,2,9216]{2,1,0:T(2,128)(2,1)S(1)}, u32[]{:S(2)}, u32[]{:S(2)}) async-start(bf16[4,2,9216]{2,1,0:T(2,128)(2,1)} %reshape.554), calls=%async_computation | async-start | bytes 294912 | tf_op jit(solution)/shard_map/all_to_all | solution.py:206
  85.0 6.7 %collective-permute-start.7 = (f32[37,128]{1,0:T(8,128)S(1)}, f32[37,128]{1,0:T(8,128)S(1)}, u32[]{:S(2)}, u32[]{:S(2)}) collective-permute-start(f32[37,128]{1,0:T(8,128)S(1)} %pad_maximum_fusion.5), channel_id=1, source_target_pairs={{0,16},{4,20},{8,24},{12,28},{16,0},{20,4},{24,8},{28,12},{1,17},{... | collective-permute-start | bytes 56840 | tf_op jit(solution)/shard_map/ppermute | solution.py:19
  89.8 1.9 %copy-start.35 = (s32[3,128]{1,0:T(4,128)S(1)}, s32[3,128]{1,0:T(4,128)}, u32[]{:S(2)}) copy-start(s32[3,128]{1,0:T(4,128)} %param.11) | copy-start | bytes 4612

commit v15 on v13

--- a/solution.py
+++ b/solution.py
@@ -219,6 +219,8 @@
         "lxc,xlbi->clbi", mixing, dz_packed, preferred_element_type=jnp.float32
     )
     grad_rad = jnp.einsum("bclki,clbi->ck", msg_acc, moment_grad_all)
+    for level_bit in range(levels):
+        grad_rad = grad_rad + partner(grad_rad, "space", level_bit)
     grad_blocks = jnp.moveaxis(moment_grad_all, 2, 0)
     tile_grad = jnp.take(grad_blocks, target_idx, axis=0, mode="clip")
     weighted = (
@@ -249,23 +251,13 @@
     grad_src, (dpos_src, grad_rad) = halving_with(grad_part, (dpos_src, grad_rad), "chan")
     grad_rad = lax.dynamic_slice_in_dim(grad_rad, offset, chan_dev, 0)
     own_both = jnp.concatenate([grad_src[:, :atoms_dev], dpos_src[:, :atoms_dev]], axis=0)
-    ghost_rows = chan_dev + 3
     back_list = []
     for level_bit in range(levels):
         low = atoms_dev + level_bit * block_size
         ghost_both = jnp.concatenate(
-            [
-                grad_src[:, low : low + block_size],
-                dpos_src[:, low : low + block_size],
-                as_rows(grad_rad, block_size),
-            ],
-            axis=0,
+            [grad_src[:, low : low + block_size], dpos_src[:, low : low + block_size]], axis=0
         )
-        back_both = partner(ghost_both, "space", level_bit)
-        grad_rad = grad_rad + back_both[ghost_rows:].reshape(-1)[: grad_rad.size].reshape(
-            grad_rad.shape
-        )
-        back_list.append(back_both[:ghost_rows])
+        back_list.append(partner(ghost_both, "space", level_bit))
     all_rows = send_rows[:levels].reshape(-1)
     ghost_hot = (all_rows[:, None] == jnp.arange(atoms_dev, dtype=jnp.int32)[None]).astype(
         jnp.float32

time: 88.2 us -> 94.5 us (1.071)
  waiting for transfers between devices: 11.9 us -> 16.1 us
    ppermute x8 -> x11, waiting for transfers between devices: 7.8 us -> 13 us  [partner(): return lax.ppermute(value, axis, pairs)]
    dot_general x1, local copies, waits for them, and re-layouts: 0.1 us -> 1.42 us  [body(): grad_rad = jnp.einsum('bclki,clbi->ck', msg_acc, moment_grad_all)]
    reduce_sum x1, other arithmetic: 1.47 us -> 0.29 us  [body(): jnp.sum(source_hot[:, None, :, None] * grad_source[:, :, None, :], axis=0)]
    unnamed x88 -> x92, local copies, waits for them, and re-layouts: 7.25 us -> 8.33 us
    another operation x1, local copies, waits for them, and re-layouts: 1.13 us -> 0.09 us  [halving_with(): groups = value.reshape(-1, 2, chunk, width)]
    all_to_all x1, waiting for transfers between devices: 4.15 us -> 3.11 us  [body(): lax.all_to_all(result_rows.reshape(all_chan, components, own_blocks, 1, r...]
    ppermute x8 -> x11, starting transfers between devices: 10.9 us -> 11.7 us  [partner(): return lax.ppermute(value, axis, pairs)]
  transfers between devices with their start and end apart: 10 -> 13, of which waited for: 4 -> 6; matrix products, arithmetic and copies ran while one was open for 22% -> 26% of each run, Pallas kernels for 0% -> 0%
where the time goes in v15:
time: 94.5 us; the launch traced here: 93.8 us
  local copies, waits for them, and re-layouts  22.8 us (24%)
  starting transfers between devices  19.1 us (20%)
  other arithmetic  18.4 us (19%)
  waiting for transfers between devices  16.1 us (17%)
  matrix products  9.73 us (10%)
  blocking collectives  5.85 us (6%)
  between operations  1.69 us (2%)
    ppermute x11, waiting for transfers between devices, partner(): return lax.ppermute(value, axis, pairs)  13 us
    ppermute x11, starting transfers between devices, partner(): return lax.ppermute(value, axis, pairs)  11.7 us
    unnamed x92, local copies, waits for them, and re-layouts  8.33 us
    all_gather x1, blocking collectives, body(): lax.all_gather(jnp.concatenate([src_feat, weight_high, weight_mid, weight...  5.85 us
    reduce_sum x1, other arithmetic, body(): harm_grad = jnp.sum(value_grad * radial[None], axis=1)  5.25 us
    all_to_all x1, starting transfers between devices, body(): lax.all_to_all(out_grad.reshape(chan_dev, components, own_blocks, chan_co...  4.09 us
    all_to_all x1, starting transfers between devices, body(): lax.all_to_all(result_rows.reshape(all_chan, components, own_blocks, 1, r...  3.34 us
    all_to_all x1, waiting for transfers between devices, body(): lax.all_to_all(result_rows.reshape(all_chan, components, own_blocks, 1, r...  3.11 us
  transfers between devices with their start and end apart: 13, of which 6 were waited for; matrix products, arithmetic and copies ran while one was open for 26% of the time, Pallas kernels for 0%

profile of v15, /device:TPU:0, one launch (start us, length us, event | category | flops | bytes accessed | tf_op | source)
XLA Modules:
  0.0 93.8 jit_solution(18372992839564124779)
XLA Ops:
  0.6 0.8 convert_element_type.99
  1.4 1.0 %fusion.26 = f32[35,384]{1,0:T(8,128)S(1)} fusion(s32[384]{0:T(512)} %bitcast.382, f32[3,256]{1,0:T(4,128)} %param.9, f32[32,256]{1,0:T(8,128)S(1)} %convert_element_type.99), kind=kOutput, calls=%fused_computation.42 | convolution fusion | flops 41394944 | bytes 91136 | tf_op jit(solution)/shard_map/dot_general | solution.py:119
  2.4 3.0 %collective-permute-start = (f32[35,128]{1,0:T(8,128)S(1)}, f32[35,128]{1,0:T(8,128)S(1)}, u32[]{:S(2)}, u32[]{:S(2)}) collective-permute-start(f32[35,128]{1,0:T(8,128)S(1)} %get-tuple-element.42), channel_id=1, source_target_pairs={{0,4},{4,0},{8,12},{12,8},{16,20},{20,16},{24,28},{28,24},{1,5},{5... | collective-permute-start | bytes 53768 | tf_op jit(solution)/shard_map/ppermute | solution.py:19
  5.4 2.6 %collective-permute-start.2 = (f32[35,128]{1,0:T(8,128)S(1)}, f32[35,128]{1,0:T(8,128)S(1)}, u32[]{:S(2)}, u32[]{:S(2)}) collective-permute-start(f32[35,128]{1,0:T(8,128)S(1)} %get-tuple-element.43), channel_id=1, source_target_pairs={{0,16},{4,20},{8,24},{12,28},{16,0},{20,4},{24,8},{28,12},{1,17},{... | collective-permute-start | bytes 53768 | tf_op jit(solution)/shard_map/ppermute | solution.py:19
  8.0 1.6 %collective-permute-start.1 = (f32[35,128]{1,0:T(8,128)S(1)}, f32[35,128]{1,0:T(8,128)S(1)}, u32[]{:S(2)}, u32[]{:S(2)}) collective-permute-start(f32[35,128]{1,0:T(8,128)S(1)} %get-tuple-element.44), channel_id=1, source_target_pairs={{0,8},{4,12},{8,0},{12,4},{16,24},{20,28},{24,16},{28,20},{1,9},{5... | collective-permute-start | bytes 53768 | tf_op jit(solution)/shard_map/ppermute | solution.py:19
  9.6 1.3 %reshape.504 = bf16[32,9,2,4,32]{4,3,2,0,1:T(4,128)(2,1)S(1)} reshape(bf16[32,9,256]{2,0,1:T(8,128)(2,1)} %param.16) | data formatting | bytes 294912 | tf_op jit(solution)/shard_map/reshape | solution.py:206
  10.9 0.7 copy.171
  11.6 1.2 %reshape.568 = bf16[4,2,9216]{2,1,0:T(2,128)(2,1)} reshape(bf16[4,9,2,32,32]{4,3,2,1,0:T(8,128)(2,1)S(1)} %bitcast.373) | data formatting | bytes 294912
  12.8 4.1 %all-to-all-start.1 = ((bf16[4,2,9216]{2,1,0:T(2,128)(2,1)}), bf16[4,2,9216]{2,1,0:T(2,128)(2,1)}, u32[]{:S(2)}, u32[]{:S(2)}) async-start(bf16[4,2,9216]{2,1,0:T(2,128)(2,1)} %reshape.568), calls=%async_computation.1 | async-start | bytes 294912 | tf_op jit(solution)/shard_map/all_to_all | solution.py:205
  17.0 0.5 compare_convert_fusion
  17.6 0.6 pad_clamp_fusion
  18.3 0.6 add_multiply_fusion
  18.9 0.7 copy.176
  19.6 0.6 copy.158
  20.2 0.7 copy.184
  21.1 0.6 gather_fusion.3
  21.9 5.9 %all_gather.3 = bf16[128,664]{1,0:T(8,128)(2,1)S(1)} all-gather(bf16[32,664]{1,0:T(8,128)(2,1)S(1)} %concatenate.53), channel_id=1, replica_groups=mesh['space'=8,'chan'=4] {'chan'}, dimensions={0}, use_global_device_ids=true | all-gather | bytes 212480 | tf_op jit(solution)/shard_map/all_gather | solution.py:139
  27.8 0.6 gather_fusion.1
  28.5 0.6 gather_fusion.2
  29.5 0.7 copy.213
  30.2 0.6 gather_fusion
  31.7 0.7 copy-done.10
  32.7 3.0 %fusion.7 = (bf16[128,2,9,32]{0,3,2,1:T(8,128)(2,1)S(1)}, f32[2,128,9,8,32,1]{1,4,5,3,2,0:T(8,128)}) fusion(f32[128,8]{0,1:T(8,128)S(1)} %copy-done.25, f32[8,128,128]{2,1,0:T(8,128)S(1)} %convert_element_type.107, f32[8,2]{0,1:T(2,128)S(1)} %copy-done.36, f32[8,8,32,128]{3,2,0,1:T(8,128)S(1)} %fusion.17, ...), kind=kOutput, calls=%fused_computation.19 | convolution fusion | flops 1214308352 | bytes 5263424 | tf_op jit(solution)/shard_map/lktij,tbcj->bclki/dot_general | solution.py:182
  35.8 1.0 %convolution_bitcast_fusion = f32[128,9,2,32]{0,3,2,1:T(8,128)} fusion(bf16[9,128,128]{2,1,0:T(8,128)(2,1)S(1)} %gather_fusion.3, bf16[128,2,9,32]{0,3,2,1:T(8,128)(2,1)S(1)} %get-tuple-element.63), kind=kOutput, calls=%fused_computation.24 | convolution fusion | flops 18874368 | bytes 737280 | tf_op jit(solution)/shard_map/lxc,clbi->xlbi/dot_general | solution.py:189
  36.8 0.7 broadcast_multiply_fusion
  37.5 1.3 %reshape.569 = bf16[4,9,2,32,32]{4,3,2,1,0:T(8,128)(2,1)S(1)} reshape(bf16[4,2,9216]{2,1,0:T(2,128)(2,1)} %all-to-all-done.1) | data formatting | bytes 294912
  38.9 0.8 copy.172
  39.8 0.5 reshape.513
  40.3 0.4 copy-done.4
  40.8 0.6 fusion.103
  41.4 0.7 multiply_convert_fusion.3
  42.4 0.9 gather_fusion.4
  43.3 1.4 %multiply_convert_fusion = bf16[8,128,9,8,32]{1,4,3,2,0:T(8,128)(2,1)S(1)} fusion(f32[8,128,9,32]{1,3,2,0:T(8,128)S(1)} %gather_fusion.4, f32[8,128,8]{1,2,0:T(8,128)S(1)} %copy-done.16), kind=kLoop, calls=%fused_computation.7 | loop fusion | flops 4718592 | bytes 5931008 | tf_op jit(solution)/shard_map/convert_element_type | solution.py:230
  44.8 2.9 %fusion.8 = f32[8,128,128]{2,1,0:T(8,128)} fusion(bf16[8,128,9,8,32]{1,4,3,2,0:T(8,128)(2,1)S(1)} %multiply_convert_fusion, f32[8,8,32,128]{3,2,0,1:T(8,128)S(1)} %copy-done.2, f32[9,8,32,128]{3,2,1,0:T(8,128)S(1)} %copy-done.7), kind=kOutput, calls=%fused_computation.22 | convolution fusion | flops 608698368 | bytes 7471104 | tf_op jit(solution)/shard_map/tclki,lktij->tcj/dot_general | solution.py:231
  47.7 1.4 %fusion.121 = f32[8,128,2304]{1,2,0:S(1)} fusion(bf16[8,128,2304]{1,2,0:T(8,128)(2,1)S(1)} %bitcast.372, bf16[8,128,128]{2,1,0:T(8,128)(2,1)S(1)} %gather_fusion), kind=kOutput, calls=%fused_computation.238 | convolution fusion | flops 603979776 | bytes 14417920
  49.1 5.2 %multiply_reduce_fusion.1 = (f32[9,8,32,128]{3,2,0,1:T(8,128)S(1)}, f32[8,8,32,128]{3,2,0,1:T(8,128)}) fusion(f32[9,8,8,32,128]{4,3,1,0,2:T(8,128)S(1)} %bitcast.371, f32[8,8,32,128]{3,2,0,1:T(8,128)S(1)} %copy-done.2, f32[9,8,32,128]{3,2,1,0:T(8,128)} %copy-done.6), kind=kLoop, calls=%fused_computation.6 | loop fusion | flops 8880128 | bytes 13893632 | tf_op jit(solution)/shard_map/reduce_sum | solution.py:237
  54.4 0.9 fusion.76
  55.3 0.7 copy-done.5
  56.1 0.9 fusion.6
  57.0 1.4 %copy.204 = f32[128,8]{1,0:T(8,128)} copy(f32[128,8]{0,1:T(8,128)} %fusion.6) | data formatting | bytes 8192 | tf_op jit(solution)/shard_map/bclki,clbi->ck/dot_general | solution.py:221
  58.4 0.5 collective-permute-start.3
  58.9 1.2 %fusion.18 = (f32[8,32,128]{2,1,0:T(8,128)S(1)}, f32[8,32,128]{2,1,0:T(8,128)S(1)}) fusion(f32[8,8,32,128]{3,2,0,1:T(8,128)S(1)} %copy-done.3, f32[8]{0:T(128)} %add_multiply_fusion, f32[8,32,128]{2,1,0:T(8,128)S(1)} %copy-done.9, f32[8,32,128]{2,1,0:T(8,128)S(1)} %copy-done.11), kind=kLoop, calls=%fused_computation.30 | loop fusion | flops 2818048 | bytes 1572896 | tf_op jit(solution)/shard_map/transpose(jvp())/reduce_sum | solution.py:86
  60.2 0.3 fusion.55
  60.6 0.5 copy-done.14
  61.1 0.3 fusion.88
  62.3 0.8 collective-permute-done.3
  63.1 0.9 add.178
  64.0 0.5 collective-permute-start.4
  64.5 3.8 %collective-permute-done.4 = f32[128,8]{1,0:T(8,128)S(1)} collective-permute-done((f32[128,8]{1,0:T(8,128)S(1)}, f32[128,8]{1,0:T(8,128)S(1)}, u32[]{:S(2)}, u32[]{:S(2)}) %collective-permute-start.4) | collective-permute-done | bytes 4128 | tf_op jit(solution)/shard_map/ppermute | solution.py:19
  68.3 0.4 collective-permute-start.5
  68.9 5.2 %collective-permute-done.5 = f32[128,8]{1,0:T(8,128)S(1)} collective-permute-done((f32[128,8]{1,0:T(8,128)S(1)}, f32[128,8]{1,0:T(8,128)S(1)}, u32[]{:S(2)}, u32[]{:S(2)}) %collective-permute-start.5) | collective-permute-done | bytes 4128 | tf_op jit(solution)/shard_map/ppermute | solution.py:19
  74.4 0.8 copy.168
  75.2 1.2 %reshape.566 = bf16[4,2,9216]{2,1,0:T(2,128)(2,1)} reshape(bf16[128,1,9,2,32]{4,3,2,1,0:T(2,128)(2,1)S(1)} %bitcast.374) | data formatting | bytes 294912
  76.5 3.3 %all-to-all-start = ((bf16[4,2,9216]{2,1,0:T(2,128)(2,1)}), bf16[4,2,9216]{2,1,0:T(2,128)(2,1)S(1)}, u32[]{:S(2)}, u32[]{:S(2)}) async-start(bf16[4,2,9216]{2,1,0:T(2,128)(2,1)} %reshape.566), calls=%async_computation | async-start | bytes 294912 | tf_op jit(solution)/shard_map/all_to_all | solution.py:198
  79.9 2.0 %collective-permute-start.7 = (f32[37,640]{1,0:T(8,128)S(1)}, f32[37,640]{1,0:T(8,128)S(1)}, u32[]{:S(2)}, u32[]{:S(2)}) collective-permute-start(f32[37,640]{1,0:T(8,128)S(1)} %pad_maximum_fusion.2), channel_id=1, source_target_pairs={{0,2},{1,3},{2,0},{3,1},{4,6},{5,7},{6,4},{7,5},{8,10},{9,11},{10,... | collective-permute-start | bytes 284168 | tf_op jit(solution)/shard_map/ppermute | solution.py:19
  81.9 3.1 %all-to-all-done = bf16[4,2,9216]{2,1,0:T(2,128)(2,1)S(1)} async-done(((bf16[4,2,9216]{2,1,0:T(2,128)(2,1)}), bf16[4,2,9216]{2,1,0:T(2,128)(2,1)S(1)}, u32[]{:S(2)}, u32[]{:S(2)}) %all-to-all-start) | async-done | bytes 147488 | tf_op jit(solution)/shard_map/all_to_all | solution.py:198
  85.3 0.8 copy.169
  86.1 1.1 %reshape.503 = bf16[32,9,256]{2,0,1:T(8,128)(2,1)} reshape(bf16[32,9,2,4,1,32]{5,3,2,0,1,4:T(4,128)(2,1)S(1)} %copy.169) | data formatting | bytes 294912 | tf_op jit(solution)/shard_map/reshape | solution.py:204
  87.7 0.7 collective-permute-start.8
  88.4 0.7 copy.185
  89.1 2.1 %collective-permute-done.9 = f32[35,128]{1,0:T(8,128)S(1)} collective-permute-done((f32[35,128]{1,0:T(8,128)S(1)}, f32[35,128]{1,0:T(8,128)S(1)}, u32[]{:S(2)}, u32[]{:S(2)}) %collective-permute-start.9) | collective-permute-done | bytes 17952 | tf_op jit(solution)/shard_map/ppermute | solution.py:19
  91.2 1.0 %collective-permute-done.10 = f32[35,128]{1,0:T(8,128)S(1)} collective-permute-done((f32[35,128]{1,0:T(8,128)S(1)}, f32[35,128]{1,0:T(8,128)S(1)}, u32[]{:S(2)}, u32[]{:S(2)}) %collective-permute-start.10) | collective-permute-done | bytes 17952 | tf_op jit(solution)/shard_map/ppermute | solution.py:19
  92.6 0.6 slice_negate_fusion
  93.2 0.6 slice.307
  (171 shorter events, 5.3 us)
Async XLA Ops:
  0.6 20.5 %copy-start = (bf16[3,128,128]{2,1,0:T(8,128)(2,1)S(1)}, bf16[3,128,128]{2,1,0:T(8,128)(2,1)}, u32[]{:S(2)}) copy-start(bf16[3,128,128]{2,1,0:T(8,128)(2,1)} %param.15) | copy-start | bytes 294916
  2.4 19.3 %collective-permute-start = (f32[35,128]{1,0:T(8,128)S(1)}, f32[35,128]{1,0:T(8,128)S(1)}, u32[]{:S(2)}, u32[]{:S(2)}) collective-permute-start(f32[35,128]{1,0:T(8,128)S(1)} %get-tuple-element.42), channel_id=1, source_target_pairs={{0,4},{4,0},{8,12},{12,8},{16,20},{20,16},{24,28},{28,24},{1,5},{5... | collective-permute-start | bytes 53768 | tf_op jit(solution)/shard_map/ppermute | solution.py:19
  5.4 16.3 %collective-permute-start.2 = (f32[35,128]{1,0:T(8,128)S(1)}, f32[35,128]{1,0:T(8,128)S(1)}, u32[]{:S(2)}, u32[]{:S(2)}) collective-permute-start(f32[35,128]{1,0:T(8,128)S(1)} %get-tuple-element.43), channel_id=1, source_target_pairs={{0,16},{4,20},{8,24},{12,28},{16,0},{20,4},{24,8},{28,12},{1,17},{... | collective-permute-start | bytes 53768 | tf_op jit(solution)/shard_map/ppermute | solution.py:19
  8.0 13.8 %collective-permute-start.1 = (f32[35,128]{1,0:T(8,128)S(1)}, f32[35,128]{1,0:T(8,128)S(1)}, u32[]{:S(2)}, u32[]{:S(2)}) collective-permute-start(f32[35,128]{1,0:T(8,128)S(1)} %get-tuple-element.44), channel_id=1, source_target_pairs={{0,8},{4,12},{8,0},{12,4},{16,24},{20,28},{24,16},{28,20},{1,9},{5... | collective-permute-start | bytes 53768 | tf_op jit(solution)/shard_map/ppermute | solution.py:19
  10.8 6.1 %copy-start.37 = (s32[8,2]{0,1:T(2,128)S(1)}, s32[8,2]{0,1:T(2,128)}, u32[]{:S(2)}) copy-start(s32[8,2]{0,1:T(2,128)} %param.12) | copy-start | bytes 196
  10.8 6.7 %copy-start.41 = (s32[8]{0:T(128)S(1)}, s32[8]{0:T(128)}, u32[]{:S(2)}) copy-start(s32[8]{0:T(128)} %param.13) | copy-start | bytes 100
  10.9 6.7 %copy-start.32 = (f32[32,8]{0,1:T(8,128)S(1)}, f32[32,8]{0,1:T(8,128)}, u32[]{:S(2)}) copy-start(f32[32,8]{0,1:T(8,128)} %param.14) | copy-start | bytes 3076
  10.9 6.8 %copy-start.39 = (s32[9]{0:T(128)S(1)}, s32[9]{0:T(128)}, u32[]{:S(2)}) copy-start(s32[9]{0:T(128)} %constant.95) | copy-start | bytes 112
  11.6 10.2 %copy-start.21 = (bf16[32,256]{1,0:T(8,128)(2,1)S(1)}, bf16[32,256]{1,0:T(8,128)(2,1)}, u32[]{:S(2)}) copy-start(bf16[32,256]{1,0:T(8,128)(2,1)} %param.10) | copy-start | bytes 49156
  12.8 15.0 %copy-start.31 = (f32[3,256]{1,0:T(4,128)S(1)}, f32[3,256]{1,0:T(4,128)}, u32[]{:S(2)}) copy-start(f32[3,256]{1,0:T(4,128)} %param.9) | copy-start | bytes 9220
  12.8 24.7 %all-to-all-start.1 = ((bf16[4,2,9216]{2,1,0:T(2,128)(2,1)}), bf16[4,2,9216]{2,1,0:T(2,128)(2,1)}, u32[]{:S(2)}, u32[]{:S(2)}) async-start(bf16[4,2,9216]{2,1,0:T(2,128)(2,1)} %reshape.568), calls=%async_computation.1 | async-start | bytes 294912 | tf_op jit(solution)/shard_map/all_to_all | solution.py:205
  16.9 14.6 %copy-start.33 = (f32[8]{0:T(128)}, f32[8]{0:T(128)S(1)}, u32[]{:S(2)}) copy-start(f32[8]{0:T(128)S(1)} %compare_convert_fusion.1) | copy-start | bytes 100
  17.5 14.0 %copy-start.28 = (f32[8]{0:T(128)}, f32[8]{0:T(128)S(1)}, u32[]{:S(2)}) copy-start(f32[8]{0:T(128)S(1)} %convert_element_type.106) | copy-start | bytes 100
  17.6 11.8 %copy-start.23 = (f32[8,5]{1,0:T(8,128)}, f32[8,5]{1,0:T(8,128)S(1)}, u32[]{:S(2)}) copy-start(f32[8,5]{1,0:T(8,128)S(1)} %get-tuple-element.59) | copy-start | bytes 484
  28.4 2.5 %copy-start.17 = (f32[8,3,128]{2,0,1:T(8,128)}, f32[8,3,128]{2,0,1:T(8,128)S(1)}, u32[]{:S(2)}) copy-start(f32[8,3,128]{2,0,1:T(8,128)S(1)} %copy.162) | copy-start | bytes 36868
  29.1 2.0 %copy-start.19 = (f32[8,3,32]{2,0,1:T(8,128)}, f32[8,3,32]{2,0,1:T(8,128)S(1)}, u32[]{:S(2)}) copy-start(f32[8,3,32]{2,0,1:T(8,128)S(1)} %copy.164) | copy-start | bytes 9220
  31.2 1.2 %copy-start.35 = (f32[8]{0:T(128)S(1)}, f32[8]{0:T(128)}, u32[]{:S(2)}) copy-start(f32[8]{0:T(128)} %add_multiply_fusion) | copy-start | bytes 100
  31.4 1.3 %copy-start.25 = (f32[128,8]{0,1:T(8,128)S(1)}, f32[128,8]{0,1:T(8,128)}, u32[]{:S(2)}) copy-start(f32[128,8]{0,1:T(8,128)} %copy.213) | copy-start | bytes 12292
  31.4 1.3 %copy-start.36 = (f32[8,2]{0,1:T(2,128)S(1)}, f32[8,2]{0,1:T(2,128)}, u32[]{:S(2)}) copy-start(f32[8,2]{0,1:T(2,128)} %copy.158) | copy-start | bytes 196
  31.5 4.2 %copy-start.6 = (f32[9,8,32,128]{3,2,1,0:T(8,128)}, f32[9,8,32,128]{3,2,1,0:T(8,128)S(1)}, u32[]{:S(2)}) copy-start(f32[9,8,32,128]{3,2,1,0:T(8,128)S(1)} %multiply_dynamic-update-slice_fusion) | copy-start | bytes 3538948
  31.7 0.8 copy-start.10
  31.7 4.1 %copy-start.8 = (f32[8,32,128]{2,1,0:T(8,128)}, f32[8,32,128]{2,1,0:T(8,128)S(1)}, u32[]{:S(2)}) copy-start(f32[8,32,128]{2,1,0:T(8,128)S(1)} %get-tuple-element.37) | copy-start | bytes 393220
  32.7 3.0 %copy-start.1 = (f32[8,8,32,128]{3,2,0,1:T(8,128)}, f32[8,8,32,128]{3,2,0,1:T(8,128)S(1)}, u32[]{:S(2)}) copy-start(f32[8,8,32,128]{3,2,0,1:T(8,128)S(1)} %fusion.17) | copy-start | bytes 3145732
  32.7 4.1 %copy-start.29 = (f32[8]{0:T(128)S(1)}, f32[8]{0:T(128)}, u32[]{:S(2)}) copy-start(f32[8]{0:T(128)} %copy-done.28) | copy-start | bytes 100
  39.8 1.0 %copy-start.4 = (f32[128,9,2,32]{0,3,2,1:T(8,128)S(1)}, f32[128,9,2,32]{0,3,2,1:T(8,128)}, u32[]{:S(2)}) copy-start(f32[128,9,2,32]{0,3,2,1:T(8,128)} %convolution_bitcast_fusion) | copy-start | bytes 884740
  42.4 0.9 copy-start.16
  43.3 1.4 %copy-start.2 = (f32[8,8,32,128]{3,2,0,1:T(8,128)S(1)}, f32[8,8,32,128]{3,2,0,1:T(8,128)}, u32[]{:S(2)}) copy-start(f32[8,8,32,128]{3,2,0,1:T(8,128)} %copy-done.1) | copy-start | bytes 3145732
  43.3 1.6 %copy-start.7 = (f32[9,8,32,128]{3,2,1,0:T(8,128)S(1)}, f32[9,8,32,128]{3,2,1,0:T(8,128)}, u32[]{:S(2)}) copy-start(f32[9,8,32,128]{3,2,1,0:T(8,128)} %copy-done.6) | copy-start | bytes 3538948
  54.3 1.8 %copy-start.5 = (f32[2,128,9,8,32,1]{1,4,5,3,2,0:T(8,128)S(1)}, f32[2,128,9,8,32,1]{1,4,5,3,2,0:T(8,128)}, u32[]{:S(2)}) copy-start(f32[2,128,9,8,32,1]{1,4,5,3,2,0:T(8,128)} %get-tuple-element.64) | copy-start | bytes 7077892
  56.1 2.8 %copy-start.3 = (f32[8,8,32,128]{3,2,0,1:T(8,128)S(1)}, f32[8,8,32,128]{3,2,0,1:T(8,128)}, u32[]{:S(2)}) copy-start(f32[8,8,32,128]{3,2,0,1:T(8,128)} %get-tuple-element.25) | copy-start | bytes 3145732
  56.1 2.8 %copy-start.9 = (f32[8,32,128]{2,1,0:T(8,128)S(1)}, f32[8,32,128]{2,1,0:T(8,128)}, u32[]{:S(2)}) copy-start(f32[8,32,128]{2,1,0:T(8,128)} %copy-done.8) | copy-start | bytes 393220
  56.1 2.8 %copy-start.11 = (f32[8,32,128]{2,1,0:T(8,128)S(1)}, f32[8,32,128]{2,1,0:T(8,128)}, u32[]{:S(2)}) copy-start(f32[8,32,128]{2,1,0:T(8,128)} %copy-done.10) | copy-start | bytes 393220
  58.4 1.7 %copy-start.30 = (f32[8]{0:T(128)S(1)}, f32[8]{0:T(128)}, u32[]{:S(2)}) copy-start(f32[8]{0:T(128)} %copy-done.28) | copy-start | bytes 100
  58.4 1.7 %copy-start.34 = (f32[8]{0:T(128)S(1)}, f32[8]{0:T(128)}, u32[]{:S(2)}) copy-start(f32[8]{0:T(128)} %copy-done.33) | copy-start | bytes 100
  58.4 4.7 %collective-permute-start.3 = (f32[128,8]{1,0:T(8,128)}, f32[128,8]{1,0:T(8,128)}, u32[]{:S(2)}, u32[]{:S(2)}) collective-permute-start(f32[128,8]{1,0:T(8,128)} %copy.204), channel_id=1, source_target_pairs={{0,4},{4,0},{8,12},{12,8},{16,20},{20,16},{24,28},{28,24},{1,5},{5... | collective-permute-start | bytes 12296 | tf_op jit(solution)/shard_map/ppermute | solution.py:19
  60.1 0.9 copy-start.14
  60.1 1.0 %copy-start.15 = (f32[8,1,32,128]{3,2,0,1:T(8,128)S(1)}, f32[8,1,32,128]{3,2,0,1:T(8,128)}, u32[]{:S(2)}) copy-start(f32[8,1,32,128]{3,2,0,1:T(8,128)} %get-tuple-element.31) | copy-start | bytes 393220
  60.1 1.0 %copy-start.18 = (f32[8,3,128]{2,0,1:T(8,128)S(1)}, f32[8,3,128]{2,0,1:T(8,128)}, u32[]{:S(2)}) copy-start(f32[8,3,128]{2,0,1:T(8,128)} %copy-done.17) | copy-start | bytes 36868
  60.1 0.9 %copy-start.20 = (f32[8,3,32]{2,0,1:T(8,128)S(1)}, f32[8,3,32]{2,0,1:T(8,128)}, u32[]{:S(2)}) copy-start(f32[8,3,32]{2,0,1:T(8,128)} %copy-done.19) | copy-start | bytes 9220
  60.2 1.3 %copy-start.27 = (f32[8,5]{0,1:T(8,128)S(1)}, f32[8,5]{0,1:T(8,128)}, u32[]{:S(2)}) copy-start(f32[8,5]{0,1:T(8,128)} %copy.176) | copy-start | bytes 484
  60.2 1.4 %copy-start.38 = (f32[4]{0:T(128)S(1)}, f32[4]{0:T(128)}, u32[]{:S(2)}) copy-start(f32[4]{0:T(128)} %compare_convert_fusion) | copy-start | bytes 52
  60.2 1.4 %copy-start.13 = (f32[8,128,128]{2,1,0:T(8,128)S(1)}, f32[8,128,128]{2,1,0:T(8,128)}, u32[]{:S(2)}) copy-start(f32[8,128,128]{2,1,0:T(8,128)} %fusion.8) | copy-start | bytes 1572868
  60.2 1.4 %copy-start.24 = (f32[8,5]{1,0:T(8,128)S(1)}, f32[8,5]{1,0:T(8,128)}, u32[]{:S(2)}) copy-start(f32[8,5]{1,0:T(8,128)} %copy-done.23) | copy-start | bytes 484
  61.9 6.8 %copy-start.26 = (f32[8,5]{0,1:T(8,128)S(1)}, f32[8,5]{0,1:T(8,128)}, u32[]{:S(2)}) copy-start(f32[8,5]{0,1:T(8,128)} %copy.184) | copy-start | bytes 484
  62.1 12.2 %copy-start.12 = (bf16[128,8,2,1,32]{0,4,2,1,3:T(8,128)(2,1)S(1)}, bf16[128,8,2,1,32]{0,4,2,1,3:T(8,128)(2,1)}, u32[]{:S(2)}) copy-start(bf16[128,8,2,1,32]{0,4,2,1,3:T(8,128)(2,1)} %get-tuple-element.46) | copy-start | bytes 393220
  62.2 12.2 %copy-start.22 = (bf16[128,1,2,1,32]{0,4,2,1,3:T(8,128)(2,1)S(1)}, bf16[128,1,2,1,32]{0,4,2,1,3:T(8,128)(2,1)}, u32[]{:S(2)}) copy-start(bf16[128,1,2,1,32]{0,4,2,1,3:T(8,128)(2,1)} %get-tuple-element.35) | copy-start | bytes 49156
  64.0 4.3 %collective-permute-start.4 = (f32[128,8]{1,0:T(8,128)S(1)}, f32[128,8]{1,0:T(8,128)S(1)}, u32[]{:S(2)}, u32[]{:S(2)}) collective-permute-start(f32[128,8]{1,0:T(8,128)S(1)} %add.178), channel_id=1, source_target_pairs={{0,8},{4,12},{8,0},{12,4},{16,24},{20,28},{24,16},{28,20},{1,9},{5... | collective-permute-start | bytes 12296 | tf_op jit(solution)/shard_map/ppermute | solution.py:19
  68.3 5.8 %collective-permute-start.5 = (f32[128,8]{1,0:T(8,128)S(1)}, f32[128,8]{1,0:T(8,128)S(1)}, u32[]{:S(2)}, u32[]{:S(2)}) collective-permute-start(f32[128,8]{1,0:T(8,128)S(1)} %add.179), channel_id=1, source_target_pairs={{0,16},{4,20},{8,24},{12,28},{16,0},{20,4},{24,8},{28,12},{1,17},{... | collective-permute-start | bytes 12296 | tf_op jit(solution)/shard_map/ppermute | solution.py:19
  74.3 5.5 %collective-permute-start.6 = (f32[69,640]{1,0:T(8,128)S(1)}, f32[69,640]{1,0:T(8,128)S(1)}, u32[]{:S(2)}, u32[]{:S(2)}) collective-permute-start(f32[69,640]{1,0:T(8,128)S(1)} %pad_maximum_fusion), channel_id=1, source_target_pairs={{0,1},{1,0},{2,3},{3,2},{4,5},{5,4},{6,7},{7,6},{8,9},{9,8},{10,11... | collective-permute-start | bytes 529928 | tf_op jit(solution)/shard_map/ppermute | solution.py:19
  76.5 8.6 %all-to-all-start = ((bf16[4,2,9216]{2,1,0:T(2,128)(2,1)}), bf16[4,2,9216]{2,1,0:T(2,128)(2,1)S(1)}, u32[]{:S(2)}, u32[]{:S(2)}) async-start(bf16[4,2,9216]{2,1,0:T(2,128)(2,1)} %reshape.566), calls=%async_computation | async-start | bytes 294912 | tf_op jit(solution)/shard_map/all_to_all | solution.py:198
  79.9 7.3 %collective-permute-start.7 = (f32[37,640]{1,0:T(8,128)S(1)}, f32[37,640]{1,0:T(8,128)S(1)}, u32[]{:S(2)}, u32[]{:S(2)}) collective-permute-start(f32[37,640]{1,0:T(8,128)S(1)} %pad_maximum_fusion.2), channel_id=1, source_target_pairs={{0,2},{1,3},{2,0},{3,1},{4,6},{5,7},{6,4},{7,5},{8,10},{9,11},{10,... | collective-permute-start | bytes 284168 | tf_op jit(solution)/shard_map/ppermute | solution.py:19
  85.3 6.9 %copy-start.40 = (s32[3,128]{1,0:T(4,128)S(1)}, s32[3,128]{1,0:T(4,128)}, u32[]{:S(2)}) copy-start(s32[3,128]{1,0:T(4,128)} %param.11) | copy-start | bytes 4612
  87.4 3.8 %collective-permute-start.9 = (f32[35,128]{1,0:T(8,128)S(1)}, f32[35,128]{1,0:T(8,128)S(1)}, u32[]{:S(2)}, u32[]{:S(2)}) collective-permute-start(f32[35,128]{1,0:T(8,128)S(1)} %pad_maximum_fusion.4), channel_id=1, source_target_pairs={{0,8},{4,12},{8,0},{12,4},{16,24},{20,28},{24,16},{28,20},{1,9},{5... | collective-permute-start | bytes 53768 | tf_op jit(solution)/shard_map/ppermute | solution.py:19
  87.5 4.7 %collective-permute-start.10 = (f32[35,128]{1,0:T(8,128)S(1)}, f32[35,128]{1,0:T(8,128)S(1)}, u32[]{:S(2)}, u32[]{:S(2)}) collective-permute-start(f32[35,128]{1,0:T(8,128)S(1)} %pad_maximum_fusion.5), channel_id=1, source_target_pairs={{0,16},{4,20},{8,24},{12,28},{16,0},{20,4},{24,8},{28,12},{1,17},{... | collective-permute-start | bytes 53768 | tf_op jit(solution)/shard_map/ppermute | solution.py:19
  87.7 4.6 %collective-permute-start.8 = (f32[35,128]{1,0:T(8,128)S(1)}, f32[35,128]{1,0:T(8,128)S(1)}, u32[]{:S(2)}, u32[]{:S(2)}) collective-permute-start(f32[35,128]{1,0:T(8,128)S(1)} %pad_maximum_fusion.3), channel_id=1, source_target_pairs={{0,4},{4,0},{8,12},{12,8},{16,20},{20,16},{24,28},{28,24},{1,5},{5... | collective-permute-start | bytes 53768 | tf_op jit(solution)/shard_map/ppermute | solution.py:19

commit v16 on v13

--- a/solution.py
+++ b/solution.py
@@ -218,6 +218,7 @@
     moment_grad_all = jnp.einsum(
         "lxc,xlbi->clbi", mixing, dz_packed, preferred_element_type=jnp.float32
     )
+    result, moment_grad_all = lax.optimization_barrier((result, moment_grad_all))
     grad_rad = jnp.einsum("bclki,clbi->ck", msg_acc, moment_grad_all)
     grad_blocks = jnp.moveaxis(moment_grad_all, 2, 0)
     tile_grad = jnp.take(grad_blocks, target_idx, axis=0, mode="clip")

time: 88.2 us -> 94.8 us (1.075)
  waiting for transfers between devices: 11.9 us -> 21.5 us
  other arithmetic: 17.7 us -> 16.2 us
  starting transfers between devices: 18.3 us -> 16.8 us
    ppermute x8, waiting for transfers between devices: 7.8 us -> 17.1 us  [partner(): return lax.ppermute(value, axis, pairs)]
    ppermute x8, starting transfers between devices: 10.9 us -> 9.19 us  [partner(): return lax.ppermute(value, axis, pairs)]
    another operation x2, other arithmetic: 1.35 us -> 0.09 us
    unnamed x88 -> x84, local copies, waits for them, and re-layouts: 7.25 us -> 7.24 us
  transfers between devices with their start and end apart: 10 -> 10, of which waited for: 4 -> 6; matrix products, arithmetic and copies ran while one was open for 22% -> 16% of each run, Pallas kernels for 0% -> 0%
where the time goes in v16:
time: 94.8 us; the launch traced here: 94 us
  local copies, waits for them, and re-layouts  22.3 us (24%)
  waiting for transfers between devices  21.5 us (23%)
  starting transfers between devices  16.8 us (18%)
  other arithmetic  16.2 us (17%)
  matrix products  9.72 us (10%)
  blocking collectives  5.85 us (6%)
  between operations  1.64 us (2%)
    ppermute x8, waiting for transfers between devices, partner(): return lax.ppermute(value, axis, pairs)  17.1 us
    ppermute x8, starting transfers between devices, partner(): return lax.ppermute(value, axis, pairs)  9.19 us
    unnamed x84, local copies, waits for them, and re-layouts  7.24 us
    all_gather x1, blocking collectives, body(): lax.all_gather(jnp.concatenate([src_feat, weight_high, weight_mid, weight...  5.85 us
    reduce_sum x1, other arithmetic, body(): harm_grad = jnp.sum(value_grad * radial[None], axis=1)  5.08 us
    all_to_all x1, waiting for transfers between devices, body(): lax.all_to_all(result_rows.reshape(all_chan, components, own_blocks, 1, r...  4.38 us
    all_to_all x1, starting transfers between devices, body(): lax.all_to_all(out_grad.reshape(chan_dev, components, own_blocks, chan_co...  4.1 us
    all_to_all x1, starting transfers between devices, body(): lax.all_to_all(result_rows.reshape(all_chan, components, own_blocks, 1, r...  3.52 us
  transfers between devices with their start and end apart: 10, of which 6 were waited for; matrix products, arithmetic and copies ran while one was open for 16% of the time, Pallas kernels for 0%

profile of v16, /device:TPU:0, one launch (start us, length us, event | category | flops | bytes accessed | tf_op | source)
XLA Modules:
  0.0 94.0 jit_solution(7066602499994981433)
XLA Ops:
  0.6 0.8 convert_element_type.99
  1.4 1.0 %fusion.26 = f32[35,384]{1,0:T(8,128)S(1)} fusion(s32[384]{0:T(512)} %bitcast.388, f32[3,256]{1,0:T(4,128)} %param.9, f32[32,256]{1,0:T(8,128)S(1)} %convert_element_type.99), kind=kOutput, calls=%fused_computation.43 | convolution fusion | flops 41394944 | bytes 91136 | tf_op jit(solution)/shard_map/dot_general | solution.py:119
  2.4 3.0 %collective-permute-start = (f32[35,128]{1,0:T(8,128)S(1)}, f32[35,128]{1,0:T(8,128)S(1)}, u32[]{:S(2)}, u32[]{:S(2)}) collective-permute-start(f32[35,128]{1,0:T(8,128)S(1)} %get-tuple-element.46), channel_id=1, source_target_pairs={{0,4},{4,0},{8,12},{12,8},{16,20},{20,16},{24,28},{28,24},{1,5},{5... | collective-permute-start | bytes 53768 | tf_op jit(solution)/shard_map/ppermute | solution.py:19
  5.4 2.6 %collective-permute-start.2 = (f32[35,128]{1,0:T(8,128)S(1)}, f32[35,128]{1,0:T(8,128)S(1)}, u32[]{:S(2)}, u32[]{:S(2)}) collective-permute-start(f32[35,128]{1,0:T(8,128)S(1)} %get-tuple-element.47), channel_id=1, source_target_pairs={{0,16},{4,20},{8,24},{12,28},{16,0},{20,4},{24,8},{28,12},{1,17},{... | collective-permute-start | bytes 53768 | tf_op jit(solution)/shard_map/ppermute | solution.py:19
  8.0 1.6 %collective-permute-start.1 = (f32[35,128]{1,0:T(8,128)S(1)}, f32[35,128]{1,0:T(8,128)S(1)}, u32[]{:S(2)}, u32[]{:S(2)}) collective-permute-start(f32[35,128]{1,0:T(8,128)S(1)} %get-tuple-element.48), channel_id=1, source_target_pairs={{0,8},{4,12},{8,0},{12,4},{16,24},{20,28},{24,16},{28,20},{1,9},{5... | collective-permute-start | bytes 53768 | tf_op jit(solution)/shard_map/ppermute | solution.py:19
  9.6 1.3 %reshape.519 = bf16[32,9,2,4,32]{4,3,2,0,1:T(4,128)(2,1)S(1)} reshape(bf16[32,9,256]{2,0,1:T(8,128)(2,1)} %param.16) | data formatting | bytes 294912 | tf_op jit(solution)/shard_map/reshape | solution.py:206
  10.9 0.7 copy.176
  11.6 1.2 %reshape.586 = bf16[4,2,9216]{2,1,0:T(2,128)(2,1)} reshape(bf16[4,9,2,32,32]{4,3,2,1,0:T(8,128)(2,1)S(1)} %bitcast.376) | data formatting | bytes 294912
  12.8 4.1 %all-to-all-start.1 = ((bf16[4,2,9216]{2,1,0:T(2,128)(2,1)}), bf16[4,2,9216]{2,1,0:T(2,128)(2,1)}, u32[]{:S(2)}, u32[]{:S(2)}) async-start(bf16[4,2,9216]{2,1,0:T(2,128)(2,1)} %reshape.586), calls=%async_computation.1 | async-start | bytes 294912 | tf_op jit(solution)/shard_map/all_to_all | solution.py:205
  17.0 0.5 compare_convert_fusion
  17.6 0.6 pad_clamp_fusion
  18.4 0.7 copy.182
  19.2 0.7 copy.190
  20.0 0.6 gather_fusion.3
  20.8 5.9 %all_gather.3 = bf16[128,664]{1,0:T(8,128)(2,1)S(1)} all-gather(bf16[32,664]{1,0:T(8,128)(2,1)S(1)} %concatenate.53), channel_id=1, replica_groups=mesh['space'=8,'chan'=4] {'chan'}, dimensions={0}, use_global_device_ids=true | all-gather | bytes 212480 | tf_op jit(solution)/shard_map/all_gather | solution.py:139
  26.7 0.6 gather_fusion.1
  27.4 0.6 gather_fusion.2
  28.5 0.6 gather_fusion
  30.0 0.8 copy-done.10
  30.7 0.3 fusion.17
  31.0 3.0 %fusion.7 = (bf16[128,2,9,32]{0,3,2,1:T(8,128)(2,1)S(1)}, f32[2,128,9,8,32,1]{1,4,5,3,2,0:T(8,128)}) fusion(f32[128,8]{0,1:T(8,128)S(1)} %copy.219, f32[8,128,128]{2,1,0:T(8,128)S(1)} %convert_element_type.107, f32[8,2]{0,1:T(2,128)S(1)} %copy.164, f32[8,8,32,128]{3,2,0,1:T(8,128)S(1)} %fusion.17, f32[9,8,32,128]{3,2,1,0:T(8,128)S(1)} %multiply_dynamic-update-slice_fusion), kind=kOutput, calls=%fused_computation.19 | convolution fusion | flops 1214308352 | bytes 5263424 | tf_op jit(solution)/shard_map/lktij,tbcj->bclki/dot_general | solution.py:182
  34.1 1.0 %convolution_bitcast_fusion.1 = f32[128,9,2,32]{0,3,2,1:T(8,128)} fusion(bf16[9,128,128]{2,1,0:T(8,128)(2,1)S(1)} %gather_fusion.3, bf16[128,2,9,32]{0,3,2,1:T(8,128)(2,1)S(1)} %get-tuple-element.67), kind=kOutput, calls=%fused_computation.25 | convolution fusion | flops 18874368 | bytes 737280 | tf_op jit(solution)/shard_map/lxc,clbi->xlbi/dot_general | solution.py:189
  35.1 0.7 broadcast_multiply_fusion
  35.8 1.3 %reshape.587 = bf16[4,9,2,32,32]{4,3,2,1,0:T(8,128)(2,1)S(1)} reshape(bf16[4,2,9216]{2,1,0:T(2,128)(2,1)} %all-to-all-done.1) | data formatting | bytes 294912
  37.2 0.8 copy.177
  38.1 0.5 reshape.531
  38.6 0.4 copy-done.4
  39.2 0.8 copy.174
  40.0 1.2 %reshape.584 = bf16[4,2,9216]{2,1,0:T(2,128)(2,1)} reshape(bf16[128,1,9,2,32]{4,3,2,1,0:T(2,128)(2,1)S(1)} %bitcast.377) | data formatting | bytes 294912
  41.3 3.5 %all-to-all-start = ((bf16[4,2,9216]{2,1,0:T(2,128)(2,1)}), bf16[4,2,9216]{2,1,0:T(2,128)(2,1)S(1)}, u32[]{:S(2)}, u32[]{:S(2)}) async-start(bf16[4,2,9216]{2,1,0:T(2,128)(2,1)} %reshape.584), calls=%async_computation | async-start | bytes 294912 | tf_op jit(solution)/shard_map/all_to_all | solution.py:198
  44.8 0.2 convolution_bitcast_fusion
  45.0 4.4 %all-to-all-done = bf16[4,2,9216]{2,1,0:T(2,128)(2,1)S(1)} async-done(((bf16[4,2,9216]{2,1,0:T(2,128)(2,1)}), bf16[4,2,9216]{2,1,0:T(2,128)(2,1)S(1)}, u32[]{:S(2)}, u32[]{:S(2)}) %all-to-all-start) | async-done | bytes 147488 | tf_op jit(solution)/shard_map/all_to_all | solution.py:198
  49.4 0.3 reshape.585
  49.7 0.8 copy.175
  50.4 1.1 %reshape.518 = bf16[32,9,256]{2,0,1:T(8,128)(2,1)} reshape(bf16[32,9,2,4,1,32]{5,3,2,0,1,4:T(4,128)(2,1)S(1)} %copy.175) | data formatting | bytes 294912 | tf_op jit(solution)/shard_map/reshape | solution.py:204
  51.5 0.9 gather_fusion.4
  52.4 1.4 %multiply_convert_fusion = bf16[8,128,9,8,32]{1,4,3,2,0:T(8,128)(2,1)S(1)} fusion(f32[8,128,9,32]{1,3,2,0:T(8,128)S(1)} %gather_fusion.4, f32[8,128,8]{1,2,0:T(8,128)S(1)} %copy-done.15), kind=kLoop, calls=%fused_computation.7 | loop fusion | flops 4718592 | bytes 5931008 | tf_op jit(solution)/shard_map/convert_element_type | solution.py:229
  53.8 0.2 copy-done.7
  54.0 2.8 %fusion.8 = f32[8,128,128]{2,1,0:T(8,128)} fusion(bf16[8,128,9,8,32]{1,4,3,2,0:T(8,128)(2,1)S(1)} %multiply_convert_fusion, f32[8,8,32,128]{3,2,0,1:T(8,128)S(1)} %copy-done.2, f32[9,8,32,128]{3,2,1,0:T(8,128)S(1)} %copy-done.7), kind=kOutput, calls=%fused_computation.22 | convolution fusion | flops 608698368 | bytes 7471104 | tf_op jit(solution)/shard_map/tclki,lktij->tcj/dot_general | solution.py:230
  56.8 1.4 %fusion.120 = f32[8,128,2304]{1,2,0:S(1)} fusion(bf16[8,128,2304]{1,2,0:T(8,128)(2,1)S(1)} %bitcast.375, bf16[8,128,128]{2,1,0:T(8,128)(2,1)S(1)} %gather_fusion), kind=kOutput, calls=%fused_computation.238 | convolution fusion | flops 603979776 | bytes 14417920
  58.2 5.1 %multiply_reduce_fusion.1 = (f32[9,8,32,128]{3,2,0,1:T(8,128)S(1)}, f32[8,8,32,128]{3,2,0,1:T(8,128)}) fusion(f32[9,8,8,32,128]{4,3,1,0,2:T(8,128)S(1)} %bitcast.374, f32[8,8,32,128]{3,2,0,1:T(8,128)S(1)} %copy-done.2, f32[9,8,32,128]{3,2,1,0:T(8,128)} %copy-done.6), kind=kLoop, calls=%fused_computation.6 | loop fusion | flops 8880128 | bytes 13893632 | tf_op jit(solution)/shard_map/reduce_sum | solution.py:236
  63.3 0.8 fusion.42
  64.0 0.9 fusion.75
  65.0 0.3 fusion.6
  65.7 1.5 %multiply_reduce_fusion.2 = f32[128,5,128]{2,0,1:T(8,128)S(1)} fusion(f32[8,128,128]{2,1,0:T(8,128)} %fusion.8, f32[8,5]{1,0:T(8,128)S(1)} %copy-done.22), kind=kLoop, calls=%fused_computation.15 | loop fusion | flops 1228800 | bytes 852128 | tf_op jit(solution)/shard_map/reduce_sum | solution.py:239
  67.1 1.0 %copy.181 = f32[128,5,128]{2,1,0:T(8,128)} copy(f32[128,5,128]{2,0,1:T(8,128)S(1)} %multiply_reduce_fusion.2) | data formatting | bytes 655360 | tf_op jit(solution)/shard_map/reduce_sum | solution.py:239
  68.2 1.1 %reshape_reshape.13 = f32[2,2,32,640]{3,2,1,0:T(8,128)S(1)} reshape(f32[128,5,128]{2,1,0:T(8,128)} %copy.181) | data formatting | bytes 655360 | tf_op jit(solution)/shard_map/reshape;reshape | solution.py:46
  69.3 0.5 fusion.18
  70.0 0.3 fusion.54
  70.3 0.5 copy-done.12
  70.9 0.3 fusion.87
  71.8 1.4 %collective-permute-done.3 = f32[69,640]{1,0:T(8,128)S(1)} collective-permute-done((f32[69,640]{1,0:T(8,128)S(1)}, f32[69,640]{1,0:T(8,128)S(1)}, u32[]{:S(2)}, u32[]{:S(2)}) %collective-permute-start.3) | collective-permute-done | bytes 176672 | tf_op jit(solution)/shard_map/ppermute | solution.py:19
  73.3 0.4 collective-permute-start.4
  73.7 4.6 %collective-permute-done.4 = f32[37,640]{1,0:T(8,128)S(1)} collective-permute-done((f32[37,640]{1,0:T(8,128)S(1)}, f32[37,640]{1,0:T(8,128)S(1)}, u32[]{:S(2)}, u32[]{:S(2)}) %collective-permute-start.4) | collective-permute-done | bytes 94752 | tf_op jit(solution)/shard_map/ppermute | solution.py:19
  78.6 0.6 collective-permute-start.5
  79.2 3.3 %collective-permute-done.5 = f32[37,128]{1,0:T(8,128)S(1)} collective-permute-done((f32[37,128]{1,0:T(8,128)S(1)}, f32[37,128]{1,0:T(8,128)S(1)}, u32[]{:S(2)}, u32[]{:S(2)}) %collective-permute-start.5) | collective-permute-done | bytes 18976 | tf_op jit(solution)/shard_map/ppermute | solution.py:19
  82.7 0.5 collective-permute-start.6
  83.2 3.3 %collective-permute-done.6 = f32[37,128]{1,0:T(8,128)S(1)} collective-permute-done((f32[37,128]{1,0:T(8,128)S(1)}, f32[37,128]{1,0:T(8,128)S(1)}, u32[]{:S(2)}, u32[]{:S(2)}) %collective-permute-start.6) | collective-permute-done | bytes 18976 | tf_op jit(solution)/shard_map/ppermute | solution.py:19
  86.8 0.4 collective-permute-start.7
  87.2 4.6 %collective-permute-done.7 = f32[37,128]{1,0:T(8,128)S(1)} collective-permute-done((f32[37,128]{1,0:T(8,128)S(1)}, f32[37,128]{1,0:T(8,128)S(1)}, u32[]{:S(2)}, u32[]{:S(2)}) %collective-permute-start.7) | collective-permute-done | bytes 18976 | tf_op jit(solution)/shard_map/ppermute | solution.py:19
  91.7 0.3 maximum_add_fusion
  92.0 0.6 slice_negate_fusion
  92.6 0.6 slice.337
  93.3 0.7 copy.191
  (166 shorter events, 4.3 us)
Async XLA Ops:
  0.6 19.4 %copy-start = (bf16[3,128,128]{2,1,0:T(8,128)(2,1)S(1)}, bf16[3,128,128]{2,1,0:T(8,128)(2,1)}, u32[]{:S(2)}) copy-start(bf16[3,128,128]{2,1,0:T(8,128)(2,1)} %param.15) | copy-start | bytes 294916
  2.4 18.3 %collective-permute-start = (f32[35,128]{1,0:T(8,128)S(1)}, f32[35,128]{1,0:T(8,128)S(1)}, u32[]{:S(2)}, u32[]{:S(2)}) collective-permute-start(f32[35,128]{1,0:T(8,128)S(1)} %get-tuple-element.46), channel_id=1, source_target_pairs={{0,4},{4,0},{8,12},{12,8},{16,20},{20,16},{24,28},{28,24},{1,5},{5... | collective-permute-start | bytes 53768 | tf_op jit(solution)/shard_map/ppermute | solution.py:19
  5.4 15.3 %collective-permute-start.2 = (f32[35,128]{1,0:T(8,128)S(1)}, f32[35,128]{1,0:T(8,128)S(1)}, u32[]{:S(2)}, u32[]{:S(2)}) collective-permute-start(f32[35,128]{1,0:T(8,128)S(1)} %get-tuple-element.47), channel_id=1, source_target_pairs={{0,16},{4,20},{8,24},{12,28},{16,0},{20,4},{24,8},{28,12},{1,17},{... | collective-permute-start | bytes 53768 | tf_op jit(solution)/shard_map/ppermute | solution.py:19
  8.0 12.7 %collective-permute-start.1 = (f32[35,128]{1,0:T(8,128)S(1)}, f32[35,128]{1,0:T(8,128)S(1)}, u32[]{:S(2)}, u32[]{:S(2)}) collective-permute-start(f32[35,128]{1,0:T(8,128)S(1)} %get-tuple-element.48), channel_id=1, source_target_pairs={{0,8},{4,12},{8,0},{12,4},{16,24},{20,28},{24,16},{28,20},{1,9},{5... | collective-permute-start | bytes 53768 | tf_op jit(solution)/shard_map/ppermute | solution.py:19
  10.8 6.1 %copy-start.33 = (s32[8,2]{0,1:T(2,128)S(1)}, s32[8,2]{0,1:T(2,128)}, u32[]{:S(2)}) copy-start(s32[8,2]{0,1:T(2,128)} %param.12) | copy-start | bytes 196
  10.8 6.7 %copy-start.37 = (s32[8]{0:T(128)S(1)}, s32[8]{0:T(128)}, u32[]{:S(2)}) copy-start(s32[8]{0:T(128)} %param.13) | copy-start | bytes 100
  10.9 6.7 %copy-start.28 = (f32[32,8]{0,1:T(8,128)S(1)}, f32[32,8]{0,1:T(8,128)}, u32[]{:S(2)}) copy-start(f32[32,8]{0,1:T(8,128)} %param.14) | copy-start | bytes 3076
  10.9 6.8 %copy-start.35 = (s32[9]{0:T(128)S(1)}, s32[9]{0:T(128)}, u32[]{:S(2)}) copy-start(s32[9]{0:T(128)} %constant.95) | copy-start | bytes 112
  11.6 9.1 %copy-start.20 = (bf16[32,256]{1,0:T(8,128)(2,1)S(1)}, bf16[32,256]{1,0:T(8,128)(2,1)}, u32[]{:S(2)}) copy-start(bf16[32,256]{1,0:T(8,128)(2,1)} %param.10) | copy-start | bytes 49156
  12.8 13.9 %copy-start.27 = (f32[3,256]{1,0:T(4,128)S(1)}, f32[3,256]{1,0:T(4,128)}, u32[]{:S(2)}) copy-start(f32[3,256]{1,0:T(4,128)} %param.9) | copy-start | bytes 9220
  12.8 23.0 %all-to-all-start.1 = ((bf16[4,2,9216]{2,1,0:T(2,128)(2,1)}), bf16[4,2,9216]{2,1,0:T(2,128)(2,1)}, u32[]{:S(2)}, u32[]{:S(2)}) async-start(bf16[4,2,9216]{2,1,0:T(2,128)(2,1)} %reshape.586), calls=%async_computation.1 | async-start | bytes 294912 | tf_op jit(solution)/shard_map/all_to_all | solution.py:205
  16.9 12.9 %copy-start.29 = (f32[8]{0:T(128)}, f32[8]{0:T(128)S(1)}, u32[]{:S(2)}) copy-start(f32[8]{0:T(128)S(1)} %compare_convert_fusion.1) | copy-start | bytes 100
  17.5 17.6 %copy-start.25 = (f32[8]{0:T(128)}, f32[8]{0:T(128)S(1)}, u32[]{:S(2)}) copy-start(f32[8]{0:T(128)S(1)} %convert_element_type.106) | copy-start | bytes 100
  17.6 2.4 %copy-start.21 = (f32[8,5]{1,0:T(8,128)}, f32[8,5]{1,0:T(8,128)S(1)}, u32[]{:S(2)}) copy-start(f32[8,5]{1,0:T(8,128)S(1)} %get-tuple-element.63) | copy-start | bytes 484
  18.3 11.7 %copy-start.31 = (f32[8]{0:T(128)}, f32[8]{0:T(128)S(1)}, u32[]{:S(2)}) copy-start(f32[8]{0:T(128)S(1)} %add_multiply_fusion) | copy-start | bytes 100
  27.3 1.9 %copy-start.16 = (f32[8,3,128]{2,0,1:T(8,128)}, f32[8,3,128]{2,0,1:T(8,128)S(1)}, u32[]{:S(2)}) copy-start(f32[8,3,128]{2,0,1:T(8,128)S(1)} %copy.168) | copy-start | bytes 36868
  28.0 1.4 %copy-start.18 = (f32[8,3,32]{2,0,1:T(8,128)}, f32[8,3,32]{2,0,1:T(8,128)S(1)}, u32[]{:S(2)}) copy-start(f32[8,3,32]{2,0,1:T(8,128)S(1)} %copy.170) | copy-start | bytes 9220
  29.8 4.2 %copy-start.6 = (f32[9,8,32,128]{3,2,1,0:T(8,128)}, f32[9,8,32,128]{3,2,1,0:T(8,128)S(1)}, u32[]{:S(2)}) copy-start(f32[9,8,32,128]{3,2,1,0:T(8,128)S(1)} %multiply_dynamic-update-slice_fusion) | copy-start | bytes 3538948
  30.0 0.8 copy-start.10
  30.0 4.1 %copy-start.8 = (f32[8,32,128]{2,1,0:T(8,128)}, f32[8,32,128]{2,1,0:T(8,128)S(1)}, u32[]{:S(2)}) copy-start(f32[8,32,128]{2,1,0:T(8,128)S(1)} %get-tuple-element.41) | copy-start | bytes 393220
  31.0 3.0 %copy-start.1 = (f32[8,8,32,128]{3,2,0,1:T(8,128)}, f32[8,8,32,128]{3,2,0,1:T(8,128)S(1)}, u32[]{:S(2)}) copy-start(f32[8,8,32,128]{3,2,0,1:T(8,128)S(1)} %fusion.17) | copy-start | bytes 3145732
  38.1 1.0 %copy-start.4 = (f32[128,9,2,32]{0,3,2,1:T(8,128)S(1)}, f32[128,9,2,32]{0,3,2,1:T(8,128)}, u32[]{:S(2)}) copy-start(f32[128,9,2,32]{0,3,2,1:T(8,128)} %convolution_bitcast_fusion.1) | copy-start | bytes 884740
  41.3 8.1 %all-to-all-start = ((bf16[4,2,9216]{2,1,0:T(2,128)(2,1)}), bf16[4,2,9216]{2,1,0:T(2,128)(2,1)S(1)}, u32[]{:S(2)}, u32[]{:S(2)}) async-start(bf16[4,2,9216]{2,1,0:T(2,128)(2,1)} %reshape.584), calls=%async_computation | async-start | bytes 294912 | tf_op jit(solution)/shard_map/all_to_all | solution.py:198
  51.5 0.9 copy-start.15
  52.4 1.4 %copy-start.2 = (f32[8,8,32,128]{3,2,0,1:T(8,128)S(1)}, f32[8,8,32,128]{3,2,0,1:T(8,128)}, u32[]{:S(2)}) copy-start(f32[8,8,32,128]{3,2,0,1:T(8,128)} %copy-done.1) | copy-start | bytes 3145732
  52.4 1.6 %copy-start.7 = (f32[9,8,32,128]{3,2,1,0:T(8,128)S(1)}, f32[9,8,32,128]{3,2,1,0:T(8,128)}, u32[]{:S(2)}) copy-start(f32[9,8,32,128]{3,2,1,0:T(8,128)} %copy-done.6) | copy-start | bytes 3538948
  63.3 1.7 %copy-start.5 = (f32[2,128,9,8,32,1]{1,4,5,3,2,0:T(8,128)S(1)}, f32[2,128,9,8,32,1]{1,4,5,3,2,0:T(8,128)}, u32[]{:S(2)}) copy-start(f32[2,128,9,8,32,1]{1,4,5,3,2,0:T(8,128)} %get-tuple-element.68) | copy-start | bytes 7077892
  65.0 0.7 copy-start.22
  65.7 3.6 %copy-start.3 = (f32[8,8,32,128]{3,2,0,1:T(8,128)S(1)}, f32[8,8,32,128]{3,2,0,1:T(8,128)}, u32[]{:S(2)}) copy-start(f32[8,8,32,128]{3,2,0,1:T(8,128)} %get-tuple-element.29) | copy-start | bytes 3145732
  65.7 3.7 %copy-start.9 = (f32[8,32,128]{2,1,0:T(8,128)S(1)}, f32[8,32,128]{2,1,0:T(8,128)}, u32[]{:S(2)}) copy-start(f32[8,32,128]{2,1,0:T(8,128)} %copy-done.8) | copy-start | bytes 393220
  65.7 3.7 %copy-start.11 = (f32[8,32,128]{2,1,0:T(8,128)S(1)}, f32[8,32,128]{2,1,0:T(8,128)}, u32[]{:S(2)}) copy-start(f32[8,32,128]{2,1,0:T(8,128)} %copy-done.10) | copy-start | bytes 393220
  65.7 3.7 %copy-start.32 = (f32[8]{0:T(128)S(1)}, f32[8]{0:T(128)}, u32[]{:S(2)}) copy-start(f32[8]{0:T(128)} %copy-done.31) | copy-start | bytes 100
  68.2 1.8 %copy-start.26 = (f32[8]{0:T(128)S(1)}, f32[8]{0:T(128)}, u32[]{:S(2)}) copy-start(f32[8]{0:T(128)} %copy-done.25) | copy-start | bytes 100
  68.2 1.8 %copy-start.30 = (f32[8]{0:T(128)S(1)}, f32[8]{0:T(128)}, u32[]{:S(2)}) copy-start(f32[8]{0:T(128)} %copy-done.29) | copy-start | bytes 100
  69.9 0.9 copy-start.12
  69.9 1.0 %copy-start.13 = (f32[8,1,32,128]{3,2,0,1:T(8,128)S(1)}, f32[8,1,32,128]{3,2,0,1:T(8,128)}, u32[]{:S(2)}) copy-start(f32[8,1,32,128]{3,2,0,1:T(8,128)} %get-tuple-element.34) | copy-start | bytes 393220
  69.9 1.0 %copy-start.14 = (f32[8,1,32,128]{3,2,0,1:T(8,128)S(1)}, f32[8,1,32,128]{3,2,0,1:T(8,128)}, u32[]{:S(2)}) copy-start(f32[8,1,32,128]{3,2,0,1:T(8,128)} %get-tuple-element.35) | copy-start | bytes 393220
  69.9 1.0 %copy-start.17 = (f32[8,3,128]{2,0,1:T(8,128)S(1)}, f32[8,3,128]{2,0,1:T(8,128)}, u32[]{:S(2)}) copy-start(f32[8,3,128]{2,0,1:T(8,128)} %copy-done.16) | copy-start | bytes 36868
  69.9 1.0 %copy-start.19 = (f32[8,3,32]{2,0,1:T(8,128)S(1)}, f32[8,3,32]{2,0,1:T(8,128)}, u32[]{:S(2)}) copy-start(f32[8,3,32]{2,0,1:T(8,128)} %copy-done.18) | copy-start | bytes 9220
  69.9 1.3 %copy-start.24 = (f32[8,5]{0,1:T(8,128)S(1)}, f32[8,5]{0,1:T(8,128)}, u32[]{:S(2)}) copy-start(f32[8,5]{0,1:T(8,128)} %copy.190) | copy-start | bytes 484
  69.9 1.4 %copy-start.23 = (f32[8,5]{0,1:T(8,128)S(1)}, f32[8,5]{0,1:T(8,128)}, u32[]{:S(2)}) copy-start(f32[8,5]{0,1:T(8,128)} %copy.182) | copy-start | bytes 484
  70.0 1.5 %copy-start.34 = (f32[4]{0:T(128)S(1)}, f32[4]{0:T(128)}, u32[]{:S(2)}) copy-start(f32[4]{0:T(128)} %compare_convert_fusion) | copy-start | bytes 52
  71.7 20.0 %copy-start.36 = (s32[3,128]{1,0:T(4,128)S(1)}, s32[3,128]{1,0:T(4,128)}, u32[]{:S(2)}) copy-start(s32[3,128]{1,0:T(4,128)} %param.11) | copy-start | bytes 4612
  71.7 1.5 %collective-permute-start.3 = (f32[69,640]{1,0:T(8,128)S(1)}, f32[69,640]{1,0:T(8,128)S(1)}, u32[]{:S(2)}, u32[]{:S(2)}) collective-permute-start(f32[69,640]{1,0:T(8,128)S(1)} %pad_maximum_fusion), channel_id=1, source_target_pairs={{0,1},{1,0},{2,3},{3,2},{4,5},{5,4},{6,7},{7,6},{8,9},{9,8},{10,11... | collective-permute-start | bytes 529928 | tf_op jit(solution)/shard_map/ppermute | solution.py:19
  73.3 5.0 %collective-permute-start.4 = (f32[37,640]{1,0:T(8,128)S(1)}, f32[37,640]{1,0:T(8,128)S(1)}, u32[]{:S(2)}, u32[]{:S(2)}) collective-permute-start(f32[37,640]{1,0:T(8,128)S(1)} %pad_maximum_fusion.2), channel_id=1, source_target_pairs={{0,2},{1,3},{2,0},{3,1},{4,6},{5,7},{6,4},{7,5},{8,10},{9,11},{10,... | collective-permute-start | bytes 284168 | tf_op jit(solution)/shard_map/ppermute | solution.py:19
  78.6 3.8 %collective-permute-start.5 = (f32[37,128]{1,0:T(8,128)S(1)}, f32[37,128]{1,0:T(8,128)S(1)}, u32[]{:S(2)}, u32[]{:S(2)}) collective-permute-start(f32[37,128]{1,0:T(8,128)S(1)} %pad_maximum_fusion.3), channel_id=1, source_target_pairs={{0,4},{4,0},{8,12},{12,8},{16,20},{20,16},{24,28},{28,24},{1,5},{5... | collective-permute-start | bytes 56840 | tf_op jit(solution)/shard_map/ppermute | solution.py:19
  82.7 3.8 %collective-permute-start.6 = (f32[37,128]{1,0:T(8,128)S(1)}, f32[37,128]{1,0:T(8,128)S(1)}, u32[]{:S(2)}, u32[]{:S(2)}) collective-permute-start(f32[37,128]{1,0:T(8,128)S(1)} %pad_maximum_fusion.4), channel_id=1, source_target_pairs={{0,8},{4,12},{8,0},{12,4},{16,24},{20,28},{24,16},{28,20},{1,9},{5... | collective-permute-start | bytes 56840 | tf_op jit(solution)/shard_map/ppermute | solution.py:19
  86.8 5.0 %collective-permute-start.7 = (f32[37,128]{1,0:T(8,128)S(1)}, f32[37,128]{1,0:T(8,128)S(1)}, u32[]{:S(2)}, u32[]{:S(2)}) collective-permute-start(f32[37,128]{1,0:T(8,128)S(1)} %pad_maximum_fusion.5), channel_id=1, source_target_pairs={{0,16},{4,20},{8,24},{12,28},{16,0},{20,4},{24,8},{28,12},{1,17},{... | collective-permute-start | bytes 56840 | tf_op jit(solution)/shard_map/ppermute | solution.py:19

commit v17 on v13

--- a/solution.py
+++ b/solution.py
@@ -34,6 +34,31 @@
     flat = value.reshape(-1)
     count = -(-flat.shape[0] // width)
     return jnp.pad(flat, (0, count * width - flat.shape[0])).reshape(count, width)
+
+
+def order_groups(count):
+    groups = []
+    for component, order in enumerate(ORDER_OF[:count]):
+        if groups and groups[-1][0] == order:
+            groups[-1] = (order, groups[-1][1], component + 1)
+        else:
+            groups.append((order, component, component + 1))
+    return groups
+
+
+def mix_orders(weights, values, spec):
+    return jnp.concatenate(
+        [
+            jnp.einsum(
+                spec,
+                weights[order],
+                values[:, low:high],
+                preferred_element_type=jnp.float32,
+            )
+            for order, low, high in order_groups(values.shape[1])
+        ],
+        axis=1,
+    )
 
 
 def halving_with(value, extras, axis):
@@ -184,11 +209,8 @@
     )
     moments = jnp.einsum("bclki,ck->clbi", msg_acc, full_weight)
     packed = moments.astype(jnp.bfloat16)
-    mixing = jnp.take(mix_weight, jnp.array(ORDER_OF, dtype=jnp.int32), axis=0)
     offset = chan_index * chan_dev
-    mixed_out = jnp.einsum(
-        "lxc,clbi->xlbi", mixing, packed, preferred_element_type=jnp.float32
-    )
+    mixed_out = mix_orders(mix_weight, packed, "xc,clbi->xlbi")
     scalar_part = mixed_out[:, 0]
     gate_value = jax.nn.sigmoid(scalar_part)
     result_rows = jnp.concatenate(
@@ -215,9 +237,7 @@
     ) + gate_value * (1.0 - gate_value) * jnp.sum(upstream[:, 1:] * mixed_out[:, 1:], axis=1)
     rest_grad = upstream[:, 1:] * gate_value[:, None]
     dz_packed = jnp.concatenate([scalar_grad[:, None], rest_grad], axis=1).astype(jnp.bfloat16)
-    moment_grad_all = jnp.einsum(
-        "lxc,xlbi->clbi", mixing, dz_packed, preferred_element_type=jnp.float32
-    )
+    moment_grad_all = mix_orders(mix_weight, dz_packed, "xc,xlbi->clbi")
     grad_rad = jnp.einsum("bclki,clbi->ck", msg_acc, moment_grad_all)
     grad_blocks = jnp.moveaxis(moment_grad_all, 2, 0)
     tile_grad = jnp.take(grad_blocks, target_idx, axis=0, mode="clip")

time: 88.2 us -> 86.6 us (0.982)
  local copies, waits for them, and re-layouts: 22.3 us -> 19.9 us
  matrix products: 9.7 us -> 11.5 us
    dot_general x2 -> x6, matrix products: 1.23 us -> 3.82 us  [mix_orders(): jnp.einsum(spec, weights[order], values[:, low:high], preferred_element_t...]
    reduce_sum x1, other arithmetic: 0.03 us -> 1.61 us  [body(): jnp.sum(upstream[:, 1:] * mixed_out[:, 1:], axis=1)]
    reduce_sum x1, other arithmetic: 5.25 us -> 3.76 us  [body(): harm_grad = jnp.sum(value_grad * radial[None], axis=1)]
    another operation x2 -> x0, other arithmetic: 1.35 us -> none
    unnamed x88 -> x84, local copies, waits for them, and re-layouts: 7.25 us -> 6.07 us
where the time goes in v17:
time: 86.6 us; the launch traced here: 85.8 us
  local copies, waits for them, and re-layouts  19.9 us (23%)
  starting transfers between devices  17.5 us (20%)
  other arithmetic  17.4 us (20%)
  waiting for transfers between devices  11.9 us (14%)
  matrix products  11.5 us (13%)
  blocking collectives  5.86 us (7%)
  between operations  1.62 us (2%)
    ppermute x8, starting transfers between devices, partner(): return lax.ppermute(value, axis, pairs)  10.9 us
    ppermute x8, waiting for transfers between devices, partner(): return lax.ppermute(value, axis, pairs)  7.79 us
    unnamed x84, local copies, waits for them, and re-layouts  6.07 us
    all_gather x1, blocking collectives, body(): lax.all_gather(jnp.concatenate([src_feat, weight_high, weight_mid, weight...  5.86 us
    all_to_all x1, waiting for transfers between devices, body(): lax.all_to_all(result_rows.reshape(all_chan, components, own_blocks, 1, r...  4.15 us
    dot_general x6, matrix products, mix_orders(): jnp.einsum(spec, weights[order], values[:, low:high], preferred_element_t...  3.82 us
    reduce_sum x1, other arithmetic, body(): harm_grad = jnp.sum(value_grad * radial[None], axis=1)  3.76 us
    all_to_all x1, starting transfers between devices, body(): lax.all_to_all(result_rows.reshape(all_chan, components, own_blocks, 1, r...  3.34 us
  transfers between devices with their start and end apart: 10, of which 4 were waited for; matrix products, arithmetic and copies ran while one was open for 22% of the time, Pallas kernels for 0%

profile of v17, /device:TPU:0, one launch (start us, length us, event | category | flops | bytes accessed | tf_op | source)
XLA Modules:
  0.0 85.8 jit_solution(13452558351018569712)
XLA Ops:
  0.6 0.7 convert_element_type.99
  1.4 1.0 %fusion.26 = f32[35,384]{1,0:T(8,128)S(1)} fusion(s32[384]{0:T(512)} %bitcast.420, f32[3,256]{1,0:T(4,128)} %param.8, f32[32,256]{1,0:T(8,128)S(1)} %convert_element_type.99), kind=kOutput, calls=%fused_computation.46 | convolution fusion | flops 41394944 | bytes 91136 | tf_op jit(solution)/shard_map/dot_general | solution.py:144
  2.3 3.0 %collective-permute-start = (f32[35,128]{1,0:T(8,128)S(1)}, f32[35,128]{1,0:T(8,128)S(1)}, u32[]{:S(2)}, u32[]{:S(2)}) collective-permute-start(f32[35,128]{1,0:T(8,128)S(1)} %get-tuple-element.43), channel_id=1, source_target_pairs={{0,4},{4,0},{8,12},{12,8},{16,20},{20,16},{24,28},{28,24},{1,5},{5... | collective-permute-start | bytes 53768 | tf_op jit(solution)/shard_map/ppermute | solution.py:19
  5.4 2.6 %collective-permute-start.2 = (f32[35,128]{1,0:T(8,128)S(1)}, f32[35,128]{1,0:T(8,128)S(1)}, u32[]{:S(2)}, u32[]{:S(2)}) collective-permute-start(f32[35,128]{1,0:T(8,128)S(1)} %get-tuple-element.44), channel_id=1, source_target_pairs={{0,16},{4,20},{8,24},{12,28},{16,0},{20,4},{24,8},{28,12},{1,17},{... | collective-permute-start | bytes 53768 | tf_op jit(solution)/shard_map/ppermute | solution.py:19
  7.9 1.6 %collective-permute-start.1 = (f32[35,128]{1,0:T(8,128)S(1)}, f32[35,128]{1,0:T(8,128)S(1)}, u32[]{:S(2)}, u32[]{:S(2)}) collective-permute-start(f32[35,128]{1,0:T(8,128)S(1)} %get-tuple-element.45), channel_id=1, source_target_pairs={{0,8},{4,12},{8,0},{12,4},{16,24},{20,28},{24,16},{28,20},{1,9},{5... | collective-permute-start | bytes 53768 | tf_op jit(solution)/shard_map/ppermute | solution.py:19
  9.5 1.3 %reshape.536 = bf16[32,9,2,4,32]{4,3,2,0,1:T(4,128)(2,1)S(1)} reshape(bf16[32,9,256]{2,0,1:T(8,128)(2,1)} %param.15) | data formatting | bytes 294912 | tf_op jit(solution)/shard_map/reshape | solution.py:228
  10.8 0.7 copy.176
  11.5 1.2 %reshape.597 = bf16[4,2,9216]{2,1,0:T(2,128)(2,1)} reshape(bf16[4,9,2,32,32]{4,3,2,1,0:T(8,128)(2,1)S(1)} %bitcast.407) | data formatting | bytes 294912
  12.8 3.3 %all-to-all-start.1 = ((bf16[4,2,9216]{2,1,0:T(2,128)(2,1)}), bf16[4,2,9216]{2,1,0:T(2,128)(2,1)S(1)}, u32[]{:S(2)}, u32[]{:S(2)}) async-start(bf16[4,2,9216]{2,1,0:T(2,128)(2,1)} %reshape.597), calls=%async_computation.1 | async-start | bytes 294912 | tf_op jit(solution)/shard_map/all_to_all | solution.py:227
  16.2 0.6 compare_convert_fusion
  16.8 0.6 pad_clamp_fusion
  17.8 0.7 copy.181
  18.6 0.7 copy.189
  19.4 5.9 %all_gather.3 = bf16[128,664]{1,0:T(8,128)(2,1)S(1)} all-gather(bf16[32,664]{1,0:T(8,128)(2,1)S(1)} %concatenate.64), channel_id=1, replica_groups=mesh['space'=8,'chan'=4] {'chan'}, dimensions={0}, use_global_device_ids=true | all-gather | bytes 212480 | tf_op jit(solution)/shard_map/all_gather | solution.py:164
  25.4 0.6 gather_fusion.1
  26.0 0.6 gather_fusion.2
  27.1 0.6 gather_fusion
  28.6 0.8 copy-done.5
  29.4 0.3 fusion.17
  29.7 3.0 %fusion.7 = (bf16[128,2,9,32]{0,3,2,1:T(8,128)(2,1)S(1)}, f32[2,128,9,8,32,1]{1,4,5,3,2,0:T(8,128)}) fusion(f32[128,8]{0,1:T(8,128)S(1)} %copy.219, f32[8,128,128]{2,1,0:T(8,128)S(1)} %convert_element_type.107, f32[8,2]{0,1:T(2,128)S(1)} %copy.163, f32[8,8,32,128]{3,2,0,1:T(8,128)S(1)} %fusion.17, f32[9,8,32,128]{3,2,1,0:T(8,128)S(1)} %multiply_dynamic-update-slice_fusion), kind=kOutput, calls=%fused_computation.18 | convolution fusion | flops 1214308352 | bytes 5263424 | tf_op jit(solution)/shard_map/lktij,tbcj->bclki/dot_general | solution.py:207
  32.7 0.8 convolution_bitcast_fusion.3
  33.8 0.6 copy-done.15
  34.5 0.6 fusion.112
  35.2 0.3 reshape.598
  35.6 0.8 copy.177
  36.5 0.5 reshape.548
  37.0 0.9 %convolution_bitcast_fusion.2 = f32[128,3,2,32]{0,3,2,1:T(8,128)S(1)} fusion(bf16[3,128,128]{2,1,0:T(8,128)(2,1)} %param.14, f32[128,9,2,32]{0,3,2,1:T(8,128)S(1)} %reshape.548, f32[128,2,32]{0,2,1:T(8,128)S(1)} %get-tuple-element.47), kind=kOutput, calls=%fused_computation.25 | convolution fusion | flops 6422528 | bytes 425984 | tf_op jit(solution)/shard_map/xc,xlbi->clbi/dot_general | solution.py:52
  37.9 0.9 %convolution_bitcast_fusion = f32[128,5,2,32]{0,3,2,1:T(8,128)S(1)} fusion(bf16[3,128,128]{2,1,0:T(8,128)(2,1)} %param.14, f32[128,9,2,32]{0,3,2,1:T(8,128)S(1)} %reshape.548, f32[128,2,32]{0,2,1:T(8,128)S(1)} %get-tuple-element.47), kind=kOutput, calls=%fused_computation.23 | convolution fusion | flops 10616832 | bytes 491520 | tf_op jit(solution)/shard_map/xc,xlbi->clbi/dot_general | solution.py:52
  38.8 1.6 %multiply_reduce_fusion.4 = (f32[128,2,32]{0,2,1:T(8,128)S(1)}, bf16[128,8,2,1,32]{0,4,2,1,3:T(8,128)(2,1)}) fusion(f32[128,9,2,32]{0,3,2,1:T(8,128)S(1)} %reshape.548, f32[128,5,2,32]{0,3,2,1:T(8,128)S(1)} %convolution_bitcast_fusion.1, f32[128,3,2,32]{0,3,2,1:T(8,128)} %convolution_bitcast_fusion.3, f32[128,2,32]{0,2,1:T(8,128)S(1)} %get-tuple-element.47), kind=kLoop, calls=%fused_computation.52 | loop fusion | flops 319488 | bytes 720896 | tf_op jit(solution)/shard_map/reduce_sum | solution.py:237
  40.4 0.9 %convolution_bitcast_fusion.4 = f32[128,1,2,32]{0,3,2,1:T(8,128)S(1)} fusion(bf16[3,128,128]{2,1,0:T(8,128)(2,1)} %param.14, f32[128,2,32]{0,2,1:T(8,128)S(1)} %copy-done.16, f32[128,2,32]{0,2,1:T(8,128)S(1)} %get-tuple-element.36, f32[128,9,2,32]{0,3,2,1:T(8,128)S(1)} %reshape.548), kind=kOutput, calls=%fused_computation.27 | convolution fusion | flops 2195456 | bytes 163840 | tf_op jit(solution)/shard_map/xc,xlbi->clbi/dot_general | solution.py:52
  41.3 0.8 fusion.29
  42.1 0.7 gather_fusion.3
  42.8 1.4 %multiply_convert_fusion = bf16[8,128,9,8,32]{1,4,3,2,0:T(8,128)(2,1)S(1)} fusion(f32[8,128,9,32]{1,3,2,0:T(8,128)S(1)} %gather_fusion.3, f32[8,128,8]{1,2,0:T(8,128)S(1)} %broadcast_multiply_fusion), kind=kLoop, calls=%fused_computation.6 | loop fusion | flops 4718592 | bytes 5931008 | tf_op jit(solution)/shard_map/convert_element_type | solution.py:248
  44.2 2.1 %fusion.8 = f32[8,128,128]{2,1,0:T(8,128)S(1)} fusion(bf16[8,128,9,8,32]{1,4,3,2,0:T(8,128)(2,1)S(1)} %multiply_convert_fusion, f32[8,8,32,128]{3,2,0,1:T(8,128)S(1)} %fusion.17, f32[9,8,32,128]{3,2,1,0:T(8,128)S(1)} %copy-done.3), kind=kOutput, calls=%fused_computation.21 | convolution fusion | flops 608698368 | bytes 7471104 | tf_op jit(solution)/shard_map/tclki,lktij->tcj/dot_general | solution.py:249
  46.3 1.4 %fusion.131 = f32[8,128,2304]{1,2,0:S(1)} fusion(bf16[8,128,2304]{1,2,0:T(8,128)(2,1)S(1)} %bitcast.406, bf16[8,128,128]{2,1,0:T(8,128)(2,1)S(1)} %gather_fusion), kind=kOutput, calls=%fused_computation.253 | convolution fusion | flops 603979776 | bytes 14417920
  47.7 3.8 %multiply_reduce_fusion.1 = (f32[9,8,32,128]{3,2,0,1:T(8,128)S(1)}, f32[8,8,32,128]{3,2,0,1:T(8,128)}) fusion(f32[9,8,8,32,128]{4,3,1,0,2:T(8,128)S(1)} %bitcast.405, f32[8,8,32,128]{3,2,0,1:T(8,128)S(1)} %fusion.17, f32[9,8,32,128]{3,2,1,0:T(8,128)S(1)} %copy-done.3), kind=kLoop, calls=%fused_computation.5 | loop fusion | flops 8880128 | bytes 13893632 | tf_op jit(solution)/shard_map/reduce_sum | solution.py:255
  51.4 0.8 fusion.38
  52.2 0.9 %fusion.71 = (f32[8,1,32,128]{3,2,0,1:T(8,128)}, f32[8,1,32,128]{3,2,0,1:T(8,128)}) fusion(f32[9,8,32,128]{3,2,0,1:T(8,128)S(1)} %get-tuple-element.24, f32[8,3,32,128]{3,2,0,1:T(8,128)S(1)} %get-tuple-element.48, f32[8,32,128]{2,1,0:T(8,128)S(1)} %get-tuple-element.49), kind=kLoop, calls=%fused_computation.119 | loop fusion | flops 950272 | bytes 1703936 | tf_op jit(solution)/shard_map/transpose(jvp())/div | solution.py:94
  53.2 0.3 fusion.6
  53.6 0.7 reshape.540
  54.3 1.1 %multiply_reduce_fusion.2 = f32[128,5,128]{2,0,1:T(8,128)S(1)} fusion(f32[8,128,128]{2,1,0:T(8,128)S(1)} %fusion.8, f32[8,5]{1,0:T(8,128)} %copy-done.23), kind=kLoop, calls=%fused_computation.14 | loop fusion | flops 1228800 | bytes 852128 | tf_op jit(solution)/shard_map/reduce_sum | solution.py:258
  55.6 0.8 reshape_reshape.13
  56.4 1.1 %fusion.18 = (f32[8,32,128]{2,1,0:T(8,128)S(1)}, f32[8,32,128]{2,1,0:T(8,128)S(1)}) fusion(f32[8,8,32,128]{3,2,0,1:T(8,128)S(1)} %copy-done, f32[8]{0:T(128)} %copy-done.33, f32[8,32,128]{2,1,0:T(8,128)S(1)} %copy-done.6, f32[8,32,128]{2,1,0:T(8,128)S(1)} %copy-done.8), kind=kLoop, calls=%fused_computation.34 | loop fusion | flops 2818048 | bytes 1572896 | tf_op jit(solution)/shard_map/transpose(jvp())/reduce_sum | solution.py:111
  57.7 0.3 fusion.50
  58.1 0.4 copy-done.10
  58.6 0.3 fusion.83
  59.5 0.4 collective-permute-start.3
  59.9 1.1 %collective-permute-done.3 = f32[69,640]{1,0:T(8,128)S(1)} collective-permute-done((f32[69,640]{1,0:T(8,128)S(1)}, f32[69,640]{1,0:T(8,128)S(1)}, u32[]{:S(2)}, u32[]{:S(2)}) %collective-permute-start.3) | collective-permute-done | bytes 176672 | tf_op jit(solution)/shard_map/ppermute | solution.py:19
  61.1 1.8 %collective-permute-start.4 = (f32[37,640]{1,0:T(8,128)S(1)}, f32[37,640]{1,0:T(8,128)S(1)}, u32[]{:S(2)}, u32[]{:S(2)}) collective-permute-start(f32[37,640]{1,0:T(8,128)S(1)} %pad_maximum_fusion.4), channel_id=1, source_target_pairs={{0,2},{1,3},{2,0},{3,1},{4,6},{5,7},{6,4},{7,5},{8,10},{9,11},{10,... | collective-permute-start | bytes 284168 | tf_op jit(solution)/shard_map/ppermute | solution.py:19
  62.8 3.4 %collective-permute-done.4 = f32[37,640]{1,0:T(8,128)S(1)} collective-permute-done((f32[37,640]{1,0:T(8,128)S(1)}, f32[37,640]{1,0:T(8,128)S(1)}, u32[]{:S(2)}, u32[]{:S(2)}) %collective-permute-start.4) | collective-permute-done | bytes 94752 | tf_op jit(solution)/shard_map/ppermute | solution.py:19
  66.6 0.6 collective-permute-start.5
  67.2 3.3 %collective-permute-done.5 = f32[37,128]{1,0:T(8,128)S(1)} collective-permute-done((f32[37,128]{1,0:T(8,128)S(1)}, f32[37,128]{1,0:T(8,128)S(1)}, u32[]{:S(2)}, u32[]{:S(2)}) %collective-permute-start.5) | collective-permute-done | bytes 18976 | tf_op jit(solution)/shard_map/ppermute | solution.py:19
  70.7 0.5 collective-permute-start.6
  71.2 0.8 copy.173
  72.0 1.2 %reshape.595 = bf16[4,2,9216]{2,1,0:T(2,128)(2,1)} reshape(bf16[128,1,9,2,32]{4,3,2,1,0:T(2,128)(2,1)S(1)} %bitcast.408) | data formatting | bytes 294912
  73.3 3.3 %all-to-all-start = ((bf16[4,2,9216]{2,1,0:T(2,128)(2,1)}), bf16[4,2,9216]{2,1,0:T(2,128)(2,1)S(1)}, u32[]{:S(2)}, u32[]{:S(2)}) async-start(bf16[4,2,9216]{2,1,0:T(2,128)(2,1)} %reshape.595), calls=%async_computation | async-start | bytes 294912 | tf_op jit(solution)/shard_map/all_to_all | solution.py:220
  76.8 0.4 collective-permute-start.7
  77.2 4.1 %all-to-all-done = bf16[4,2,9216]{2,1,0:T(2,128)(2,1)S(1)} async-done(((bf16[4,2,9216]{2,1,0:T(2,128)(2,1)}), bf16[4,2,9216]{2,1,0:T(2,128)(2,1)S(1)}, u32[]{:S(2)}, u32[]{:S(2)}) %all-to-all-start) | async-done | bytes 147488 | tf_op jit(solution)/shard_map/all_to_all | solution.py:220
  81.7 0.8 copy.174
  82.4 1.1 %reshape.535 = bf16[32,9,256]{2,0,1:T(8,128)(2,1)} reshape(bf16[32,9,2,4,1,32]{5,3,2,0,1,4:T(4,128)(2,1)S(1)} %copy.174) | data formatting | bytes 294912 | tf_op jit(solution)/shard_map/reshape | solution.py:226
  83.5 0.3 maximum_add_fusion
  83.8 0.6 slice_negate_fusion
  84.4 0.6 slice.382
  85.1 0.7 copy.190
  (169 shorter events, 4.7 us)
Async XLA Ops:
  2.3 16.9 %collective-permute-start = (f32[35,128]{1,0:T(8,128)S(1)}, f32[35,128]{1,0:T(8,128)S(1)}, u32[]{:S(2)}, u32[]{:S(2)}) collective-permute-start(f32[35,128]{1,0:T(8,128)S(1)} %get-tuple-element.43), channel_id=1, source_target_pairs={{0,4},{4,0},{8,12},{12,8},{16,20},{20,16},{24,28},{28,24},{1,5},{5... | collective-permute-start | bytes 53768 | tf_op jit(solution)/shard_map/ppermute | solution.py:19
  5.4 13.9 %collective-permute-start.2 = (f32[35,128]{1,0:T(8,128)S(1)}, f32[35,128]{1,0:T(8,128)S(1)}, u32[]{:S(2)}, u32[]{:S(2)}) collective-permute-start(f32[35,128]{1,0:T(8,128)S(1)} %get-tuple-element.44), channel_id=1, source_target_pairs={{0,16},{4,20},{8,24},{12,28},{16,0},{20,4},{24,8},{28,12},{1,17},{... | collective-permute-start | bytes 53768 | tf_op jit(solution)/shard_map/ppermute | solution.py:19
  7.9 11.3 %collective-permute-start.1 = (f32[35,128]{1,0:T(8,128)S(1)}, f32[35,128]{1,0:T(8,128)S(1)}, u32[]{:S(2)}, u32[]{:S(2)}) collective-permute-start(f32[35,128]{1,0:T(8,128)S(1)} %get-tuple-element.45), channel_id=1, source_target_pairs={{0,8},{4,12},{8,0},{12,4},{16,24},{20,28},{24,16},{28,20},{1,9},{5... | collective-permute-start | bytes 53768 | tf_op jit(solution)/shard_map/ppermute | solution.py:19
  10.8 5.3 %copy-start.34 = (s32[8,2]{0,1:T(2,128)S(1)}, s32[8,2]{0,1:T(2,128)}, u32[]{:S(2)}) copy-start(s32[8,2]{0,1:T(2,128)} %param.11) | copy-start | bytes 196
  10.8 6.0 %copy-start.37 = (s32[8]{0:T(128)S(1)}, s32[8]{0:T(128)}, u32[]{:S(2)}) copy-start(s32[8]{0:T(128)} %param.12) | copy-start | bytes 100
  10.8 6.0 %copy-start.30 = (f32[32,8]{0,1:T(8,128)S(1)}, f32[32,8]{0,1:T(8,128)}, u32[]{:S(2)}) copy-start(f32[32,8]{0,1:T(8,128)} %param.13) | copy-start | bytes 3076
  10.8 8.5 %copy-start.21 = (bf16[32,256]{1,0:T(8,128)(2,1)S(1)}, bf16[32,256]{1,0:T(8,128)(2,1)}, u32[]{:S(2)}) copy-start(bf16[32,256]{1,0:T(8,128)(2,1)} %param.9) | copy-start | bytes 49156
  11.5 13.8 %copy-start.29 = (f32[3,256]{1,0:T(4,128)S(1)}, f32[3,256]{1,0:T(4,128)}, u32[]{:S(2)}) copy-start(f32[3,256]{1,0:T(4,128)} %param.8) | copy-start | bytes 9220
  12.8 22.4 %all-to-all-start.1 = ((bf16[4,2,9216]{2,1,0:T(2,128)(2,1)}), bf16[4,2,9216]{2,1,0:T(2,128)(2,1)S(1)}, u32[]{:S(2)}, u32[]{:S(2)}) async-start(bf16[4,2,9216]{2,1,0:T(2,128)(2,1)} %reshape.597), calls=%async_computation.1 | async-start | bytes 294912 | tf_op jit(solution)/shard_map/all_to_all | solution.py:227
  16.1 12.3 %copy-start.31 = (f32[8]{0:T(128)}, f32[8]{0:T(128)S(1)}, u32[]{:S(2)}) copy-start(f32[8]{0:T(128)S(1)} %compare_convert_fusion.1) | copy-start | bytes 100
  16.8 18.3 %copy-start.27 = (f32[8]{0:T(128)}, f32[8]{0:T(128)S(1)}, u32[]{:S(2)}) copy-start(f32[8]{0:T(128)S(1)} %convert_element_type.106) | copy-start | bytes 100
  17.5 7.9 %copy-start.23 = (f32[8,5]{1,0:T(8,128)}, f32[8,5]{1,0:T(8,128)S(1)}, u32[]{:S(2)}) copy-start(f32[8,5]{1,0:T(8,128)S(1)} %get-tuple-element.60) | copy-start | bytes 484
  17.6 11.0 %copy-start.33 = (f32[8]{0:T(128)}, f32[8]{0:T(128)S(1)}, u32[]{:S(2)}) copy-start(f32[8]{0:T(128)S(1)} %add_multiply_fusion) | copy-start | bytes 100
  26.0 1.9 %copy-start.17 = (f32[8,3,128]{2,0,1:T(8,128)}, f32[8,3,128]{2,0,1:T(8,128)S(1)}, u32[]{:S(2)}) copy-start(f32[8,3,128]{2,0,1:T(8,128)S(1)} %copy.167) | copy-start | bytes 36868
  26.6 1.4 %copy-start.19 = (f32[8,3,32]{2,0,1:T(8,128)}, f32[8,3,32]{2,0,1:T(8,128)S(1)}, u32[]{:S(2)}) copy-start(f32[8,3,32]{2,0,1:T(8,128)S(1)} %copy.169) | copy-start | bytes 9220
  28.5 4.2 %copy-start.2 = (f32[9,8,32,128]{3,2,1,0:T(8,128)}, f32[9,8,32,128]{3,2,1,0:T(8,128)S(1)}, u32[]{:S(2)}) copy-start(f32[9,8,32,128]{3,2,1,0:T(8,128)S(1)} %multiply_dynamic-update-slice_fusion) | copy-start | bytes 3538948
  28.6 0.8 copy-start.5
  28.6 0.8 copy-start.7
  29.7 3.0 %copy-start.14 = (bf16[3,128,128]{2,1,0:T(8,128)(2,1)S(1)}, bf16[3,128,128]{2,1,0:T(8,128)(2,1)}, u32[]{:S(2)}) copy-start(bf16[3,128,128]{2,1,0:T(8,128)(2,1)} %param.14) | copy-start | bytes 294916
  33.8 0.6 copy-start.15
  37.0 3.4 %copy-start.16 = (f32[128,2,32]{0,2,1:T(8,128)S(1)}, f32[128,2,32]{0,2,1:T(8,128)}, u32[]{:S(2)}) copy-start(f32[128,2,32]{0,2,1:T(8,128)} %copy-done.15) | copy-start | bytes 98308
  42.8 1.4 %copy-start.3 = (f32[9,8,32,128]{3,2,1,0:T(8,128)S(1)}, f32[9,8,32,128]{3,2,1,0:T(8,128)}, u32[]{:S(2)}) copy-start(f32[9,8,32,128]{3,2,1,0:T(8,128)} %copy-done.2) | copy-start | bytes 3538948
  51.4 1.7 %copy-start.1 = (f32[2,128,9,8,32,1]{1,4,5,3,2,0:T(8,128)S(1)}, f32[2,128,9,8,32,1]{1,4,5,3,2,0:T(8,128)}, u32[]{:S(2)}) copy-start(f32[2,128,9,8,32,1]{1,4,5,3,2,0:T(8,128)} %get-tuple-element.65) | copy-start | bytes 7077892
  51.4 1.7 %copy-start.9 = (f32[128,2,32,9]{0,2,1,3:T(8,128)S(1)}, f32[128,2,32,9]{0,2,1,3:T(8,128)}, u32[]{:S(2)}) copy-start(f32[128,2,32,9]{0,2,1,3:T(8,128)} %get-tuple-element.35) | copy-start | bytes 884740
  54.3 2.2 %copy-start = (f32[8,8,32,128]{3,2,0,1:T(8,128)S(1)}, f32[8,8,32,128]{3,2,0,1:T(8,128)}, u32[]{:S(2)}) copy-start(f32[8,8,32,128]{3,2,0,1:T(8,128)} %get-tuple-element.25) | copy-start | bytes 3145732
  54.3 2.2 %copy-start.6 = (f32[8,32,128]{2,1,0:T(8,128)S(1)}, f32[8,32,128]{2,1,0:T(8,128)}, u32[]{:S(2)}) copy-start(f32[8,32,128]{2,1,0:T(8,128)} %copy-done.5) | copy-start | bytes 393220
  54.3 2.2 %copy-start.8 = (f32[8,32,128]{2,1,0:T(8,128)S(1)}, f32[8,32,128]{2,1,0:T(8,128)}, u32[]{:S(2)}) copy-start(f32[8,32,128]{2,1,0:T(8,128)} %copy-done.7) | copy-start | bytes 393220
  56.4 1.2 %copy-start.28 = (f32[8]{0:T(128)S(1)}, f32[8]{0:T(128)}, u32[]{:S(2)}) copy-start(f32[8]{0:T(128)} %copy-done.27) | copy-start | bytes 100
  56.4 1.2 %copy-start.32 = (f32[8]{0:T(128)S(1)}, f32[8]{0:T(128)}, u32[]{:S(2)}) copy-start(f32[8]{0:T(128)} %copy-done.31) | copy-start | bytes 100
  57.6 0.9 %copy-start.10 = (f32[8,1,32,128]{3,2,0,1:T(8,128)S(1)}, f32[8,1,32,128]{3,2,0,1:T(8,128)}, u32[]{:S(2)}) copy-start(f32[8,1,32,128]{3,2,0,1:T(8,128)} %fusion.38) | copy-start | bytes 393220
  57.6 1.0 %copy-start.12 = (f32[8,1,32,128]{3,2,0,1:T(8,128)S(1)}, f32[8,1,32,128]{3,2,0,1:T(8,128)}, u32[]{:S(2)}) copy-start(f32[8,1,32,128]{3,2,0,1:T(8,128)} %get-tuple-element.30) | copy-start | bytes 393220
  57.6 1.0 %copy-start.13 = (f32[8,1,32,128]{3,2,0,1:T(8,128)S(1)}, f32[8,1,32,128]{3,2,0,1:T(8,128)}, u32[]{:S(2)}) copy-start(f32[8,1,32,128]{3,2,0,1:T(8,128)} %get-tuple-element.31) | copy-start | bytes 393220
  57.6 1.0 %copy-start.18 = (f32[8,3,128]{2,0,1:T(8,128)S(1)}, f32[8,3,128]{2,0,1:T(8,128)}, u32[]{:S(2)}) copy-start(f32[8,3,128]{2,0,1:T(8,128)} %copy-done.17) | copy-start | bytes 36868
  57.6 1.0 %copy-start.20 = (f32[8,3,32]{2,0,1:T(8,128)S(1)}, f32[8,3,32]{2,0,1:T(8,128)}, u32[]{:S(2)}) copy-start(f32[8,3,32]{2,0,1:T(8,128)} %copy-done.19) | copy-start | bytes 9220
  57.7 1.3 %copy-start.26 = (f32[8,5]{0,1:T(8,128)S(1)}, f32[8,5]{0,1:T(8,128)}, u32[]{:S(2)}) copy-start(f32[8,5]{0,1:T(8,128)} %copy.189) | copy-start | bytes 484
  57.7 1.4 %copy-start.25 = (f32[8,5]{0,1:T(8,128)S(1)}, f32[8,5]{0,1:T(8,128)}, u32[]{:S(2)}) copy-start(f32[8,5]{0,1:T(8,128)} %copy.181) | copy-start | bytes 484
  57.7 1.5 %copy-start.35 = (f32[4]{0:T(128)S(1)}, f32[4]{0:T(128)}, u32[]{:S(2)}) copy-start(f32[4]{0:T(128)} %compare_convert_fusion) | copy-start | bytes 52
  57.7 1.7 %copy-start.24 = (f32[1024]{0:T(1024)S(1)}, f32[1024]{0:T(1024)}, u32[]{:S(2)}) copy-start(f32[1024]{0:T(1024)} %reshape.540) | copy-start | bytes 12292
  57.7 1.7 %copy-start.4 = (f32[2,2,32,640]{3,2,1,0:T(8,128)S(1)}, f32[2,2,32,640]{3,2,1,0:T(8,128)}, u32[]{:S(2)}) copy-start(f32[2,2,32,640]{3,2,1,0:T(8,128)} %reshape_reshape.13) | copy-start | bytes 983044
  59.4 11.7 %copy-start.11 = (bf16[128,8,2,1,32]{0,4,2,1,3:T(8,128)(2,1)S(1)}, bf16[128,8,2,1,32]{0,4,2,1,3:T(8,128)(2,1)}, u32[]{:S(2)}) copy-start(bf16[128,8,2,1,32]{0,4,2,1,3:T(8,128)(2,1)} %get-tuple-element.37) | copy-start | bytes 393220
  59.5 11.7 %copy-start.22 = (bf16[128,1,2,1,32]{0,4,2,1,3:T(8,128)(2,1)S(1)}, bf16[128,1,2,1,32]{0,4,2,1,3:T(8,128)(2,1)}, u32[]{:S(2)}) copy-start(bf16[128,1,2,1,32]{0,4,2,1,3:T(8,128)(2,1)} %get-tuple-element.46) | copy-start | bytes 49156
  59.5 1.5 %collective-permute-start.3 = (f32[69,640]{1,0:T(8,128)S(1)}, f32[69,640]{1,0:T(8,128)S(1)}, u32[]{:S(2)}, u32[]{:S(2)}) collective-permute-start(f32[69,640]{1,0:T(8,128)S(1)} %pad_maximum_fusion.2), channel_id=1, source_target_pairs={{0,1},{1,0},{2,3},{3,2},{4,5},{5,4},{6,7},{7,6},{8,9},{9,8},{10,11... | collective-permute-start | bytes 529928 | tf_op jit(solution)/shard_map/ppermute | solution.py:19
  61.1 5.2 %collective-permute-start.4 = (f32[37,640]{1,0:T(8,128)S(1)}, f32[37,640]{1,0:T(8,128)S(1)}, u32[]{:S(2)}, u32[]{:S(2)}) collective-permute-start(f32[37,640]{1,0:T(8,128)S(1)} %pad_maximum_fusion.4), channel_id=1, source_target_pairs={{0,2},{1,3},{2,0},{3,1},{4,6},{5,7},{6,4},{7,5},{8,10},{9,11},{10,... | collective-permute-start | bytes 284168 | tf_op jit(solution)/shard_map/ppermute | solution.py:19
  66.6 3.8 %collective-permute-start.5 = (f32[37,128]{1,0:T(8,128)S(1)}, f32[37,128]{1,0:T(8,128)S(1)}, u32[]{:S(2)}, u32[]{:S(2)}) collective-permute-start(f32[37,128]{1,0:T(8,128)S(1)} %pad_maximum_fusion.5), channel_id=1, source_target_pairs={{0,4},{4,0},{8,12},{12,8},{16,20},{20,16},{24,28},{28,24},{1,5},{5... | collective-permute-start | bytes 56840 | tf_op jit(solution)/shard_map/ppermute | solution.py:19
  70.7 5.9 %collective-permute-start.6 = (f32[37,128]{1,0:T(8,128)S(1)}, f32[37,128]{1,0:T(8,128)S(1)}, u32[]{:S(2)}, u32[]{:S(2)}) collective-permute-start(f32[37,128]{1,0:T(8,128)S(1)} %pad_maximum_fusion.6), channel_id=1, source_target_pairs={{0,8},{4,12},{8,0},{12,4},{16,24},{20,28},{24,16},{28,20},{1,9},{5... | collective-permute-start | bytes 56840 | tf_op jit(solution)/shard_map/ppermute | solution.py:19
  73.3 8.1 %all-to-all-start = ((bf16[4,2,9216]{2,1,0:T(2,128)(2,1)}), bf16[4,2,9216]{2,1,0:T(2,128)(2,1)S(1)}, u32[]{:S(2)}, u32[]{:S(2)}) async-start(bf16[4,2,9216]{2,1,0:T(2,128)(2,1)} %reshape.595), calls=%async_computation | async-start | bytes 294912 | tf_op jit(solution)/shard_map/all_to_all | solution.py:220
  76.8 6.7 %collective-permute-start.7 = (f32[37,128]{1,0:T(8,128)S(1)}, f32[37,128]{1,0:T(8,128)S(1)}, u32[]{:S(2)}, u32[]{:S(2)}) collective-permute-start(f32[37,128]{1,0:T(8,128)S(1)} %pad_maximum_fusion.7), channel_id=1, source_target_pairs={{0,16},{4,20},{8,24},{12,28},{16,0},{20,4},{24,8},{28,12},{1,17},{... | collective-permute-start | bytes 56840 | tf_op jit(solution)/shard_map/ppermute | solution.py:19
  81.6 1.9 %copy-start.36 = (s32[3,128]{1,0:T(4,128)S(1)}, s32[3,128]{1,0:T(4,128)}, u32[]{:S(2)}) copy-start(s32[3,128]{1,0:T(4,128)} %param.10) | copy-start | bytes 4612

commit v18 on v17

--- a/solution.py
+++ b/solution.py
@@ -258,13 +258,13 @@
     grad_part = jnp.sum(
         source_hot[:, None, :, None] * grad_source[:, :, None, :], axis=0
     ).reshape(all_chan, src_atoms)
-    row_hot = (jnp.arange(chan_count, dtype=jnp.int32) == chan_index).astype(jnp.float32)
     target_part = jnp.sum(target_hot[:, None, :, None] * target_grad[:, :, None, :], axis=0)
-    dpos_src = (
-        row_hot[None, None, :, None] * target_part[:, :, None, :]
-        + jnp.sum(source_hot[:, None, :, None] * source_grad_pos[:, :, None, :], axis=0).reshape(
-            3, src_blocks, chan_count, rows
-        )
+    source_part = jnp.sum(
+        source_hot[:, None, :, None] * source_grad_pos[:, :, None, :], axis=0
+    ).reshape(3, src_blocks, chan_count, rows)
+    own_rows = lax.dynamic_index_in_dim(source_part, chan_index, 2, keepdims=False)
+    dpos_src = lax.dynamic_update_index_in_dim(
+        source_part, own_rows + target_part, chan_index, 2
     ).reshape(3, src_atoms)
     grad_src, (dpos_src, grad_rad) = halving_with(grad_part, (dpos_src, grad_rad), "chan")
     grad_rad = lax.dynamic_slice_in_dim(grad_rad, offset, chan_dev, 0)

time: 86.6 us -> 86.1 us (level)
    unnamed x84 -> x82, local copies, waits for them, and re-layouts: 6.07 us -> 6.12 us
  transfers between devices with their start and end apart: 10 -> 10, of which waited for: 4 -> 4; matrix products, arithmetic and copies ran while one was open for 22% -> 21% of each run, Pallas kernels for 0% -> 0%
where the time goes in v18:
time: 86.1 us; the launch traced here: 85.4 us
  local copies, waits for them, and re-layouts  20.1 us (23%)
  starting transfers between devices  17.5 us (20%)
  other arithmetic  16.8 us (20%)
  waiting for transfers between devices  11.9 us (14%)
  matrix products  11.5 us (13%)
  blocking collectives  5.86 us (7%)
  between operations  1.64 us (2%)
    ppermute x8, starting transfers between devices, partner(): return lax.ppermute(value, axis, pairs)  10.9 us
    ppermute x8, waiting for transfers between devices, partner(): return lax.ppermute(value, axis, pairs)  7.8 us
    unnamed x82, local copies, waits for them, and re-layouts  6.12 us
    all_gather x1, blocking collectives, body(): lax.all_gather(jnp.concatenate([src_feat, weight_high, weight_mid, weight...  5.86 us
    all_to_all x1, waiting for transfers between devices, body(): lax.all_to_all(result_rows.reshape(all_chan, components, own_blocks, 1, r...  4.15 us
    dot_general x6, matrix products, mix_orders(): jnp.einsum(spec, weights[order], values[:, low:high], preferred_element_t...  3.81 us
    reduce_sum x1, other arithmetic, body(): harm_grad = jnp.sum(value_grad * radial[None], axis=1)  3.77 us
    all_to_all x1, starting transfers between devices, body(): lax.all_to_all(out_grad.reshape(chan_dev, components, own_blocks, chan_co...  3.34 us
  transfers between devices with their start and end apart: 10, of which 4 were waited for; matrix products, arithmetic and copies ran while one was open for 21% of the time, Pallas kernels for 0%

profile of v18, /device:TPU:0, one launch (start us, length us, event | category | flops | bytes accessed | tf_op | source)
XLA Modules:
  0.0 85.4 jit_solution(2475403925200944863)
XLA Ops:
  0.6 0.7 convert_element_type.92
  1.4 1.0 %fusion.26 = f32[35,384]{1,0:T(8,128)S(1)} fusion(s32[384]{0:T(512)} %bitcast.424, f32[3,256]{1,0:T(4,128)} %param.8, f32[32,256]{1,0:T(8,128)S(1)} %convert_element_type.92), kind=kOutput, calls=%fused_computation.46 | convolution fusion | flops 41394944 | bytes 91136 | tf_op jit(solution)/shard_map/dot_general | solution.py:144
  2.3 3.0 %collective-permute-start = (f32[35,128]{1,0:T(8,128)S(1)}, f32[35,128]{1,0:T(8,128)S(1)}, u32[]{:S(2)}, u32[]{:S(2)}) collective-permute-start(f32[35,128]{1,0:T(8,128)S(1)} %get-tuple-element.47), channel_id=1, source_target_pairs={{0,4},{4,0},{8,12},{12,8},{16,20},{20,16},{24,28},{28,24},{1,5},{5... | collective-permute-start | bytes 53768 | tf_op jit(solution)/shard_map/ppermute | solution.py:19
  5.4 2.6 %collective-permute-start.2 = (f32[35,128]{1,0:T(8,128)S(1)}, f32[35,128]{1,0:T(8,128)S(1)}, u32[]{:S(2)}, u32[]{:S(2)}) collective-permute-start(f32[35,128]{1,0:T(8,128)S(1)} %get-tuple-element.48), channel_id=1, source_target_pairs={{0,16},{4,20},{8,24},{12,28},{16,0},{20,4},{24,8},{28,12},{1,17},{... | collective-permute-start | bytes 53768 | tf_op jit(solution)/shard_map/ppermute | solution.py:19
  7.9 1.6 %collective-permute-start.1 = (f32[35,128]{1,0:T(8,128)S(1)}, f32[35,128]{1,0:T(8,128)S(1)}, u32[]{:S(2)}, u32[]{:S(2)}) collective-permute-start(f32[35,128]{1,0:T(8,128)S(1)} %get-tuple-element.49), channel_id=1, source_target_pairs={{0,8},{4,12},{8,0},{12,4},{16,24},{20,28},{24,16},{28,20},{1,9},{5... | collective-permute-start | bytes 53768 | tf_op jit(solution)/shard_map/ppermute | solution.py:19
  9.5 1.3 %reshape.527 = bf16[32,9,2,4,32]{4,3,2,0,1:T(4,128)(2,1)S(1)} reshape(bf16[32,9,256]{2,0,1:T(8,128)(2,1)} %param.15) | data formatting | bytes 294912 | tf_op jit(solution)/shard_map/reshape | solution.py:228
  10.8 0.7 copy.215
  11.5 1.2 %reshape.588 = bf16[4,2,9216]{2,1,0:T(2,128)(2,1)} reshape(bf16[4,9,2,32,32]{4,3,2,1,0:T(8,128)(2,1)S(1)} %bitcast.410) | data formatting | bytes 294912
  12.8 3.3 %all-to-all-start.1 = ((bf16[4,2,9216]{2,1,0:T(2,128)(2,1)}), bf16[4,2,9216]{2,1,0:T(2,128)(2,1)S(1)}, u32[]{:S(2)}, u32[]{:S(2)}) async-start(bf16[4,2,9216]{2,1,0:T(2,128)(2,1)} %reshape.588), calls=%async_computation.1 | async-start | bytes 294912 | tf_op jit(solution)/shard_map/all_to_all | solution.py:227
  16.2 0.6 pad_clamp_fusion
  17.3 0.7 copy.229
  18.0 0.7 copy.220
  18.8 5.9 %all_gather.3 = bf16[128,664]{1,0:T(8,128)(2,1)S(1)} all-gather(bf16[32,664]{1,0:T(8,128)(2,1)S(1)} %concatenate.64), channel_id=1, replica_groups=mesh['space'=8,'chan'=4] {'chan'}, dimensions={0}, use_global_device_ids=true | all-gather | bytes 212480 | tf_op jit(solution)/shard_map/all_gather | solution.py:164
  24.8 0.6 gather_fusion.1
  25.5 0.6 gather_fusion.2
  26.6 0.6 gather_fusion
  28.0 0.7 copy-done.5
  28.8 0.3 fusion.17
  29.1 3.0 %fusion.7 = (bf16[128,2,9,32]{0,3,2,1:T(8,128)(2,1)S(1)}, f32[2,128,9,8,32,1]{1,4,5,3,2,0:T(8,128)}) fusion(f32[128,8]{0,1:T(8,128)S(1)} %copy.264, f32[8,128,128]{2,1,0:T(8,128)S(1)} %convert_element_type.100, f32[8,2]{0,1:T(2,128)S(1)} %copy.202, f32[8,8,32,128]{3,2,0,1:T(8,128)S(1)} %fusion.17, f32[9,8,32,128]{3,2,1,0:T(8,128)S(1)} %multiply_dynamic-update-slice_fusion), kind=kOutput, calls=%fused_computation.18 | convolution fusion | flops 1214308352 | bytes 5263424 | tf_op jit(solution)/shard_map/lktij,tbcj->bclki/dot_general | solution.py:207
  32.2 0.8 convolution_bitcast_fusion.3
  33.3 0.6 copy-done.15
  33.9 0.6 fusion.112
  34.6 0.3 reshape.589
  35.0 0.8 copy.216
  35.9 0.5 reshape.539
  36.4 0.9 %convolution_bitcast_fusion.2 = f32[128,3,2,32]{0,3,2,1:T(8,128)S(1)} fusion(bf16[3,128,128]{2,1,0:T(8,128)(2,1)} %param.14, f32[128,9,2,32]{0,3,2,1:T(8,128)S(1)} %reshape.539, f32[128,2,32]{0,2,1:T(8,128)S(1)} %get-tuple-element.51), kind=kOutput, calls=%fused_computation.25 | convolution fusion | flops 6422528 | bytes 425984 | tf_op jit(solution)/shard_map/xc,xlbi->clbi/dot_general | solution.py:52
  37.3 0.9 %convolution_bitcast_fusion = f32[128,5,2,32]{0,3,2,1:T(8,128)S(1)} fusion(bf16[3,128,128]{2,1,0:T(8,128)(2,1)} %param.14, f32[128,9,2,32]{0,3,2,1:T(8,128)S(1)} %reshape.539, f32[128,2,32]{0,2,1:T(8,128)S(1)} %get-tuple-element.51), kind=kOutput, calls=%fused_computation.23 | convolution fusion | flops 10616832 | bytes 491520 | tf_op jit(solution)/shard_map/xc,xlbi->clbi/dot_general | solution.py:52
  38.2 1.6 %multiply_reduce_fusion.4 = (f32[128,2,32]{0,2,1:T(8,128)S(1)}, bf16[128,8,2,1,32]{0,4,2,1,3:T(8,128)(2,1)}) fusion(f32[128,9,2,32]{0,3,2,1:T(8,128)S(1)} %reshape.539, f32[128,5,2,32]{0,3,2,1:T(8,128)S(1)} %convolution_bitcast_fusion.1, f32[128,3,2,32]{0,3,2,1:T(8,128)} %convolution_bitcast_fusion.3, f32[128,2,32]{0,2,1:T(8,128)S(1)} %get-tuple-element.51), kind=kLoop, calls=%fused_computation.52 | loop fusion | flops 319488 | bytes 720896 | tf_op jit(solution)/shard_map/reduce_sum | solution.py:237
  39.8 0.9 %convolution_bitcast_fusion.4 = f32[128,1,2,32]{0,3,2,1:T(8,128)S(1)} fusion(bf16[3,128,128]{2,1,0:T(8,128)(2,1)} %param.14, f32[128,2,32]{0,2,1:T(8,128)S(1)} %copy-done.16, f32[128,2,32]{0,2,1:T(8,128)S(1)} %get-tuple-element.40, f32[128,9,2,32]{0,3,2,1:T(8,128)S(1)} %reshape.539), kind=kOutput, calls=%fused_computation.27 | convolution fusion | flops 2195456 | bytes 163840 | tf_op jit(solution)/shard_map/xc,xlbi->clbi/dot_general | solution.py:52
  40.7 0.8 fusion.29
  41.5 0.7 gather_fusion.3
  42.3 1.4 %multiply_convert_fusion = bf16[8,128,9,8,32]{1,4,3,2,0:T(8,128)(2,1)S(1)} fusion(f32[8,128,9,32]{1,3,2,0:T(8,128)S(1)} %gather_fusion.3, f32[8,128,8]{1,2,0:T(8,128)S(1)} %broadcast_multiply_fusion), kind=kLoop, calls=%fused_computation.6 | loop fusion | flops 4718592 | bytes 5931008 | tf_op jit(solution)/shard_map/convert_element_type | solution.py:248
  43.6 2.1 %fusion.8 = f32[8,128,128]{2,1,0:T(8,128)S(1)} fusion(bf16[8,128,9,8,32]{1,4,3,2,0:T(8,128)(2,1)S(1)} %multiply_convert_fusion, f32[8,8,32,128]{3,2,0,1:T(8,128)S(1)} %fusion.17, f32[9,8,32,128]{3,2,1,0:T(8,128)S(1)} %copy-done.3), kind=kOutput, calls=%fused_computation.21 | convolution fusion | flops 608698368 | bytes 7471104 | tf_op jit(solution)/shard_map/tclki,lktij->tcj/dot_general | solution.py:249
  45.7 1.4 %fusion.131 = f32[8,128,2304]{1,2,0:S(1)} fusion(bf16[8,128,2304]{1,2,0:T(8,128)(2,1)S(1)} %bitcast.409, bf16[8,128,128]{2,1,0:T(8,128)(2,1)S(1)} %gather_fusion), kind=kOutput, calls=%fused_computation.252 | convolution fusion | flops 603979776 | bytes 14417920
  47.1 3.8 %multiply_reduce_fusion.1 = (f32[9,8,32,128]{3,2,0,1:T(8,128)S(1)}, f32[8,8,32,128]{3,2,0,1:T(8,128)}) fusion(f32[9,8,8,32,128]{4,3,1,0,2:T(8,128)S(1)} %bitcast.408, f32[8,8,32,128]{3,2,0,1:T(8,128)S(1)} %fusion.17, f32[9,8,32,128]{3,2,1,0:T(8,128)S(1)} %copy-done.3), kind=kLoop, calls=%fused_computation.5 | loop fusion | flops 8880128 | bytes 13893632 | tf_op jit(solution)/shard_map/reduce_sum | solution.py:255
  50.9 0.8 fusion.38
  51.7 0.9 %fusion.71 = (f32[8,1,32,128]{3,2,0,1:T(8,128)}, f32[8,1,32,128]{3,2,0,1:T(8,128)}) fusion(f32[9,8,32,128]{3,2,0,1:T(8,128)S(1)} %get-tuple-element.28, f32[8,3,32,128]{3,2,0,1:T(8,128)S(1)} %get-tuple-element.52, f32[8,32,128]{2,1,0:T(8,128)S(1)} %get-tuple-element.53), kind=kLoop, calls=%fused_computation.119 | loop fusion | flops 950272 | bytes 1703936 | tf_op jit(solution)/shard_map/transpose(jvp())/div | solution.py:94
  52.6 0.3 fusion.6
  53.0 0.7 reshape.531
  53.7 1.1 %multiply_reduce_fusion.2 = f32[128,5,128]{2,0,1:T(8,128)S(1)} fusion(f32[8,128,128]{2,1,0:T(8,128)S(1)} %fusion.8, f32[8,5]{1,0:T(8,128)} %copy-done.23), kind=kLoop, calls=%fused_computation.14 | loop fusion | flops 1228800 | bytes 852128 | tf_op jit(solution)/shard_map/reduce_sum | solution.py:258
  55.0 0.8 reshape_reshape.15
  55.9 1.2 %fusion.18 = (f32[8,32,128]{2,1,0:T(8,128)S(1)}, f32[8,32,128]{2,1,0:T(8,128)S(1)}) fusion(f32[8,8,32,128]{3,2,0,1:T(8,128)S(1)} %copy-done, f32[8]{0:T(128)} %copy-done.33, f32[8,32,128]{2,1,0:T(8,128)S(1)} %copy-done.6, f32[8,32,128]{2,1,0:T(8,128)S(1)} %copy-done.8), kind=kLoop, calls=%fused_computation.34 | loop fusion | flops 2818048 | bytes 1572896 | tf_op jit(solution)/shard_map/transpose(jvp())/reduce_sum | solution.py:111
  57.2 0.3 fusion.50
  57.5 0.4 copy-done.10
  58.1 0.3 fusion.83
  59.0 0.4 collective-permute-start.3
  59.4 1.1 %collective-permute-done.3 = f32[69,640]{1,0:T(8,128)S(1)} collective-permute-done((f32[69,640]{1,0:T(8,128)S(1)}, f32[69,640]{1,0:T(8,128)S(1)}, u32[]{:S(2)}, u32[]{:S(2)}) %collective-permute-start.3) | collective-permute-done | bytes 176672 | tf_op jit(solution)/shard_map/ppermute | solution.py:19
  60.6 1.8 %collective-permute-start.4 = (f32[37,640]{1,0:T(8,128)S(1)}, f32[37,640]{1,0:T(8,128)S(1)}, u32[]{:S(2)}, u32[]{:S(2)}) collective-permute-start(f32[37,640]{1,0:T(8,128)S(1)} %pad_maximum_fusion.4), channel_id=1, source_target_pairs={{0,2},{1,3},{2,0},{3,1},{4,6},{5,7},{6,4},{7,5},{8,10},{9,11},{10,... | collective-permute-start | bytes 284168 | tf_op jit(solution)/shard_map/ppermute | solution.py:19
  62.4 3.4 %collective-permute-done.4 = f32[37,640]{1,0:T(8,128)S(1)} collective-permute-done((f32[37,640]{1,0:T(8,128)S(1)}, f32[37,640]{1,0:T(8,128)S(1)}, u32[]{:S(2)}, u32[]{:S(2)}) %collective-permute-start.4) | collective-permute-done | bytes 94752 | tf_op jit(solution)/shard_map/ppermute | solution.py:19
  66.1 0.6 collective-permute-start.5
  66.7 3.3 %collective-permute-done.5 = f32[37,128]{1,0:T(8,128)S(1)} collective-permute-done((f32[37,128]{1,0:T(8,128)S(1)}, f32[37,128]{1,0:T(8,128)S(1)}, u32[]{:S(2)}, u32[]{:S(2)}) %collective-permute-start.5) | collective-permute-done | bytes 18976 | tf_op jit(solution)/shard_map/ppermute | solution.py:19
  70.2 0.5 collective-permute-start.6
  70.7 0.8 copy.212
  71.6 1.2 %reshape.586 = bf16[4,2,9216]{2,1,0:T(2,128)(2,1)} reshape(bf16[128,1,9,2,32]{4,3,2,1,0:T(2,128)(2,1)S(1)} %bitcast.411) | data formatting | bytes 294912
  72.8 3.3 %all-to-all-start = ((bf16[4,2,9216]{2,1,0:T(2,128)(2,1)}), bf16[4,2,9216]{2,1,0:T(2,128)(2,1)S(1)}, u32[]{:S(2)}, u32[]{:S(2)}) async-start(bf16[4,2,9216]{2,1,0:T(2,128)(2,1)} %reshape.586), calls=%async_computation | async-start | bytes 294912 | tf_op jit(solution)/shard_map/all_to_all | solution.py:220
  76.4 0.4 collective-permute-start.7
  76.8 4.1 %all-to-all-done = bf16[4,2,9216]{2,1,0:T(2,128)(2,1)S(1)} async-done(((bf16[4,2,9216]{2,1,0:T(2,128)(2,1)}), bf16[4,2,9216]{2,1,0:T(2,128)(2,1)S(1)}, u32[]{:S(2)}, u32[]{:S(2)}) %all-to-all-start) | async-done | bytes 147488 | tf_op jit(solution)/shard_map/all_to_all | solution.py:220
  80.9 0.3 reshape.587
  81.2 0.8 copy.213
  82.0 1.1 %reshape.526 = bf16[32,9,256]{2,0,1:T(8,128)(2,1)} reshape(bf16[32,9,2,4,1,32]{5,3,2,0,1,4:T(4,128)(2,1)S(1)} %copy.213) | data formatting | bytes 294912 | tf_op jit(solution)/shard_map/reshape | solution.py:226
  83.1 0.3 maximum_add_fusion
  83.4 0.6 slice_negate_fusion
  84.0 0.6 slice.382
  84.7 0.7 copy.233
  (168 shorter events, 4.6 us)
Async XLA Ops:
  2.3 16.4 %collective-permute-start = (f32[35,128]{1,0:T(8,128)S(1)}, f32[35,128]{1,0:T(8,128)S(1)}, u32[]{:S(2)}, u32[]{:S(2)}) collective-permute-start(f32[35,128]{1,0:T(8,128)S(1)} %get-tuple-element.47), channel_id=1, source_target_pairs={{0,4},{4,0},{8,12},{12,8},{16,20},{20,16},{24,28},{28,24},{1,5},{5... | collective-permute-start | bytes 53768 | tf_op jit(solution)/shard_map/ppermute | solution.py:19
  5.4 13.3 %collective-permute-start.2 = (f32[35,128]{1,0:T(8,128)S(1)}, f32[35,128]{1,0:T(8,128)S(1)}, u32[]{:S(2)}, u32[]{:S(2)}) collective-permute-start(f32[35,128]{1,0:T(8,128)S(1)} %get-tuple-element.48), channel_id=1, source_target_pairs={{0,16},{4,20},{8,24},{12,28},{16,0},{20,4},{24,8},{28,12},{1,17},{... | collective-permute-start | bytes 53768 | tf_op jit(solution)/shard_map/ppermute | solution.py:19
  7.9 10.8 %collective-permute-start.1 = (f32[35,128]{1,0:T(8,128)S(1)}, f32[35,128]{1,0:T(8,128)S(1)}, u32[]{:S(2)}, u32[]{:S(2)}) collective-permute-start(f32[35,128]{1,0:T(8,128)S(1)} %get-tuple-element.49), channel_id=1, source_target_pairs={{0,8},{4,12},{8,0},{12,4},{16,24},{20,28},{24,16},{28,20},{1,9},{5... | collective-permute-start | bytes 53768 | tf_op jit(solution)/shard_map/ppermute | solution.py:19
  10.8 5.3 %copy-start.34 = (s32[8,2]{0,1:T(2,128)S(1)}, s32[8,2]{0,1:T(2,128)}, u32[]{:S(2)}) copy-start(s32[8,2]{0,1:T(2,128)} %param.11) | copy-start | bytes 196
  10.8 5.4 %copy-start.36 = (s32[8]{0:T(128)S(1)}, s32[8]{0:T(128)}, u32[]{:S(2)}) copy-start(s32[8]{0:T(128)} %param.12) | copy-start | bytes 100
  10.8 5.4 %copy-start.30 = (f32[32,8]{0,1:T(8,128)S(1)}, f32[32,8]{0,1:T(8,128)}, u32[]{:S(2)}) copy-start(f32[32,8]{0,1:T(8,128)} %param.13) | copy-start | bytes 3076
  10.8 7.9 %copy-start.21 = (bf16[32,256]{1,0:T(8,128)(2,1)S(1)}, bf16[32,256]{1,0:T(8,128)(2,1)}, u32[]{:S(2)}) copy-start(bf16[32,256]{1,0:T(8,128)(2,1)} %param.9) | copy-start | bytes 49156
  11.5 13.2 %copy-start.29 = (f32[3,256]{1,0:T(4,128)S(1)}, f32[3,256]{1,0:T(4,128)}, u32[]{:S(2)}) copy-start(f32[3,256]{1,0:T(4,128)} %param.8) | copy-start | bytes 9220
  12.8 21.8 %all-to-all-start.1 = ((bf16[4,2,9216]{2,1,0:T(2,128)(2,1)}), bf16[4,2,9216]{2,1,0:T(2,128)(2,1)S(1)}, u32[]{:S(2)}, u32[]{:S(2)}) async-start(bf16[4,2,9216]{2,1,0:T(2,128)(2,1)} %reshape.588), calls=%async_computation.1 | async-start | bytes 294912 | tf_op jit(solution)/shard_map/all_to_all | solution.py:227
  16.1 11.8 %copy-start.31 = (f32[8]{0:T(128)}, f32[8]{0:T(128)S(1)}, u32[]{:S(2)}) copy-start(f32[8]{0:T(128)S(1)} %compare_convert_fusion) | copy-start | bytes 100
  16.2 18.3 %copy-start.27 = (f32[8]{0:T(128)}, f32[8]{0:T(128)S(1)}, u32[]{:S(2)}) copy-start(f32[8]{0:T(128)S(1)} %convert_element_type.99) | copy-start | bytes 100
  16.9 7.9 %copy-start.23 = (f32[8,5]{1,0:T(8,128)}, f32[8,5]{1,0:T(8,128)S(1)}, u32[]{:S(2)}) copy-start(f32[8,5]{1,0:T(8,128)S(1)} %get-tuple-element.64) | copy-start | bytes 484
  17.0 11.0 %copy-start.33 = (f32[8]{0:T(128)}, f32[8]{0:T(128)S(1)}, u32[]{:S(2)}) copy-start(f32[8]{0:T(128)S(1)} %add_multiply_fusion) | copy-start | bytes 100
  25.4 1.9 %copy-start.17 = (f32[8,3,128]{2,0,1:T(8,128)}, f32[8,3,128]{2,0,1:T(8,128)S(1)}, u32[]{:S(2)}) copy-start(f32[8,3,128]{2,0,1:T(8,128)S(1)} %copy.206) | copy-start | bytes 36868
  26.1 1.4 %copy-start.19 = (f32[8,3,32]{2,0,1:T(8,128)}, f32[8,3,32]{2,0,1:T(8,128)S(1)}, u32[]{:S(2)}) copy-start(f32[8,3,32]{2,0,1:T(8,128)S(1)} %copy.208) | copy-start | bytes 9220
  27.9 4.2 %copy-start.2 = (f32[9,8,32,128]{3,2,1,0:T(8,128)}, f32[9,8,32,128]{3,2,1,0:T(8,128)S(1)}, u32[]{:S(2)}) copy-start(f32[9,8,32,128]{3,2,1,0:T(8,128)S(1)} %multiply_dynamic-update-slice_fusion) | copy-start | bytes 3538948
  28.0 0.8 copy-start.5
  28.0 0.8 copy-start.7
  29.1 3.0 %copy-start.14 = (bf16[3,128,128]{2,1,0:T(8,128)(2,1)S(1)}, bf16[3,128,128]{2,1,0:T(8,128)(2,1)}, u32[]{:S(2)}) copy-start(bf16[3,128,128]{2,1,0:T(8,128)(2,1)} %param.14) | copy-start | bytes 294916
  33.3 0.6 copy-start.15
  36.4 3.4 %copy-start.16 = (f32[128,2,32]{0,2,1:T(8,128)S(1)}, f32[128,2,32]{0,2,1:T(8,128)}, u32[]{:S(2)}) copy-start(f32[128,2,32]{0,2,1:T(8,128)} %copy-done.15) | copy-start | bytes 98308
  42.3 1.4 %copy-start.3 = (f32[9,8,32,128]{3,2,1,0:T(8,128)S(1)}, f32[9,8,32,128]{3,2,1,0:T(8,128)}, u32[]{:S(2)}) copy-start(f32[9,8,32,128]{3,2,1,0:T(8,128)} %copy-done.2) | copy-start | bytes 3538948
  50.9 1.7 %copy-start.1 = (f32[2,128,9,8,32,1]{1,4,5,3,2,0:T(8,128)S(1)}, f32[2,128,9,8,32,1]{1,4,5,3,2,0:T(8,128)}, u32[]{:S(2)}) copy-start(f32[2,128,9,8,32,1]{1,4,5,3,2,0:T(8,128)} %get-tuple-element.69) | copy-start | bytes 7077892
  50.9 1.7 %copy-start.9 = (f32[128,2,32,9]{0,2,1,3:T(8,128)S(1)}, f32[128,2,32,9]{0,2,1,3:T(8,128)}, u32[]{:S(2)}) copy-start(f32[128,2,32,9]{0,2,1,3:T(8,128)} %get-tuple-element.39) | copy-start | bytes 884740
  53.7 2.1 %copy-start = (f32[8,8,32,128]{3,2,0,1:T(8,128)S(1)}, f32[8,8,32,128]{3,2,0,1:T(8,128)}, u32[]{:S(2)}) copy-start(f32[8,8,32,128]{3,2,0,1:T(8,128)} %get-tuple-element.29) | copy-start | bytes 3145732
  53.7 2.1 %copy-start.6 = (f32[8,32,128]{2,1,0:T(8,128)S(1)}, f32[8,32,128]{2,1,0:T(8,128)}, u32[]{:S(2)}) copy-start(f32[8,32,128]{2,1,0:T(8,128)} %copy-done.5) | copy-start | bytes 393220
  53.7 2.1 %copy-start.8 = (f32[8,32,128]{2,1,0:T(8,128)S(1)}, f32[8,32,128]{2,1,0:T(8,128)}, u32[]{:S(2)}) copy-start(f32[8,32,128]{2,1,0:T(8,128)} %copy-done.7) | copy-start | bytes 393220
  55.9 1.2 %copy-start.28 = (f32[8]{0:T(128)S(1)}, f32[8]{0:T(128)}, u32[]{:S(2)}) copy-start(f32[8]{0:T(128)} %copy-done.27) | copy-start | bytes 100
  55.9 1.2 %copy-start.32 = (f32[8]{0:T(128)S(1)}, f32[8]{0:T(128)}, u32[]{:S(2)}) copy-start(f32[8]{0:T(128)} %copy-done.31) | copy-start | bytes 100
  57.0 0.9 %copy-start.10 = (f32[8,1,32,128]{3,2,0,1:T(8,128)S(1)}, f32[8,1,32,128]{3,2,0,1:T(8,128)}, u32[]{:S(2)}) copy-start(f32[8,1,32,128]{3,2,0,1:T(8,128)} %fusion.38) | copy-start | bytes 393220
  57.0 1.0 %copy-start.12 = (f32[8,1,32,128]{3,2,0,1:T(8,128)S(1)}, f32[8,1,32,128]{3,2,0,1:T(8,128)}, u32[]{:S(2)}) copy-start(f32[8,1,32,128]{3,2,0,1:T(8,128)} %get-tuple-element.34) | copy-start | bytes 393220
  57.1 1.0 %copy-start.13 = (f32[8,1,32,128]{3,2,0,1:T(8,128)S(1)}, f32[8,1,32,128]{3,2,0,1:T(8,128)}, u32[]{:S(2)}) copy-start(f32[8,1,32,128]{3,2,0,1:T(8,128)} %get-tuple-element.35) | copy-start | bytes 393220
  57.1 1.0 %copy-start.18 = (f32[8,3,128]{2,0,1:T(8,128)S(1)}, f32[8,3,128]{2,0,1:T(8,128)}, u32[]{:S(2)}) copy-start(f32[8,3,128]{2,0,1:T(8,128)} %copy-done.17) | copy-start | bytes 36868
  57.1 1.0 %copy-start.20 = (f32[8,3,32]{2,0,1:T(8,128)S(1)}, f32[8,3,32]{2,0,1:T(8,128)}, u32[]{:S(2)}) copy-start(f32[8,3,32]{2,0,1:T(8,128)} %copy-done.19) | copy-start | bytes 9220
  57.1 1.3 %copy-start.26 = (f32[8,5]{0,1:T(8,128)S(1)}, f32[8,5]{0,1:T(8,128)}, u32[]{:S(2)}) copy-start(f32[8,5]{0,1:T(8,128)} %copy.220) | copy-start | bytes 484
  57.1 1.5 %copy-start.25 = (f32[8,5]{0,1:T(8,128)S(1)}, f32[8,5]{0,1:T(8,128)}, u32[]{:S(2)}) copy-start(f32[8,5]{0,1:T(8,128)} %copy.229) | copy-start | bytes 484
  57.1 1.8 %copy-start.24 = (f32[1024]{0:T(1024)S(1)}, f32[1024]{0:T(1024)}, u32[]{:S(2)}) copy-start(f32[1024]{0:T(1024)} %reshape.531) | copy-start | bytes 12292
  57.1 1.8 %copy-start.4 = (f32[2,2,32,640]{3,2,1,0:T(8,128)S(1)}, f32[2,2,32,640]{3,2,1,0:T(8,128)}, u32[]{:S(2)}) copy-start(f32[2,2,32,640]{3,2,1,0:T(8,128)} %reshape_reshape.15) | copy-start | bytes 983044
  59.0 11.7 %copy-start.11 = (bf16[128,8,2,1,32]{0,4,2,1,3:T(8,128)(2,1)S(1)}, bf16[128,8,2,1,32]{0,4,2,1,3:T(8,128)(2,1)}, u32[]{:S(2)}) copy-start(bf16[128,8,2,1,32]{0,4,2,1,3:T(8,128)(2,1)} %get-tuple-element.41) | copy-start | bytes 393220
  59.0 11.7 %copy-start.22 = (bf16[128,1,2,1,32]{0,4,2,1,3:T(8,128)(2,1)S(1)}, bf16[128,1,2,1,32]{0,4,2,1,3:T(8,128)(2,1)}, u32[]{:S(2)}) copy-start(bf16[128,1,2,1,32]{0,4,2,1,3:T(8,128)(2,1)} %get-tuple-element.50) | copy-start | bytes 49156
  59.0 1.5 %collective-permute-start.3 = (f32[69,640]{1,0:T(8,128)S(1)}, f32[69,640]{1,0:T(8,128)S(1)}, u32[]{:S(2)}, u32[]{:S(2)}) collective-permute-start(f32[69,640]{1,0:T(8,128)S(1)} %pad_maximum_fusion.2), channel_id=1, source_target_pairs={{0,1},{1,0},{2,3},{3,2},{4,5},{5,4},{6,7},{7,6},{8,9},{9,8},{10,11... | collective-permute-start | bytes 529928 | tf_op jit(solution)/shard_map/ppermute | solution.py:19
  60.6 5.2 %collective-permute-start.4 = (f32[37,640]{1,0:T(8,128)S(1)}, f32[37,640]{1,0:T(8,128)S(1)}, u32[]{:S(2)}, u32[]{:S(2)}) collective-permute-start(f32[37,640]{1,0:T(8,128)S(1)} %pad_maximum_fusion.4), channel_id=1, source_target_pairs={{0,2},{1,3},{2,0},{3,1},{4,6},{5,7},{6,4},{7,5},{8,10},{9,11},{10,... | collective-permute-start | bytes 284168 | tf_op jit(solution)/shard_map/ppermute | solution.py:19
  66.1 3.8 %collective-permute-start.5 = (f32[37,128]{1,0:T(8,128)S(1)}, f32[37,128]{1,0:T(8,128)S(1)}, u32[]{:S(2)}, u32[]{:S(2)}) collective-permute-start(f32[37,128]{1,0:T(8,128)S(1)} %pad_maximum_fusion.5), channel_id=1, source_target_pairs={{0,4},{4,0},{8,12},{12,8},{16,20},{20,16},{24,28},{28,24},{1,5},{5... | collective-permute-start | bytes 56840 | tf_op jit(solution)/shard_map/ppermute | solution.py:19
  70.2 5.9 %collective-permute-start.6 = (f32[37,128]{1,0:T(8,128)S(1)}, f32[37,128]{1,0:T(8,128)S(1)}, u32[]{:S(2)}, u32[]{:S(2)}) collective-permute-start(f32[37,128]{1,0:T(8,128)S(1)} %pad_maximum_fusion.6), channel_id=1, source_target_pairs={{0,8},{4,12},{8,0},{12,4},{16,24},{20,28},{24,16},{28,20},{1,9},{5... | collective-permute-start | bytes 56840 | tf_op jit(solution)/shard_map/ppermute | solution.py:19
  72.8 8.1 %all-to-all-start = ((bf16[4,2,9216]{2,1,0:T(2,128)(2,1)}), bf16[4,2,9216]{2,1,0:T(2,128)(2,1)S(1)}, u32[]{:S(2)}, u32[]{:S(2)}) async-start(bf16[4,2,9216]{2,1,0:T(2,128)(2,1)} %reshape.586), calls=%async_computation | async-start | bytes 294912 | tf_op jit(solution)/shard_map/all_to_all | solution.py:220
  76.4 6.7 %collective-permute-start.7 = (f32[37,128]{1,0:T(8,128)S(1)}, f32[37,128]{1,0:T(8,128)S(1)}, u32[]{:S(2)}, u32[]{:S(2)}) collective-permute-start(f32[37,128]{1,0:T(8,128)S(1)} %pad_maximum_fusion.7), channel_id=1, source_target_pairs={{0,16},{4,20},{8,24},{12,28},{16,0},{20,4},{24,8},{28,12},{1,17},{... | collective-permute-start | bytes 56840 | tf_op jit(solution)/shard_map/ppermute | solution.py:19
  81.2 1.9 %copy-start.35 = (s32[3,128]{1,0:T(4,128)S(1)}, s32[3,128]{1,0:T(4,128)}, u32[]{:S(2)}) copy-start(s32[3,128]{1,0:T(4,128)} %param.10) | copy-start | bytes 4612

commit v19 on v18

--- a/solution.py
+++ b/solution.py
@@ -64,7 +64,11 @@
 def halving_with(value, extras, axis):
     index = lax.axis_index(axis)
     width = value.shape[1]
-    extra_rows = as_rows(jnp.concatenate([extra.reshape(-1) for extra in extras]), width)
+    pieces = [
+        extra if extra.ndim == 2 and extra.shape[1] == width else as_rows(extra, width)
+        for extra in extras
+    ]
+    extra_rows = jnp.concatenate(pieces, axis=0)
     count = lax.axis_size(axis)
     chunk = value.shape[0] // count
     for bit in range(count.bit_length() - 1):
@@ -76,12 +80,12 @@
         got = partner(jnp.concatenate([give, extra_rows], axis=0), axis, bit)
         value = keep + got[:half]
         extra_rows = extra_rows + got[half:]
-    flat = extra_rows.reshape(-1)
     sums = []
     start = 0
-    for extra in extras:
-        sums.append(flat[start : start + extra.size].reshape(extra.shape))
-        start += extra.size
+    for extra, piece in zip(extras, pieces):
+        rows = extra_rows[start : start + piece.shape[0]]
+        sums.append(rows.reshape(-1)[: extra.size].reshape(extra.shape))
+        start += piece.shape[0]
     return value, sums
 
 

time: 86.1 us -> 86.1 us (level)
  no operation moved by 1% of the time
where the time goes in v19:
time: 86.1 us; the launch traced here: 85.3 us
  local copies, waits for them, and re-layouts  20.1 us (23%)
  starting transfers between devices  17.5 us (20%)
  other arithmetic  16.8 us (20%)
  waiting for transfers between devices  11.9 us (14%)
  matrix products  11.5 us (13%)
  blocking collectives  5.86 us (7%)
  between operations  1.64 us (2%)
    ppermute x8, starting transfers between devices, partner(): return lax.ppermute(value, axis, pairs)  10.9 us
    ppermute x8, waiting for transfers between devices, partner(): return lax.ppermute(value, axis, pairs)  7.8 us
    unnamed x82, local copies, waits for them, and re-layouts  6.12 us
    all_gather x1, blocking collectives, body(): lax.all_gather(jnp.concatenate([src_feat, weight_high, weight_mid, weight...  5.86 us
    all_to_all x1, waiting for transfers between devices, body(): lax.all_to_all(result_rows.reshape(all_chan, components, own_blocks, 1, r...  4.15 us
    dot_general x6, matrix products, mix_orders(): jnp.einsum(spec, weights[order], values[:, low:high], preferred_element_t...  3.81 us
    reduce_sum x1, other arithmetic, body(): harm_grad = jnp.sum(value_grad * radial[None], axis=1)  3.77 us
    all_to_all x1, starting transfers between devices, body(): lax.all_to_all(result_rows.reshape(all_chan, components, own_blocks, 1, r...  3.34 us
  transfers between devices with their start and end apart: 10, of which 4 were waited for; matrix products, arithmetic and copies ran while one was open for 21% of the time, Pallas kernels for 0%

profile of v19, /device:TPU:0, one launch (start us, length us, event | category | flops | bytes accessed | tf_op | source)
XLA Modules:
  0.0 85.3 jit_solution(16056262765794224382)
XLA Ops:
  0.6 0.7 convert_element_type.92
  1.4 1.0 %fusion.26 = f32[35,384]{1,0:T(8,128)S(1)} fusion(s32[384]{0:T(512)} %bitcast.424, f32[3,256]{1,0:T(4,128)} %param.8, f32[32,256]{1,0:T(8,128)S(1)} %convert_element_type.92), kind=kOutput, calls=%fused_computation.46 | convolution fusion | flops 41394944 | bytes 91136 | tf_op jit(solution)/shard_map/dot_general | solution.py:148
  2.3 3.0 %collective-permute-start = (f32[35,128]{1,0:T(8,128)S(1)}, f32[35,128]{1,0:T(8,128)S(1)}, u32[]{:S(2)}, u32[]{:S(2)}) collective-permute-start(f32[35,128]{1,0:T(8,128)S(1)} %get-tuple-element.43), channel_id=1, source_target_pairs={{0,4},{4,0},{8,12},{12,8},{16,20},{20,16},{24,28},{28,24},{1,5},{5... | collective-permute-start | bytes 53768 | tf_op jit(solution)/shard_map/ppermute | solution.py:19
  5.4 2.6 %collective-permute-start.2 = (f32[35,128]{1,0:T(8,128)S(1)}, f32[35,128]{1,0:T(8,128)S(1)}, u32[]{:S(2)}, u32[]{:S(2)}) collective-permute-start(f32[35,128]{1,0:T(8,128)S(1)} %get-tuple-element.44), channel_id=1, source_target_pairs={{0,16},{4,20},{8,24},{12,28},{16,0},{20,4},{24,8},{28,12},{1,17},{... | collective-permute-start | bytes 53768 | tf_op jit(solution)/shard_map/ppermute | solution.py:19
  7.9 1.6 %collective-permute-start.1 = (f32[35,128]{1,0:T(8,128)S(1)}, f32[35,128]{1,0:T(8,128)S(1)}, u32[]{:S(2)}, u32[]{:S(2)}) collective-permute-start(f32[35,128]{1,0:T(8,128)S(1)} %get-tuple-element.45), channel_id=1, source_target_pairs={{0,8},{4,12},{8,0},{12,4},{16,24},{20,28},{24,16},{28,20},{1,9},{5... | collective-permute-start | bytes 53768 | tf_op jit(solution)/shard_map/ppermute | solution.py:19
  9.5 1.3 %reshape.527 = bf16[32,9,2,4,32]{4,3,2,0,1:T(4,128)(2,1)S(1)} reshape(bf16[32,9,256]{2,0,1:T(8,128)(2,1)} %param.15) | data formatting | bytes 294912 | tf_op jit(solution)/shard_map/reshape | solution.py:232
  10.8 0.7 copy.186
  11.5 1.2 %reshape.589 = bf16[4,2,9216]{2,1,0:T(2,128)(2,1)} reshape(bf16[4,9,2,32,32]{4,3,2,1,0:T(8,128)(2,1)S(1)} %bitcast.410) | data formatting | bytes 294912
  12.8 3.3 %all-to-all-start.1 = ((bf16[4,2,9216]{2,1,0:T(2,128)(2,1)}), bf16[4,2,9216]{2,1,0:T(2,128)(2,1)S(1)}, u32[]{:S(2)}, u32[]{:S(2)}) async-start(bf16[4,2,9216]{2,1,0:T(2,128)(2,1)} %reshape.589), calls=%async_computation.1 | async-start | bytes 294912 | tf_op jit(solution)/shard_map/all_to_all | solution.py:231
  16.2 0.6 pad_clamp_fusion
  17.3 0.7 copy.200
  18.0 0.7 copy.191
  18.8 5.9 %all_gather.3 = bf16[128,664]{1,0:T(8,128)(2,1)S(1)} all-gather(bf16[32,664]{1,0:T(8,128)(2,1)S(1)} %concatenate.65), channel_id=1, replica_groups=mesh['space'=8,'chan'=4] {'chan'}, dimensions={0}, use_global_device_ids=true | all-gather | bytes 212480 | tf_op jit(solution)/shard_map/all_gather | solution.py:168
  24.8 0.6 gather_fusion.1
  25.5 0.6 gather_fusion.2
  26.6 0.6 gather_fusion
  28.0 0.7 copy-done.5
  28.8 0.3 fusion.17
  29.1 3.0 %fusion.7 = (bf16[128,2,9,32]{0,3,2,1:T(8,128)(2,1)S(1)}, f32[2,128,9,8,32,1]{1,4,5,3,2,0:T(8,128)}) fusion(f32[128,8]{0,1:T(8,128)S(1)} %copy.235, f32[8,128,128]{2,1,0:T(8,128)S(1)} %convert_element_type.100, f32[8,2]{0,1:T(2,128)S(1)} %copy.173, f32[8,8,32,128]{3,2,0,1:T(8,128)S(1)} %fusion.17, f32[9,8,32,128]{3,2,1,0:T(8,128)S(1)} %multiply_dynamic-update-slice_fusion), kind=kOutput, calls=%fused_computation.18 | convolution fusion | flops 1214308352 | bytes 5263424 | tf_op jit(solution)/shard_map/lktij,tbcj->bclki/dot_general | solution.py:211
  32.2 0.8 convolution_bitcast_fusion.3
  33.3 0.6 copy-done.15
  33.9 0.6 fusion.112
  34.6 0.3 reshape.590
  35.0 0.8 copy.187
  35.9 0.5 reshape.540
  36.4 0.9 %convolution_bitcast_fusion.2 = f32[128,3,2,32]{0,3,2,1:T(8,128)S(1)} fusion(bf16[3,128,128]{2,1,0:T(8,128)(2,1)} %param.14, f32[128,9,2,32]{0,3,2,1:T(8,128)S(1)} %reshape.540, f32[128,2,32]{0,2,1:T(8,128)S(1)} %get-tuple-element.47), kind=kOutput, calls=%fused_computation.25 | convolution fusion | flops 6422528 | bytes 425984 | tf_op jit(solution)/shard_map/xc,xlbi->clbi/dot_general | solution.py:52
  37.3 0.9 %convolution_bitcast_fusion = f32[128,5,2,32]{0,3,2,1:T(8,128)S(1)} fusion(bf16[3,128,128]{2,1,0:T(8,128)(2,1)} %param.14, f32[128,9,2,32]{0,3,2,1:T(8,128)S(1)} %reshape.540, f32[128,2,32]{0,2,1:T(8,128)S(1)} %get-tuple-element.47), kind=kOutput, calls=%fused_computation.23 | convolution fusion | flops 10616832 | bytes 491520 | tf_op jit(solution)/shard_map/xc,xlbi->clbi/dot_general | solution.py:52
  38.2 1.6 %multiply_reduce_fusion.4 = (f32[128,2,32]{0,2,1:T(8,128)S(1)}, bf16[128,8,2,1,32]{0,4,2,1,3:T(8,128)(2,1)}) fusion(f32[128,9,2,32]{0,3,2,1:T(8,128)S(1)} %reshape.540, f32[128,5,2,32]{0,3,2,1:T(8,128)S(1)} %convolution_bitcast_fusion.1, f32[128,3,2,32]{0,3,2,1:T(8,128)} %convolution_bitcast_fusion.3, f32[128,2,32]{0,2,1:T(8,128)S(1)} %get-tuple-element.47), kind=kLoop, calls=%fused_computation.52 | loop fusion | flops 319488 | bytes 720896 | tf_op jit(solution)/shard_map/reduce_sum | solution.py:241
  39.8 0.9 %convolution_bitcast_fusion.4 = f32[128,1,2,32]{0,3,2,1:T(8,128)S(1)} fusion(bf16[3,128,128]{2,1,0:T(8,128)(2,1)} %param.14, f32[128,2,32]{0,2,1:T(8,128)S(1)} %copy-done.16, f32[128,2,32]{0,2,1:T(8,128)S(1)} %get-tuple-element.36, f32[128,9,2,32]{0,3,2,1:T(8,128)S(1)} %reshape.540), kind=kOutput, calls=%fused_computation.27 | convolution fusion | flops 2195456 | bytes 163840 | tf_op jit(solution)/shard_map/xc,xlbi->clbi/dot_general | solution.py:52
  40.7 0.8 fusion.29
  41.5 0.7 gather_fusion.3
  42.3 1.4 %multiply_convert_fusion = bf16[8,128,9,8,32]{1,4,3,2,0:T(8,128)(2,1)S(1)} fusion(f32[8,128,9,32]{1,3,2,0:T(8,128)S(1)} %gather_fusion.3, f32[8,128,8]{1,2,0:T(8,128)S(1)} %broadcast_multiply_fusion), kind=kLoop, calls=%fused_computation.6 | loop fusion | flops 4718592 | bytes 5931008 | tf_op jit(solution)/shard_map/convert_element_type | solution.py:252
  43.6 2.1 %fusion.8 = f32[8,128,128]{2,1,0:T(8,128)S(1)} fusion(bf16[8,128,9,8,32]{1,4,3,2,0:T(8,128)(2,1)S(1)} %multiply_convert_fusion, f32[8,8,32,128]{3,2,0,1:T(8,128)S(1)} %fusion.17, f32[9,8,32,128]{3,2,1,0:T(8,128)S(1)} %copy-done.3), kind=kOutput, calls=%fused_computation.21 | convolution fusion | flops 608698368 | bytes 7471104 | tf_op jit(solution)/shard_map/tclki,lktij->tcj/dot_general | solution.py:253
  45.7 1.4 %fusion.131 = f32[8,128,2304]{1,2,0:S(1)} fusion(bf16[8,128,2304]{1,2,0:T(8,128)(2,1)S(1)} %bitcast.409, bf16[8,128,128]{2,1,0:T(8,128)(2,1)S(1)} %gather_fusion), kind=kOutput, calls=%fused_computation.250 | convolution fusion | flops 603979776 | bytes 14417920
  47.1 3.8 %multiply_reduce_fusion.1 = (f32[9,8,32,128]{3,2,0,1:T(8,128)S(1)}, f32[8,8,32,128]{3,2,0,1:T(8,128)}) fusion(f32[9,8,8,32,128]{4,3,1,0,2:T(8,128)S(1)} %bitcast.408, f32[8,8,32,128]{3,2,0,1:T(8,128)S(1)} %fusion.17, f32[9,8,32,128]{3,2,1,0:T(8,128)S(1)} %copy-done.3), kind=kLoop, calls=%fused_computation.5 | loop fusion | flops 8880128 | bytes 13893632 | tf_op jit(solution)/shard_map/reduce_sum | solution.py:259
  50.9 0.8 fusion.38
  51.7 0.9 %fusion.71 = (f32[8,1,32,128]{3,2,0,1:T(8,128)}, f32[8,1,32,128]{3,2,0,1:T(8,128)}) fusion(f32[9,8,32,128]{3,2,0,1:T(8,128)S(1)} %get-tuple-element.24, f32[8,3,32,128]{3,2,0,1:T(8,128)S(1)} %get-tuple-element.48, f32[8,32,128]{2,1,0:T(8,128)S(1)} %get-tuple-element.49), kind=kLoop, calls=%fused_computation.119 | loop fusion | flops 950272 | bytes 1703936 | tf_op jit(solution)/shard_map/transpose(jvp())/div | solution.py:98
  52.6 0.3 fusion.6
  53.1 0.6 reshape.533
  53.7 1.1 %multiply_reduce_fusion.2 = f32[128,5,128]{2,0,1:T(8,128)S(1)} fusion(f32[8,128,128]{2,1,0:T(8,128)S(1)} %fusion.8, f32[8,5]{1,0:T(8,128)} %copy-done.24), kind=kLoop, calls=%fused_computation.14 | loop fusion | flops 1228800 | bytes 852128 | tf_op jit(solution)/shard_map/reduce_sum | solution.py:262
  55.1 0.8 reshape_reshape.12
  55.9 1.2 %fusion.18 = (f32[8,32,128]{2,1,0:T(8,128)S(1)}, f32[8,32,128]{2,1,0:T(8,128)S(1)}) fusion(f32[8,8,32,128]{3,2,0,1:T(8,128)S(1)} %copy-done, f32[8]{0:T(128)} %copy-done.33, f32[8,32,128]{2,1,0:T(8,128)S(1)} %copy-done.6, f32[8,32,128]{2,1,0:T(8,128)S(1)} %copy-done.8), kind=kLoop, calls=%fused_computation.34 | loop fusion | flops 2818048 | bytes 1572896 | tf_op jit(solution)/shard_map/transpose(jvp())/reduce_sum | solution.py:115
  57.2 0.3 fusion.50
  57.5 0.4 copy-done.10
  58.1 0.3 fusion.83
  59.0 0.4 collective-permute-start.3
  59.5 1.1 %collective-permute-done.3 = f32[69,640]{1,0:T(8,128)S(1)} collective-permute-done((f32[69,640]{1,0:T(8,128)S(1)}, f32[69,640]{1,0:T(8,128)S(1)}, u32[]{:S(2)}, u32[]{:S(2)}) %collective-permute-start.3) | collective-permute-done | bytes 176672 | tf_op jit(solution)/shard_map/ppermute | solution.py:19
  60.6 1.8 %collective-permute-start.4 = (f32[37,640]{1,0:T(8,128)S(1)}, f32[37,640]{1,0:T(8,128)S(1)}, u32[]{:S(2)}, u32[]{:S(2)}) collective-permute-start(f32[37,640]{1,0:T(8,128)S(1)} %pad_maximum_fusion.4), channel_id=1, source_target_pairs={{0,2},{1,3},{2,0},{3,1},{4,6},{5,7},{6,4},{7,5},{8,10},{9,11},{10,... | collective-permute-start | bytes 284168 | tf_op jit(solution)/shard_map/ppermute | solution.py:19
  62.4 3.4 %collective-permute-done.4 = f32[37,640]{1,0:T(8,128)S(1)} collective-permute-done((f32[37,640]{1,0:T(8,128)S(1)}, f32[37,640]{1,0:T(8,128)S(1)}, u32[]{:S(2)}, u32[]{:S(2)}) %collective-permute-start.4) | collective-permute-done | bytes 94752 | tf_op jit(solution)/shard_map/ppermute | solution.py:19
  66.1 0.6 collective-permute-start.5
  66.7 3.3 %collective-permute-done.5 = f32[37,128]{1,0:T(8,128)S(1)} collective-permute-done((f32[37,128]{1,0:T(8,128)S(1)}, f32[37,128]{1,0:T(8,128)S(1)}, u32[]{:S(2)}, u32[]{:S(2)}) %collective-permute-start.5) | collective-permute-done | bytes 18976 | tf_op jit(solution)/shard_map/ppermute | solution.py:19
  70.2 0.5 collective-permute-start.6
  70.7 0.8 copy.183
  71.6 1.2 %reshape.587 = bf16[4,2,9216]{2,1,0:T(2,128)(2,1)} reshape(bf16[128,1,9,2,32]{4,3,2,1,0:T(2,128)(2,1)S(1)} %bitcast.411) | data formatting | bytes 294912
  72.8 3.3 %all-to-all-start = ((bf16[4,2,9216]{2,1,0:T(2,128)(2,1)}), bf16[4,2,9216]{2,1,0:T(2,128)(2,1)S(1)}, u32[]{:S(2)}, u32[]{:S(2)}) async-start(bf16[4,2,9216]{2,1,0:T(2,128)(2,1)} %reshape.587), calls=%async_computation | async-start | bytes 294912 | tf_op jit(solution)/shard_map/all_to_all | solution.py:224
  76.4 0.4 collective-permute-start.7
  76.8 4.1 %all-to-all-done = bf16[4,2,9216]{2,1,0:T(2,128)(2,1)S(1)} async-done(((bf16[4,2,9216]{2,1,0:T(2,128)(2,1)}), bf16[4,2,9216]{2,1,0:T(2,128)(2,1)S(1)}, u32[]{:S(2)}, u32[]{:S(2)}) %all-to-all-start) | async-done | bytes 147488 | tf_op jit(solution)/shard_map/all_to_all | solution.py:224
  80.9 0.3 reshape.588
  81.2 0.8 copy.184
  82.0 1.1 %reshape.526 = bf16[32,9,256]{2,0,1:T(8,128)(2,1)} reshape(bf16[32,9,2,4,1,32]{5,3,2,0,1,4:T(4,128)(2,1)S(1)} %copy.184) | data formatting | bytes 294912 | tf_op jit(solution)/shard_map/reshape | solution.py:230
  83.1 0.3 maximum_add_fusion
  83.4 0.6 slice_negate_fusion
  84.0 0.6 slice.386
  84.7 0.7 copy.204
  (169 shorter events, 4.6 us)
Async XLA Ops:
  2.3 16.4 %collective-permute-start = (f32[35,128]{1,0:T(8,128)S(1)}, f32[35,128]{1,0:T(8,128)S(1)}, u32[]{:S(2)}, u32[]{:S(2)}) collective-permute-start(f32[35,128]{1,0:T(8,128)S(1)} %get-tuple-element.43), channel_id=1, source_target_pairs={{0,4},{4,0},{8,12},{12,8},{16,20},{20,16},{24,28},{28,24},{1,5},{5... | collective-permute-start | bytes 53768 | tf_op jit(solution)/shard_map/ppermute | solution.py:19
  5.4 13.3 %collective-permute-start.2 = (f32[35,128]{1,0:T(8,128)S(1)}, f32[35,128]{1,0:T(8,128)S(1)}, u32[]{:S(2)}, u32[]{:S(2)}) collective-permute-start(f32[35,128]{1,0:T(8,128)S(1)} %get-tuple-element.44), channel_id=1, source_target_pairs={{0,16},{4,20},{8,24},{12,28},{16,0},{20,4},{24,8},{28,12},{1,17},{... | collective-permute-start | bytes 53768 | tf_op jit(solution)/shard_map/ppermute | solution.py:19
  7.9 10.8 %collective-permute-start.1 = (f32[35,128]{1,0:T(8,128)S(1)}, f32[35,128]{1,0:T(8,128)S(1)}, u32[]{:S(2)}, u32[]{:S(2)}) collective-permute-start(f32[35,128]{1,0:T(8,128)S(1)} %get-tuple-element.45), channel_id=1, source_target_pairs={{0,8},{4,12},{8,0},{12,4},{16,24},{20,28},{24,16},{28,20},{1,9},{5... | collective-permute-start | bytes 53768 | tf_op jit(solution)/shard_map/ppermute | solution.py:19
  10.8 5.3 %copy-start.34 = (s32[8,2]{0,1:T(2,128)S(1)}, s32[8,2]{0,1:T(2,128)}, u32[]{:S(2)}) copy-start(s32[8,2]{0,1:T(2,128)} %param.11) | copy-start | bytes 196
  10.8 5.4 %copy-start.36 = (s32[8]{0:T(128)S(1)}, s32[8]{0:T(128)}, u32[]{:S(2)}) copy-start(s32[8]{0:T(128)} %param.12) | copy-start | bytes 100
  10.8 5.4 %copy-start.30 = (f32[32,8]{0,1:T(8,128)S(1)}, f32[32,8]{0,1:T(8,128)}, u32[]{:S(2)}) copy-start(f32[32,8]{0,1:T(8,128)} %param.13) | copy-start | bytes 3076
  10.8 7.9 %copy-start.21 = (bf16[32,256]{1,0:T(8,128)(2,1)S(1)}, bf16[32,256]{1,0:T(8,128)(2,1)}, u32[]{:S(2)}) copy-start(bf16[32,256]{1,0:T(8,128)(2,1)} %param.9) | copy-start | bytes 49156
  11.5 13.2 %copy-start.29 = (f32[3,256]{1,0:T(4,128)S(1)}, f32[3,256]{1,0:T(4,128)}, u32[]{:S(2)}) copy-start(f32[3,256]{1,0:T(4,128)} %param.8) | copy-start | bytes 9220
  12.8 21.8 %all-to-all-start.1 = ((bf16[4,2,9216]{2,1,0:T(2,128)(2,1)}), bf16[4,2,9216]{2,1,0:T(2,128)(2,1)S(1)}, u32[]{:S(2)}, u32[]{:S(2)}) async-start(bf16[4,2,9216]{2,1,0:T(2,128)(2,1)} %reshape.589), calls=%async_computation.1 | async-start | bytes 294912 | tf_op jit(solution)/shard_map/all_to_all | solution.py:231
  16.1 11.8 %copy-start.31 = (f32[8]{0:T(128)}, f32[8]{0:T(128)S(1)}, u32[]{:S(2)}) copy-start(f32[8]{0:T(128)S(1)} %compare_convert_fusion) | copy-start | bytes 100
  16.2 18.3 %copy-start.27 = (f32[8]{0:T(128)}, f32[8]{0:T(128)S(1)}, u32[]{:S(2)}) copy-start(f32[8]{0:T(128)S(1)} %convert_element_type.99) | copy-start | bytes 100
  16.9 7.9 %copy-start.24 = (f32[8,5]{1,0:T(8,128)}, f32[8,5]{1,0:T(8,128)S(1)}, u32[]{:S(2)}) copy-start(f32[8,5]{1,0:T(8,128)S(1)} %get-tuple-element.60) | copy-start | bytes 484
  17.0 11.0 %copy-start.33 = (f32[8]{0:T(128)}, f32[8]{0:T(128)S(1)}, u32[]{:S(2)}) copy-start(f32[8]{0:T(128)S(1)} %add_multiply_fusion) | copy-start | bytes 100
  25.4 1.9 %copy-start.17 = (f32[8,3,128]{2,0,1:T(8,128)}, f32[8,3,128]{2,0,1:T(8,128)S(1)}, u32[]{:S(2)}) copy-start(f32[8,3,128]{2,0,1:T(8,128)S(1)} %copy.177) | copy-start | bytes 36868
  26.1 1.4 %copy-start.19 = (f32[8,3,32]{2,0,1:T(8,128)}, f32[8,3,32]{2,0,1:T(8,128)S(1)}, u32[]{:S(2)}) copy-start(f32[8,3,32]{2,0,1:T(8,128)S(1)} %copy.179) | copy-start | bytes 9220
  27.9 4.2 %copy-start.2 = (f32[9,8,32,128]{3,2,1,0:T(8,128)}, f32[9,8,32,128]{3,2,1,0:T(8,128)S(1)}, u32[]{:S(2)}) copy-start(f32[9,8,32,128]{3,2,1,0:T(8,128)S(1)} %multiply_dynamic-update-slice_fusion) | copy-start | bytes 3538948
  28.0 0.8 copy-start.5
  28.0 0.8 copy-start.7
  29.1 3.0 %copy-start.14 = (bf16[3,128,128]{2,1,0:T(8,128)(2,1)S(1)}, bf16[3,128,128]{2,1,0:T(8,128)(2,1)}, u32[]{:S(2)}) copy-start(bf16[3,128,128]{2,1,0:T(8,128)(2,1)} %param.14) | copy-start | bytes 294916
  33.3 0.6 copy-start.15
  36.4 3.4 %copy-start.16 = (f32[128,2,32]{0,2,1:T(8,128)S(1)}, f32[128,2,32]{0,2,1:T(8,128)}, u32[]{:S(2)}) copy-start(f32[128,2,32]{0,2,1:T(8,128)} %copy-done.15) | copy-start | bytes 98308
  42.3 1.4 %copy-start.3 = (f32[9,8,32,128]{3,2,1,0:T(8,128)S(1)}, f32[9,8,32,128]{3,2,1,0:T(8,128)}, u32[]{:S(2)}) copy-start(f32[9,8,32,128]{3,2,1,0:T(8,128)} %copy-done.2) | copy-start | bytes 3538948
  50.9 1.7 %copy-start.1 = (f32[2,128,9,8,32,1]{1,4,5,3,2,0:T(8,128)S(1)}, f32[2,128,9,8,32,1]{1,4,5,3,2,0:T(8,128)}, u32[]{:S(2)}) copy-start(f32[2,128,9,8,32,1]{1,4,5,3,2,0:T(8,128)} %get-tuple-element.65) | copy-start | bytes 7077892
  50.9 1.7 %copy-start.9 = (f32[128,2,32,9]{0,2,1,3:T(8,128)S(1)}, f32[128,2,32,9]{0,2,1,3:T(8,128)}, u32[]{:S(2)}) copy-start(f32[128,2,32,9]{0,2,1,3:T(8,128)} %get-tuple-element.35) | copy-start | bytes 884740
  53.7 2.1 %copy-start = (f32[8,8,32,128]{3,2,0,1:T(8,128)S(1)}, f32[8,8,32,128]{3,2,0,1:T(8,128)}, u32[]{:S(2)}) copy-start(f32[8,8,32,128]{3,2,0,1:T(8,128)} %get-tuple-element.25) | copy-start | bytes 3145732
  53.7 2.1 %copy-start.6 = (f32[8,32,128]{2,1,0:T(8,128)S(1)}, f32[8,32,128]{2,1,0:T(8,128)}, u32[]{:S(2)}) copy-start(f32[8,32,128]{2,1,0:T(8,128)} %copy-done.5) | copy-start | bytes 393220
  53.7 2.1 %copy-start.8 = (f32[8,32,128]{2,1,0:T(8,128)S(1)}, f32[8,32,128]{2,1,0:T(8,128)}, u32[]{:S(2)}) copy-start(f32[8,32,128]{2,1,0:T(8,128)} %copy-done.7) | copy-start | bytes 393220
  55.9 1.2 %copy-start.28 = (f32[8]{0:T(128)S(1)}, f32[8]{0:T(128)}, u32[]{:S(2)}) copy-start(f32[8]{0:T(128)} %copy-done.27) | copy-start | bytes 100
  55.9 1.2 %copy-start.32 = (f32[8]{0:T(128)S(1)}, f32[8]{0:T(128)}, u32[]{:S(2)}) copy-start(f32[8]{0:T(128)} %copy-done.31) | copy-start | bytes 100
  57.1 0.9 %copy-start.10 = (f32[8,1,32,128]{3,2,0,1:T(8,128)S(1)}, f32[8,1,32,128]{3,2,0,1:T(8,128)}, u32[]{:S(2)}) copy-start(f32[8,1,32,128]{3,2,0,1:T(8,128)} %fusion.38) | copy-start | bytes 393220
  57.1 1.0 %copy-start.12 = (f32[8,1,32,128]{3,2,0,1:T(8,128)S(1)}, f32[8,1,32,128]{3,2,0,1:T(8,128)}, u32[]{:S(2)}) copy-start(f32[8,1,32,128]{3,2,0,1:T(8,128)} %get-tuple-element.30) | copy-start | bytes 393220
  57.1 1.0 %copy-start.13 = (f32[8,1,32,128]{3,2,0,1:T(8,128)S(1)}, f32[8,1,32,128]{3,2,0,1:T(8,128)}, u32[]{:S(2)}) copy-start(f32[8,1,32,128]{3,2,0,1:T(8,128)} %get-tuple-element.31) | copy-start | bytes 393220
  57.1 1.0 %copy-start.18 = (f32[8,3,128]{2,0,1:T(8,128)S(1)}, f32[8,3,128]{2,0,1:T(8,128)}, u32[]{:S(2)}) copy-start(f32[8,3,128]{2,0,1:T(8,128)} %copy-done.17) | copy-start | bytes 36868
  57.1 1.0 %copy-start.20 = (f32[8,3,32]{2,0,1:T(8,128)S(1)}, f32[8,3,32]{2,0,1:T(8,128)}, u32[]{:S(2)}) copy-start(f32[8,3,32]{2,0,1:T(8,128)} %copy-done.19) | copy-start | bytes 9220
  57.1 1.3 %copy-start.26 = (f32[8,5]{0,1:T(8,128)S(1)}, f32[8,5]{0,1:T(8,128)}, u32[]{:S(2)}) copy-start(f32[8,5]{0,1:T(8,128)} %copy.191) | copy-start | bytes 484
  57.1 1.5 %copy-start.25 = (f32[8,5]{0,1:T(8,128)S(1)}, f32[8,5]{0,1:T(8,128)}, u32[]{:S(2)}) copy-start(f32[8,5]{0,1:T(8,128)} %copy.200) | copy-start | bytes 484
  57.2 1.8 %copy-start.4 = (f32[2,2,32,640]{3,2,1,0:T(8,128)S(1)}, f32[2,2,32,640]{3,2,1,0:T(8,128)}, u32[]{:S(2)}) copy-start(f32[2,2,32,640]{3,2,1,0:T(8,128)} %reshape_reshape.12) | copy-start | bytes 983044
  57.5 1.5 %copy-start.23 = (f32[2,640]{1,0:T(2,128)S(1)}, f32[2,640]{1,0:T(2,128)}, u32[]{:S(2)}) copy-start(f32[2,640]{1,0:T(2,128)} %reshape.533) | copy-start | bytes 15364
  59.0 11.7 %copy-start.11 = (bf16[128,8,2,1,32]{0,4,2,1,3:T(8,128)(2,1)S(1)}, bf16[128,8,2,1,32]{0,4,2,1,3:T(8,128)(2,1)}, u32[]{:S(2)}) copy-start(bf16[128,8,2,1,32]{0,4,2,1,3:T(8,128)(2,1)} %get-tuple-element.37) | copy-start | bytes 393220
  59.0 11.7 %copy-start.22 = (bf16[128,1,2,1,32]{0,4,2,1,3:T(8,128)(2,1)S(1)}, bf16[128,1,2,1,32]{0,4,2,1,3:T(8,128)(2,1)}, u32[]{:S(2)}) copy-start(bf16[128,1,2,1,32]{0,4,2,1,3:T(8,128)(2,1)} %get-tuple-element.46) | copy-start | bytes 49156
  59.0 1.5 %collective-permute-start.3 = (f32[69,640]{1,0:T(8,128)S(1)}, f32[69,640]{1,0:T(8,128)S(1)}, u32[]{:S(2)}, u32[]{:S(2)}) collective-permute-start(f32[69,640]{1,0:T(8,128)S(1)} %pad_maximum_fusion.2), channel_id=1, source_target_pairs={{0,1},{1,0},{2,3},{3,2},{4,5},{5,4},{6,7},{7,6},{8,9},{9,8},{10,11... | collective-permute-start | bytes 529928 | tf_op jit(solution)/shard_map/ppermute | solution.py:19
  60.6 5.2 %collective-permute-start.4 = (f32[37,640]{1,0:T(8,128)S(1)}, f32[37,640]{1,0:T(8,128)S(1)}, u32[]{:S(2)}, u32[]{:S(2)}) collective-permute-start(f32[37,640]{1,0:T(8,128)S(1)} %pad_maximum_fusion.4), channel_id=1, source_target_pairs={{0,2},{1,3},{2,0},{3,1},{4,6},{5,7},{6,4},{7,5},{8,10},{9,11},{10,... | collective-permute-start | bytes 284168 | tf_op jit(solution)/shard_map/ppermute | solution.py:19
  66.1 3.8 %collective-permute-start.5 = (f32[37,128]{1,0:T(8,128)S(1)}, f32[37,128]{1,0:T(8,128)S(1)}, u32[]{:S(2)}, u32[]{:S(2)}) collective-permute-start(f32[37,128]{1,0:T(8,128)S(1)} %pad_maximum_fusion.5), channel_id=1, source_target_pairs={{0,4},{4,0},{8,12},{12,8},{16,20},{20,16},{24,28},{28,24},{1,5},{5... | collective-permute-start | bytes 56840 | tf_op jit(solution)/shard_map/ppermute | solution.py:19
  70.2 5.9 %collective-permute-start.6 = (f32[37,128]{1,0:T(8,128)S(1)}, f32[37,128]{1,0:T(8,128)S(1)}, u32[]{:S(2)}, u32[]{:S(2)}) collective-permute-start(f32[37,128]{1,0:T(8,128)S(1)} %pad_maximum_fusion.6), channel_id=1, source_target_pairs={{0,8},{4,12},{8,0},{12,4},{16,24},{20,28},{24,16},{28,20},{1,9},{5... | collective-permute-start | bytes 56840 | tf_op jit(solution)/shard_map/ppermute | solution.py:19
  72.8 8.1 %all-to-all-start = ((bf16[4,2,9216]{2,1,0:T(2,128)(2,1)}), bf16[4,2,9216]{2,1,0:T(2,128)(2,1)S(1)}, u32[]{:S(2)}, u32[]{:S(2)}) async-start(bf16[4,2,9216]{2,1,0:T(2,128)(2,1)} %reshape.587), calls=%async_computation | async-start | bytes 294912 | tf_op jit(solution)/shard_map/all_to_all | solution.py:224
  76.4 6.7 %collective-permute-start.7 = (f32[37,128]{1,0:T(8,128)S(1)}, f32[37,128]{1,0:T(8,128)S(1)}, u32[]{:S(2)}, u32[]{:S(2)}) collective-permute-start(f32[37,128]{1,0:T(8,128)S(1)} %pad_maximum_fusion.7), channel_id=1, source_target_pairs={{0,16},{4,20},{8,24},{12,28},{16,0},{20,4},{24,8},{28,12},{1,17},{... | collective-permute-start | bytes 56840 | tf_op jit(solution)/shard_map/ppermute | solution.py:19
  81.2 1.9 %copy-start.35 = (s32[3,128]{1,0:T(4,128)S(1)}, s32[3,128]{1,0:T(4,128)}, u32[]{:S(2)}) copy-start(s32[3,128]{1,0:T(4,128)} %param.10) | copy-start | bytes 4612
